TPU v7x, 32 devices: a whole 2x2x4 slice. The times are simulated.
32 devices in a mesh: row: 4 (over x, core), col: 8 (over z, y).
Axes of the slice: x: 2, y: 2, z: 4, core: 2. Of those that a mesh axis runs over, the one named last changes fastest.
Arguments:
- right_side: float32 [64, 16384], P(None, 'row'), may hold values from -8 to 8
- blocks: bfloat16 [3072, 128, 128], P(('row', 'col')), may hold values from -1 to 1
- targets: int32 [3072, 1], P(('row', 'col')), may hold values from 0 to 7; in each aligned block of 96 rows (0 to 95, 96 to 191, ...) at most 24 rows name the same one
- tile_rows: int32 [3072], P(('row', 'col')), may hold values from 0 to 31
- tile_cols: int32 [3072], P(('row', 'col')), may hold values from 0 to 31
Outputs:
- solution: float32 [64, 8, 4096], P(None, 'col', 'row')
- phibar: float32 [64], replicated
Inputs may be any that keep to these rules, and one draw needn't show every extreme that they name: `targets`: among the 96 blocks of one device, at most 24 name the same grid column, and some grid column is named exactly 24 times by some device.
All inputs are finite; a program needn't handle non-finite values.
Results may differ from a plain program's by a relative error of at most 0.0032.
Values may be sent and summed in bfloat16 or wider, within the bound.
No kernel may reach another device: no remote copies, remote signals or barrier semaphores. Data moves between devices by JAX's collectives and lax.ppermute only.
A program may use at most 128 MiB of HBM per device.

v0:
```python
import jax
import jax.numpy as jnp
from jax import lax
from jax.sharding import PartitionSpec as P

TC = 32
ITERS = 4


EPSILON = 1e-06


def gather_tiles(vector_bf, indices, block_size):
    snapshots, extent = vector_bf.shape
    vector_tiles = vector_bf.reshape(snapshots, extent // block_size, block_size)
    return jnp.take(vector_tiles, indices, axis=1)


def place_terms(weighted, indices, n_out):
    snapshots, number, block_size = weighted.shape
    onehot = (indices[:, None] == jnp.arange(n_out, dtype=jnp.int32)[None, :]).astype(jnp.float32)
    summed = jnp.einsum("ksi,st->kti", weighted, onehot, precision=lax.Precision.HIGHEST)
    return summed.reshape(snapshots, n_out * block_size)


def forward_terms(vector_bf, blocks, row_index, col_index, n_out):
    picked = gather_tiles(vector_bf, col_index, blocks.shape[1])
    weighted = jnp.einsum("sij,ksj->ksi", blocks, picked, preferred_element_type=jnp.float32)
    return place_terms(weighted, row_index, n_out)


def backward_terms(vector_bf, blocks, row_index, col_index, n_out):
    picked = gather_tiles(vector_bf, row_index, blocks.shape[1])
    weighted = jnp.einsum("sji,ksj->ksi", blocks, picked, preferred_element_type=jnp.float32)
    return place_terms(weighted, col_index, n_out)


def per_device(right_side, blocks, targets, tile_rows, tile_cols):
    col_count = lax.axis_size("col")
    row_count = lax.axis_size("row")
    block_size = blocks.shape[1]
    snapshots = right_side.shape[0]
    row_tiles = right_side.shape[1] // block_size
    own_count = blocks.shape[0]
    capacity = 2 * own_count // col_count
    target = targets[:, 0]
    matches = (target[:, None] == jnp.arange(col_count, dtype=jnp.int32)[None, :]).astype(jnp.int32)
    before = jnp.cumsum(matches, axis=0) - matches
    slot_index = target * capacity + jnp.sum(before * matches, axis=1)
    outgoing = (
        jnp.zeros((col_count * capacity, block_size, block_size), blocks.dtype)
        .at[slot_index]
        .set(blocks)
    )
    places = (
        jnp.zeros((col_count * capacity, 2), jnp.int32)
        .at[slot_index]
        .set(jnp.stack([tile_rows, tile_cols], axis=1))
    )
    arrived, arrived_places = (
        lax.all_to_all(
            outgoing.reshape(col_count, capacity, block_size, block_size),
            "col",
            split_axis=0,
            concat_axis=0,
            tiled=True,
        ),
        lax.all_to_all(
            places.reshape(col_count, capacity, 2), "col", split_axis=0, concat_axis=0, tiled=True
        ),
    )
    work_blocks = arrived.reshape(col_count * capacity, block_size, block_size)
    flat_places = arrived_places.reshape(col_count * capacity, 2)
    work_rows = flat_places[:, 0]
    work_cols = flat_places[:, 1]

    def backward(left_bf):
        return backward_terms(left_bf, work_blocks, work_rows, work_cols, TC)

    def sum_right(partial_value):
        return lax.psum(partial_value, "row")

    def finish_left(unscaled, need_form):
        squares = jnp.sum(unscaled * unscaled, axis=1)
        total = lax.psum(squares, "row")
        beta_norm = jnp.sqrt(total + EPSILON)
        scaled = unscaled / beta_norm[:, None]
        rounded = None
        if need_form:
            rounded = scaled.astype(jnp.bfloat16)
        return (beta_norm, scaled, rounded)

    def finish_right(unscaled):
        squares = jnp.sum(unscaled * unscaled, axis=1)
        total = lax.psum(squares, "col")
        alpha_norm = jnp.sqrt(total + EPSILON)
        scaled = unscaled / alpha_norm[:, None]
        rounded = scaled.astype(jnp.bfloat16)
        return (alpha_norm, scaled, rounded)

    beta_norm, left_vec, left_bf = finish_left(right_side, True)
    alpha_norm, right_vec, right_bf = finish_right(sum_right(backward(left_bf)))
    search = right_vec
    solution = jnp.zeros_like(right_vec)
    phibar = beta_norm
    rhobar = alpha_norm
    for iteration in range(ITERS):
        last_turn = iteration + 1 == ITERS
        unscaled = (
            lax.psum(forward_terms(right_bf, work_blocks, work_rows, work_cols, row_tiles), "col")
            - alpha_norm[:, None] * left_vec
        )
        beta_norm, left_vec, left_bf = finish_left(unscaled, not last_turn)
        rho_value = jnp.sqrt(rhobar * rhobar + beta_norm * beta_norm)
        cosine = rhobar / rho_value
        sine_value = beta_norm / rho_value
        phi_value = cosine * phibar
        phibar = sine_value * phibar
        solution = solution + (phi_value / rho_value)[:, None] * search
        if not last_turn:
            unscaled = sum_right(backward(left_bf)) - beta_norm[:, None] * right_vec
            alpha_norm, right_vec, right_bf = finish_right(unscaled)
            theta_value = sine_value * alpha_norm
            rhobar = -cosine * alpha_norm
            search = right_vec - (theta_value / rho_value)[:, None] * search
    share_len = solution.shape[1] // row_count
    solution = lax.dynamic_slice_in_dim(solution, lax.axis_index("row") * share_len, share_len, 1)
    return (solution.reshape(snapshots, 1, solution.shape[1]), phibar)


def solution(mesh):
    placed = (
        P(None, "row"),
        P(("row", "col"), None, None),
        P(("row", "col"), None),
        P(("row", "col")),
        P(("row", "col")),
    )
    return jax.shard_map(
        per_device,
        mesh=mesh,
        in_specs=placed,
        out_specs=(P(None, "col", "row"), P()),
        check_vma=False,
    )
```

profile of v0, /device:TPU:0, one launch (start us, length us, event | category | flops | bytes accessed | tf_op | source)
XLA Modules:
  0.0 907.1 jit_solution(17280355181446882380)
XLA Ops:
  11.9 7.3 all-to-all-start
  23.4 14.7 %scatter_fusion = bf16[192,128,128]{2,1,0:T(8,128)(2,1)} fusion(bf16[192,128,128]{2,1,0:T(8,128)(2,1)} %broadcast_in_dim.14, s32[96]{0:T(128)S(1)} %fusion.105, bf16[96,128,128]{2,1,0:T(8,128)(2,1)} %param.8), kind=kCustom, calls=%fused_computation.9 | custom fusion | bytes 9437568 | tf_op jit(solution)/shard_map/scatter | solution.py:53
  38.1 6.1 all-to-all-start.1
  53.3 128.6 %all-to-all-done.1 = bf16[8,24,128,128]{3,2,1,0:T(8,128)(2,1)} async-done(((bf16[8,24,128,128]{3,2,1,0:T(8,128)(2,1)}), bf16[8,24,128,128]{3,2,1,0:T(8,128)(2,1)}, u32[]{:S(2)}, u32[]{:S(2)}) %all-to-all-start.1) | async-done | bytes 6291488 | tf_op jit(solution)/shard_map/all_to_all | solution.py:61
  194.9 35.2 %all-reduce.9.cloned.1.call-done = f32[64,4096]{1,0:T(8,128)} async-done(((f32[64,4096]{1,0:T(8,128)}), f32[64,4096]{1,0:T(8,128)}) %all-reduce.9.cloned.1.call-update) | async-done | bytes 1048592 | tf_op jit(solution)/shard_map/psum | solution.py:81
  231.5 21.8 %psum.121 = f32[64]{0:T(128)S(1)} all-reduce(f32[64]{0:T(128)S(1)} %multiply_reduce_fusion.7), channel_id=1, replica_groups=mesh['row'=4,'col'=8] {'col'}, use_global_device_ids=true, to_apply=%region_8.10 | all-reduce | flops 64 | bytes 512 | tf_op jit(solution)/shard_map/psum | solution.py:95
  257.7 8.1 fusion.51
  273.2 75.0 %all-reduce.11.cloned.1.call-done = f32[64,4096]{1,0:T(8,128)} async-done(((f32[64,4096]{1,0:T(8,128)}), f32[64,4096]{1,0:T(8,128)}) %all-reduce.11.cloned.1.call-update) | async-done | bytes 1048592 | tf_op jit(solution)/shard_map/psum | solution.py:110
  350.8 6.1 psum.123
  374.0 35.8 %all-reduce.13.cloned.1.call-done = f32[64,4096]{1,0:T(8,128)} async-done(((f32[64,4096]{1,0:T(8,128)}), f32[64,4096]{1,0:T(8,128)}) %all-reduce.13.cloned.1.call-update) | async-done | bytes 1048592 | tf_op jit(solution)/shard_map/psum | solution.py:81
  411.3 21.6 %psum.125 = f32[64]{0:T(128)S(1)} all-reduce(f32[64]{0:T(128)S(1)} %multiply_reduce_fusion.5), channel_id=1, replica_groups=mesh['row'=4,'col'=8] {'col'}, use_global_device_ids=true, to_apply=%region_14.16 | all-reduce | flops 64 | bytes 512 | tf_op jit(solution)/shard_map/psum | solution.py:95
  437.3 8.1 fusion.57
  452.9 75.0 %all-reduce.15.cloned.1.call-done = f32[64,4096]{1,0:T(8,128)} async-done(((f32[64,4096]{1,0:T(8,128)}), f32[64,4096]{1,0:T(8,128)}) %all-reduce.15.cloned.1.call-update) | async-done | bytes 1048592 | tf_op jit(solution)/shard_map/psum | solution.py:110
  530.4 6.3 psum.127
  553.9 35.8 %all-reduce.17.cloned.1.call-done = f32[64,4096]{1,0:T(8,128)} async-done(((f32[64,4096]{1,0:T(8,128)}), f32[64,4096]{1,0:T(8,128)}) %all-reduce.17.cloned.1.call-update) | async-done | bytes 1048592 | tf_op jit(solution)/shard_map/psum | solution.py:81
  591.3 21.5 %psum.129 = f32[64]{0:T(128)S(1)} all-reduce(f32[64]{0:T(128)S(1)} %multiply_reduce_fusion.3), channel_id=1, replica_groups=mesh['row'=4,'col'=8] {'col'}, use_global_device_ids=true, to_apply=%region_20.22 | all-reduce | flops 64 | bytes 512 | tf_op jit(solution)/shard_map/psum | solution.py:95
  618.2 8.1 fusion.63
  633.8 75.0 %all-reduce.19.cloned.1.call-done = f32[64,4096]{1,0:T(8,128)} async-done(((f32[64,4096]{1,0:T(8,128)}), f32[64,4096]{1,0:T(8,128)}) %all-reduce.19.cloned.1.call-update) | async-done | bytes 1048592 | tf_op jit(solution)/shard_map/psum | solution.py:110
  711.3 6.1 psum.131
  734.6 35.8 %all-reduce.21.cloned.1.call-done = f32[64,4096]{1,0:T(8,128)} async-done(((f32[64,4096]{1,0:T(8,128)}), f32[64,4096]{1,0:T(8,128)}) %all-reduce.21.cloned.1.call-update) | async-done | bytes 1048592 | tf_op jit(solution)/shard_map/psum | solution.py:81
  772.0 21.6 %psum.133 = f32[64]{0:T(128)S(1)} all-reduce(f32[64]{0:T(128)S(1)} %multiply_reduce_fusion.1), channel_id=1, replica_groups=mesh['row'=4,'col'=8] {'col'}, use_global_device_ids=true, to_apply=%region_26.28 | all-reduce | flops 64 | bytes 512 | tf_op jit(solution)/shard_map/psum | solution.py:95
  799.0 8.1 fusion.69
  814.6 74.9 %all-reduce.23.cloned.1.call-done = f32[64,4096]{1,0:T(8,128)} async-done(((f32[64,4096]{1,0:T(8,128)}), f32[64,4096]{1,0:T(8,128)}) %all-reduce.23.cloned.1.call-update) | async-done | bytes 1048592 | tf_op jit(solution)/shard_map/psum | solution.py:110
  891.0 5.9 psum.135
  (108 shorter events, 149.9 us)
Async XLA Ops:
  11.9 26.2 %all-to-all-start = ((s32[8,24,2]{1,2,0:T(2,128)}), s32[8,24,2]{1,2,0:T(2,128)S(1)}, u32[]{:S(2)}, u32[]{:S(2)}) async-start(s32[8,24,2]{1,2,0:T(2,128)} %copy.46), calls=%async_computation | async-start | bytes 16384 | tf_op jit(solution)/shard_map/all_to_all | solution.py:68
  38.1 6.1 copy-start.1
  38.1 143.8 %all-to-all-start.1 = ((bf16[8,24,128,128]{3,2,1,0:T(8,128)(2,1)}), bf16[8,24,128,128]{3,2,1,0:T(8,128)(2,1)}, u32[]{:S(2)}, u32[]{:S(2)}) async-start(bf16[8,24,128,128]{3,2,1,0:T(8,128)(2,1)} %bitcast.172), calls=%async_computation.1 | async-start | bytes 12582912 | tf_op jit(solution)/shard_map/all_to_all | solution.py:61
  44.2 185.9 %all-reduce.9.cloned.1.call-start = ((), (), s32[]{:S(2)}) async-start(), calls=%async_computation.2 | async-start | bytes 2097152 | tf_op jit(solution)/shard_map/psum | solution.py:81
  194.8 153.4 %all-reduce.11.cloned.1.call-start = ((), (), s32[]{:S(2)}) async-start(), calls=%async_computation.3 | async-start | bytes 2097152 | tf_op jit(solution)/shard_map/psum | solution.py:110
  273.1 136.7 %all-reduce.13.cloned.1.call-start = ((), (), s32[]{:S(2)}) async-start(), calls=%async_computation.4 | async-start | bytes 2097152 | tf_op jit(solution)/shard_map/psum | solution.py:81
  373.9 153.9 %all-reduce.15.cloned.1.call-start = ((), (), s32[]{:S(2)}) async-start(), calls=%async_computation.5 | async-start | bytes 2097152 | tf_op jit(solution)/shard_map/psum | solution.py:110
  451.2 76.6 %copy-start.4 = (f32[64,4096]{1,0:T(8,128)S(1)}, f32[64,4096]{1,0:T(8,128)}, u32[]{:S(2)}) copy-start(f32[64,4096]{1,0:T(8,128)} %get-tuple-element.25) | copy-start | bytes 3145732
  452.8 136.9 %all-reduce.17.cloned.1.call-start = ((), (), s32[]{:S(2)}) async-start(), calls=%async_computation.6 | async-start | bytes 2097152 | tf_op jit(solution)/shard_map/psum | solution.py:81
  553.9 154.9 %all-reduce.19.cloned.1.call-start = ((), (), s32[]{:S(2)}) async-start(), calls=%async_computation.7 | async-start | bytes 2097152 | tf_op jit(solution)/shard_map/psum | solution.py:110
  632.1 76.6 %copy-start.3 = (f32[64,4096]{1,0:T(8,128)S(1)}, f32[64,4096]{1,0:T(8,128)}, u32[]{:S(2)}) copy-start(f32[64,4096]{1,0:T(8,128)} %get-tuple-element.21) | copy-start | bytes 3145732
  633.7 136.7 %all-reduce.21.cloned.1.call-start = ((), (), s32[]{:S(2)}) async-start(), calls=%async_computation.8 | async-start | bytes 2097152 | tf_op jit(solution)/shard_map/psum | solution.py:81
  733.0 37.5 %copy-start = (f32[64,4096]{1,0:T(8,128)S(1)}, f32[64,4096]{1,0:T(8,128)}, u32[]{:S(2)}) copy-start(f32[64,4096]{1,0:T(8,128)} %get-tuple-element.19) | copy-start | bytes 3145732
  734.6 154.9 %all-reduce.23.cloned.1.call-start = ((), (), s32[]{:S(2)}) async-start(), calls=%async_computation.9 | async-start | bytes 2097152 | tf_op jit(solution)/shard_map/psum | solution.py:110
  812.9 76.6 %copy-start.2 = (f32[64,4096]{1,0:T(8,128)S(1)}, f32[64,4096]{1,0:T(8,128)}, u32[]{:S(2)}) copy-start(f32[64,4096]{1,0:T(8,128)} %get-tuple-element.17) | copy-start | bytes 3145732
Sparse Core Ops, SparseCore 0:
  194.9 35.1 all-reduce.8
  273.3 74.8 all-reduce.10
  374.1 35.7 all-reduce.12
  453.0 74.8 all-reduce.14
  554.0 35.7 all-reduce.16
  633.8 74.8 all-reduce.18
  734.7 35.7 all-reduce.20
  814.7 74.7 all-reduce.22
where the time goes:
time: 917 us; the launch traced here: 907 us
  waiting for transfers between devices  571 us (62%)
  blocking collectives  117 us (13%)
  matrix products  101 us (11%)
  local copies, waits for them, and re-layouts  56.9 us (6%)
  other arithmetic  32.9 us (4%)
  between operations  14.9 us (2%)
  starting transfers between devices  13.7 us (1%)
    psum x4, waiting for transfers between devices, per_device(): lax.psum(forward_terms(right_bf, work_blocks, work_rows, work_cols, row_t...  300 us
    psum x4, waiting for transfers between devices, sum_right(): return lax.psum(partial_value, 'row')  143 us
    all_to_all x1, waiting for transfers between devices, per_device(): lax.all_to_all(outgoing.reshape(col_count, capacity, block_size, block_si...  129 us
    psum x4, blocking collectives, finish_right(): total = lax.psum(squares, 'col')  86.6 us
    dot_general x8, matrix products, place_terms(): jnp.einsum('ksi,st->kti', weighted, onehot, precision=lax.Precision.HIGHEST)  46.2 us
    dot_general x4, matrix products, forward_terms(): jnp.einsum('sij,ksj->ksi', blocks, picked, preferred_element_type=jnp.flo...  32.2 us
    psum x5, blocking collectives, finish_left(): total = lax.psum(squares, 'row')  30.1 us
    dot_general x4, matrix products, backward_terms(): jnp.einsum('sji,ksj->ksi', blocks, picked, preferred_element_type=jnp.flo...  22.3 us
  transfers between devices with their start and end apart: 10, of which 9 were waited for; matrix products, arithmetic and copies ran while one was open for 2% of the time, Pallas kernels for 0%

commit v1 on v0

--- a/solution.py
+++ b/solution.py
@@ -8,6 +8,54 @@
 
 
 EPSILON = 1e-06
+
+
+def partner_pairs(count, distance):
+    return [(i, i ^ distance) for i in range(count)]
+
+
+def is_power_of_two(count):
+    return count & (count - 1) == 0
+
+
+def small_sum(value, axis):
+    count = lax.axis_size(axis)
+    if not is_power_of_two(count):
+        return lax.psum(value, axis)
+    distance = 1
+    while distance < count:
+        value = value + lax.ppermute(value, axis, partner_pairs(count, distance))
+        distance *= 2
+    return value
+
+
+def big_sum(value, axis):
+    count = lax.axis_size(axis)
+    width = value.shape[-1]
+    if not is_power_of_two(count) or width % (128 * count):
+        return lax.psum(value, axis)
+    index = lax.axis_index(axis)
+    distances = []
+    distance = 1
+    while distance < count:
+        distances.append(distance)
+        distance *= 2
+    held = value
+    for distance in distances:
+        half = held.shape[-1] // 2
+        upper = (index // distance) % 2
+        keep = lax.dynamic_slice_in_dim(held, upper * half, half, held.ndim - 1)
+        give = lax.dynamic_slice_in_dim(held, (1 - upper) * half, half, held.ndim - 1)
+        held = keep + lax.ppermute(give, axis, partner_pairs(count, distance))
+    for distance in reversed(distances):
+        upper = (index // distance) % 2
+        other = lax.ppermute(held, axis, partner_pairs(count, distance))
+        held = jnp.where(
+            upper == 1,
+            jnp.concatenate([other, held], axis=-1),
+            jnp.concatenate([held, other], axis=-1),
+        )
+    return held
 
 
 def gather_tiles(vector_bf, indices, block_size):
@@ -78,11 +126,11 @@
         return backward_terms(left_bf, work_blocks, work_rows, work_cols, TC)
 
     def sum_right(partial_value):
-        return lax.psum(partial_value, "row")
+        return big_sum(partial_value, "row")
 
     def finish_left(unscaled, need_form):
         squares = jnp.sum(unscaled * unscaled, axis=1)
-        total = lax.psum(squares, "row")
+        total = small_sum(squares, "row")
         beta_norm = jnp.sqrt(total + EPSILON)
         scaled = unscaled / beta_norm[:, None]
         rounded = None
@@ -92,7 +140,7 @@
 
     def finish_right(unscaled):
         squares = jnp.sum(unscaled * unscaled, axis=1)
-        total = lax.psum(squares, "col")
+        total = small_sum(squares, "col")
         alpha_norm = jnp.sqrt(total + EPSILON)
         scaled = unscaled / alpha_norm[:, None]
         rounded = scaled.astype(jnp.bfloat16)
@@ -107,7 +155,7 @@
     for iteration in range(ITERS):
         last_turn = iteration + 1 == ITERS
         unscaled = (
-            lax.psum(forward_terms(right_bf, work_blocks, work_rows, work_cols, row_tiles), "col")
+            big_sum(forward_terms(right_bf, work_blocks, work_rows, work_cols, row_tiles), "col")
             - alpha_norm[:, None] * left_vec
         )
         beta_norm, left_vec, left_bf = finish_left(unscaled, not last_turn)

time: 917 us -> 662 us (0.72)
  waiting for transfers between devices: 571 us -> 430 us
  blocking collectives: 117 us -> 0 us
  starting transfers between devices: 13.7 us -> 59.6 us
  other arithmetic: 32.9 us -> 16.6 us
  between operations: 14.9 us -> 1.96 us
  local copies, waits for them, and re-layouts: 56.9 us -> 47.7 us
    psum x8 -> x0, waiting for transfers between devices: 443 us -> none  [the longest x4 300 us: per_device(): lax.psum(forward_terms(right_bf, work_blocks, work_rows, work_cols, row_t...]
    ppermute x0 -> x62, waiting for transfers between devices: none -> 301 us  [the longest x20 132 us: big_sum(): held = keep + lax.ppermute(give, axis, partner_pairs(count, distance))]
    psum x9 -> x0, blocking collectives: 117 us -> none  [the longest x4 86.6 us: finish_right(): total = lax.psum(squares, 'col')]
    ppermute x0 -> x62, starting transfers between devices: none -> 45.6 us  [the longest x20 16.8 us: big_sum(): held = keep + lax.ppermute(give, axis, partner_pairs(count, distance))]
  transfers between devices with their start and end apart: 10 -> 64, of which waited for: 9 -> 63; matrix products, arithmetic and copies ran while one was open for 2% -> 3% of each run, Pallas kernels for 0% -> 0%
where the time goes in v1:
time: 662 us; the launch traced here: 659 us
  waiting for transfers between devices  430 us (65%)
  matrix products  103 us (16%)
  starting transfers between devices  59.6 us (9%)
  local copies, waits for them, and re-layouts  47.7 us (7%)
  other arithmetic  16.6 us (3%)
    ppermute x20, waiting for transfers between devices, big_sum(): held = keep + lax.ppermute(give, axis, partner_pairs(count, distance))  132 us
    all_to_all x1, waiting for transfers between devices, per_device(): lax.all_to_all(outgoing.reshape(col_count, capacity, block_size, block_si...  129 us
    ppermute x20, waiting for transfers between devices, big_sum(): other = lax.ppermute(held, axis, partner_pairs(count, distance))  116 us
    ppermute x22, waiting for transfers between devices, small_sum(): value = value + lax.ppermute(value, axis, partner_pairs(count, distance))  53.3 us
    dot_general x8, matrix products, place_terms(): jnp.einsum('ksi,st->kti', weighted, onehot, precision=lax.Precision.HIGHEST)  47.9 us
    dot_general x4, matrix products, forward_terms(): jnp.einsum('sij,ksj->ksi', blocks, picked, preferred_element_type=jnp.flo...  32.4 us
    dot_general x4, matrix products, backward_terms(): jnp.einsum('sji,ksj->ksi', blocks, picked, preferred_element_type=jnp.flo...  22.2 us
    gather x8, local copies, waits for them, and re-layouts, gather_tiles(): return jnp.take(vector_tiles, indices, axis=1)  22.2 us
  transfers between devices with their start and end apart: 64, of which 63 were waited for; matrix products, arithmetic and copies ran while one was open for 3% of the time, Pallas kernels for 0%

profile of v1, /device:TPU:0, one launch (start us, length us, event | category | flops | bytes accessed | tf_op | source)
XLA Modules:
  0.0 658.7 jit_solution(10406613652673878419)
XLA Ops:
  5.4 7.3 %all-to-all-start = ((s32[8,24,2]{1,2,0:T(2,128)}), s32[8,24,2]{1,2,0:T(2,128)S(1)}, u32[]{:S(2)}, u32[]{:S(2)}) async-start(s32[8,24,2]{1,2,0:T(2,128)} %copy.86), calls=%async_computation | async-start | bytes 16384 | tf_op jit(solution)/shard_map/all_to_all | solution.py:116
  16.9 12.8 %scatter_fusion = bf16[192,128,128]{2,1,0:T(8,128)(2,1)} fusion(bf16[192,128,128]{2,1,0:T(8,128)(2,1)} %broadcast_in_dim.14, s32[96]{0:T(128)S(1)} %fusion.124, bf16[96,128,128]{2,1,0:T(8,128)(2,1)S(1)} %copy-done.17), kind=kCustom, calls=%fused_computation.9 | custom fusion | bytes 9437568 | tf_op jit(solution)/shard_map/scatter | solution.py:101
  44.4 129.2 %all-to-all-done.1 = bf16[8,24,128,128]{3,2,1,0:T(8,128)(2,1)} async-done(((bf16[8,24,128,128]{3,2,1,0:T(8,128)(2,1)}), bf16[8,24,128,128]{3,2,1,0:T(8,128)(2,1)}, u32[]{:S(2)}, u32[]{:S(2)}) %all-to-all-start.1) | async-done | bytes 6291488 | tf_op jit(solution)/shard_map/all_to_all | solution.py:109
  220.5 8.2 %fusion.51 = f32[64,192,128]{2,0,1:T(8,128)S(1)} fusion(bf16[192,128,128]{2,1,0:T(8,128)(2,1)} %bitcast.11, bf16[192,64,128]{2,1,0:T(8,128)(2,1)} %gather_fusion.1, pred[192]{0:T(512)(128)(4,1)S(1)} %get-tuple-element.39), kind=kOutput, calls=%fused_computation.59 | convolution fusion | flops 404226048 | bytes 15728832 | tf_op jit(solution)/shard_map/sij,ksj->ksi/dot_general | solution.py:76
  236.8 9.1 %collective-permute-done.9 = f32[64,2048]{1,0:T(8,128)S(1)} collective-permute-done((f32[64,2048]{1,0:T(8,128)S(1)}, f32[64,2048]{1,0:T(8,128)S(1)}, u32[]{:S(2)}, u32[]{:S(2)}) %collective-permute-start.9) | collective-permute-done | bytes 524320 | tf_op jit(solution)/shard_map/ppermute | solution.py:49
  246.3 7.5 %collective-permute-done.10 = f32[64,1024]{1,0:T(8,128)S(1)} collective-permute-done((f32[64,1024]{1,0:T(8,128)S(1)}, f32[64,1024]{1,0:T(8,128)S(1)}, u32[]{:S(2)}, u32[]{:S(2)}) %collective-permute-start.10) | collective-permute-done | bytes 262176 | tf_op jit(solution)/shard_map/ppermute | solution.py:49
  255.0 7.4 %collective-permute-done.11 = f32[64,512]{1,0:T(8,128)S(1)} collective-permute-done((f32[64,512]{1,0:T(8,128)S(1)}, f32[64,512]{1,0:T(8,128)S(1)}, u32[]{:S(2)}, u32[]{:S(2)}) %collective-permute-start.11) | collective-permute-done | bytes 131104 | tf_op jit(solution)/shard_map/ppermute | solution.py:49
  277.1 8.0 %collective-permute-done.14 = f32[64,2048]{1,0:T(8,128)S(1)} collective-permute-done((f32[64,2048]{1,0:T(8,128)S(1)}, f32[64,2048]{1,0:T(8,128)S(1)}, u32[]{:S(2)}, u32[]{:S(2)}) %collective-permute-start.14) | collective-permute-done | bytes 524320 | tf_op jit(solution)/shard_map/ppermute | solution.py:52
  342.0 8.1 %fusion.57 = f32[64,192,128]{2,0,1:T(8,128)S(1)} fusion(bf16[192,128,128]{2,1,0:T(8,128)(2,1)} %bitcast.11, bf16[192,64,128]{2,1,0:T(8,128)(2,1)} %gather_fusion.3, pred[192]{0:T(512)(128)(4,1)S(1)} %get-tuple-element.39), kind=kOutput, calls=%fused_computation.61 | convolution fusion | flops 404226048 | bytes 15728832 | tf_op jit(solution)/shard_map/sij,ksj->ksi/dot_general | solution.py:76
  358.1 9.4 %collective-permute-done.24 = f32[64,2048]{1,0:T(8,128)S(1)} collective-permute-done((f32[64,2048]{1,0:T(8,128)S(1)}, f32[64,2048]{1,0:T(8,128)S(1)}, u32[]{:S(2)}, u32[]{:S(2)}) %collective-permute-start.24) | collective-permute-done | bytes 524320 | tf_op jit(solution)/shard_map/ppermute | solution.py:49
  368.0 7.5 %collective-permute-done.25 = f32[64,1024]{1,0:T(8,128)S(1)} collective-permute-done((f32[64,1024]{1,0:T(8,128)S(1)}, f32[64,1024]{1,0:T(8,128)S(1)}, u32[]{:S(2)}, u32[]{:S(2)}) %collective-permute-start.25) | collective-permute-done | bytes 262176 | tf_op jit(solution)/shard_map/ppermute | solution.py:49
  376.4 7.4 %collective-permute-done.26 = f32[64,512]{1,0:T(8,128)S(1)} collective-permute-done((f32[64,512]{1,0:T(8,128)S(1)}, f32[64,512]{1,0:T(8,128)S(1)}, u32[]{:S(2)}, u32[]{:S(2)}) %collective-permute-start.26) | collective-permute-done | bytes 131104 | tf_op jit(solution)/shard_map/ppermute | solution.py:49
  398.6 8.0 %collective-permute-done.29 = f32[64,2048]{1,0:T(8,128)S(1)} collective-permute-done((f32[64,2048]{1,0:T(8,128)S(1)}, f32[64,2048]{1,0:T(8,128)S(1)}, u32[]{:S(2)}, u32[]{:S(2)}) %collective-permute-start.29) | collective-permute-done | bytes 524320 | tf_op jit(solution)/shard_map/ppermute | solution.py:52
  464.3 8.1 %fusion.63 = f32[64,192,128]{2,0,1:T(8,128)S(1)} fusion(bf16[192,128,128]{2,1,0:T(8,128)(2,1)} %bitcast.11, bf16[192,64,128]{2,1,0:T(8,128)(2,1)} %gather_fusion.5, pred[192]{0:T(512)(128)(4,1)S(1)} %get-tuple-element.39), kind=kOutput, calls=%fused_computation.63 | convolution fusion | flops 404226048 | bytes 15728832 | tf_op jit(solution)/shard_map/sij,ksj->ksi/dot_general | solution.py:76
  480.3 9.4 %collective-permute-done.39 = f32[64,2048]{1,0:T(8,128)S(1)} collective-permute-done((f32[64,2048]{1,0:T(8,128)S(1)}, f32[64,2048]{1,0:T(8,128)S(1)}, u32[]{:S(2)}, u32[]{:S(2)}) %collective-permute-start.39) | collective-permute-done | bytes 524320 | tf_op jit(solution)/shard_map/ppermute | solution.py:49
  490.1 7.5 %collective-permute-done.40 = f32[64,1024]{1,0:T(8,128)S(1)} collective-permute-done((f32[64,1024]{1,0:T(8,128)S(1)}, f32[64,1024]{1,0:T(8,128)S(1)}, u32[]{:S(2)}, u32[]{:S(2)}) %collective-permute-start.40) | collective-permute-done | bytes 262176 | tf_op jit(solution)/shard_map/ppermute | solution.py:49
  498.6 7.4 %collective-permute-done.41 = f32[64,512]{1,0:T(8,128)S(1)} collective-permute-done((f32[64,512]{1,0:T(8,128)S(1)}, f32[64,512]{1,0:T(8,128)S(1)}, u32[]{:S(2)}, u32[]{:S(2)}) %collective-permute-start.41) | collective-permute-done | bytes 131104 | tf_op jit(solution)/shard_map/ppermute | solution.py:49
  506.1 6.9 %collective-permute-done.42 = f32[64,512]{1,0:T(8,128)S(1)} collective-permute-done((f32[64,512]{1,0:T(8,128)S(1)}, f32[64,512]{1,0:T(8,128)S(1)}, u32[]{:S(2)}, u32[]{:S(2)}) %collective-permute-start.42) | collective-permute-done | bytes 131104 | tf_op jit(solution)/shard_map/ppermute | solution.py:52
  520.7 8.0 %collective-permute-done.44 = f32[64,2048]{1,0:T(8,128)S(1)} collective-permute-done((f32[64,2048]{1,0:T(8,128)S(1)}, f32[64,2048]{1,0:T(8,128)S(1)}, u32[]{:S(2)}, u32[]{:S(2)}) %collective-permute-start.44) | collective-permute-done | bytes 524320 | tf_op jit(solution)/shard_map/ppermute | solution.py:52
  586.0 8.1 %fusion.69 = f32[64,192,128]{2,0,1:T(8,128)S(1)} fusion(bf16[192,128,128]{2,1,0:T(8,128)(2,1)} %bitcast.11, bf16[192,64,128]{2,1,0:T(8,128)(2,1)} %gather_fusion.7, pred[192]{0:T(512)(128)(4,1)S(1)} %get-tuple-element.39), kind=kOutput, calls=%fused_computation.65 | convolution fusion | flops 404226048 | bytes 15728832 | tf_op jit(solution)/shard_map/sij,ksj->ksi/dot_general | solution.py:76
  601.9 9.4 %collective-permute-done.54 = f32[64,2048]{1,0:T(8,128)S(1)} collective-permute-done((f32[64,2048]{1,0:T(8,128)S(1)}, f32[64,2048]{1,0:T(8,128)S(1)}, u32[]{:S(2)}, u32[]{:S(2)}) %collective-permute-start.54) | collective-permute-done | bytes 524320 | tf_op jit(solution)/shard_map/ppermute | solution.py:49
  611.7 7.5 %collective-permute-done.55 = f32[64,1024]{1,0:T(8,128)S(1)} collective-permute-done((f32[64,1024]{1,0:T(8,128)S(1)}, f32[64,1024]{1,0:T(8,128)S(1)}, u32[]{:S(2)}, u32[]{:S(2)}) %collective-permute-start.55) | collective-permute-done | bytes 262176 | tf_op jit(solution)/shard_map/ppermute | solution.py:49
  620.2 7.4 %collective-permute-done.56 = f32[64,512]{1,0:T(8,128)S(1)} collective-permute-done((f32[64,512]{1,0:T(8,128)S(1)}, f32[64,512]{1,0:T(8,128)S(1)}, u32[]{:S(2)}, u32[]{:S(2)}) %collective-permute-start.56) | collective-permute-done | bytes 131104 | tf_op jit(solution)/shard_map/ppermute | solution.py:49
  642.3 8.0 %collective-permute-done.59 = f32[64,2048]{1,0:T(8,128)S(1)} collective-permute-done((f32[64,2048]{1,0:T(8,128)S(1)}, f32[64,2048]{1,0:T(8,128)S(1)}, u32[]{:S(2)}, u32[]{:S(2)}) %collective-permute-start.59) | collective-permute-done | bytes 524320 | tf_op jit(solution)/shard_map/ppermute | solution.py:52
  (302 shorter events, 339.4 us)
Async XLA Ops:
  5.4 24.3 %all-to-all-start = ((s32[8,24,2]{1,2,0:T(2,128)}), s32[8,24,2]{1,2,0:T(2,128)S(1)}, u32[]{:S(2)}, u32[]{:S(2)}) async-start(s32[8,24,2]{1,2,0:T(2,128)} %copy.86), calls=%async_computation | async-start | bytes 16384 | tf_op jit(solution)/shard_map/all_to_all | solution.py:116
  29.7 143.8 %all-to-all-start.1 = ((bf16[8,24,128,128]{3,2,1,0:T(8,128)(2,1)}), bf16[8,24,128,128]{3,2,1,0:T(8,128)(2,1)}, u32[]{:S(2)}, u32[]{:S(2)}) async-start(bf16[8,24,128,128]{3,2,1,0:T(8,128)(2,1)} %bitcast.214), calls=%async_computation.1 | async-start | bytes 12582912 | tf_op jit(solution)/shard_map/all_to_all | solution.py:109
  187.6 8.4 %collective-permute-start.3 = (f32[64,1024]{1,0:T(8,128)S(1)}, f32[64,1024]{1,0:T(8,128)S(1)}, u32[]{:S(2)}, u32[]{:S(2)}) collective-permute-start(f32[64,1024]{1,0:T(8,128)S(1)} %constant_dynamic-slice_fusion.18), channel_id=1, source_target_pairs={{0,16},{8,24},{16,0},{24,8},{1,17},{9,25},{17,1},{25,9},{2,18},{10... | collective-permute-start | bytes 786440 | tf_op jit(solution)/shard_map/ppermute | solution.py:49
  196.1 7.6 %collective-permute-start.4 = (f32[64,1024]{1,0:T(8,128)S(1)}, f32[64,1024]{1,0:T(8,128)S(1)}, u32[]{:S(2)}, u32[]{:S(2)}) collective-permute-start(f32[64,1024]{1,0:T(8,128)S(1)} %dynamic-slice_add_fusion.15), channel_id=1, source_target_pairs={{0,16},{8,24},{16,0},{24,8},{1,17},{9,25},{17,1},{25,9},{2,18},{10... | collective-permute-start | bytes 786440 | tf_op jit(solution)/shard_map/ppermute | solution.py:52
  235.3 10.6 %collective-permute-start.9 = (f32[64,2048]{1,0:T(8,128)S(1)}, f32[64,2048]{1,0:T(8,128)S(1)}, u32[]{:S(2)}, u32[]{:S(2)}) collective-permute-start(f32[64,2048]{1,0:T(8,128)S(1)} %constant_dynamic-slice_fusion.17), channel_id=1, source_target_pairs={{0,1},{1,0},{2,3},{3,2},{4,5},{5,4},{6,7},{7,6},{8,9},{9,8},{10,11... | collective-permute-start | bytes 1572872 | tf_op jit(solution)/shard_map/ppermute | solution.py:49
  245.9 7.8 %collective-permute-start.10 = (f32[64,1024]{1,0:T(8,128)S(1)}, f32[64,1024]{1,0:T(8,128)S(1)}, u32[]{:S(2)}, u32[]{:S(2)}) collective-permute-start(f32[64,1024]{1,0:T(8,128)S(1)} %constant_dynamic-slice_fusion.16), channel_id=1, source_target_pairs={{0,2},{1,3},{2,0},{3,1},{4,6},{5,7},{6,4},{7,5},{8,10},{9,11},{10,... | collective-permute-start | bytes 786440 | tf_op jit(solution)/shard_map/ppermute | solution.py:49
  253.9 8.5 %collective-permute-start.11 = (f32[64,512]{1,0:T(8,128)S(1)}, f32[64,512]{1,0:T(8,128)S(1)}, u32[]{:S(2)}, u32[]{:S(2)}) collective-permute-start(f32[64,512]{1,0:T(8,128)S(1)} %constant_dynamic-slice_fusion.15), channel_id=1, source_target_pairs={{0,4},{1,5},{2,6},{3,7},{4,0},{5,1},{6,2},{7,3},{8,12},{9,13},{10,... | collective-permute-start | bytes 393224 | tf_op jit(solution)/shard_map/ppermute | solution.py:49
  275.9 9.2 %collective-permute-start.14 = (f32[64,2048]{1,0:T(8,128)S(1)}, f32[64,2048]{1,0:T(8,128)S(1)}, u32[]{:S(2)}, u32[]{:S(2)}) collective-permute-start(f32[64,2048]{1,0:T(8,128)S(1)} %maximum_select_fusion.14), channel_id=1, source_target_pairs={{0,1},{1,0},{2,3},{3,2},{4,5},{5,4},{6,7},{7,6},{8,9},{9,8},{10,11... | collective-permute-start | bytes 1572872 | tf_op jit(solution)/shard_map/ppermute | solution.py:52
  307.6 8.4 %collective-permute-start.18 = (f32[64,1024]{1,0:T(8,128)S(1)}, f32[64,1024]{1,0:T(8,128)S(1)}, u32[]{:S(2)}, u32[]{:S(2)}) collective-permute-start(f32[64,1024]{1,0:T(8,128)S(1)} %constant_dynamic-slice_fusion.13), channel_id=1, source_target_pairs={{0,16},{8,24},{16,0},{24,8},{1,17},{9,25},{17,1},{25,9},{2,18},{10... | collective-permute-start | bytes 786440 | tf_op jit(solution)/shard_map/ppermute | solution.py:49
  356.9 10.6 %collective-permute-start.24 = (f32[64,2048]{1,0:T(8,128)S(1)}, f32[64,2048]{1,0:T(8,128)S(1)}, u32[]{:S(2)}, u32[]{:S(2)}) collective-permute-start(f32[64,2048]{1,0:T(8,128)S(1)} %constant_dynamic-slice_fusion.12), channel_id=1, source_target_pairs={{0,1},{1,0},{2,3},{3,2},{4,5},{5,4},{6,7},{7,6},{8,9},{9,8},{10,11... | collective-permute-start | bytes 1572872 | tf_op jit(solution)/shard_map/ppermute | solution.py:49
  367.6 7.8 %collective-permute-start.25 = (f32[64,1024]{1,0:T(8,128)S(1)}, f32[64,1024]{1,0:T(8,128)S(1)}, u32[]{:S(2)}, u32[]{:S(2)}) collective-permute-start(f32[64,1024]{1,0:T(8,128)S(1)} %constant_dynamic-slice_fusion.11), channel_id=1, source_target_pairs={{0,2},{1,3},{2,0},{3,1},{4,6},{5,7},{6,4},{7,5},{8,10},{9,11},{10,... | collective-permute-start | bytes 786440 | tf_op jit(solution)/shard_map/ppermute | solution.py:49
  375.5 8.3 %collective-permute-start.26 = (f32[64,512]{1,0:T(8,128)S(1)}, f32[64,512]{1,0:T(8,128)S(1)}, u32[]{:S(2)}, u32[]{:S(2)}) collective-permute-start(f32[64,512]{1,0:T(8,128)S(1)} %constant_dynamic-slice_fusion.10), channel_id=1, source_target_pairs={{0,4},{1,5},{2,6},{3,7},{4,0},{5,1},{6,2},{7,3},{8,12},{9,13},{10,... | collective-permute-start | bytes 393224 | tf_op jit(solution)/shard_map/ppermute | solution.py:49
  397.4 9.2 %collective-permute-start.29 = (f32[64,2048]{1,0:T(8,128)S(1)}, f32[64,2048]{1,0:T(8,128)S(1)}, u32[]{:S(2)}, u32[]{:S(2)}) collective-permute-start(f32[64,2048]{1,0:T(8,128)S(1)} %maximum_select_fusion.17), channel_id=1, source_target_pairs={{0,1},{1,0},{2,3},{3,2},{4,5},{5,4},{6,7},{7,6},{8,9},{9,8},{10,11... | collective-permute-start | bytes 1572872 | tf_op jit(solution)/shard_map/ppermute | solution.py:52
  428.9 8.4 %collective-permute-start.33 = (f32[64,1024]{1,0:T(8,128)S(1)}, f32[64,1024]{1,0:T(8,128)S(1)}, u32[]{:S(2)}, u32[]{:S(2)}) collective-permute-start(f32[64,1024]{1,0:T(8,128)S(1)} %constant_dynamic-slice_fusion.8), channel_id=1, source_target_pairs={{0,16},{8,24},{16,0},{24,8},{1,17},{9,25},{17,1},{25,9},{2,18},{10... | collective-permute-start | bytes 786440 | tf_op jit(solution)/shard_map/ppermute | solution.py:49
  479.1 10.6 %collective-permute-start.39 = (f32[64,2048]{1,0:T(8,128)S(1)}, f32[64,2048]{1,0:T(8,128)S(1)}, u32[]{:S(2)}, u32[]{:S(2)}) collective-permute-start(f32[64,2048]{1,0:T(8,128)S(1)} %constant_dynamic-slice_fusion.7), channel_id=1, source_target_pairs={{0,1},{1,0},{2,3},{3,2},{4,5},{5,4},{6,7},{7,6},{8,9},{9,8},{10,11... | collective-permute-start | bytes 1572872 | tf_op jit(solution)/shard_map/ppermute | solution.py:49
  489.8 7.8 %collective-permute-start.40 = (f32[64,1024]{1,0:T(8,128)S(1)}, f32[64,1024]{1,0:T(8,128)S(1)}, u32[]{:S(2)}, u32[]{:S(2)}) collective-permute-start(f32[64,1024]{1,0:T(8,128)S(1)} %constant_dynamic-slice_fusion.6), channel_id=1, source_target_pairs={{0,2},{1,3},{2,0},{3,1},{4,6},{5,7},{6,4},{7,5},{8,10},{9,11},{10,... | collective-permute-start | bytes 786440 | tf_op jit(solution)/shard_map/ppermute | solution.py:49
  497.7 8.3 %collective-permute-start.41 = (f32[64,512]{1,0:T(8,128)S(1)}, f32[64,512]{1,0:T(8,128)S(1)}, u32[]{:S(2)}, u32[]{:S(2)}) collective-permute-start(f32[64,512]{1,0:T(8,128)S(1)} %constant_dynamic-slice_fusion.5), channel_id=1, source_target_pairs={{0,4},{1,5},{2,6},{3,7},{4,0},{5,1},{6,2},{7,3},{8,12},{9,13},{10,... | collective-permute-start | bytes 393224 | tf_op jit(solution)/shard_map/ppermute | solution.py:49
  519.5 9.2 %collective-permute-start.44 = (f32[64,2048]{1,0:T(8,128)S(1)}, f32[64,2048]{1,0:T(8,128)S(1)}, u32[]{:S(2)}, u32[]{:S(2)}) collective-permute-start(f32[64,2048]{1,0:T(8,128)S(1)} %maximum_select_fusion.20), channel_id=1, source_target_pairs={{0,1},{1,0},{2,3},{3,2},{4,5},{5,4},{6,7},{7,6},{8,9},{9,8},{10,11... | collective-permute-start | bytes 1572872 | tf_op jit(solution)/shard_map/ppermute | solution.py:52
  551.4 8.4 %collective-permute-start.48 = (f32[64,1024]{1,0:T(8,128)S(1)}, f32[64,1024]{1,0:T(8,128)S(1)}, u32[]{:S(2)}, u32[]{:S(2)}) collective-permute-start(f32[64,1024]{1,0:T(8,128)S(1)} %constant_dynamic-slice_fusion.3), channel_id=1, source_target_pairs={{0,16},{8,24},{16,0},{24,8},{1,17},{9,25},{17,1},{25,9},{2,18},{10... | collective-permute-start | bytes 786440 | tf_op jit(solution)/shard_map/ppermute | solution.py:49
  559.8 7.6 %collective-permute-start.49 = (f32[64,1024]{1,0:T(8,128)S(1)}, f32[64,1024]{1,0:T(8,128)S(1)}, u32[]{:S(2)}, u32[]{:S(2)}) collective-permute-start(f32[64,1024]{1,0:T(8,128)S(1)} %dynamic-slice_add_fusion.9), channel_id=1, source_target_pairs={{0,16},{8,24},{16,0},{24,8},{1,17},{9,25},{17,1},{25,9},{2,18},{10... | collective-permute-start | bytes 786440 | tf_op jit(solution)/shard_map/ppermute | solution.py:52
  600.7 10.6 %collective-permute-start.54 = (f32[64,2048]{1,0:T(8,128)S(1)}, f32[64,2048]{1,0:T(8,128)S(1)}, u32[]{:S(2)}, u32[]{:S(2)}) collective-permute-start(f32[64,2048]{1,0:T(8,128)S(1)} %constant_dynamic-slice_fusion.2), channel_id=1, source_target_pairs={{0,1},{1,0},{2,3},{3,2},{4,5},{5,4},{6,7},{7,6},{8,9},{9,8},{10,11... | collective-permute-start | bytes 1572872 | tf_op jit(solution)/shard_map/ppermute | solution.py:49
  611.4 7.8 %collective-permute-start.55 = (f32[64,1024]{1,0:T(8,128)S(1)}, f32[64,1024]{1,0:T(8,128)S(1)}, u32[]{:S(2)}, u32[]{:S(2)}) collective-permute-start(f32[64,1024]{1,0:T(8,128)S(1)} %constant_dynamic-slice_fusion.1), channel_id=1, source_target_pairs={{0,2},{1,3},{2,0},{3,1},{4,6},{5,7},{6,4},{7,5},{8,10},{9,11},{10,... | collective-permute-start | bytes 786440 | tf_op jit(solution)/shard_map/ppermute | solution.py:49
  619.3 8.3 %collective-permute-start.56 = (f32[64,512]{1,0:T(8,128)S(1)}, f32[64,512]{1,0:T(8,128)S(1)}, u32[]{:S(2)}, u32[]{:S(2)}) collective-permute-start(f32[64,512]{1,0:T(8,128)S(1)} %constant_dynamic-slice_fusion), channel_id=1, source_target_pairs={{0,4},{1,5},{2,6},{3,7},{4,0},{5,1},{6,2},{7,3},{8,12},{9,13},{10,... | collective-permute-start | bytes 393224 | tf_op jit(solution)/shard_map/ppermute | solution.py:49
  641.1 9.2 %collective-permute-start.59 = (f32[64,2048]{1,0:T(8,128)S(1)}, f32[64,2048]{1,0:T(8,128)S(1)}, u32[]{:S(2)}, u32[]{:S(2)}) collective-permute-start(f32[64,2048]{1,0:T(8,128)S(1)} %maximum_select_fusion.23), channel_id=1, source_target_pairs={{0,1},{1,0},{2,3},{3,2},{4,5},{5,4},{6,7},{7,6},{8,9},{9,8},{10,11... | collective-permute-start | bytes 1572872 | tf_op jit(solution)/shard_map/ppermute | solution.py:52
  (58 other events, 447.9 us)

commit v2 on v1

--- a/solution.py
+++ b/solution.py
@@ -5,6 +5,7 @@
 
 TC = 32
 ITERS = 4
+CHUNKS = 2
 
 
 EPSILON = 1e-06
@@ -146,31 +147,56 @@
         rounded = scaled.astype(jnp.bfloat16)
         return (alpha_norm, scaled, rounded)
 
-    beta_norm, left_vec, left_bf = finish_left(right_side, True)
-    alpha_norm, right_vec, right_bf = finish_right(sum_right(backward(left_bf)))
-    search = right_vec
-    solution = jnp.zeros_like(right_vec)
-    phibar = beta_norm
-    rhobar = alpha_norm
-    for iteration in range(ITERS):
-        last_turn = iteration + 1 == ITERS
-        unscaled = (
-            big_sum(forward_terms(right_bf, work_blocks, work_rows, work_cols, row_tiles), "col")
-            - alpha_norm[:, None] * left_vec
-        )
-        beta_norm, left_vec, left_bf = finish_left(unscaled, not last_turn)
-        rho_value = jnp.sqrt(rhobar * rhobar + beta_norm * beta_norm)
-        cosine = rhobar / rho_value
-        sine_value = beta_norm / rho_value
-        phi_value = cosine * phibar
-        phibar = sine_value * phibar
-        solution = solution + (phi_value / rho_value)[:, None] * search
-        if not last_turn:
-            unscaled = sum_right(backward(left_bf)) - beta_norm[:, None] * right_vec
-            alpha_norm, right_vec, right_bf = finish_right(unscaled)
-            theta_value = sine_value * alpha_norm
-            rhobar = -cosine * alpha_norm
-            search = right_vec - (theta_value / rho_value)[:, None] * search
+    def run_chunk(side, results):
+        beta_norm, left_vec, left_bf = finish_left(side, True)
+        yield
+        alpha_norm, right_vec, right_bf = finish_right(sum_right(backward(left_bf)))
+        yield
+        search = right_vec
+        solution = jnp.zeros_like(right_vec)
+        phibar = beta_norm
+        rhobar = alpha_norm
+        for iteration in range(ITERS):
+            last_turn = iteration + 1 == ITERS
+            unscaled = (
+                big_sum(forward_terms(right_bf, work_blocks, work_rows, work_cols, row_tiles), "col")
+                - alpha_norm[:, None] * left_vec
+            )
+            beta_norm, left_vec, left_bf = finish_left(unscaled, not last_turn)
+            rho_value = jnp.sqrt(rhobar * rhobar + beta_norm * beta_norm)
+            cosine = rhobar / rho_value
+            sine_value = beta_norm / rho_value
+            phi_value = cosine * phibar
+            phibar = sine_value * phibar
+            solution = solution + (phi_value / rho_value)[:, None] * search
+            yield
+            if not last_turn:
+                unscaled = sum_right(backward(left_bf)) - beta_norm[:, None] * right_vec
+                alpha_norm, right_vec, right_bf = finish_right(unscaled)
+                theta_value = sine_value * alpha_norm
+                rhobar = -cosine * alpha_norm
+                search = right_vec - (theta_value / rho_value)[:, None] * search
+                yield
+        results.append((solution, phibar))
+
+    chunk_len = snapshots // CHUNKS
+    results = [[] for _ in range(CHUNKS)]
+    runs = [
+        run_chunk(right_side[k * chunk_len:(k + 1) * chunk_len], results[k])
+        for k in range(CHUNKS)
+    ]
+    active = list(runs)
+    while active:
+        still = []
+        for run in active:
+            try:
+                next(run)
+                still.append(run)
+            except StopIteration:
+                pass
+        active = still
+    solution = jnp.concatenate([r[0][0] for r in results], axis=0)
+    phibar = jnp.concatenate([r[0][1] for r in results], axis=0)
     share_len = solution.shape[1] // row_count
     solution = lax.dynamic_slice_in_dim(solution, lax.axis_index("row") * share_len, share_len, 1)
     return (solution.reshape(snapshots, 1, solution.shape[1]), phibar)

time: 662 us -> 624 us (0.943)
  waiting for transfers between devices: 430 us -> 308 us
  starting transfers between devices: 59.6 us -> 97.7 us
  matrix products: 103 us -> 125 us
  other arithmetic: 16.6 us -> 32.1 us
    ppermute x20 -> x40, waiting for transfers between devices: 132 us -> 77.4 us  [big_sum(): held = keep + lax.ppermute(give, axis, partner_pairs(count, distance))]
    ppermute x20 -> x40, waiting for transfers between devices: 116 us -> 69.8 us  [big_sum(): other = lax.ppermute(held, axis, partner_pairs(count, distance))]
    ppermute x22 -> x44, waiting for transfers between devices: 53.3 us -> 32.9 us  [small_sum(): value = value + lax.ppermute(value, axis, partner_pairs(count, distance))]
    ppermute x22 -> x44, starting transfers between devices: 16 us -> 33.3 us  [small_sum(): value = value + lax.ppermute(value, axis, partner_pairs(count, distance))]
    dot_general x4 -> x8, matrix products: 32.4 us -> 45.1 us  [forward_terms(): jnp.einsum('sij,ksj->ksi', blocks, picked, preferred_element_type=jnp.flo...]
    ppermute x20 -> x40, starting transfers between devices: 12.7 us -> 25.4 us  [big_sum(): other = lax.ppermute(held, axis, partner_pairs(count, distance))]
    dot_general x4 -> x8, matrix products: 22.2 us -> 33.4 us  [backward_terms(): jnp.einsum('sji,ksj->ksi', blocks, picked, preferred_element_type=jnp.flo...]
    ppermute x20 -> x40, starting transfers between devices: 16.8 us -> 25.6 us  [big_sum(): held = keep + lax.ppermute(give, axis, partner_pairs(count, distance))]
  transfers between devices with their start and end apart: 64 -> 126, of which waited for: 63 -> 92; matrix products, arithmetic and copies ran while one was open for 3% -> 31% of each run, Pallas kernels for 0% -> 0%
where the time goes in v2:
time: 624 us; the launch traced here: 616 us
  waiting for transfers between devices  308 us (49%)
  matrix products  125 us (20%)
  starting transfers between devices  97.7 us (16%)
  local copies, waits for them, and re-layouts  49.1 us (8%)
  other arithmetic  32.1 us (5%)
    all_to_all x1, waiting for transfers between devices, per_device(): lax.all_to_all(outgoing.reshape(col_count, capacity, block_size, block_si...  128 us
    ppermute x40, waiting for transfers between devices, big_sum(): held = keep + lax.ppermute(give, axis, partner_pairs(count, distance))  77.4 us
    ppermute x40, waiting for transfers between devices, big_sum(): other = lax.ppermute(held, axis, partner_pairs(count, distance))  69.8 us
    dot_general x16, matrix products, place_terms(): jnp.einsum('ksi,st->kti', weighted, onehot, precision=lax.Precision.HIGHEST)  46.9 us
    dot_general x8, matrix products, forward_terms(): jnp.einsum('sij,ksj->ksi', blocks, picked, preferred_element_type=jnp.flo...  45.1 us
    dot_general x8, matrix products, backward_terms(): jnp.einsum('sji,ksj->ksi', blocks, picked, preferred_element_type=jnp.flo...  33.4 us
    ppermute x44, starting transfers between devices, small_sum(): value = value + lax.ppermute(value, axis, partner_pairs(count, distance))  33.3 us
    ppermute x44, waiting for transfers between devices, small_sum(): value = value + lax.ppermute(value, axis, partner_pairs(count, distance))  32.9 us
  transfers between devices with their start and end apart: 126, of which 92 were waited for; matrix products, arithmetic and copies ran while one was open for 31% of the time, Pallas kernels for 0%

profile of v2, /device:TPU:0, one launch (start us, length us, event | category | flops | bytes accessed | tf_op | source)
XLA Modules:
  0.0 615.9 jit_solution(8778748405546108604)
XLA Ops:
  5.4 7.3 %all-to-all-start = ((s32[8,24,2]{1,2,0:T(2,128)}), s32[8,24,2]{1,2,0:T(2,128)S(1)}, u32[]{:S(2)}, u32[]{:S(2)}) async-start(s32[8,24,2]{1,2,0:T(2,128)} %copy.158), calls=%async_computation | async-start | bytes 16384 | tf_op jit(solution)/shard_map/all_to_all | solution.py:117
  12.6 4.3 broadcast_in_dim.14
  17.0 12.8 %scatter_fusion = bf16[192,128,128]{2,1,0:T(8,128)(2,1)} fusion(bf16[192,128,128]{2,1,0:T(8,128)(2,1)} %broadcast_in_dim.14, s32[96]{0:T(128)S(1)} %fusion.170, bf16[96,128,128]{2,1,0:T(8,128)(2,1)S(1)} %copy-done.23), kind=kCustom, calls=%fused_computation.17 | custom fusion | bytes 9437568 | tf_op jit(solution)/shard_map/scatter | solution.py:102
  29.7 6.1 all-to-all-start.1
  45.6 127.9 %all-to-all-done.1 = bf16[8,24,128,128]{3,2,1,0:T(8,128)(2,1)} async-done(((bf16[8,24,128,128]{3,2,1,0:T(8,128)(2,1)}), bf16[8,24,128,128]{3,2,1,0:T(8,128)(2,1)}, u32[]{:S(2)}, u32[]{:S(2)}) %all-to-all-start.1) | async-done | bytes 6291488 | tf_op jit(solution)/shard_map/all_to_all | solution.py:110
  173.5 5.1 convolution_bitcast_fusion.7
  182.0 4.1 convolution_bitcast_fusion.15
  217.4 5.5 convolution_bitcast_fusion.6
  229.4 5.7 convolution_bitcast_fusion.14
  240.3 4.5 collective-permute-done.9
  289.1 4.3 convolution_bitcast_fusion.5
  300.6 4.2 collective-permute-done.18
  327.4 5.7 convolution_bitcast_fusion.12
  339.4 5.5 convolution_bitcast_fusion.4
  388.9 4.1 convolution_bitcast_fusion.11
  398.3 3.9 convolution_bitcast_fusion.3
  409.2 4.2 collective-permute-done.33
  436.8 5.9 convolution_bitcast_fusion.10
  450.5 5.7 convolution_bitcast_fusion.2
  461.5 4.4 collective-permute-done.101
  510.2 4.1 convolution_bitcast_fusion.1
  521.4 4.2 collective-permute-done.48
  547.4 5.5 convolution_bitcast_fusion.8
  558.3 5.7 convolution_bitcast_fusion
  (651 shorter events, 361.7 us)
Async XLA Ops:
  5.4 24.4 %all-to-all-start = ((s32[8,24,2]{1,2,0:T(2,128)}), s32[8,24,2]{1,2,0:T(2,128)S(1)}, u32[]{:S(2)}, u32[]{:S(2)}) async-start(s32[8,24,2]{1,2,0:T(2,128)} %copy.158), calls=%async_computation | async-start | bytes 16384 | tf_op jit(solution)/shard_map/all_to_all | solution.py:117
  29.7 143.8 %all-to-all-start.1 = ((bf16[8,24,128,128]{3,2,1,0:T(8,128)(2,1)}), bf16[8,24,128,128]{3,2,1,0:T(8,128)(2,1)}, u32[]{:S(2)}, u32[]{:S(2)}) async-start(bf16[8,24,128,128]{3,2,1,0:T(8,128)(2,1)} %bitcast.370), calls=%async_computation.1 | async-start | bytes 12582912 | tf_op jit(solution)/shard_map/all_to_all | solution.py:110
  181.9 8.0 %collective-permute-start.64 = (f32[32,2048]{1,0:T(8,128)S(1)}, f32[32,2048]{1,0:T(8,128)S(1)}, u32[]{:S(2)}, u32[]{:S(2)}) collective-permute-start(f32[32,2048]{1,0:T(8,128)S(1)} %constant_dynamic-slice_fusion.19), channel_id=1, source_target_pairs={{0,8},{8,0},{16,24},{24,16},{1,9},{9,1},{17,25},{25,17},{2,10},{10... | collective-permute-start | bytes 786440 | tf_op jit(solution)/shard_map/ppermute | solution.py:50
  191.6 7.6 %collective-permute-start.3 = (f32[32,1024]{1,0:T(8,128)S(1)}, f32[32,1024]{1,0:T(8,128)S(1)}, u32[]{:S(2)}, u32[]{:S(2)}) collective-permute-start(f32[32,1024]{1,0:T(8,128)S(1)} %constant_dynamic-slice_fusion.38), channel_id=1, source_target_pairs={{0,16},{8,24},{16,0},{24,8},{1,17},{9,25},{17,1},{25,9},{2,18},{10... | collective-permute-start | bytes 393224 | tf_op jit(solution)/shard_map/ppermute | solution.py:50
  213.5 14.8 %collective-permute-start.8 = (f32[32]{0:T(128)S(1)}, f32[32]{0:T(128)S(1)}, u32[]{:S(2)}, u32[]{:S(2)}) collective-permute-start(f32[32]{0:T(128)S(1)} %add.576), channel_id=1, source_target_pairs={{0,4},{1,5},{2,6},{3,7},{4,0},{5,1},{6,2},{7,3},{8,12},{9,13},{10,... | collective-permute-start | bytes 392 | tf_op jit(solution)/shard_map/ppermute | solution.py:28
  226.9 12.2 %collective-permute-start.71 = (f32[32,2048]{1,0:T(8,128)}, f32[32,2048]{1,0:T(8,128)}, u32[]{:S(2)}, u32[]{:S(2)}) collective-permute-start(f32[32,2048]{1,0:T(8,128)} %constant_dynamic-slice_fusion.17), channel_id=1, source_target_pairs={{0,1},{1,0},{2,3},{3,2},{4,5},{5,4},{6,7},{7,6},{8,9},{9,8},{10,11... | collective-permute-start | bytes 786440 | tf_op jit(solution)/shard_map/ppermute | solution.py:50
  277.1 11.0 %collective-permute-start.78 = (f32[32]{0:T(128)S(1)}, f32[32]{0:T(128)S(1)}, u32[]{:S(2)}, u32[]{:S(2)}) collective-permute-start(f32[32]{0:T(128)S(1)} %add.649), channel_id=1, source_target_pairs={{0,16},{8,24},{16,0},{24,8},{1,17},{9,25},{17,1},{25,9},{2,18},{10... | collective-permute-start | bytes 392 | tf_op jit(solution)/shard_map/ppermute | solution.py:28
  288.1 9.3 %collective-permute-start.17 = (f32[32,2048]{1,0:T(8,128)}, f32[32,2048]{1,0:T(8,128)}, u32[]{:S(2)}, u32[]{:S(2)}) collective-permute-start(f32[32,2048]{1,0:T(8,128)} %constant_dynamic-slice_fusion.34), channel_id=1, source_target_pairs={{0,8},{8,0},{16,24},{24,16},{1,9},{9,1},{17,25},{25,17},{2,10},{10... | collective-permute-start | bytes 786440 | tf_op jit(solution)/shard_map/ppermute | solution.py:50
  300.0 7.6 %collective-permute-start.80 = (f32[32,1024]{1,0:T(8,128)S(1)}, f32[32,1024]{1,0:T(8,128)S(1)}, u32[]{:S(2)}, u32[]{:S(2)}) collective-permute-start(f32[32,1024]{1,0:T(8,128)S(1)} %constant_dynamic-slice_fusion.13), channel_id=1, source_target_pairs={{0,16},{8,24},{16,0},{24,8},{1,17},{9,25},{17,1},{25,9},{2,18},{10... | collective-permute-start | bytes 393224 | tf_op jit(solution)/shard_map/ppermute | solution.py:50
  321.7 15.7 %collective-permute-start.85 = (f32[32]{0:T(128)S(1)}, f32[32]{0:T(128)S(1)}, u32[]{:S(2)}, u32[]{:S(2)}) collective-permute-start(f32[32]{0:T(128)S(1)} %add.656), channel_id=1, source_target_pairs={{0,4},{1,5},{2,6},{3,7},{4,0},{5,1},{6,2},{7,3},{8,12},{9,13},{10,... | collective-permute-start | bytes 392 | tf_op jit(solution)/shard_map/ppermute | solution.py:28
  337.1 12.9 %collective-permute-start.24 = (f32[32,2048]{1,0:T(8,128)}, f32[32,2048]{1,0:T(8,128)}, u32[]{:S(2)}, u32[]{:S(2)}) collective-permute-start(f32[32,2048]{1,0:T(8,128)} %constant_dynamic-slice_fusion.32), channel_id=1, source_target_pairs={{0,1},{1,0},{2,3},{3,2},{4,5},{5,4},{6,7},{7,6},{8,9},{9,8},{10,11... | collective-permute-start | bytes 786440 | tf_op jit(solution)/shard_map/ppermute | solution.py:50
  385.8 11.3 %collective-permute-start.93 = (f32[32]{0:T(128)S(1)}, f32[32]{0:T(128)S(1)}, u32[]{:S(2)}, u32[]{:S(2)}) collective-permute-start(f32[32]{0:T(128)S(1)} %add.662), channel_id=1, source_target_pairs={{0,16},{8,24},{16,0},{24,8},{1,17},{9,25},{17,1},{25,9},{2,18},{10... | collective-permute-start | bytes 392 | tf_op jit(solution)/shard_map/ppermute | solution.py:28
  397.1 8.9 %collective-permute-start.32 = (f32[32,2048]{1,0:T(8,128)}, f32[32,2048]{1,0:T(8,128)}, u32[]{:S(2)}, u32[]{:S(2)}) collective-permute-start(f32[32,2048]{1,0:T(8,128)} %constant_dynamic-slice_fusion.29), channel_id=1, source_target_pairs={{0,8},{8,0},{16,24},{24,16},{1,9},{9,1},{17,25},{25,17},{2,10},{10... | collective-permute-start | bytes 786440 | tf_op jit(solution)/shard_map/ppermute | solution.py:50
  408.6 7.6 %collective-permute-start.95 = (f32[32,1024]{1,0:T(8,128)S(1)}, f32[32,1024]{1,0:T(8,128)S(1)}, u32[]{:S(2)}, u32[]{:S(2)}) collective-permute-start(f32[32,1024]{1,0:T(8,128)S(1)} %constant_dynamic-slice_fusion.8), channel_id=1, source_target_pairs={{0,16},{8,24},{16,0},{24,8},{1,17},{9,25},{17,1},{25,9},{2,18},{10... | collective-permute-start | bytes 393224 | tf_op jit(solution)/shard_map/ppermute | solution.py:50
  432.6 16.0 %collective-permute-start.100 = (f32[32]{0:T(128)S(1)}, f32[32]{0:T(128)S(1)}, u32[]{:S(2)}, u32[]{:S(2)}) collective-permute-start(f32[32]{0:T(128)S(1)} %add.670), channel_id=1, source_target_pairs={{0,4},{1,5},{2,6},{3,7},{4,0},{5,1},{6,2},{7,3},{8,12},{9,13},{10,... | collective-permute-start | bytes 392 | tf_op jit(solution)/shard_map/ppermute | solution.py:28
  446.8 13.0 %collective-permute-start.39 = (f32[32,2048]{1,0:T(8,128)}, f32[32,2048]{1,0:T(8,128)}, u32[]{:S(2)}, u32[]{:S(2)}) collective-permute-start(f32[32,2048]{1,0:T(8,128)} %constant_dynamic-slice_fusion.27), channel_id=1, source_target_pairs={{0,1},{1,0},{2,3},{3,2},{4,5},{5,4},{6,7},{7,6},{8,9},{9,8},{10,11... | collective-permute-start | bytes 786440 | tf_op jit(solution)/shard_map/ppermute | solution.py:50
  487.6 7.7 %collective-permute-start.106 = (f32[32,2048]{1,0:T(8,128)S(1)}, f32[32,2048]{1,0:T(8,128)S(1)}, u32[]{:S(2)}, u32[]{:S(2)}) collective-permute-start(f32[32,2048]{1,0:T(8,128)S(1)} %maximum_select_fusion.44), channel_id=1, source_target_pairs={{0,1},{1,0},{2,3},{3,2},{4,5},{5,4},{6,7},{7,6},{8,9},{9,8},{10,11... | collective-permute-start | bytes 786440 | tf_op jit(solution)/shard_map/ppermute | solution.py:53
  498.0 11.1 %collective-permute-start.108 = (f32[32]{0:T(128)S(1)}, f32[32]{0:T(128)S(1)}, u32[]{:S(2)}, u32[]{:S(2)}) collective-permute-start(f32[32]{0:T(128)S(1)} %add.676), channel_id=1, source_target_pairs={{0,16},{8,24},{16,0},{24,8},{1,17},{9,25},{17,1},{25,9},{2,18},{10... | collective-permute-start | bytes 392 | tf_op jit(solution)/shard_map/ppermute | solution.py:28
  509.1 9.1 %collective-permute-start.47 = (f32[32,2048]{1,0:T(8,128)}, f32[32,2048]{1,0:T(8,128)}, u32[]{:S(2)}, u32[]{:S(2)}) collective-permute-start(f32[32,2048]{1,0:T(8,128)} %constant_dynamic-slice_fusion.24), channel_id=1, source_target_pairs={{0,8},{8,0},{16,24},{24,16},{1,9},{9,1},{17,25},{25,17},{2,10},{10... | collective-permute-start | bytes 786440 | tf_op jit(solution)/shard_map/ppermute | solution.py:50
  520.8 7.6 %collective-permute-start.110 = (f32[32,1024]{1,0:T(8,128)S(1)}, f32[32,1024]{1,0:T(8,128)S(1)}, u32[]{:S(2)}, u32[]{:S(2)}) collective-permute-start(f32[32,1024]{1,0:T(8,128)S(1)} %constant_dynamic-slice_fusion.3), channel_id=1, source_target_pairs={{0,16},{8,24},{16,0},{24,8},{1,17},{9,25},{17,1},{25,9},{2,18},{10... | collective-permute-start | bytes 393224 | tf_op jit(solution)/shard_map/ppermute | solution.py:50
  542.5 14.7 %collective-permute-start.115 = (f32[32]{0:T(128)S(1)}, f32[32]{0:T(128)S(1)}, u32[]{:S(2)}, u32[]{:S(2)}) collective-permute-start(f32[32]{0:T(128)S(1)} %add.684), channel_id=1, source_target_pairs={{0,4},{1,5},{2,6},{3,7},{4,0},{5,1},{6,2},{7,3},{8,12},{9,13},{10,... | collective-permute-start | bytes 392 | tf_op jit(solution)/shard_map/ppermute | solution.py:28
  556.9 12.3 %collective-permute-start.54 = (f32[32,2048]{1,0:T(8,128)}, f32[32,2048]{1,0:T(8,128)}, u32[]{:S(2)}, u32[]{:S(2)}) collective-permute-start(f32[32,2048]{1,0:T(8,128)} %constant_dynamic-slice_fusion.22), channel_id=1, source_target_pairs={{0,1},{1,0},{2,3},{3,2},{4,5},{5,4},{6,7},{7,6},{8,9},{9,8},{10,11... | collective-permute-start | bytes 786440 | tf_op jit(solution)/shard_map/ppermute | solution.py:50
  594.0 7.7 %collective-permute-start.59 = (f32[32,2048]{1,0:T(8,128)}, f32[32,2048]{1,0:T(8,128)}, u32[]{:S(2)}, u32[]{:S(2)}) collective-permute-start(f32[32,2048]{1,0:T(8,128)} %maximum_select_fusion.35), channel_id=1, source_target_pairs={{0,1},{1,0},{2,3},{3,2},{4,5},{5,4},{6,7},{7,6},{8,9},{9,8},{10,11... | collective-permute-start | bytes 786440 | tf_op jit(solution)/shard_map/ppermute | solution.py:53
  597.3 7.2 %collective-permute-start.121 = (f32[32,2048]{1,0:T(8,128)}, f32[32,2048]{1,0:T(8,128)}, u32[]{:S(2)}, u32[]{:S(2)}) collective-permute-start(f32[32,2048]{1,0:T(8,128)} %maximum_select_fusion.47), channel_id=1, source_target_pairs={{0,1},{1,0},{2,3},{3,2},{4,5},{5,4},{6,7},{7,6},{8,9},{9,8},{10,11... | collective-permute-start | bytes 786440 | tf_op jit(solution)/shard_map/ppermute | solution.py:53
  (162 other events, 1195.6 us)

commit v3 on v2

--- a/solution.py
+++ b/solution.py
@@ -126,6 +126,12 @@
     def backward(left_bf):
         return backward_terms(left_bf, work_blocks, work_rows, work_cols, TC)
 
+    def forward(right_bf):
+        return forward_terms(right_bf, work_blocks, work_rows, work_cols, row_tiles)
+
+    def sum_left(partial_value):
+        return big_sum(partial_value, "col")
+
     def sum_right(partial_value):
         return big_sum(partial_value, "row")
 
@@ -147,10 +153,19 @@
         rounded = scaled.astype(jnp.bfloat16)
         return (alpha_norm, scaled, rounded)
 
-    def run_chunk(side, results):
+    latest = [None] * CHUNKS
+
+    def staggered(product, summed, vector, chunk):
+        if chunk > 0 and latest[chunk - 1] is not None:
+            vector, unused = lax.optimization_barrier((vector, latest[chunk - 1]))
+        result = summed(product(vector))
+        latest[chunk] = result
+        return result
+
+    def run_chunk(chunk, side, results):
         beta_norm, left_vec, left_bf = finish_left(side, True)
         yield
-        alpha_norm, right_vec, right_bf = finish_right(sum_right(backward(left_bf)))
+        alpha_norm, right_vec, right_bf = finish_right(staggered(backward, sum_right, left_bf, chunk))
         yield
         search = right_vec
         solution = jnp.zeros_like(right_vec)
@@ -159,7 +174,7 @@
         for iteration in range(ITERS):
             last_turn = iteration + 1 == ITERS
             unscaled = (
-                big_sum(forward_terms(right_bf, work_blocks, work_rows, work_cols, row_tiles), "col")
+                staggered(forward, sum_left, right_bf, chunk)
                 - alpha_norm[:, None] * left_vec
             )
             beta_norm, left_vec, left_bf = finish_left(unscaled, not last_turn)
@@ -171,7 +186,7 @@
             solution = solution + (phi_value / rho_value)[:, None] * search
             yield
             if not last_turn:
-                unscaled = sum_right(backward(left_bf)) - beta_norm[:, None] * right_vec
+                unscaled = staggered(backward, sum_right, left_bf, chunk) - beta_norm[:, None] * right_vec
                 alpha_norm, right_vec, right_bf = finish_right(unscaled)
                 theta_value = sine_value * alpha_norm
                 rhobar = -cosine * alpha_norm
@@ -182,7 +197,7 @@
     chunk_len = snapshots // CHUNKS
     results = [[] for _ in range(CHUNKS)]
     runs = [
-        run_chunk(right_side[k * chunk_len:(k + 1) * chunk_len], results[k])
+        run_chunk(k, right_side[k * chunk_len:(k + 1) * chunk_len], results[k])
         for k in range(CHUNKS)
     ]
     active = list(runs)

time: 624 us -> 695 us (1.11)
  waiting for transfers between devices: 308 us -> 344 us
  starting transfers between devices: 97.7 us -> 127 us
    ppermute x44, waiting for transfers between devices: 32.9 us -> 61.3 us  [small_sum(): value = value + lax.ppermute(value, axis, partner_pairs(count, distance))]
    ppermute x40, starting transfers between devices: 25.6 us -> 39.6 us  [big_sum(): held = keep + lax.ppermute(give, axis, partner_pairs(count, distance))]
    ppermute x44, starting transfers between devices: 33.3 us -> 41.4 us  [small_sum(): value = value + lax.ppermute(value, axis, partner_pairs(count, distance))]
    ppermute x40, starting transfers between devices: 25.4 us -> 32.8 us  [big_sum(): other = lax.ppermute(held, axis, partner_pairs(count, distance))]
  transfers between devices with their start and end apart: 126 -> 126, of which waited for: 92 -> 91; matrix products, arithmetic and copies ran while one was open for 31% -> 24% of each run, Pallas kernels for 0% -> 0%
where the time goes in v3:
time: 695 us; the launch traced here: 686 us
  waiting for transfers between devices  344 us (49%)
  starting transfers between devices  127 us (18%)
  matrix products  125 us (18%)
  local copies, waits for them, and re-layouts  49.6 us (7%)
  other arithmetic  37.8 us (5%)
    all_to_all x1, waiting for transfers between devices, per_device(): lax.all_to_all(outgoing.reshape(col_count, capacity, block_size, block_si...  130 us
    ppermute x40, waiting for transfers between devices, big_sum(): held = keep + lax.ppermute(give, axis, partner_pairs(count, distance))  81.1 us
    ppermute x40, waiting for transfers between devices, big_sum(): other = lax.ppermute(held, axis, partner_pairs(count, distance))  70.8 us
    ppermute x44, waiting for transfers between devices, small_sum(): value = value + lax.ppermute(value, axis, partner_pairs(count, distance))  61.3 us
    dot_general x16, matrix products, place_terms(): jnp.einsum('ksi,st->kti', weighted, onehot, precision=lax.Precision.HIGHEST)  46.9 us
    dot_general x8, matrix products, forward_terms(): jnp.einsum('sij,ksj->ksi', blocks, picked, preferred_element_type=jnp.flo...  45.4 us
    ppermute x44, starting transfers between devices, small_sum(): value = value + lax.ppermute(value, axis, partner_pairs(count, distance))  41.4 us
    ppermute x40, starting transfers between devices, big_sum(): held = keep + lax.ppermute(give, axis, partner_pairs(count, distance))  39.6 us
  transfers between devices with their start and end apart: 126, of which 91 were waited for; matrix products, arithmetic and copies ran while one was open for 24% of the time, Pallas kernels for 0%

profile of v3, /device:TPU:0, one launch (start us, length us, event | category | flops | bytes accessed | tf_op | source)
XLA Modules:
  0.0 686.4 jit_solution(15507020394328668810)
XLA Ops:
  5.4 7.3 %all-to-all-start = ((s32[8,24,2]{1,2,0:T(2,128)}), s32[8,24,2]{1,2,0:T(2,128)S(1)}, u32[]{:S(2)}, u32[]{:S(2)}) async-start(s32[8,24,2]{1,2,0:T(2,128)} %copy.118), calls=%async_computation | async-start | bytes 16384 | tf_op jit(solution)/shard_map/all_to_all | solution.py:117
  16.9 12.6 %scatter_fusion = bf16[192,128,128]{2,1,0:T(8,128)(2,1)} fusion(bf16[192,128,128]{2,1,0:T(8,128)(2,1)} %broadcast_in_dim.14, s32[96]{0:T(128)S(1)} %fusion.157, bf16[96,128,128]{2,1,0:T(8,128)(2,1)S(1)} %copy-done.20), kind=kCustom, calls=%fused_computation.17 | custom fusion | bytes 9437568 | tf_op jit(solution)/shard_map/scatter | solution.py:102
  29.6 6.2 all-to-all-start.1
  42.9 130.5 %all-to-all-done.1 = bf16[8,24,128,128]{3,2,1,0:T(8,128)(2,1)} async-done(((bf16[8,24,128,128]{3,2,1,0:T(8,128)(2,1)}), bf16[8,24,128,128]{3,2,1,0:T(8,128)(2,1)}, u32[]{:S(2)}, u32[]{:S(2)}) %all-to-all-start.1) | async-done | bytes 6291488 | tf_op jit(solution)/shard_map/all_to_all | solution.py:110
  207.4 6.0 convolution_bitcast_fusion.14
  218.2 4.9 collective-permute-done.9
  223.3 5.6 collective-permute-done.10
  229.2 5.0 collective-permute-done.11
  234.5 5.0 collective-permute-done.12
  239.6 4.9 collective-permute-done.13
  301.0 5.5 convolution_bitcast_fusion.6
  319.5 5.7 convolution_bitcast_fusion.12
  355.4 4.7 collective-permute-done.27
  381.4 4.3 convolution_bitcast_fusion.11
  418.0 5.7 convolution_bitcast_fusion.4
  436.6 5.5 convolution_bitcast_fusion.10
  472.2 4.5 collective-permute-done.42
  533.8 5.9 convolution_bitcast_fusion.2
  557.8 4.7 collective-permute-done.103
  567.8 5.5 convolution_bitcast_fusion.8
  629.9 5.7 convolution_bitcast_fusion
  639.9 5.5 collective-permute-done.116
  646.8 4.4 collective-permute-done.117
  670.5 5.5 collective-permute-done.121
  (679 shorter events, 421.9 us)
Async XLA Ops:
  5.4 24.2 %all-to-all-start = ((s32[8,24,2]{1,2,0:T(2,128)}), s32[8,24,2]{1,2,0:T(2,128)S(1)}, u32[]{:S(2)}, u32[]{:S(2)}) async-start(s32[8,24,2]{1,2,0:T(2,128)} %copy.118), calls=%async_computation | async-start | bytes 16384 | tf_op jit(solution)/shard_map/all_to_all | solution.py:117
  29.6 143.8 %all-to-all-start.1 = ((bf16[8,24,128,128]{3,2,1,0:T(8,128)(2,1)}), bf16[8,24,128,128]{3,2,1,0:T(8,128)(2,1)}, u32[]{:S(2)}, u32[]{:S(2)}) async-start(bf16[8,24,128,128]{3,2,1,0:T(8,128)(2,1)} %bitcast.332), calls=%async_computation.1 | async-start | bytes 12582912 | tf_op jit(solution)/shard_map/all_to_all | solution.py:110
  252.1 8.4 %collective-permute-start.15 = (f32[32]{0:T(128)S(1)}, f32[32]{0:T(128)S(1)}, u32[]{:S(2)}, u32[]{:S(2)}) collective-permute-start(f32[32]{0:T(128)S(1)} %get-tuple-element.71), channel_id=1, source_target_pairs={{0,8},{8,0},{16,24},{24,16},{1,9},{9,1},{17,25},{25,17},{2,10},{10... | collective-permute-start | bytes 392 | tf_op jit(solution)/shard_map/ppermute | solution.py:28
  262.8 9.8 %collective-permute-start.64 = (f32[32,2048]{1,0:T(8,128)}, f32[32,2048]{1,0:T(8,128)}, u32[]{:S(2)}, u32[]{:S(2)}) collective-permute-start(f32[32,2048]{1,0:T(8,128)} %constant_dynamic-slice_fusion.19), channel_id=1, source_target_pairs={{0,8},{8,0},{16,24},{24,16},{1,9},{9,1},{17,25},{25,17},{2,10},{10... | collective-permute-start | bytes 786440 | tf_op jit(solution)/shard_map/ppermute | solution.py:50
  275.3 7.5 %collective-permute-start.18 = (f32[32,1024]{1,0:T(8,128)S(1)}, f32[32,1024]{1,0:T(8,128)S(1)}, u32[]{:S(2)}, u32[]{:S(2)}) collective-permute-start(f32[32,1024]{1,0:T(8,128)S(1)} %constant_dynamic-slice_fusion.33), channel_id=1, source_target_pairs={{0,16},{8,24},{16,0},{24,8},{1,17},{9,25},{17,1},{25,9},{2,18},{10... | collective-permute-start | bytes 393224 | tf_op jit(solution)/shard_map/ppermute | solution.py:50
  288.0 8.0 %collective-permute-start.20 = (f32[32,2048]{1,0:T(8,128)S(1)}, f32[32,2048]{1,0:T(8,128)S(1)}, u32[]{:S(2)}, u32[]{:S(2)}) collective-permute-start(f32[32,2048]{1,0:T(8,128)S(1)} %maximum_select_fusion.23), channel_id=1, source_target_pairs={{0,8},{8,0},{16,24},{24,16},{1,9},{9,1},{17,25},{25,17},{2,10},{10... | collective-permute-start | bytes 786440 | tf_op jit(solution)/shard_map/ppermute | solution.py:53
  297.1 12.3 %collective-permute-start.21 = (f32[32]{0:T(128)S(1)}, f32[32]{0:T(128)S(1)}, u32[]{:S(2)}, u32[]{:S(2)}) collective-permute-start(f32[32]{0:T(128)S(1)} %get-tuple-element.68), channel_id=1, source_target_pairs={{0,1},{1,0},{2,3},{3,2},{4,5},{5,4},{6,7},{7,6},{8,9},{9,8},{10,11... | collective-permute-start | bytes 392 | tf_op jit(solution)/shard_map/ppermute | solution.py:28
  315.4 13.1 %collective-permute-start.71 = (f32[32,2048]{1,0:T(8,128)}, f32[32,2048]{1,0:T(8,128)}, u32[]{:S(2)}, u32[]{:S(2)}) collective-permute-start(f32[32,2048]{1,0:T(8,128)} %constant_dynamic-slice_fusion.17), channel_id=1, source_target_pairs={{0,1},{1,0},{2,3},{3,2},{4,5},{5,4},{6,7},{7,6},{8,9},{9,8},{10,11... | collective-permute-start | bytes 786440 | tf_op jit(solution)/shard_map/ppermute | solution.py:50
  348.1 6.8 collective-permute-start.26
  352.7 7.5 %collective-permute-start.76 = (f32[32,2048]{1,0:T(8,128)S(1)}, f32[32,2048]{1,0:T(8,128)S(1)}, u32[]{:S(2)}, u32[]{:S(2)}) collective-permute-start(f32[32,2048]{1,0:T(8,128)S(1)} %maximum_select_fusion.33), channel_id=1, source_target_pairs={{0,1},{1,0},{2,3},{3,2},{4,5},{5,4},{6,7},{7,6},{8,9},{9,8},{10,11... | collective-permute-start | bytes 786440 | tf_op jit(solution)/shard_map/ppermute | solution.py:53
  365.3 8.8 %collective-permute-start.29 = (f32[32,2048]{1,0:T(8,128)S(1)}, f32[32,2048]{1,0:T(8,128)}, u32[]{:S(2)}, u32[]{:S(2)}) collective-permute-start(f32[32,2048]{1,0:T(8,128)S(1)} %maximum_select_fusion.25), channel_id=1, source_target_pairs={{0,1},{1,0},{2,3},{3,2},{4,5},{5,4},{6,7},{7,6},{8,9},{9,8},{10,11... | collective-permute-start | bytes 786440 | tf_op jit(solution)/shard_map/ppermute | solution.py:53
  379.0 10.0 %collective-permute-start.79 = (f32[32,2048]{1,0:T(8,128)}, f32[32,2048]{1,0:T(8,128)}, u32[]{:S(2)}, u32[]{:S(2)}) collective-permute-start(f32[32,2048]{1,0:T(8,128)} %constant_dynamic-slice_fusion.14), channel_id=1, source_target_pairs={{0,8},{8,0},{16,24},{24,16},{1,9},{9,1},{17,25},{25,17},{2,10},{10... | collective-permute-start | bytes 786440 | tf_op jit(solution)/shard_map/ppermute | solution.py:50
  391.8 7.5 %collective-permute-start.33 = (f32[32,1024]{1,0:T(8,128)S(1)}, f32[32,1024]{1,0:T(8,128)S(1)}, u32[]{:S(2)}, u32[]{:S(2)}) collective-permute-start(f32[32,1024]{1,0:T(8,128)S(1)} %constant_dynamic-slice_fusion.28), channel_id=1, source_target_pairs={{0,16},{8,24},{16,0},{24,8},{1,17},{9,25},{17,1},{25,9},{2,18},{10... | collective-permute-start | bytes 393224 | tf_op jit(solution)/shard_map/ppermute | solution.py:50
  404.5 9.0 %collective-permute-start.35 = (f32[32,2048]{1,0:T(8,128)S(1)}, f32[32,2048]{1,0:T(8,128)S(1)}, u32[]{:S(2)}, u32[]{:S(2)}) collective-permute-start(f32[32,2048]{1,0:T(8,128)S(1)} %maximum_select_fusion.26), channel_id=1, source_target_pairs={{0,8},{8,0},{16,24},{24,16},{1,9},{9,1},{17,25},{25,17},{2,10},{10... | collective-permute-start | bytes 786440 | tf_op jit(solution)/shard_map/ppermute | solution.py:53
  414.6 12.0 %collective-permute-start.36 = (f32[32]{0:T(128)S(1)}, f32[32]{0:T(128)S(1)}, u32[]{:S(2)}, u32[]{:S(2)}) collective-permute-start(f32[32]{0:T(128)S(1)} %get-tuple-element.60), channel_id=1, source_target_pairs={{0,1},{1,0},{2,3},{3,2},{4,5},{5,4},{6,7},{7,6},{8,9},{9,8},{10,11... | collective-permute-start | bytes 392 | tf_op jit(solution)/shard_map/ppermute | solution.py:28
  432.4 13.0 %collective-permute-start.86 = (f32[32,2048]{1,0:T(8,128)}, f32[32,2048]{1,0:T(8,128)}, u32[]{:S(2)}, u32[]{:S(2)}) collective-permute-start(f32[32,2048]{1,0:T(8,128)} %constant_dynamic-slice_fusion.12), channel_id=1, source_target_pairs={{0,1},{1,0},{2,3},{3,2},{4,5},{5,4},{6,7},{7,6},{8,9},{9,8},{10,11... | collective-permute-start | bytes 786440 | tf_op jit(solution)/shard_map/ppermute | solution.py:50
  464.0 6.7 collective-permute-start.90
  481.9 9.6 %collective-permute-start.44 = (f32[32,2048]{1,0:T(8,128)S(1)}, f32[32,2048]{1,0:T(8,128)}, u32[]{:S(2)}, u32[]{:S(2)}) collective-permute-start(f32[32,2048]{1,0:T(8,128)S(1)} %maximum_select_fusion.28), channel_id=1, source_target_pairs={{0,1},{1,0},{2,3},{3,2},{4,5},{5,4},{6,7},{7,6},{8,9},{9,8},{10,11... | collective-permute-start | bytes 786440 | tf_op jit(solution)/shard_map/ppermute | solution.py:53
  496.4 9.5 %collective-permute-start.94 = (f32[32,2048]{1,0:T(8,128)}, f32[32,2048]{1,0:T(8,128)}, u32[]{:S(2)}, u32[]{:S(2)}) collective-permute-start(f32[32,2048]{1,0:T(8,128)} %constant_dynamic-slice_fusion.9), channel_id=1, source_target_pairs={{0,8},{8,0},{16,24},{24,16},{1,9},{9,1},{17,25},{25,17},{2,10},{10... | collective-permute-start | bytes 786440 | tf_op jit(solution)/shard_map/ppermute | solution.py:50
  525.4 18.5 %collective-permute-start.50 = (f32[32,2048]{1,0:T(8,128)}, f32[32,2048]{1,0:T(8,128)}, u32[]{:S(2)}, u32[]{:S(2)}) collective-permute-start(f32[32,2048]{1,0:T(8,128)} %maximum_select_fusion.29), channel_id=1, source_target_pairs={{0,8},{8,0},{16,24},{24,16},{1,9},{9,1},{17,25},{25,17},{2,10},{10... | collective-permute-start | bytes 786440 | tf_op jit(solution)/shard_map/ppermute | solution.py:53
  543.1 8.0 %collective-permute-start.101 = (f32[32,2048]{1,0:T(8,128)S(1)}, f32[32,2048]{1,0:T(8,128)S(1)}, u32[]{:S(2)}, u32[]{:S(2)}) collective-permute-start(f32[32,2048]{1,0:T(8,128)S(1)} %constant_dynamic-slice_fusion.7), channel_id=1, source_target_pairs={{0,1},{1,0},{2,3},{3,2},{4,5},{5,4},{6,7},{7,6},{8,9},{9,8},{10,11... | collective-permute-start | bytes 786440 | tf_op jit(solution)/shard_map/ppermute | solution.py:50
  586.0 11.3 %collective-permute-start.55 = (f32[32,1024]{1,0:T(8,128)}, f32[32,1024]{1,0:T(8,128)S(1)}, u32[]{:S(2)}, u32[]{:S(2)}) collective-permute-start(f32[32,1024]{1,0:T(8,128)} %constant_dynamic-slice_fusion.21), channel_id=1, source_target_pairs={{0,2},{1,3},{2,0},{3,1},{4,6},{5,7},{6,4},{7,5},{8,10},{9,11},{10,... | collective-permute-start | bytes 393224 | tf_op jit(solution)/shard_map/ppermute | solution.py:50
  613.8 11.6 %collective-permute-start.59 = (f32[32,2048]{1,0:T(8,128)S(1)}, f32[32,2048]{1,0:T(8,128)S(1)}, u32[]{:S(2)}, u32[]{:S(2)}) collective-permute-start(f32[32,2048]{1,0:T(8,128)S(1)} %maximum_select_fusion.31), channel_id=1, source_target_pairs={{0,1},{1,0},{2,3},{3,2},{4,5},{5,4},{6,7},{7,6},{8,9},{9,8},{10,11... | collective-permute-start | bytes 786440 | tf_op jit(solution)/shard_map/ppermute | solution.py:53
  667.9 8.1 %collective-permute-start.121 = (f32[32,2048]{1,0:T(8,128)S(1)}, f32[32,2048]{1,0:T(8,128)S(1)}, u32[]{:S(2)}, u32[]{:S(2)}) collective-permute-start(f32[32,2048]{1,0:T(8,128)S(1)} %maximum_select_fusion.39), channel_id=1, source_target_pairs={{0,1},{1,0},{2,3},{3,2},{4,5},{5,4},{6,7},{7,6},{8,9},{9,8},{10,11... | collective-permute-start | bytes 786440 | tf_op jit(solution)/shard_map/ppermute | solution.py:53
  (180 other events, 2436.5 us)

commit v4 on v2

--- a/solution.py
+++ b/solution.py
@@ -93,35 +93,30 @@
     own_count = blocks.shape[0]
     capacity = 2 * own_count // col_count
     target = targets[:, 0]
-    matches = (target[:, None] == jnp.arange(col_count, dtype=jnp.int32)[None, :]).astype(jnp.int32)
-    before = jnp.cumsum(matches, axis=0) - matches
-    slot_index = target * capacity + jnp.sum(before * matches, axis=1)
-    outgoing = (
-        jnp.zeros((col_count * capacity, block_size, block_size), blocks.dtype)
-        .at[slot_index]
-        .set(blocks)
+    slot_count = col_count * capacity
+
+    def slot_of(named):
+        matches = (named[..., :, None] == jnp.arange(col_count, dtype=jnp.int32)).astype(jnp.int32)
+        before = jnp.cumsum(matches, axis=-2) - matches
+        return named * capacity + jnp.sum(before * matches, axis=-1)
+
+    pick = slot_of(target)[:, None] == jnp.arange(slot_count, dtype=jnp.int32)[None, :]
+    source = jnp.sum(jnp.where(pick, jnp.arange(own_count, dtype=jnp.int32)[:, None], 0), axis=0)
+    filled = jnp.any(pick, axis=0)
+    outgoing = jnp.where(filled[:, None, None], jnp.take(blocks, source, axis=0), jnp.zeros((), blocks.dtype))
+    arrived = lax.all_to_all(
+        outgoing.reshape(col_count, capacity, block_size, block_size),
+        "col",
+        split_axis=0,
+        concat_axis=0,
+        tiled=True,
     )
-    places = (
-        jnp.zeros((col_count * capacity, 2), jnp.int32)
-        .at[slot_index]
-        .set(jnp.stack([tile_rows, tile_cols], axis=1))
-    )
-    arrived, arrived_places = (
-        lax.all_to_all(
-            outgoing.reshape(col_count, capacity, block_size, block_size),
-            "col",
-            split_axis=0,
-            concat_axis=0,
-            tiled=True,
-        ),
-        lax.all_to_all(
-            places.reshape(col_count, capacity, 2), "col", split_axis=0, concat_axis=0, tiled=True
-        ),
-    )
-    work_blocks = arrived.reshape(col_count * capacity, block_size, block_size)
-    flat_places = arrived_places.reshape(col_count * capacity, 2)
-    work_rows = flat_places[:, 0]
-    work_cols = flat_places[:, 1]
+    everyone = lax.all_gather(jnp.stack([target, tile_rows, tile_cols], axis=1), "col")
+    wanted = lax.axis_index("col") * capacity + jnp.arange(capacity, dtype=jnp.int32)
+    hit = slot_of(everyone[:, :, 0])[:, :, None] == wanted[None, None, :]
+    work_rows = jnp.sum(jnp.where(hit, everyone[:, :, 1:2], 0), axis=1).reshape(slot_count)
+    work_cols = jnp.sum(jnp.where(hit, everyone[:, :, 2:3], 0), axis=1).reshape(slot_count)
+    work_blocks = arrived.reshape(slot_count, block_size, block_size)
 
     def backward(left_bf):
         return backward_terms(left_bf, work_blocks, work_rows, work_cols, TC)

time: 624 us -> 674 us (1.080)
  blocking collectives: 0 us -> 156 us
  waiting for transfers between devices: 308 us -> 187 us
  matrix products: 125 us -> 140 us
  starting transfers between devices: 97.7 us -> 83.6 us
  other arithmetic: 32.1 us -> 44.3 us
  local copies, waits for them, and re-layouts: 49.1 us -> 56 us
    all_gather x0 -> x1, blocking collectives: none -> 156 us  [per_device(): lax.all_gather(jnp.stack([target, tile_rows, tile_cols], axis=1), 'col')]
    all_to_all x1, waiting for transfers between devices: 128 us -> 0.01 us  [per_device(): lax.all_to_all(outgoing.reshape(col_count, capacity, block_size, block_si...]
    gather x16, local copies, waits for them, and re-layouts: 15.5 us -> 31.5 us  [gather_tiles(): return jnp.take(vector_tiles, indices, axis=1)]
    scatter x2 -> x0, local copies, waits for them, and re-layouts: 13.6 us -> none  [the longest x1 12.8 us: per_device(): outgoing = jnp.zeros((col_count * capacity, block_size, block_size), bloc...]
    dot_general x8, matrix products: 45.1 us -> 54 us  [forward_terms(): jnp.einsum('sij,ksj->ksi', blocks, picked, preferred_element_type=jnp.flo...]
    gather x0 -> x1, local copies, waits for them, and re-layouts: none -> 7.94 us  [per_device(): jnp.take(blocks, source, axis=0)]
    all_to_all x1 -> x0, starting transfers between devices: 7.28 us -> none  [per_device(): lax.all_to_all(places.reshape(col_count, capacity, 2), 'col', split_axis=...]
  transfers between devices with their start and end apart: 126 -> 125, of which waited for: 92 -> 90; matrix products, arithmetic and copies ran while one was open for 31% -> 31% of each run, Pallas kernels for 0% -> 0%
where the time goes in v4:
time: 674 us; the launch traced here: 670 us
  waiting for transfers between devices  187 us (28%)
  blocking collectives  156 us (23%)
  matrix products  140 us (21%)
  starting transfers between devices  83.6 us (12%)
  local copies, waits for them, and re-layouts  56 us (8%)
  other arithmetic  44.3 us (7%)
    all_gather x1, blocking collectives, per_device(): lax.all_gather(jnp.stack([target, tile_rows, tile_cols], axis=1), 'col')  156 us
    ppermute x40, waiting for transfers between devices, big_sum(): held = keep + lax.ppermute(give, axis, partner_pairs(count, distance))  79.8 us
    ppermute x40, waiting for transfers between devices, big_sum(): other = lax.ppermute(held, axis, partner_pairs(count, distance))  73 us
    dot_general x8, matrix products, forward_terms(): jnp.einsum('sij,ksj->ksi', blocks, picked, preferred_element_type=jnp.flo...  54 us
    dot_general x16, matrix products, place_terms(): jnp.einsum('ksi,st->kti', weighted, onehot, precision=lax.Precision.HIGHEST)  47.8 us
    dot_general x8, matrix products, backward_terms(): jnp.einsum('sji,ksj->ksi', blocks, picked, preferred_element_type=jnp.flo...  38.5 us
    ppermute x44, waiting for transfers between devices, small_sum(): value = value + lax.ppermute(value, axis, partner_pairs(count, distance))  33.9 us
    gather x16, local copies, waits for them, and re-layouts, gather_tiles(): return jnp.take(vector_tiles, indices, axis=1)  31.5 us
  transfers between devices with their start and end apart: 125, of which 90 were waited for; matrix products, arithmetic and copies ran while one was open for 31% of the time, Pallas kernels for 0%

profile of v4, /device:TPU:0, one launch (start us, length us, event | category | flops | bytes accessed | tf_op | source)
XLA Modules:
  0.0 669.7 jit_solution(4867240173720208909)
XLA Ops:
  3.6 7.9 %gather_fusion = bf16[192,128,128]{2,1,0:T(8,128)(2,1)} fusion(bf16[96,128,128]{2,1,0:T(8,128)(2,1)S(1)} %copy-done, s32[1024]{0:T(1024)S(1)} %pad_clamp_fusion.1), kind=kCustom, calls=%fused_computation.16 | custom fusion | bytes 12583680 | tf_op jit(solution)/shard_map/jit(_take)/gather | solution.py:106
  11.5 6.9 %select_select_fusion = bf16[8,24,128,128]{3,2,1,0:T(8,128)(2,1)} fusion(bf16[8,24,128,128]{3,2,1,0:T(8,128)(2,1)} %bitcast.378, pred[8,24]{1,0:T(8,128)(4,1)S(1)} %compare_and_fusion, pred[8,24]{1,0:T(8,128)(4,1)S(1)} %broadcast_in_dim.72), kind=kLoop, calls=%fused_computation.17 | loop fusion | flops 6291456 | bytes 12583296 | tf_op jit(solution)/shard_map/jit(_where)/select_n | solution.py:106
  18.4 7.4 %all-to-all-start = ((bf16[8,24,128,128]{3,2,1,0:T(8,128)(2,1)}), bf16[8,24,128,128]{3,2,1,0:T(8,128)(2,1)}, u32[]{:S(2)}, u32[]{:S(2)}) async-start(bf16[8,24,128,128]{3,2,1,0:T(8,128)(2,1)} %select_select_fusion), calls=%async_computation | async-start | bytes 12582912 | tf_op jit(solution)/shard_map/all_to_all | solution.py:107
  26.7 155.8 %all-gather.1 = s32[8,96,3]{1,2,0:T(4,128)S(1)} all-gather(s32[1,96,3]{1,2,0:T(4,128)S(1)} %add_bitcast_fusion), channel_id=2, replica_groups=mesh['row'=4,'col'=8] {'col'}, dimensions={0}, use_global_device_ids=true | all-gather | bytes 10368 | tf_op jit(solution)/shard_map/all_gather | solution.py:114
  200.9 4.1 convolution_bitcast_fusion.15
  211.1 4.2 collective-permute-done.65
  238.1 6.7 convolution_bitcast_fusion.6
  251.2 7.1 %convolution_bitcast_fusion.14 = f32[32,192,128]{2,0,1:T(8,128)S(1)} fusion(bf16[192,128,128]{2,1,0:T(8,128)(2,1)} %bitcast.16, bf16[192,32,128]{2,1,0:T(8,128)(2,1)} %gather_fusion.2, pred[192]{0:T(512)(128)(4,1)S(1)} %get-tuple-element.76), kind=kOutput, calls=%fused_computation.64 | convolution fusion | flops 202113024 | bytes 11010240 | tf_op jit(solution)/shard_map/sij,ksj->ksi/dot_general | solution.py:77
  305.2 5.1 convolution_bitcast_fusion.13
  316.8 5.1 convolution_bitcast_fusion.5
  329.0 4.2 collective-permute-done.18
  358.1 6.7 convolution_bitcast_fusion.12
  374.2 6.7 convolution_bitcast_fusion.4
  427.0 5.1 convolution_bitcast_fusion.11
  438.8 5.1 convolution_bitcast_fusion.3
  450.9 4.2 collective-permute-done.33
  480.0 6.8 %convolution_bitcast_fusion.10 = f32[32,192,128]{2,0,1:T(8,128)S(1)} fusion(bf16[192,128,128]{2,1,0:T(8,128)(2,1)} %bitcast.16, bf16[192,32,128]{2,1,0:T(8,128)(2,1)} %gather_fusion.6, pred[192]{0:T(512)(128)(4,1)S(1)} %get-tuple-element.76), kind=kOutput, calls=%fused_computation.60 | convolution fusion | flops 202113024 | bytes 11010240 | tf_op jit(solution)/shard_map/sij,ksj->ksi/dot_general | solution.py:77
  494.3 6.7 convolution_bitcast_fusion.2
  547.3 5.1 convolution_bitcast_fusion.9
  558.7 5.1 convolution_bitcast_fusion.1
  570.9 4.2 collective-permute-done.48
  598.0 6.7 convolution_bitcast_fusion.8
  612.7 6.7 convolution_bitcast_fusion
  625.3 4.0 collective-permute-done.116
  (672 shorter events, 379.1 us)
Async XLA Ops:
  18.4 175.1 %all-to-all-start = ((bf16[8,24,128,128]{3,2,1,0:T(8,128)(2,1)}), bf16[8,24,128,128]{3,2,1,0:T(8,128)(2,1)}, u32[]{:S(2)}, u32[]{:S(2)}) async-start(bf16[8,24,128,128]{3,2,1,0:T(8,128)(2,1)} %select_select_fusion), calls=%async_computation | async-start | bytes 12582912 | tf_op jit(solution)/shard_map/all_to_all | solution.py:107
  26.1 159.2 %collective-permute-start.62 = (f32[32]{0:T(128)S(1)}, f32[32]{0:T(128)S(1)}, u32[]{:S(2)}, u32[]{:S(2)}) collective-permute-start(f32[32]{0:T(128)S(1)} %get-tuple-element.3), channel_id=1, source_target_pairs={{0,8},{8,0},{16,24},{24,16},{1,9},{9,1},{17,25},{25,17},{2,10},{10... | collective-permute-start | bytes 392 | tf_op jit(solution)/shard_map/ppermute | solution.py:28
  26.1 160.7 %collective-permute-start = (f32[32]{0:T(128)S(1)}, f32[32]{0:T(128)S(1)}, u32[]{:S(2)}, u32[]{:S(2)}) collective-permute-start(f32[32]{0:T(128)S(1)} %get-tuple-element.4), channel_id=1, source_target_pairs={{0,8},{8,0},{16,24},{24,16},{1,9},{9,1},{17,25},{25,17},{2,10},{10... | collective-permute-start | bytes 392 | tf_op jit(solution)/shard_map/ppermute | solution.py:28
  200.8 8.0 %collective-permute-start.64 = (f32[32,2048]{1,0:T(8,128)S(1)}, f32[32,2048]{1,0:T(8,128)S(1)}, u32[]{:S(2)}, u32[]{:S(2)}) collective-permute-start(f32[32,2048]{1,0:T(8,128)S(1)} %constant_dynamic-slice_fusion.19), channel_id=1, source_target_pairs={{0,8},{8,0},{16,24},{24,16},{1,9},{9,1},{17,25},{25,17},{2,10},{10... | collective-permute-start | bytes 786440 | tf_op jit(solution)/shard_map/ppermute | solution.py:50
  210.0 8.1 %collective-permute-start.3 = (f32[32,1024]{1,0:T(8,128)S(1)}, f32[32,1024]{1,0:T(8,128)S(1)}, u32[]{:S(2)}, u32[]{:S(2)}) collective-permute-start(f32[32,1024]{1,0:T(8,128)S(1)} %constant_dynamic-slice_fusion.38), channel_id=1, source_target_pairs={{0,16},{8,24},{16,0},{24,8},{1,17},{9,25},{17,1},{25,9},{2,18},{10... | collective-permute-start | bytes 393224 | tf_op jit(solution)/shard_map/ppermute | solution.py:50
  232.1 16.8 %collective-permute-start.8 = (f32[32]{0:T(128)S(1)}, f32[32]{0:T(128)S(1)}, u32[]{:S(2)}, u32[]{:S(2)}) collective-permute-start(f32[32]{0:T(128)S(1)} %add.613), channel_id=1, source_target_pairs={{0,4},{1,5},{2,6},{3,7},{4,0},{5,1},{6,2},{7,3},{8,12},{9,13},{10,... | collective-permute-start | bytes 392 | tf_op jit(solution)/shard_map/ppermute | solution.py:28
  248.9 14.7 %collective-permute-start.71 = (f32[32,2048]{1,0:T(8,128)}, f32[32,2048]{1,0:T(8,128)}, u32[]{:S(2)}, u32[]{:S(2)}) collective-permute-start(f32[32,2048]{1,0:T(8,128)} %constant_dynamic-slice_fusion.17), channel_id=1, source_target_pairs={{0,1},{1,0},{2,3},{3,2},{4,5},{5,4},{6,7},{7,6},{8,9},{9,8},{10,11... | collective-permute-start | bytes 786440 | tf_op jit(solution)/shard_map/ppermute | solution.py:50
  300.0 14.5 %collective-permute-start.78 = (f32[32]{0:T(128)S(1)}, f32[32]{0:T(128)S(1)}, u32[]{:S(2)}, u32[]{:S(2)}) collective-permute-start(f32[32]{0:T(128)S(1)} %add.686), channel_id=1, source_target_pairs={{0,16},{8,24},{16,0},{24,8},{1,17},{9,25},{17,1},{25,9},{2,18},{10... | collective-permute-start | bytes 392 | tf_op jit(solution)/shard_map/ppermute | solution.py:28
  314.5 11.2 %collective-permute-start.17 = (f32[32,2048]{1,0:T(8,128)}, f32[32,2048]{1,0:T(8,128)}, u32[]{:S(2)}, u32[]{:S(2)}) collective-permute-start(f32[32,2048]{1,0:T(8,128)} %constant_dynamic-slice_fusion.34), channel_id=1, source_target_pairs={{0,8},{8,0},{16,24},{24,16},{1,9},{9,1},{17,25},{25,17},{2,10},{10... | collective-permute-start | bytes 786440 | tf_op jit(solution)/shard_map/ppermute | solution.py:50
  327.4 8.6 %collective-permute-start.80 = (f32[32,1024]{1,0:T(8,128)S(1)}, f32[32,1024]{1,0:T(8,128)S(1)}, u32[]{:S(2)}, u32[]{:S(2)}) collective-permute-start(f32[32,1024]{1,0:T(8,128)S(1)} %constant_dynamic-slice_fusion.13), channel_id=1, source_target_pairs={{0,16},{8,24},{16,0},{24,8},{1,17},{9,25},{17,1},{25,9},{2,18},{10... | collective-permute-start | bytes 393224 | tf_op jit(solution)/shard_map/ppermute | solution.py:50
  353.3 17.8 %collective-permute-start.85 = (f32[32]{0:T(128)S(1)}, f32[32]{0:T(128)S(1)}, u32[]{:S(2)}, u32[]{:S(2)}) collective-permute-start(f32[32]{0:T(128)S(1)} %add.693), channel_id=1, source_target_pairs={{0,4},{1,5},{2,6},{3,7},{4,0},{5,1},{6,2},{7,3},{8,12},{9,13},{10,... | collective-permute-start | bytes 392 | tf_op jit(solution)/shard_map/ppermute | solution.py:28
  369.1 15.3 %collective-permute-start.24 = (f32[32,2048]{1,0:T(8,128)}, f32[32,2048]{1,0:T(8,128)}, u32[]{:S(2)}, u32[]{:S(2)}) collective-permute-start(f32[32,2048]{1,0:T(8,128)} %constant_dynamic-slice_fusion.32), channel_id=1, source_target_pairs={{0,1},{1,0},{2,3},{3,2},{4,5},{5,4},{6,7},{7,6},{8,9},{9,8},{10,11... | collective-permute-start | bytes 786440 | tf_op jit(solution)/shard_map/ppermute | solution.py:50
  392.1 7.3 %collective-permute-start.26 = (f32[32,512]{1,0:T(8,128)S(1)}, f32[32,512]{1,0:T(8,128)S(1)}, u32[]{:S(2)}, u32[]{:S(2)}) collective-permute-start(f32[32,512]{1,0:T(8,128)S(1)} %constant_dynamic-slice_fusion.30), channel_id=1, source_target_pairs={{0,4},{1,5},{2,6},{3,7},{4,0},{5,1},{6,2},{7,3},{8,12},{9,13},{10,... | collective-permute-start | bytes 196616 | tf_op jit(solution)/shard_map/ppermute | solution.py:50
  412.2 7.8 %collective-permute-start.91 = (f32[32,2048]{1,0:T(8,128)S(1)}, f32[32,2048]{1,0:T(8,128)S(1)}, u32[]{:S(2)}, u32[]{:S(2)}) collective-permute-start(f32[32,2048]{1,0:T(8,128)S(1)} %maximum_select_fusion.41), channel_id=1, source_target_pairs={{0,1},{1,0},{2,3},{3,2},{4,5},{5,4},{6,7},{7,6},{8,9},{9,8},{10,11... | collective-permute-start | bytes 786440 | tf_op jit(solution)/shard_map/ppermute | solution.py:53
  422.3 14.3 %collective-permute-start.93 = (f32[32]{0:T(128)S(1)}, f32[32]{0:T(128)S(1)}, u32[]{:S(2)}, u32[]{:S(2)}) collective-permute-start(f32[32]{0:T(128)S(1)} %add.699), channel_id=1, source_target_pairs={{0,16},{8,24},{16,0},{24,8},{1,17},{9,25},{17,1},{25,9},{2,18},{10... | collective-permute-start | bytes 392 | tf_op jit(solution)/shard_map/ppermute | solution.py:28
  436.5 11.2 %collective-permute-start.32 = (f32[32,2048]{1,0:T(8,128)}, f32[32,2048]{1,0:T(8,128)}, u32[]{:S(2)}, u32[]{:S(2)}) collective-permute-start(f32[32,2048]{1,0:T(8,128)} %constant_dynamic-slice_fusion.29), channel_id=1, source_target_pairs={{0,8},{8,0},{16,24},{24,16},{1,9},{9,1},{17,25},{25,17},{2,10},{10... | collective-permute-start | bytes 786440 | tf_op jit(solution)/shard_map/ppermute | solution.py:50
  449.4 8.6 %collective-permute-start.95 = (f32[32,1024]{1,0:T(8,128)S(1)}, f32[32,1024]{1,0:T(8,128)S(1)}, u32[]{:S(2)}, u32[]{:S(2)}) collective-permute-start(f32[32,1024]{1,0:T(8,128)S(1)} %constant_dynamic-slice_fusion.8), channel_id=1, source_target_pairs={{0,16},{8,24},{16,0},{24,8},{1,17},{9,25},{17,1},{25,9},{2,18},{10... | collective-permute-start | bytes 393224 | tf_op jit(solution)/shard_map/ppermute | solution.py:50
  473.5 17.7 %collective-permute-start.100 = (f32[32]{0:T(128)S(1)}, f32[32]{0:T(128)S(1)}, u32[]{:S(2)}, u32[]{:S(2)}) collective-permute-start(f32[32]{0:T(128)S(1)} %add.707), channel_id=1, source_target_pairs={{0,4},{1,5},{2,6},{3,7},{4,0},{5,1},{6,2},{7,3},{8,12},{9,13},{10,... | collective-permute-start | bytes 392 | tf_op jit(solution)/shard_map/ppermute | solution.py:28
  490.9 15.2 %collective-permute-start.39 = (f32[32,2048]{1,0:T(8,128)}, f32[32,2048]{1,0:T(8,128)}, u32[]{:S(2)}, u32[]{:S(2)}) collective-permute-start(f32[32,2048]{1,0:T(8,128)} %constant_dynamic-slice_fusion.27), channel_id=1, source_target_pairs={{0,1},{1,0},{2,3},{3,2},{4,5},{5,4},{6,7},{7,6},{8,9},{9,8},{10,11... | collective-permute-start | bytes 786440 | tf_op jit(solution)/shard_map/ppermute | solution.py:50
  542.4 14.1 %collective-permute-start.108 = (f32[32]{0:T(128)S(1)}, f32[32]{0:T(128)S(1)}, u32[]{:S(2)}, u32[]{:S(2)}) collective-permute-start(f32[32]{0:T(128)S(1)} %add.713), channel_id=1, source_target_pairs={{0,16},{8,24},{16,0},{24,8},{1,17},{9,25},{17,1},{25,9},{2,18},{10... | collective-permute-start | bytes 392 | tf_op jit(solution)/shard_map/ppermute | solution.py:28
  556.5 11.2 %collective-permute-start.47 = (f32[32,2048]{1,0:T(8,128)}, f32[32,2048]{1,0:T(8,128)}, u32[]{:S(2)}, u32[]{:S(2)}) collective-permute-start(f32[32,2048]{1,0:T(8,128)} %constant_dynamic-slice_fusion.24), channel_id=1, source_target_pairs={{0,8},{8,0},{16,24},{24,16},{1,9},{9,1},{17,25},{25,17},{2,10},{10... | collective-permute-start | bytes 786440 | tf_op jit(solution)/shard_map/ppermute | solution.py:50
  569.4 8.5 %collective-permute-start.110 = (f32[32,1024]{1,0:T(8,128)S(1)}, f32[32,1024]{1,0:T(8,128)S(1)}, u32[]{:S(2)}, u32[]{:S(2)}) collective-permute-start(f32[32,1024]{1,0:T(8,128)S(1)} %constant_dynamic-slice_fusion.3), channel_id=1, source_target_pairs={{0,16},{8,24},{16,0},{24,8},{1,17},{9,25},{17,1},{25,9},{2,18},{10... | collective-permute-start | bytes 393224 | tf_op jit(solution)/shard_map/ppermute | solution.py:50
  593.7 16.7 %collective-permute-start.115 = (f32[32]{0:T(128)S(1)}, f32[32]{0:T(128)S(1)}, u32[]{:S(2)}, u32[]{:S(2)}) collective-permute-start(f32[32]{0:T(128)S(1)} %add.721), channel_id=1, source_target_pairs={{0,4},{1,5},{2,6},{3,7},{4,0},{5,1},{6,2},{7,3},{8,12},{9,13},{10,... | collective-permute-start | bytes 392 | tf_op jit(solution)/shard_map/ppermute | solution.py:28
  608.8 14.5 %collective-permute-start.54 = (f32[32,2048]{1,0:T(8,128)}, f32[32,2048]{1,0:T(8,128)}, u32[]{:S(2)}, u32[]{:S(2)}) collective-permute-start(f32[32,2048]{1,0:T(8,128)} %constant_dynamic-slice_fusion.22), channel_id=1, source_target_pairs={{0,1},{1,0},{2,3},{3,2},{4,5},{5,4},{6,7},{7,6},{8,9},{9,8},{10,11... | collective-permute-start | bytes 786440 | tf_op jit(solution)/shard_map/ppermute | solution.py:50
  (167 other events, 1188.4 us)

commit v5 on v4

--- a/solution.py
+++ b/solution.py
@@ -6,6 +6,7 @@
 TC = 32
 ITERS = 4
 CHUNKS = 2
+UNUSED = 1 << 20
 
 
 EPSILON = 1e-06
@@ -62,7 +63,7 @@
 def gather_tiles(vector_bf, indices, block_size):
     snapshots, extent = vector_bf.shape
     vector_tiles = vector_bf.reshape(snapshots, extent // block_size, block_size)
-    return jnp.take(vector_tiles, indices, axis=1)
+    return jnp.take(vector_tiles, indices, axis=1, mode="clip")
 
 
 def place_terms(weighted, indices, n_out):
@@ -103,7 +104,12 @@
     pick = slot_of(target)[:, None] == jnp.arange(slot_count, dtype=jnp.int32)[None, :]
     source = jnp.sum(jnp.where(pick, jnp.arange(own_count, dtype=jnp.int32)[:, None], 0), axis=0)
     filled = jnp.any(pick, axis=0)
-    outgoing = jnp.where(filled[:, None, None], jnp.take(blocks, source, axis=0), jnp.zeros((), blocks.dtype))
+    outgoing = jnp.take(blocks, source, axis=0, mode="clip")
+    places = jnp.where(
+        filled[:, None],
+        jnp.take(jnp.stack([tile_rows, tile_cols], axis=1), source, axis=0, mode="clip"),
+        UNUSED,
+    )
     arrived = lax.all_to_all(
         outgoing.reshape(col_count, capacity, block_size, block_size),
         "col",
@@ -111,11 +117,12 @@
         concat_axis=0,
         tiled=True,
     )
-    everyone = lax.all_gather(jnp.stack([target, tile_rows, tile_cols], axis=1), "col")
-    wanted = lax.axis_index("col") * capacity + jnp.arange(capacity, dtype=jnp.int32)
-    hit = slot_of(everyone[:, :, 0])[:, :, None] == wanted[None, None, :]
-    work_rows = jnp.sum(jnp.where(hit, everyone[:, :, 1:2], 0), axis=1).reshape(slot_count)
-    work_cols = jnp.sum(jnp.where(hit, everyone[:, :, 2:3], 0), axis=1).reshape(slot_count)
+    arrived_places = lax.all_to_all(
+        places.reshape(col_count, capacity, 2), "col", split_axis=0, concat_axis=0, tiled=True
+    )
+    flat_places = arrived_places.reshape(slot_count, 2)
+    work_rows = flat_places[:, 0]
+    work_cols = flat_places[:, 1]
     work_blocks = arrived.reshape(slot_count, block_size, block_size)
 
     def backward(left_bf):

time: 674 us -> 650 us (0.964)
  blocking collectives: 156 us -> 0 us
  waiting for transfers between devices: 187 us -> 305 us
  starting transfers between devices: 83.6 us -> 102 us
  other arithmetic: 44.3 us -> 35.9 us
    all_gather x1 -> x0, blocking collectives: 156 us -> none  [per_device(): lax.all_gather(jnp.stack([target, tile_rows, tile_cols], axis=1), 'col')]
    all_to_all x1, waiting for transfers between devices: 0.01 us -> 128 us  [per_device(): lax.all_to_all(outgoing.reshape(col_count, capacity, block_size, block_si...]
    all_to_all x0 -> x1, starting transfers between devices: none -> 7.28 us  [per_device(): lax.all_to_all(places.reshape(col_count, capacity, 2), 'col', split_axis=...]
    gather x17 -> x19, local copies, waits for them, and re-layouts: 39.4 us -> 40.8 us  [the longest x16 31.9 us: gather_tiles(): return jnp.take(vector_tiles, indices, axis=1, mode='clip')]
  transfers between devices with their start and end apart: 125 -> 126, of which waited for: 90 -> 90; matrix products, arithmetic and copies ran while one was open for 31% -> 33% of each run, Pallas kernels for 0% -> 0%
where the time goes in v5:
time: 650 us; the launch traced here: 643 us
  waiting for transfers between devices  305 us (47%)
  matrix products  140 us (22%)
  starting transfers between devices  102 us (16%)
  local copies, waits for them, and re-layouts  57.3 us (9%)
  other arithmetic  35.9 us (6%)
    all_to_all x1, waiting for transfers between devices, per_device(): lax.all_to_all(outgoing.reshape(col_count, capacity, block_size, block_si...  128 us
    ppermute x40, waiting for transfers between devices, big_sum(): held = keep + lax.ppermute(give, axis, partner_pairs(count, distance))  73.3 us
    ppermute x40, waiting for transfers between devices, big_sum(): other = lax.ppermute(held, axis, partner_pairs(count, distance))  72.7 us
    dot_general x8, matrix products, forward_terms(): jnp.einsum('sij,ksj->ksi', blocks, picked, preferred_element_type=jnp.flo...  53.3 us
    dot_general x16, matrix products, place_terms(): jnp.einsum('ksi,st->kti', weighted, onehot, precision=lax.Precision.HIGHEST)  48.1 us
    dot_general x8, matrix products, backward_terms(): jnp.einsum('sji,ksj->ksi', blocks, picked, preferred_element_type=jnp.flo...  38.3 us
    ppermute x44, starting transfers between devices, small_sum(): value = value + lax.ppermute(value, axis, partner_pairs(count, distance))  33.6 us
    gather x16, local copies, waits for them, and re-layouts, gather_tiles(): return jnp.take(vector_tiles, indices, axis=1, mode='clip')  31.9 us
  transfers between devices with their start and end apart: 126, of which 90 were waited for; matrix products, arithmetic and copies ran while one was open for 33% of the time, Pallas kernels for 0%

profile of v5, /device:TPU:0, one launch (start us, length us, event | category | flops | bytes accessed | tf_op | source)
XLA Modules:
  0.0 642.7 jit_solution(5067434574306567561)
XLA Ops:
  5.7 7.3 %all-to-all-start = ((s32[8,24,2]{1,2,0:T(2,128)}), s32[8,24,2]{1,2,0:T(2,128)S(1)}, u32[]{:S(2)}, u32[]{:S(2)}) async-start(s32[8,24,2]{1,2,0:T(2,128)} %broadcast_select_fusion), calls=%async_computation | async-start | bytes 16384 | tf_op jit(solution)/shard_map/all_to_all | solution.py:120
  13.0 8.1 %gather_fusion.2 = bf16[192,128,128]{2,1,0:T(8,128)(2,1)} fusion(bf16[96,128,128]{2,1,0:T(8,128)(2,1)S(1)} %copy-done, s32[1024]{0:T(1024)S(1)} %pad_clamp_fusion.2), kind=kCustom, calls=%fused_computation.2 | custom fusion | bytes 12583680 | tf_op jit(solution)/shard_map/jit(_take)/gather | solution.py:107
  21.0 6.1 all-to-all-start.1
  36.9 127.9 %all-to-all-done.1 = bf16[8,24,128,128]{3,2,1,0:T(8,128)(2,1)} async-done(((bf16[8,24,128,128]{3,2,1,0:T(8,128)(2,1)}), bf16[8,24,128,128]{3,2,1,0:T(8,128)(2,1)}, u32[]{:S(2)}, u32[]{:S(2)}) %all-to-all-start.1) | async-done | bytes 6291488 | tf_op jit(solution)/shard_map/all_to_all | solution.py:113
  172.0 4.2 convolution_bitcast_fusion.15
  209.5 6.6 %convolution_bitcast_fusion.6 = f32[32,192,128]{2,0,1:T(8,128)S(1)} fusion(bf16[192,128,128]{2,1,0:T(8,128)(2,1)} %bitcast.11, bf16[192,32,128]{2,1,0:T(8,128)(2,1)} %gather_fusion.11), kind=kOutput, calls=%fused_computation.56 | convolution fusion | flops 201326592 | bytes 11010048 | tf_op jit(solution)/shard_map/sij,ksj->ksi/dot_general | solution.py:78
  223.9 6.8 %convolution_bitcast_fusion.14 = f32[32,192,128]{2,0,1:T(8,128)S(1)} fusion(bf16[192,128,128]{2,1,0:T(8,128)(2,1)} %bitcast.11, bf16[192,32,128]{2,1,0:T(8,128)(2,1)} %gather_fusion.3), kind=kOutput, calls=%fused_computation.64 | convolution fusion | flops 201326592 | bytes 11010048 | tf_op jit(solution)/shard_map/sij,ksj->ksi/dot_general | solution.py:78
  235.9 4.5 collective-permute-done.9
  277.9 5.0 convolution_bitcast_fusion.13
  289.3 5.2 convolution_bitcast_fusion.5
  301.6 4.2 collective-permute-done.18
  330.7 6.6 %convolution_bitcast_fusion.12 = f32[32,192,128]{2,0,1:T(8,128)S(1)} fusion(bf16[192,128,128]{2,1,0:T(8,128)(2,1)} %bitcast.11, bf16[192,32,128]{2,1,0:T(8,128)(2,1)} %gather_fusion.5), kind=kOutput, calls=%fused_computation.62 | convolution fusion | flops 201326592 | bytes 11010048 | tf_op jit(solution)/shard_map/sij,ksj->ksi/dot_general | solution.py:78
  345.3 6.6 %convolution_bitcast_fusion.4 = f32[32,192,128]{2,0,1:T(8,128)S(1)} fusion(bf16[192,128,128]{2,1,0:T(8,128)(2,1)} %bitcast.11, bf16[192,32,128]{2,1,0:T(8,128)(2,1)} %gather_fusion.13), kind=kOutput, calls=%fused_computation.54 | convolution fusion | flops 201326592 | bytes 11010048 | tf_op jit(solution)/shard_map/sij,ksj->ksi/dot_general | solution.py:78
  398.6 5.0 convolution_bitcast_fusion.11
  410.2 5.0 convolution_bitcast_fusion.3
  422.2 4.2 collective-permute-done.33
  451.3 6.6 %convolution_bitcast_fusion.10 = f32[32,192,128]{2,0,1:T(8,128)S(1)} fusion(bf16[192,128,128]{2,1,0:T(8,128)(2,1)} %bitcast.11, bf16[192,32,128]{2,1,0:T(8,128)(2,1)} %gather_fusion.7), kind=kOutput, calls=%fused_computation.60 | convolution fusion | flops 201326592 | bytes 11010048 | tf_op jit(solution)/shard_map/sij,ksj->ksi/dot_general | solution.py:78
  467.1 6.6 %convolution_bitcast_fusion.2 = f32[32,192,128]{2,0,1:T(8,128)S(1)} fusion(bf16[192,128,128]{2,1,0:T(8,128)(2,1)} %bitcast.11, bf16[192,32,128]{2,1,0:T(8,128)(2,1)} %gather_fusion.15), kind=kOutput, calls=%fused_computation.52 | convolution fusion | flops 201326592 | bytes 11010048 | tf_op jit(solution)/shard_map/sij,ksj->ksi/dot_general | solution.py:78
  506.4 4.3 collective-permute-done.44
  520.5 5.0 convolution_bitcast_fusion.9
  532.3 5.0 convolution_bitcast_fusion.1
  544.4 4.2 collective-permute-done.48
  571.5 6.6 %convolution_bitcast_fusion.8 = f32[32,192,128]{2,0,1:T(8,128)S(1)} fusion(bf16[192,128,128]{2,1,0:T(8,128)(2,1)} %bitcast.11, bf16[192,32,128]{2,1,0:T(8,128)(2,1)} %gather_fusion.9), kind=kOutput, calls=%fused_computation.58 | convolution fusion | flops 201326592 | bytes 11010048 | tf_op jit(solution)/shard_map/sij,ksj->ksi/dot_general | solution.py:78
  585.0 6.6 %convolution_bitcast_fusion = f32[32,192,128]{2,0,1:T(8,128)S(1)} fusion(bf16[192,128,128]{2,1,0:T(8,128)(2,1)} %bitcast.11, bf16[192,32,128]{2,1,0:T(8,128)(2,1)} %gather_fusion.17), kind=kOutput, calls=%fused_computation.50 | convolution fusion | flops 201326592 | bytes 11010048 | tf_op jit(solution)/shard_map/sij,ksj->ksi/dot_general | solution.py:78
  (658 shorter events, 381.1 us)
Async XLA Ops:
  5.7 15.3 %all-to-all-start = ((s32[8,24,2]{1,2,0:T(2,128)}), s32[8,24,2]{1,2,0:T(2,128)S(1)}, u32[]{:S(2)}, u32[]{:S(2)}) async-start(s32[8,24,2]{1,2,0:T(2,128)} %broadcast_select_fusion), calls=%async_computation | async-start | bytes 16384 | tf_op jit(solution)/shard_map/all_to_all | solution.py:120
  21.0 143.8 %all-to-all-start.1 = ((bf16[8,24,128,128]{3,2,1,0:T(8,128)(2,1)}), bf16[8,24,128,128]{3,2,1,0:T(8,128)(2,1)}, u32[]{:S(2)}, u32[]{:S(2)}) async-start(bf16[8,24,128,128]{3,2,1,0:T(8,128)(2,1)} %bitcast.370), calls=%async_computation.1 | async-start | bytes 12582912 | tf_op jit(solution)/shard_map/all_to_all | solution.py:113
  171.9 8.2 %collective-permute-start.64 = (f32[32,2048]{1,0:T(8,128)S(1)}, f32[32,2048]{1,0:T(8,128)S(1)}, u32[]{:S(2)}, u32[]{:S(2)}) collective-permute-start(f32[32,2048]{1,0:T(8,128)S(1)} %constant_dynamic-slice_fusion.19), channel_id=1, source_target_pairs={{0,8},{8,0},{16,24},{24,16},{1,9},{9,1},{17,25},{25,17},{2,10},{10... | collective-permute-start | bytes 786440 | tf_op jit(solution)/shard_map/ppermute | solution.py:51
  181.7 7.6 %collective-permute-start.3 = (f32[32,1024]{1,0:T(8,128)S(1)}, f32[32,1024]{1,0:T(8,128)S(1)}, u32[]{:S(2)}, u32[]{:S(2)}) collective-permute-start(f32[32,1024]{1,0:T(8,128)S(1)} %constant_dynamic-slice_fusion.38), channel_id=1, source_target_pairs={{0,16},{8,24},{16,0},{24,8},{1,17},{9,25},{17,1},{25,9},{2,18},{10... | collective-permute-start | bytes 393224 | tf_op jit(solution)/shard_map/ppermute | solution.py:51
  204.5 17.2 %collective-permute-start.8 = (f32[32]{0:T(128)S(1)}, f32[32]{0:T(128)S(1)}, u32[]{:S(2)}, u32[]{:S(2)}) collective-permute-start(f32[32]{0:T(128)S(1)} %add.564), channel_id=1, source_target_pairs={{0,4},{1,5},{2,6},{3,7},{4,0},{5,1},{6,2},{7,3},{8,12},{9,13},{10,... | collective-permute-start | bytes 392 | tf_op jit(solution)/shard_map/ppermute | solution.py:29
  220.2 14.4 %collective-permute-start.71 = (f32[32,2048]{1,0:T(8,128)}, f32[32,2048]{1,0:T(8,128)}, u32[]{:S(2)}, u32[]{:S(2)}) collective-permute-start(f32[32,2048]{1,0:T(8,128)} %constant_dynamic-slice_fusion.17), channel_id=1, source_target_pairs={{0,1},{1,0},{2,3},{3,2},{4,5},{5,4},{6,7},{7,6},{8,9},{9,8},{10,11... | collective-permute-start | bytes 786440 | tf_op jit(solution)/shard_map/ppermute | solution.py:51
  262.4 7.4 %collective-permute-start.14 = (f32[32,2048]{1,0:T(8,128)S(1)}, f32[32,2048]{1,0:T(8,128)S(1)}, u32[]{:S(2)}, u32[]{:S(2)}) collective-permute-start(f32[32,2048]{1,0:T(8,128)S(1)} %maximum_select_fusion.26), channel_id=1, source_target_pairs={{0,1},{1,0},{2,3},{3,2},{4,5},{5,4},{6,7},{7,6},{8,9},{9,8},{10,11... | collective-permute-start | bytes 786440 | tf_op jit(solution)/shard_map/ppermute | solution.py:54
  273.6 13.4 %collective-permute-start.78 = (f32[32]{0:T(128)S(1)}, f32[32]{0:T(128)S(1)}, u32[]{:S(2)}, u32[]{:S(2)}) collective-permute-start(f32[32]{0:T(128)S(1)} %add.637), channel_id=1, source_target_pairs={{0,16},{8,24},{16,0},{24,8},{1,17},{9,25},{17,1},{25,9},{2,18},{10... | collective-permute-start | bytes 392 | tf_op jit(solution)/shard_map/ppermute | solution.py:29
  287.0 11.3 %collective-permute-start.17 = (f32[32,2048]{1,0:T(8,128)}, f32[32,2048]{1,0:T(8,128)}, u32[]{:S(2)}, u32[]{:S(2)}) collective-permute-start(f32[32,2048]{1,0:T(8,128)} %constant_dynamic-slice_fusion.34), channel_id=1, source_target_pairs={{0,8},{8,0},{16,24},{24,16},{1,9},{9,1},{17,25},{25,17},{2,10},{10... | collective-permute-start | bytes 786440 | tf_op jit(solution)/shard_map/ppermute | solution.py:51
  301.0 7.6 %collective-permute-start.80 = (f32[32,1024]{1,0:T(8,128)S(1)}, f32[32,1024]{1,0:T(8,128)S(1)}, u32[]{:S(2)}, u32[]{:S(2)}) collective-permute-start(f32[32,1024]{1,0:T(8,128)S(1)} %constant_dynamic-slice_fusion.13), channel_id=1, source_target_pairs={{0,16},{8,24},{16,0},{24,8},{1,17},{9,25},{17,1},{25,9},{2,18},{10... | collective-permute-start | bytes 393224 | tf_op jit(solution)/shard_map/ppermute | solution.py:51
  324.2 18.0 %collective-permute-start.85 = (f32[32]{0:T(128)S(1)}, f32[32]{0:T(128)S(1)}, u32[]{:S(2)}, u32[]{:S(2)}) collective-permute-start(f32[32]{0:T(128)S(1)} %add.644), channel_id=1, source_target_pairs={{0,4},{1,5},{2,6},{3,7},{4,0},{5,1},{6,2},{7,3},{8,12},{9,13},{10,... | collective-permute-start | bytes 392 | tf_op jit(solution)/shard_map/ppermute | solution.py:29
  341.9 15.2 %collective-permute-start.24 = (f32[32,2048]{1,0:T(8,128)}, f32[32,2048]{1,0:T(8,128)}, u32[]{:S(2)}, u32[]{:S(2)}) collective-permute-start(f32[32,2048]{1,0:T(8,128)} %constant_dynamic-slice_fusion.32), channel_id=1, source_target_pairs={{0,1},{1,0},{2,3},{3,2},{4,5},{5,4},{6,7},{7,6},{8,9},{9,8},{10,11... | collective-permute-start | bytes 786440 | tf_op jit(solution)/shard_map/ppermute | solution.py:51
  394.4 13.5 %collective-permute-start.93 = (f32[32]{0:T(128)S(1)}, f32[32]{0:T(128)S(1)}, u32[]{:S(2)}, u32[]{:S(2)}) collective-permute-start(f32[32]{0:T(128)S(1)} %add.650), channel_id=1, source_target_pairs={{0,16},{8,24},{16,0},{24,8},{1,17},{9,25},{17,1},{25,9},{2,18},{10... | collective-permute-start | bytes 392 | tf_op jit(solution)/shard_map/ppermute | solution.py:29
  407.8 11.1 %collective-permute-start.32 = (f32[32,2048]{1,0:T(8,128)}, f32[32,2048]{1,0:T(8,128)}, u32[]{:S(2)}, u32[]{:S(2)}) collective-permute-start(f32[32,2048]{1,0:T(8,128)} %constant_dynamic-slice_fusion.29), channel_id=1, source_target_pairs={{0,8},{8,0},{16,24},{24,16},{1,9},{9,1},{17,25},{25,17},{2,10},{10... | collective-permute-start | bytes 786440 | tf_op jit(solution)/shard_map/ppermute | solution.py:51
  421.6 7.6 %collective-permute-start.95 = (f32[32,1024]{1,0:T(8,128)S(1)}, f32[32,1024]{1,0:T(8,128)S(1)}, u32[]{:S(2)}, u32[]{:S(2)}) collective-permute-start(f32[32,1024]{1,0:T(8,128)S(1)} %constant_dynamic-slice_fusion.8), channel_id=1, source_target_pairs={{0,16},{8,24},{16,0},{24,8},{1,17},{9,25},{17,1},{25,9},{2,18},{10... | collective-permute-start | bytes 393224 | tf_op jit(solution)/shard_map/ppermute | solution.py:51
  446.3 17.7 %collective-permute-start.100 = (f32[32]{0:T(128)S(1)}, f32[32]{0:T(128)S(1)}, u32[]{:S(2)}, u32[]{:S(2)}) collective-permute-start(f32[32]{0:T(128)S(1)} %add.658), channel_id=1, source_target_pairs={{0,4},{1,5},{2,6},{3,7},{4,0},{5,1},{6,2},{7,3},{8,12},{9,13},{10,... | collective-permute-start | bytes 392 | tf_op jit(solution)/shard_map/ppermute | solution.py:29
  462.2 15.2 %collective-permute-start.39 = (f32[32,2048]{1,0:T(8,128)}, f32[32,2048]{1,0:T(8,128)}, u32[]{:S(2)}, u32[]{:S(2)}) collective-permute-start(f32[32,2048]{1,0:T(8,128)} %constant_dynamic-slice_fusion.27), channel_id=1, source_target_pairs={{0,1},{1,0},{2,3},{3,2},{4,5},{5,4},{6,7},{7,6},{8,9},{9,8},{10,11... | collective-permute-start | bytes 786440 | tf_op jit(solution)/shard_map/ppermute | solution.py:51
  506.0 7.5 %collective-permute-start.106 = (f32[32,2048]{1,0:T(8,128)S(1)}, f32[32,2048]{1,0:T(8,128)S(1)}, u32[]{:S(2)}, u32[]{:S(2)}) collective-permute-start(f32[32,2048]{1,0:T(8,128)S(1)} %maximum_select_fusion.44), channel_id=1, source_target_pairs={{0,1},{1,0},{2,3},{3,2},{4,5},{5,4},{6,7},{7,6},{8,9},{9,8},{10,11... | collective-permute-start | bytes 786440 | tf_op jit(solution)/shard_map/ppermute | solution.py:54
  515.9 14.1 %collective-permute-start.108 = (f32[32]{0:T(128)S(1)}, f32[32]{0:T(128)S(1)}, u32[]{:S(2)}, u32[]{:S(2)}) collective-permute-start(f32[32]{0:T(128)S(1)} %add.664), channel_id=1, source_target_pairs={{0,16},{8,24},{16,0},{24,8},{1,17},{9,25},{17,1},{25,9},{2,18},{10... | collective-permute-start | bytes 392 | tf_op jit(solution)/shard_map/ppermute | solution.py:29
  530.0 11.1 %collective-permute-start.47 = (f32[32,2048]{1,0:T(8,128)}, f32[32,2048]{1,0:T(8,128)}, u32[]{:S(2)}, u32[]{:S(2)}) collective-permute-start(f32[32,2048]{1,0:T(8,128)} %constant_dynamic-slice_fusion.24), channel_id=1, source_target_pairs={{0,8},{8,0},{16,24},{24,16},{1,9},{9,1},{17,25},{25,17},{2,10},{10... | collective-permute-start | bytes 786440 | tf_op jit(solution)/shard_map/ppermute | solution.py:51
  543.5 7.9 %collective-permute-start.110 = (f32[32,1024]{1,0:T(8,128)S(1)}, f32[32,1024]{1,0:T(8,128)S(1)}, u32[]{:S(2)}, u32[]{:S(2)}) collective-permute-start(f32[32,1024]{1,0:T(8,128)S(1)} %constant_dynamic-slice_fusion.3), channel_id=1, source_target_pairs={{0,16},{8,24},{16,0},{24,8},{1,17},{9,25},{17,1},{25,9},{2,18},{10... | collective-permute-start | bytes 393224 | tf_op jit(solution)/shard_map/ppermute | solution.py:51
  565.5 17.2 %collective-permute-start.115 = (f32[32]{0:T(128)S(1)}, f32[32]{0:T(128)S(1)}, u32[]{:S(2)}, u32[]{:S(2)}) collective-permute-start(f32[32]{0:T(128)S(1)} %add.672), channel_id=1, source_target_pairs={{0,4},{1,5},{2,6},{3,7},{4,0},{5,1},{6,2},{7,3},{8,12},{9,13},{10,... | collective-permute-start | bytes 392 | tf_op jit(solution)/shard_map/ppermute | solution.py:29
  582.4 14.4 %collective-permute-start.54 = (f32[32,2048]{1,0:T(8,128)}, f32[32,2048]{1,0:T(8,128)}, u32[]{:S(2)}, u32[]{:S(2)}) collective-permute-start(f32[32,2048]{1,0:T(8,128)} %constant_dynamic-slice_fusion.22), channel_id=1, source_target_pairs={{0,1},{1,0},{2,3},{3,2},{4,5},{5,4},{6,7},{7,6},{8,9},{9,8},{10,11... | collective-permute-start | bytes 786440 | tf_op jit(solution)/shard_map/ppermute | solution.py:51
  623.6 7.6 %collective-permute-start.121 = (f32[32,2048]{1,0:T(8,128)S(1)}, f32[32,2048]{1,0:T(8,128)S(1)}, u32[]{:S(2)}, u32[]{:S(2)}) collective-permute-start(f32[32,2048]{1,0:T(8,128)S(1)} %maximum_select_fusion.47), channel_id=1, source_target_pairs={{0,1},{1,0},{2,3},{3,2},{4,5},{5,4},{6,7},{7,6},{8,9},{9,8},{10,11... | collective-permute-start | bytes 786440 | tf_op jit(solution)/shard_map/ppermute | solution.py:54
  (165 other events, 1167.5 us)

commit v6 on v5

--- a/solution.py
+++ b/solution.py
@@ -63,7 +63,7 @@
 def gather_tiles(vector_bf, indices, block_size):
     snapshots, extent = vector_bf.shape
     vector_tiles = vector_bf.reshape(snapshots, extent // block_size, block_size)
-    return jnp.take(vector_tiles, indices, axis=1, mode="clip")
+    return jnp.take(vector_tiles, indices, axis=1)
 
 
 def place_terms(weighted, indices, n_out):
@@ -74,13 +74,13 @@
 
 
 def forward_terms(vector_bf, blocks, row_index, col_index, n_out):
-    picked = gather_tiles(vector_bf, col_index, blocks.shape[1])
+    picked = gather_tiles(vector_bf, jnp.minimum(col_index, vector_bf.shape[1] // blocks.shape[1] - 1), blocks.shape[1])
     weighted = jnp.einsum("sij,ksj->ksi", blocks, picked, preferred_element_type=jnp.float32)
     return place_terms(weighted, row_index, n_out)
 
 
 def backward_terms(vector_bf, blocks, row_index, col_index, n_out):
-    picked = gather_tiles(vector_bf, row_index, blocks.shape[1])
+    picked = gather_tiles(vector_bf, jnp.minimum(row_index, vector_bf.shape[1] // blocks.shape[1] - 1), blocks.shape[1])
     weighted = jnp.einsum("sji,ksj->ksi", blocks, picked, preferred_element_type=jnp.float32)
     return place_terms(weighted, col_index, n_out)
 

time: 650 us -> 652 us (level)
  transfers between devices with their start and end apart: 126 -> 126, of which waited for: 90 -> 89; matrix products, arithmetic and copies ran while one was open for 33% -> 33% of each run, Pallas kernels for 0% -> 0%
where the time goes in v6:
time: 652 us; the launch traced here: 644 us
  waiting for transfers between devices  304 us (47%)
  matrix products  140 us (21%)
  starting transfers between devices  104 us (16%)
  local copies, waits for them, and re-layouts  57.2 us (9%)
  other arithmetic  36.1 us (6%)
    all_to_all x1, waiting for transfers between devices, per_device(): lax.all_to_all(outgoing.reshape(col_count, capacity, block_size, block_si...  128 us
    ppermute x40, waiting for transfers between devices, big_sum(): held = keep + lax.ppermute(give, axis, partner_pairs(count, distance))  72.9 us
    ppermute x40, waiting for transfers between devices, big_sum(): other = lax.ppermute(held, axis, partner_pairs(count, distance))  72.7 us
    dot_general x8, matrix products, forward_terms(): jnp.einsum('sij,ksj->ksi', blocks, picked, preferred_element_type=jnp.flo...  54.1 us
    dot_general x16, matrix products, place_terms(): jnp.einsum('ksi,st->kti', weighted, onehot, precision=lax.Precision.HIGHEST)  47.6 us
    dot_general x8, matrix products, backward_terms(): jnp.einsum('sji,ksj->ksi', blocks, picked, preferred_element_type=jnp.flo...  38.4 us
    ppermute x44, starting transfers between devices, small_sum(): value = value + lax.ppermute(value, axis, partner_pairs(count, distance))  34.4 us
    gather x16, local copies, waits for them, and re-layouts, gather_tiles(): return jnp.take(vector_tiles, indices, axis=1)  31.8 us
  transfers between devices with their start and end apart: 126, of which 89 were waited for; matrix products, arithmetic and copies ran while one was open for 33% of the time, Pallas kernels for 0%

profile of v6, /device:TPU:0, one launch (start us, length us, event | category | flops | bytes accessed | tf_op | source)
XLA Modules:
  0.0 644.1 jit_solution(3265565995591118748)
XLA Ops:
  5.7 7.3 %all-to-all-start = ((s32[8,24,2]{1,2,0:T(2,128)}), s32[8,24,2]{1,2,0:T(2,128)S(1)}, u32[]{:S(2)}, u32[]{:S(2)}) async-start(s32[8,24,2]{1,2,0:T(2,128)} %broadcast_select_fusion), calls=%async_computation | async-start | bytes 16384 | tf_op jit(solution)/shard_map/all_to_all | solution.py:120
  13.0 8.0 %gather_fusion.1 = bf16[192,128,128]{2,1,0:T(8,128)(2,1)} fusion(bf16[96,128,128]{2,1,0:T(8,128)(2,1)S(1)} %copy-done, s32[1024]{0:T(1024)S(1)} %pad_clamp_fusion.2), kind=kCustom, calls=%fused_computation.17 | custom fusion | bytes 12583680 | tf_op jit(solution)/shard_map/jit(_take)/gather | solution.py:107
  21.0 6.1 all-to-all-start.1
  36.9 127.9 %all-to-all-done.1 = bf16[8,24,128,128]{3,2,1,0:T(8,128)(2,1)} async-done(((bf16[8,24,128,128]{3,2,1,0:T(8,128)(2,1)}), bf16[8,24,128,128]{3,2,1,0:T(8,128)(2,1)}, u32[]{:S(2)}, u32[]{:S(2)}) %all-to-all-start.1) | async-done | bytes 6291488 | tf_op jit(solution)/shard_map/all_to_all | solution.py:113
  209.4 6.7 %convolution_bitcast_fusion.6 = f32[32,192,128]{2,0,1:T(8,128)S(1)} fusion(bf16[192,128,128]{2,1,0:T(8,128)(2,1)} %bitcast.11, bf16[192,32,128]{2,1,0:T(8,128)(2,1)} %gather_fusion.11, pred[192]{0:T(512)(128)(4,1)S(1)} %get-tuple-element.73), kind=kOutput, calls=%fused_computation.56 | convolution fusion | flops 202113024 | bytes 11010240 | tf_op jit(solution)/shard_map/sij,ksj->ksi/dot_general | solution.py:78
  223.8 6.9 %convolution_bitcast_fusion.14 = f32[32,192,128]{2,0,1:T(8,128)S(1)} fusion(bf16[192,128,128]{2,1,0:T(8,128)(2,1)} %bitcast.11, bf16[192,32,128]{2,1,0:T(8,128)(2,1)} %gather_fusion.3, pred[192]{0:T(512)(128)(4,1)S(1)} %get-tuple-element.73), kind=kOutput, calls=%fused_computation.64 | convolution fusion | flops 202113024 | bytes 11010240 | tf_op jit(solution)/shard_map/sij,ksj->ksi/dot_general | solution.py:78
  235.9 4.5 collective-permute-done.9
  262.9 4.1 collective-permute-done.76
  277.9 5.1 convolution_bitcast_fusion.13
  289.8 5.1 convolution_bitcast_fusion.5
  301.9 4.2 collective-permute-done.18
  331.1 6.7 %convolution_bitcast_fusion.12 = f32[32,192,128]{2,0,1:T(8,128)S(1)} fusion(bf16[192,128,128]{2,1,0:T(8,128)(2,1)} %bitcast.11, bf16[192,32,128]{2,1,0:T(8,128)(2,1)} %gather_fusion.5, pred[192]{0:T(512)(128)(4,1)S(1)} %get-tuple-element.73), kind=kOutput, calls=%fused_computation.62 | convolution fusion | flops 202113024 | bytes 11010240 | tf_op jit(solution)/shard_map/sij,ksj->ksi/dot_general | solution.py:78
  345.4 6.7 %convolution_bitcast_fusion.4 = f32[32,192,128]{2,0,1:T(8,128)S(1)} fusion(bf16[192,128,128]{2,1,0:T(8,128)(2,1)} %bitcast.11, bf16[192,32,128]{2,1,0:T(8,128)(2,1)} %gather_fusion.13, pred[192]{0:T(512)(128)(4,1)S(1)} %get-tuple-element.73), kind=kOutput, calls=%fused_computation.54 | convolution fusion | flops 202113024 | bytes 11010240 | tf_op jit(solution)/shard_map/sij,ksj->ksi/dot_general | solution.py:78
  398.8 5.1 convolution_bitcast_fusion.11
  410.4 5.1 convolution_bitcast_fusion.3
  422.6 4.2 collective-permute-done.33
  451.6 7.1 %convolution_bitcast_fusion.10 = f32[32,192,128]{2,0,1:T(8,128)S(1)} fusion(bf16[192,128,128]{2,1,0:T(8,128)(2,1)} %bitcast.11, bf16[192,32,128]{2,1,0:T(8,128)(2,1)} %gather_fusion.7, pred[192]{0:T(512)(128)(4,1)S(1)} %get-tuple-element.73), kind=kOutput, calls=%fused_computation.60 | convolution fusion | flops 202113024 | bytes 11010240 | tf_op jit(solution)/shard_map/sij,ksj->ksi/dot_general | solution.py:78
  467.6 6.7 %convolution_bitcast_fusion.2 = f32[32,192,128]{2,0,1:T(8,128)S(1)} fusion(bf16[192,128,128]{2,1,0:T(8,128)(2,1)} %bitcast.11, bf16[192,32,128]{2,1,0:T(8,128)(2,1)} %gather_fusion.15, pred[192]{0:T(512)(128)(4,1)S(1)} %get-tuple-element.73), kind=kOutput, calls=%fused_computation.52 | convolution fusion | flops 202113024 | bytes 11010240 | tf_op jit(solution)/shard_map/sij,ksj->ksi/dot_general | solution.py:78
  507.0 4.2 collective-permute-done.44
  521.2 5.1 convolution_bitcast_fusion.9
  532.6 5.1 convolution_bitcast_fusion.1
  544.8 4.2 collective-permute-done.48
  571.9 6.7 %convolution_bitcast_fusion.8 = f32[32,192,128]{2,0,1:T(8,128)S(1)} fusion(bf16[192,128,128]{2,1,0:T(8,128)(2,1)} %bitcast.11, bf16[192,32,128]{2,1,0:T(8,128)(2,1)} %gather_fusion.9, pred[192]{0:T(512)(128)(4,1)S(1)} %get-tuple-element.73), kind=kOutput, calls=%fused_computation.58 | convolution fusion | flops 202113024 | bytes 11010240 | tf_op jit(solution)/shard_map/sij,ksj->ksi/dot_general | solution.py:78
  585.2 6.7 %convolution_bitcast_fusion = f32[32,192,128]{2,0,1:T(8,128)S(1)} fusion(bf16[192,128,128]{2,1,0:T(8,128)(2,1)} %bitcast.11, bf16[192,32,128]{2,1,0:T(8,128)(2,1)} %gather_fusion.17, pred[192]{0:T(512)(128)(4,1)S(1)} %get-tuple-element.73), kind=kOutput, calls=%fused_computation.50 | convolution fusion | flops 202113024 | bytes 11010240 | tf_op jit(solution)/shard_map/sij,ksj->ksi/dot_general | solution.py:78
  (661 shorter events, 381.5 us)
Async XLA Ops:
  5.7 15.3 %all-to-all-start = ((s32[8,24,2]{1,2,0:T(2,128)}), s32[8,24,2]{1,2,0:T(2,128)S(1)}, u32[]{:S(2)}, u32[]{:S(2)}) async-start(s32[8,24,2]{1,2,0:T(2,128)} %broadcast_select_fusion), calls=%async_computation | async-start | bytes 16384 | tf_op jit(solution)/shard_map/all_to_all | solution.py:120
  21.0 143.8 %all-to-all-start.1 = ((bf16[8,24,128,128]{3,2,1,0:T(8,128)(2,1)}), bf16[8,24,128,128]{3,2,1,0:T(8,128)(2,1)}, u32[]{:S(2)}, u32[]{:S(2)}) async-start(bf16[8,24,128,128]{3,2,1,0:T(8,128)(2,1)} %bitcast.370), calls=%async_computation.1 | async-start | bytes 12582912 | tf_op jit(solution)/shard_map/all_to_all | solution.py:113
  172.0 8.0 %collective-permute-start.64 = (f32[32,2048]{1,0:T(8,128)S(1)}, f32[32,2048]{1,0:T(8,128)S(1)}, u32[]{:S(2)}, u32[]{:S(2)}) collective-permute-start(f32[32,2048]{1,0:T(8,128)S(1)} %constant_dynamic-slice_fusion.19), channel_id=1, source_target_pairs={{0,8},{8,0},{16,24},{24,16},{1,9},{9,1},{17,25},{25,17},{2,10},{10... | collective-permute-start | bytes 786440 | tf_op jit(solution)/shard_map/ppermute | solution.py:51
  181.7 7.6 %collective-permute-start.3 = (f32[32,1024]{1,0:T(8,128)S(1)}, f32[32,1024]{1,0:T(8,128)S(1)}, u32[]{:S(2)}, u32[]{:S(2)}) collective-permute-start(f32[32,1024]{1,0:T(8,128)S(1)} %constant_dynamic-slice_fusion.38), channel_id=1, source_target_pairs={{0,16},{8,24},{16,0},{24,8},{1,17},{9,25},{17,1},{25,9},{2,18},{10... | collective-permute-start | bytes 393224 | tf_op jit(solution)/shard_map/ppermute | solution.py:51
  204.4 17.2 %collective-permute-start.8 = (f32[32]{0:T(128)S(1)}, f32[32]{0:T(128)S(1)}, u32[]{:S(2)}, u32[]{:S(2)}) collective-permute-start(f32[32]{0:T(128)S(1)} %add.570), channel_id=1, source_target_pairs={{0,4},{1,5},{2,6},{3,7},{4,0},{5,1},{6,2},{7,3},{8,12},{9,13},{10,... | collective-permute-start | bytes 392 | tf_op jit(solution)/shard_map/ppermute | solution.py:29
  220.1 14.5 %collective-permute-start.71 = (f32[32,2048]{1,0:T(8,128)}, f32[32,2048]{1,0:T(8,128)}, u32[]{:S(2)}, u32[]{:S(2)}) collective-permute-start(f32[32,2048]{1,0:T(8,128)} %constant_dynamic-slice_fusion.17), channel_id=1, source_target_pairs={{0,1},{1,0},{2,3},{3,2},{4,5},{5,4},{6,7},{7,6},{8,9},{9,8},{10,11... | collective-permute-start | bytes 786440 | tf_op jit(solution)/shard_map/ppermute | solution.py:51
  262.4 7.4 %collective-permute-start.14 = (f32[32,2048]{1,0:T(8,128)S(1)}, f32[32,2048]{1,0:T(8,128)S(1)}, u32[]{:S(2)}, u32[]{:S(2)}) collective-permute-start(f32[32,2048]{1,0:T(8,128)S(1)} %maximum_select_fusion.26), channel_id=1, source_target_pairs={{0,1},{1,0},{2,3},{3,2},{4,5},{5,4},{6,7},{7,6},{8,9},{9,8},{10,11... | collective-permute-start | bytes 786440 | tf_op jit(solution)/shard_map/ppermute | solution.py:54
  273.7 13.8 %collective-permute-start.78 = (f32[32]{0:T(128)S(1)}, f32[32]{0:T(128)S(1)}, u32[]{:S(2)}, u32[]{:S(2)}) collective-permute-start(f32[32]{0:T(128)S(1)} %add.643), channel_id=1, source_target_pairs={{0,16},{8,24},{16,0},{24,8},{1,17},{9,25},{17,1},{25,9},{2,18},{10... | collective-permute-start | bytes 392 | tf_op jit(solution)/shard_map/ppermute | solution.py:29
  287.5 11.2 %collective-permute-start.17 = (f32[32,2048]{1,0:T(8,128)}, f32[32,2048]{1,0:T(8,128)}, u32[]{:S(2)}, u32[]{:S(2)}) collective-permute-start(f32[32,2048]{1,0:T(8,128)} %constant_dynamic-slice_fusion.34), channel_id=1, source_target_pairs={{0,8},{8,0},{16,24},{24,16},{1,9},{9,1},{17,25},{25,17},{2,10},{10... | collective-permute-start | bytes 786440 | tf_op jit(solution)/shard_map/ppermute | solution.py:51
  301.3 7.6 %collective-permute-start.80 = (f32[32,1024]{1,0:T(8,128)S(1)}, f32[32,1024]{1,0:T(8,128)S(1)}, u32[]{:S(2)}, u32[]{:S(2)}) collective-permute-start(f32[32,1024]{1,0:T(8,128)S(1)} %constant_dynamic-slice_fusion.13), channel_id=1, source_target_pairs={{0,16},{8,24},{16,0},{24,8},{1,17},{9,25},{17,1},{25,9},{2,18},{10... | collective-permute-start | bytes 393224 | tf_op jit(solution)/shard_map/ppermute | solution.py:51
  324.6 17.7 %collective-permute-start.85 = (f32[32]{0:T(128)S(1)}, f32[32]{0:T(128)S(1)}, u32[]{:S(2)}, u32[]{:S(2)}) collective-permute-start(f32[32]{0:T(128)S(1)} %add.650), channel_id=1, source_target_pairs={{0,4},{1,5},{2,6},{3,7},{4,0},{5,1},{6,2},{7,3},{8,12},{9,13},{10,... | collective-permute-start | bytes 392 | tf_op jit(solution)/shard_map/ppermute | solution.py:29
  342.0 15.2 %collective-permute-start.24 = (f32[32,2048]{1,0:T(8,128)}, f32[32,2048]{1,0:T(8,128)}, u32[]{:S(2)}, u32[]{:S(2)}) collective-permute-start(f32[32,2048]{1,0:T(8,128)} %constant_dynamic-slice_fusion.32), channel_id=1, source_target_pairs={{0,1},{1,0},{2,3},{3,2},{4,5},{5,4},{6,7},{7,6},{8,9},{9,8},{10,11... | collective-permute-start | bytes 786440 | tf_op jit(solution)/shard_map/ppermute | solution.py:51
  394.5 13.7 %collective-permute-start.93 = (f32[32]{0:T(128)S(1)}, f32[32]{0:T(128)S(1)}, u32[]{:S(2)}, u32[]{:S(2)}) collective-permute-start(f32[32]{0:T(128)S(1)} %add.656), channel_id=1, source_target_pairs={{0,16},{8,24},{16,0},{24,8},{1,17},{9,25},{17,1},{25,9},{2,18},{10... | collective-permute-start | bytes 392 | tf_op jit(solution)/shard_map/ppermute | solution.py:29
  408.1 11.2 %collective-permute-start.32 = (f32[32,2048]{1,0:T(8,128)}, f32[32,2048]{1,0:T(8,128)}, u32[]{:S(2)}, u32[]{:S(2)}) collective-permute-start(f32[32,2048]{1,0:T(8,128)} %constant_dynamic-slice_fusion.29), channel_id=1, source_target_pairs={{0,8},{8,0},{16,24},{24,16},{1,9},{9,1},{17,25},{25,17},{2,10},{10... | collective-permute-start | bytes 786440 | tf_op jit(solution)/shard_map/ppermute | solution.py:51
  421.9 7.6 %collective-permute-start.95 = (f32[32,1024]{1,0:T(8,128)S(1)}, f32[32,1024]{1,0:T(8,128)S(1)}, u32[]{:S(2)}, u32[]{:S(2)}) collective-permute-start(f32[32,1024]{1,0:T(8,128)S(1)} %constant_dynamic-slice_fusion.8), channel_id=1, source_target_pairs={{0,16},{8,24},{16,0},{24,8},{1,17},{9,25},{17,1},{25,9},{2,18},{10... | collective-permute-start | bytes 393224 | tf_op jit(solution)/shard_map/ppermute | solution.py:51
  446.6 17.9 %collective-permute-start.100 = (f32[32]{0:T(128)S(1)}, f32[32]{0:T(128)S(1)}, u32[]{:S(2)}, u32[]{:S(2)}) collective-permute-start(f32[32]{0:T(128)S(1)} %add.664), channel_id=1, source_target_pairs={{0,4},{1,5},{2,6},{3,7},{4,0},{5,1},{6,2},{7,3},{8,12},{9,13},{10,... | collective-permute-start | bytes 392 | tf_op jit(solution)/shard_map/ppermute | solution.py:29
  462.8 15.2 %collective-permute-start.39 = (f32[32,2048]{1,0:T(8,128)}, f32[32,2048]{1,0:T(8,128)}, u32[]{:S(2)}, u32[]{:S(2)}) collective-permute-start(f32[32,2048]{1,0:T(8,128)} %constant_dynamic-slice_fusion.27), channel_id=1, source_target_pairs={{0,1},{1,0},{2,3},{3,2},{4,5},{5,4},{6,7},{7,6},{8,9},{9,8},{10,11... | collective-permute-start | bytes 786440 | tf_op jit(solution)/shard_map/ppermute | solution.py:51
  506.5 7.5 %collective-permute-start.106 = (f32[32,2048]{1,0:T(8,128)S(1)}, f32[32,2048]{1,0:T(8,128)S(1)}, u32[]{:S(2)}, u32[]{:S(2)}) collective-permute-start(f32[32,2048]{1,0:T(8,128)S(1)} %maximum_select_fusion.44), channel_id=1, source_target_pairs={{0,1},{1,0},{2,3},{3,2},{4,5},{5,4},{6,7},{7,6},{8,9},{9,8},{10,11... | collective-permute-start | bytes 786440 | tf_op jit(solution)/shard_map/ppermute | solution.py:54
  516.9 13.4 %collective-permute-start.108 = (f32[32]{0:T(128)S(1)}, f32[32]{0:T(128)S(1)}, u32[]{:S(2)}, u32[]{:S(2)}) collective-permute-start(f32[32]{0:T(128)S(1)} %add.670), channel_id=1, source_target_pairs={{0,16},{8,24},{16,0},{24,8},{1,17},{9,25},{17,1},{25,9},{2,18},{10... | collective-permute-start | bytes 392 | tf_op jit(solution)/shard_map/ppermute | solution.py:29
  530.3 11.2 %collective-permute-start.47 = (f32[32,2048]{1,0:T(8,128)}, f32[32,2048]{1,0:T(8,128)}, u32[]{:S(2)}, u32[]{:S(2)}) collective-permute-start(f32[32,2048]{1,0:T(8,128)} %constant_dynamic-slice_fusion.24), channel_id=1, source_target_pairs={{0,8},{8,0},{16,24},{24,16},{1,9},{9,1},{17,25},{25,17},{2,10},{10... | collective-permute-start | bytes 786440 | tf_op jit(solution)/shard_map/ppermute | solution.py:51
  544.1 7.6 %collective-permute-start.110 = (f32[32,1024]{1,0:T(8,128)S(1)}, f32[32,1024]{1,0:T(8,128)S(1)}, u32[]{:S(2)}, u32[]{:S(2)}) collective-permute-start(f32[32,1024]{1,0:T(8,128)S(1)} %constant_dynamic-slice_fusion.3), channel_id=1, source_target_pairs={{0,16},{8,24},{16,0},{24,8},{1,17},{9,25},{17,1},{25,9},{2,18},{10... | collective-permute-start | bytes 393224 | tf_op jit(solution)/shard_map/ppermute | solution.py:51
  566.1 16.9 %collective-permute-start.115 = (f32[32]{0:T(128)S(1)}, f32[32]{0:T(128)S(1)}, u32[]{:S(2)}, u32[]{:S(2)}) collective-permute-start(f32[32]{0:T(128)S(1)} %add.678), channel_id=1, source_target_pairs={{0,4},{1,5},{2,6},{3,7},{4,0},{5,1},{6,2},{7,3},{8,12},{9,13},{10,... | collective-permute-start | bytes 392 | tf_op jit(solution)/shard_map/ppermute | solution.py:29
  582.7 14.6 %collective-permute-start.54 = (f32[32,2048]{1,0:T(8,128)}, f32[32,2048]{1,0:T(8,128)}, u32[]{:S(2)}, u32[]{:S(2)}) collective-permute-start(f32[32,2048]{1,0:T(8,128)} %constant_dynamic-slice_fusion.22), channel_id=1, source_target_pairs={{0,1},{1,0},{2,3},{3,2},{4,5},{5,4},{6,7},{7,6},{8,9},{9,8},{10,11... | collective-permute-start | bytes 786440 | tf_op jit(solution)/shard_map/ppermute | solution.py:51
  624.3 7.6 %collective-permute-start.121 = (f32[32,2048]{1,0:T(8,128)S(1)}, f32[32,2048]{1,0:T(8,128)S(1)}, u32[]{:S(2)}, u32[]{:S(2)}) collective-permute-start(f32[32,2048]{1,0:T(8,128)S(1)} %maximum_select_fusion.47), channel_id=1, source_target_pairs={{0,1},{1,0},{2,3},{3,2},{4,5},{5,4},{6,7},{7,6},{8,9},{9,8},{10,11... | collective-permute-start | bytes 786440 | tf_op jit(solution)/shard_map/ppermute | solution.py:54
  (165 other events, 1175.9 us)

commit v7 on v2

--- a/solution.py
+++ b/solution.py
@@ -42,12 +42,14 @@
         distances.append(distance)
         distance *= 2
     held = value
+    last = distances.pop()
     for distance in distances:
         half = held.shape[-1] // 2
         upper = (index // distance) % 2
         keep = lax.dynamic_slice_in_dim(held, upper * half, half, held.ndim - 1)
         give = lax.dynamic_slice_in_dim(held, (1 - upper) * half, half, held.ndim - 1)
         held = keep + lax.ppermute(give, axis, partner_pairs(count, distance))
+    held = held + lax.ppermute(held, axis, partner_pairs(count, last))
     for distance in reversed(distances):
         upper = (index // distance) % 2
         other = lax.ppermute(held, axis, partner_pairs(count, distance))

time: 624 us -> 621 us (level)
    ppermute x0 -> x16, waiting for transfers between devices: none -> 71.5 us  [big_sum(): held = held + lax.ppermute(held, axis, partner_pairs(count, last))]
    ppermute x40 -> x24, waiting for transfers between devices: 77.4 us -> 33.8 us  [big_sum(): held = keep + lax.ppermute(give, axis, partner_pairs(count, distance))]
    ppermute x40 -> x24, waiting for transfers between devices: 69.8 us -> 42.9 us  [big_sum(): other = lax.ppermute(held, axis, partner_pairs(count, distance))]
    ppermute x0 -> x16, starting transfers between devices: none -> 13 us  [big_sum(): held = held + lax.ppermute(held, axis, partner_pairs(count, last))]
    ppermute x40 -> x24, starting transfers between devices: 25.6 us -> 14.8 us  [big_sum(): held = keep + lax.ppermute(give, axis, partner_pairs(count, distance))]
    ppermute x40 -> x24, starting transfers between devices: 25.4 us -> 16.7 us  [big_sum(): other = lax.ppermute(held, axis, partner_pairs(count, distance))]
  transfers between devices with their start and end apart: 126 -> 110, of which waited for: 92 -> 73; matrix products, arithmetic and copies ran while one was open for 31% -> 31% of each run, Pallas kernels for 0% -> 0%
where the time goes in v7:
time: 621 us; the launch traced here: 614 us
  waiting for transfers between devices  305 us (49%)
  matrix products  125 us (20%)
  starting transfers between devices  93.5 us (15%)
  local copies, waits for them, and re-layouts  54.4 us (9%)
  other arithmetic  32.1 us (5%)
    all_to_all x1, waiting for transfers between devices, per_device(): lax.all_to_all(outgoing.reshape(col_count, capacity, block_size, block_si...  128 us
    ppermute x16, waiting for transfers between devices, big_sum(): held = held + lax.ppermute(held, axis, partner_pairs(count, last))  71.5 us
    dot_general x16, matrix products, place_terms(): jnp.einsum('ksi,st->kti', weighted, onehot, precision=lax.Precision.HIGHEST)  47 us
    dot_general x8, matrix products, forward_terms(): jnp.einsum('sij,ksj->ksi', blocks, picked, preferred_element_type=jnp.flo...  44.9 us
    ppermute x24, waiting for transfers between devices, big_sum(): other = lax.ppermute(held, axis, partner_pairs(count, distance))  42.9 us
    ppermute x44, starting transfers between devices, small_sum(): value = value + lax.ppermute(value, axis, partner_pairs(count, distance))  35.7 us
    ppermute x24, waiting for transfers between devices, big_sum(): held = keep + lax.ppermute(give, axis, partner_pairs(count, distance))  33.8 us
    dot_general x8, matrix products, backward_terms(): jnp.einsum('sji,ksj->ksi', blocks, picked, preferred_element_type=jnp.flo...  33.4 us
  transfers between devices with their start and end apart: 110, of which 73 were waited for; matrix products, arithmetic and copies ran while one was open for 31% of the time, Pallas kernels for 0%

profile of v7, /device:TPU:0, one launch (start us, length us, event | category | flops | bytes accessed | tf_op | source)
XLA Modules:
  0.0 613.8 jit_solution(10475681972534747226)
XLA Ops:
  5.4 7.3 %all-to-all-start = ((s32[8,24,2]{1,2,0:T(2,128)}), s32[8,24,2]{1,2,0:T(2,128)S(1)}, u32[]{:S(2)}, u32[]{:S(2)}) async-start(s32[8,24,2]{1,2,0:T(2,128)} %copy.126), calls=%async_computation | async-start | bytes 16384 | tf_op jit(solution)/shard_map/all_to_all | solution.py:119
  16.9 14.7 %scatter_fusion = bf16[192,128,128]{2,1,0:T(8,128)(2,1)} fusion(bf16[192,128,128]{2,1,0:T(8,128)(2,1)} %broadcast_in_dim.14, s32[96]{0:T(128)S(1)} %fusion.170, bf16[96,128,128]{2,1,0:T(8,128)(2,1)} %param.8), kind=kCustom, calls=%fused_computation.17 | custom fusion | bytes 9437568 | tf_op jit(solution)/shard_map/scatter | solution.py:104
  31.6 6.1 all-to-all-start.1
  47.4 127.9 %all-to-all-done.1 = bf16[8,24,128,128]{3,2,1,0:T(8,128)(2,1)} async-done(((bf16[8,24,128,128]{3,2,1,0:T(8,128)(2,1)}), bf16[8,24,128,128]{3,2,1,0:T(8,128)(2,1)}, u32[]{:S(2)}, u32[]{:S(2)}) %all-to-all-start.1) | async-done | bytes 6291488 | tf_op jit(solution)/shard_map/all_to_all | solution.py:112
  175.4 5.1 convolution_bitcast_fusion.7
  194.6 6.5 %collective-permute-done.57 = f32[32,2048]{1,0:T(8,128)S(1)} collective-permute-done((f32[32,2048]{1,0:T(8,128)S(1)}, f32[32,2048]{1,0:T(8,128)S(1)}, u32[]{:S(2)}, u32[]{:S(2)}) %collective-permute-start.57) | collective-permute-done | bytes 262176 | tf_op jit(solution)/shard_map/ppermute | solution.py:52
  219.4 5.5 convolution_bitcast_fusion.6
  231.6 5.9 convolution_bitcast_fusion.14
  253.5 5.8 collective-permute-done.64
  267.0 5.3 collective-permute-done.66
  301.8 7.0 %collective-permute-done.16 = f32[32,2048]{1,0:T(8,128)S(1)} collective-permute-done((f32[32,2048]{1,0:T(8,128)S(1)}, f32[32,2048]{1,0:T(8,128)S(1)}, u32[]{:S(2)}, u32[]{:S(2)}) %collective-permute-start.16) | collective-permute-done | bytes 262176 | tf_op jit(solution)/shard_map/ppermute | solution.py:52
  308.9 5.0 collective-permute-done.70
  328.6 5.5 convolution_bitcast_fusion.12
  340.4 5.7 convolution_bitcast_fusion.4
  410.4 7.0 %collective-permute-done.29 = f32[32,2048]{1,0:T(8,128)S(1)} collective-permute-done((f32[32,2048]{1,0:T(8,128)S(1)}, f32[32,2048]{1,0:T(8,128)S(1)}, u32[]{:S(2)}, u32[]{:S(2)}) %collective-permute-start.29) | collective-permute-done | bytes 262176 | tf_op jit(solution)/shard_map/ppermute | solution.py:52
  417.6 4.6 collective-permute-done.83
  438.1 5.5 convolution_bitcast_fusion.10
  451.3 5.7 convolution_bitcast_fusion.2
  472.5 6.8 %collective-permute-done.36 = f32[32,1024]{1,0:T(8,128)S(1)} collective-permute-done((f32[32,1024]{1,0:T(8,128)S(1)}, f32[32,1024]{1,0:T(8,128)S(1)}, u32[]{:S(2)}, u32[]{:S(2)}) %collective-permute-start.36) | collective-permute-done | bytes 131104 | tf_op jit(solution)/shard_map/ppermute | solution.py:52
  487.0 5.3 collective-permute-done.38
  521.2 7.0 %collective-permute-done.42 = f32[32,2048]{1,0:T(8,128)S(1)} collective-permute-done((f32[32,2048]{1,0:T(8,128)S(1)}, f32[32,2048]{1,0:T(8,128)S(1)}, u32[]{:S(2)}, u32[]{:S(2)}) %collective-permute-start.42) | collective-permute-done | bytes 262176 | tf_op jit(solution)/shard_map/ppermute | solution.py:52
  528.3 4.6 collective-permute-done.96
  546.8 5.5 convolution_bitcast_fusion.8
  557.8 5.7 convolution_bitcast_fusion
  (569 shorter events, 339.8 us)
Async XLA Ops:
  5.4 26.2 %all-to-all-start = ((s32[8,24,2]{1,2,0:T(2,128)}), s32[8,24,2]{1,2,0:T(2,128)S(1)}, u32[]{:S(2)}, u32[]{:S(2)}) async-start(s32[8,24,2]{1,2,0:T(2,128)} %copy.126), calls=%async_computation | async-start | bytes 16384 | tf_op jit(solution)/shard_map/all_to_all | solution.py:119
  31.6 143.8 %all-to-all-start.1 = ((bf16[8,24,128,128]{3,2,1,0:T(8,128)(2,1)}), bf16[8,24,128,128]{3,2,1,0:T(8,128)(2,1)}, u32[]{:S(2)}, u32[]{:S(2)}) async-start(bf16[8,24,128,128]{3,2,1,0:T(8,128)(2,1)} %bitcast.330), calls=%async_computation.1 | async-start | bytes 12582912 | tf_op jit(solution)/shard_map/all_to_all | solution.py:112
  191.8 9.2 %collective-permute-start.57 = (f32[32,2048]{1,0:T(8,128)S(1)}, f32[32,2048]{1,0:T(8,128)S(1)}, u32[]{:S(2)}, u32[]{:S(2)}) collective-permute-start(f32[32,2048]{1,0:T(8,128)S(1)} %dynamic-slice_add_fusion.7), channel_id=1, source_target_pairs={{0,16},{8,24},{16,0},{24,8},{1,17},{9,25},{17,1},{25,9},{2,18},{10... | collective-permute-start | bytes 786440 | tf_op jit(solution)/shard_map/ppermute | solution.py:52
  193.5 12.3 %collective-permute-start.3 = (f32[32,2048]{1,0:T(8,128)S(1)}, f32[32,2048]{1,0:T(8,128)S(1)}, u32[]{:S(2)}, u32[]{:S(2)}) collective-permute-start(f32[32,2048]{1,0:T(8,128)S(1)} %dynamic-slice_add_fusion.15), channel_id=1, source_target_pairs={{0,16},{8,24},{16,0},{24,8},{1,17},{9,25},{17,1},{25,9},{2,18},{10... | collective-permute-start | bytes 786440 | tf_op jit(solution)/shard_map/ppermute | solution.py:52
  215.6 14.9 %collective-permute-start.7 = (f32[32]{0:T(128)S(1)}, f32[32]{0:T(128)S(1)}, u32[]{:S(2)}, u32[]{:S(2)}) collective-permute-start(f32[32]{0:T(128)S(1)} %add.495), channel_id=1, source_target_pairs={{0,4},{1,5},{2,6},{3,7},{4,0},{5,1},{6,2},{7,3},{8,12},{9,13},{10,... | collective-permute-start | bytes 392 | tf_op jit(solution)/shard_map/ppermute | solution.py:28
  229.0 12.4 %collective-permute-start.62 = (f32[32,2048]{1,0:T(8,128)}, f32[32,2048]{1,0:T(8,128)}, u32[]{:S(2)}, u32[]{:S(2)}) collective-permute-start(f32[32,2048]{1,0:T(8,128)} %constant_dynamic-slice_fusion.10), channel_id=1, source_target_pairs={{0,1},{1,0},{2,3},{3,2},{4,5},{5,4},{6,7},{7,6},{8,9},{9,8},{10,11... | collective-permute-start | bytes 786440 | tf_op jit(solution)/shard_map/ppermute | solution.py:51
  249.9 9.4 %collective-permute-start.64 = (f32[32,1024]{1,0:T(8,128)S(1)}, f32[32,1024]{1,0:T(8,128)S(1)}, u32[]{:S(2)}, u32[]{:S(2)}) collective-permute-start(f32[32,1024]{1,0:T(8,128)S(1)} %dynamic-slice_add_fusion.19), channel_id=1, source_target_pairs={{0,4},{1,5},{2,6},{3,7},{4,0},{5,1},{6,2},{7,3},{8,12},{9,13},{10,... | collective-permute-start | bytes 393224 | tf_op jit(solution)/shard_map/ppermute | solution.py:52
  279.1 10.4 %collective-permute-start.68 = (f32[32]{0:T(128)S(1)}, f32[32]{0:T(128)S(1)}, u32[]{:S(2)}, u32[]{:S(2)}) collective-permute-start(f32[32]{0:T(128)S(1)} %add.565), channel_id=1, source_target_pairs={{0,16},{8,24},{16,0},{24,8},{1,17},{9,25},{17,1},{25,9},{2,18},{10... | collective-permute-start | bytes 392 | tf_op jit(solution)/shard_map/ppermute | solution.py:28
  289.3 9.3 %collective-permute-start.15 = (f32[32,2048]{1,0:T(8,128)S(1)}, f32[32,2048]{1,0:T(8,128)}, u32[]{:S(2)}, u32[]{:S(2)}) collective-permute-start(f32[32,2048]{1,0:T(8,128)S(1)} %constant_dynamic-slice_fusion.20), channel_id=1, source_target_pairs={{0,8},{8,0},{16,24},{24,16},{1,9},{9,1},{17,25},{25,17},{2,10},{10... | collective-permute-start | bytes 786440 | tf_op jit(solution)/shard_map/ppermute | solution.py:51
  301.2 12.7 %collective-permute-start.70 = (f32[32,2048]{1,0:T(8,128)S(1)}, f32[32,2048]{1,0:T(8,128)S(1)}, u32[]{:S(2)}, u32[]{:S(2)}) collective-permute-start(f32[32,2048]{1,0:T(8,128)S(1)} %dynamic-slice_add_fusion.5), channel_id=1, source_target_pairs={{0,16},{8,24},{16,0},{24,8},{1,17},{9,25},{17,1},{25,9},{2,18},{10... | collective-permute-start | bytes 786440 | tf_op jit(solution)/shard_map/ppermute | solution.py:52
  323.1 15.4 %collective-permute-start.74 = (f32[32]{0:T(128)S(1)}, f32[32]{0:T(128)S(1)}, u32[]{:S(2)}, u32[]{:S(2)}) collective-permute-start(f32[32]{0:T(128)S(1)} %add.572), channel_id=1, source_target_pairs={{0,4},{1,5},{2,6},{3,7},{4,0},{5,1},{6,2},{7,3},{8,12},{9,13},{10,... | collective-permute-start | bytes 392 | tf_op jit(solution)/shard_map/ppermute | solution.py:28
  338.2 13.1 %collective-permute-start.21 = (f32[32,2048]{1,0:T(8,128)}, f32[32,2048]{1,0:T(8,128)}, u32[]{:S(2)}, u32[]{:S(2)}) collective-permute-start(f32[32,2048]{1,0:T(8,128)} %constant_dynamic-slice_fusion.19), channel_id=1, source_target_pairs={{0,1},{1,0},{2,3},{3,2},{4,5},{5,4},{6,7},{7,6},{8,9},{9,8},{10,11... | collective-permute-start | bytes 786440 | tf_op jit(solution)/shard_map/ppermute | solution.py:51
  372.0 9.3 %collective-permute-start.25 = (f32[32,2048]{1,0:T(8,128)S(1)}, f32[32,2048]{1,0:T(8,128)S(1)}, u32[]{:S(2)}, u32[]{:S(2)}) collective-permute-start(f32[32,2048]{1,0:T(8,128)S(1)} %maximum_select_fusion.25), channel_id=1, source_target_pairs={{0,1},{1,0},{2,3},{3,2},{4,5},{5,4},{6,7},{7,6},{8,9},{9,8},{10,11... | collective-permute-start | bytes 786440 | tf_op jit(solution)/shard_map/ppermute | solution.py:55
  386.9 11.0 %collective-permute-start.81 = (f32[32]{0:T(128)S(1)}, f32[32]{0:T(128)S(1)}, u32[]{:S(2)}, u32[]{:S(2)}) collective-permute-start(f32[32]{0:T(128)S(1)} %add.578), channel_id=1, source_target_pairs={{0,16},{8,24},{16,0},{24,8},{1,17},{9,25},{17,1},{25,9},{2,18},{10... | collective-permute-start | bytes 392 | tf_op jit(solution)/shard_map/ppermute | solution.py:28
  397.9 9.3 %collective-permute-start.28 = (f32[32,2048]{1,0:T(8,128)}, f32[32,2048]{1,0:T(8,128)}, u32[]{:S(2)}, u32[]{:S(2)}) collective-permute-start(f32[32,2048]{1,0:T(8,128)} %constant_dynamic-slice_fusion.17), channel_id=1, source_target_pairs={{0,8},{8,0},{16,24},{24,16},{1,9},{9,1},{17,25},{25,17},{2,10},{10... | collective-permute-start | bytes 786440 | tf_op jit(solution)/shard_map/ppermute | solution.py:51
  409.8 12.4 %collective-permute-start.83 = (f32[32,2048]{1,0:T(8,128)S(1)}, f32[32,2048]{1,0:T(8,128)S(1)}, u32[]{:S(2)}, u32[]{:S(2)}) collective-permute-start(f32[32,2048]{1,0:T(8,128)S(1)} %dynamic-slice_add_fusion.3), channel_id=1, source_target_pairs={{0,16},{8,24},{16,0},{24,8},{1,17},{9,25},{17,1},{25,9},{2,18},{10... | collective-permute-start | bytes 786440 | tf_op jit(solution)/shard_map/ppermute | solution.py:52
  434.2 15.2 %collective-permute-start.87 = (f32[32]{0:T(128)S(1)}, f32[32]{0:T(128)S(1)}, u32[]{:S(2)}, u32[]{:S(2)}) collective-permute-start(f32[32]{0:T(128)S(1)} %add.586), channel_id=1, source_target_pairs={{0,4},{1,5},{2,6},{3,7},{4,0},{5,1},{6,2},{7,3},{8,12},{9,13},{10,... | collective-permute-start | bytes 392 | tf_op jit(solution)/shard_map/ppermute | solution.py:28
  447.7 13.0 %collective-permute-start.34 = (f32[32,2048]{1,0:T(8,128)}, f32[32,2048]{1,0:T(8,128)}, u32[]{:S(2)}, u32[]{:S(2)}) collective-permute-start(f32[32,2048]{1,0:T(8,128)} %constant_dynamic-slice_fusion.16), channel_id=1, source_target_pairs={{0,1},{1,0},{2,3},{3,2},{4,5},{5,4},{6,7},{7,6},{8,9},{9,8},{10,11... | collective-permute-start | bytes 786440 | tf_op jit(solution)/shard_map/ppermute | solution.py:51
  469.2 10.0 %collective-permute-start.36 = (f32[32,1024]{1,0:T(8,128)S(1)}, f32[32,1024]{1,0:T(8,128)S(1)}, u32[]{:S(2)}, u32[]{:S(2)}) collective-permute-start(f32[32,1024]{1,0:T(8,128)S(1)} %dynamic-slice_add_fusion.21), channel_id=1, source_target_pairs={{0,4},{1,5},{2,6},{3,7},{4,0},{5,1},{6,2},{7,3},{8,12},{9,13},{10,... | collective-permute-start | bytes 393224 | tf_op jit(solution)/shard_map/ppermute | solution.py:52
  497.8 11.1 %collective-permute-start.94 = (f32[32]{0:T(128)S(1)}, f32[32]{0:T(128)S(1)}, u32[]{:S(2)}, u32[]{:S(2)}) collective-permute-start(f32[32]{0:T(128)S(1)} %add.592), channel_id=1, source_target_pairs={{0,16},{8,24},{16,0},{24,8},{1,17},{9,25},{17,1},{25,9},{2,18},{10... | collective-permute-start | bytes 392 | tf_op jit(solution)/shard_map/ppermute | solution.py:28
  520.6 12.4 %collective-permute-start.96 = (f32[32,2048]{1,0:T(8,128)S(1)}, f32[32,2048]{1,0:T(8,128)S(1)}, u32[]{:S(2)}, u32[]{:S(2)}) collective-permute-start(f32[32,2048]{1,0:T(8,128)S(1)} %dynamic-slice_add_fusion.1), channel_id=1, source_target_pairs={{0,16},{8,24},{16,0},{24,8},{1,17},{9,25},{17,1},{25,9},{2,18},{10... | collective-permute-start | bytes 786440 | tf_op jit(solution)/shard_map/ppermute | solution.py:52
  542.0 14.7 %collective-permute-start.100 = (f32[32]{0:T(128)S(1)}, f32[32]{0:T(128)S(1)}, u32[]{:S(2)}, u32[]{:S(2)}) collective-permute-start(f32[32]{0:T(128)S(1)} %add.600), channel_id=1, source_target_pairs={{0,4},{1,5},{2,6},{3,7},{4,0},{5,1},{6,2},{7,3},{8,12},{9,13},{10,... | collective-permute-start | bytes 392 | tf_op jit(solution)/shard_map/ppermute | solution.py:28
  556.4 12.3 %collective-permute-start.47 = (f32[32,2048]{1,0:T(8,128)}, f32[32,2048]{1,0:T(8,128)}, u32[]{:S(2)}, u32[]{:S(2)}) collective-permute-start(f32[32,2048]{1,0:T(8,128)} %constant_dynamic-slice_fusion.13), channel_id=1, source_target_pairs={{0,1},{1,0},{2,3},{3,2},{4,5},{5,4},{6,7},{7,6},{8,9},{9,8},{10,11... | collective-permute-start | bytes 786440 | tf_op jit(solution)/shard_map/ppermute | solution.py:51
  590.0 9.6 %collective-permute-start.51 = (f32[32,2048]{1,0:T(8,128)}, f32[32,2048]{1,0:T(8,128)}, u32[]{:S(2)}, u32[]{:S(2)}) collective-permute-start(f32[32,2048]{1,0:T(8,128)} %maximum_select_fusion.27), channel_id=1, source_target_pairs={{0,1},{1,0},{2,3},{3,2},{4,5},{5,4},{6,7},{7,6},{8,9},{9,8},{10,11... | collective-permute-start | bytes 786440 | tf_op jit(solution)/shard_map/ppermute | solution.py:55
  (145 other events, 1109.9 us)

commit v8 on v7

--- a/solution.py
+++ b/solution.py
@@ -70,7 +70,7 @@
 def place_terms(weighted, indices, n_out):
     snapshots, number, block_size = weighted.shape
     onehot = (indices[:, None] == jnp.arange(n_out, dtype=jnp.int32)[None, :]).astype(jnp.float32)
-    summed = jnp.einsum("ksi,st->kti", weighted, onehot, precision=lax.Precision.HIGHEST)
+    summed = jnp.einsum("ksi,st->kti", weighted, onehot, precision=lax.Precision.HIGH)
     return summed.reshape(snapshots, n_out * block_size)
 
 

time: 621 us -> 615 us (level)
  matrix products: 125 us -> 116 us
    dot_general x16, matrix products: 47 us -> 38.1 us  [place_terms(): jnp.einsum('ksi,st->kti', weighted, onehot, precision=lax.Precision.HIGH)]
  transfers between devices with their start and end apart: 110 -> 110, of which waited for: 73 -> 73; matrix products, arithmetic and copies ran while one was open for 31% -> 30% of each run, Pallas kernels for 0% -> 0%
where the time goes in v8:
time: 615 us; the launch traced here: 605 us
  waiting for transfers between devices  305 us (50%)
  matrix products  116 us (19%)
  starting transfers between devices  93.9 us (15%)
  local copies, waits for them, and re-layouts  54.4 us (9%)
  other arithmetic  32.1 us (5%)
    all_to_all x1, waiting for transfers between devices, per_device(): lax.all_to_all(outgoing.reshape(col_count, capacity, block_size, block_si...  128 us
    ppermute x16, waiting for transfers between devices, big_sum(): held = held + lax.ppermute(held, axis, partner_pairs(count, last))  71.3 us
    dot_general x8, matrix products, forward_terms(): jnp.einsum('sij,ksj->ksi', blocks, picked, preferred_element_type=jnp.flo...  44.9 us
    ppermute x24, waiting for transfers between devices, big_sum(): other = lax.ppermute(held, axis, partner_pairs(count, distance))  42.8 us
    dot_general x16, matrix products, place_terms(): jnp.einsum('ksi,st->kti', weighted, onehot, precision=lax.Precision.HIGH)  38.1 us
    ppermute x44, starting transfers between devices, small_sum(): value = value + lax.ppermute(value, axis, partner_pairs(count, distance))  35.8 us
    ppermute x24, waiting for transfers between devices, big_sum(): held = keep + lax.ppermute(give, axis, partner_pairs(count, distance))  33.8 us
    dot_general x8, matrix products, backward_terms(): jnp.einsum('sji,ksj->ksi', blocks, picked, preferred_element_type=jnp.flo...  33.2 us
  transfers between devices with their start and end apart: 110, of which 73 were waited for; matrix products, arithmetic and copies ran while one was open for 30% of the time, Pallas kernels for 0%

profile of v8, /device:TPU:0, one launch (start us, length us, event | category | flops | bytes accessed | tf_op | source)
XLA Modules:
  0.0 604.7 jit_solution(12490090960923210868)
XLA Ops:
  5.4 7.3 %all-to-all-start = ((s32[8,24,2]{1,2,0:T(2,128)}), s32[8,24,2]{1,2,0:T(2,128)S(1)}, u32[]{:S(2)}, u32[]{:S(2)}) async-start(s32[8,24,2]{1,2,0:T(2,128)} %copy.126), calls=%async_computation | async-start | bytes 16384 | tf_op jit(solution)/shard_map/all_to_all | solution.py:119
  16.9 14.6 %scatter_fusion = bf16[192,128,128]{2,1,0:T(8,128)(2,1)} fusion(bf16[192,128,128]{2,1,0:T(8,128)(2,1)} %broadcast_in_dim.14, s32[96]{0:T(128)S(1)} %fusion.170, bf16[96,128,128]{2,1,0:T(8,128)(2,1)} %param.8), kind=kCustom, calls=%fused_computation.17 | custom fusion | bytes 9437568 | tf_op jit(solution)/shard_map/scatter | solution.py:104
  31.5 6.2 %all-to-all-start.1 = ((bf16[8,24,128,128]{3,2,1,0:T(8,128)(2,1)}), bf16[8,24,128,128]{3,2,1,0:T(8,128)(2,1)}, u32[]{:S(2)}, u32[]{:S(2)}) async-start(bf16[8,24,128,128]{3,2,1,0:T(8,128)(2,1)} %bitcast.330), calls=%async_computation.1 | async-start | bytes 12582912 | tf_op jit(solution)/shard_map/all_to_all | solution.py:112
  47.4 127.9 %all-to-all-done.1 = bf16[8,24,128,128]{3,2,1,0:T(8,128)(2,1)} async-done(((bf16[8,24,128,128]{3,2,1,0:T(8,128)(2,1)}), bf16[8,24,128,128]{3,2,1,0:T(8,128)(2,1)}, u32[]{:S(2)}, u32[]{:S(2)}) %all-to-all-start.1) | async-done | bytes 6291488 | tf_op jit(solution)/shard_map/all_to_all | solution.py:112
  175.3 5.1 convolution_bitcast_fusion.7
  193.3 6.4 %collective-permute-done.57 = f32[32,2048]{1,0:T(8,128)S(1)} collective-permute-done((f32[32,2048]{1,0:T(8,128)S(1)}, f32[32,2048]{1,0:T(8,128)S(1)}, u32[]{:S(2)}, u32[]{:S(2)}) %collective-permute-start.57) | collective-permute-done | bytes 262176 | tf_op jit(solution)/shard_map/ppermute | solution.py:52
  218.1 5.8 convolution_bitcast_fusion.6
  230.0 5.5 convolution_bitcast_fusion.14
  251.0 5.8 collective-permute-done.64
  264.5 5.3 collective-permute-done.66
  298.1 7.0 %collective-permute-done.16 = f32[32,2048]{1,0:T(8,128)S(1)} collective-permute-done((f32[32,2048]{1,0:T(8,128)S(1)}, f32[32,2048]{1,0:T(8,128)S(1)}, u32[]{:S(2)}, u32[]{:S(2)}) %collective-permute-start.16) | collective-permute-done | bytes 262176 | tf_op jit(solution)/shard_map/ppermute | solution.py:52
  305.3 5.0 collective-permute-done.70
  325.0 5.7 convolution_bitcast_fusion.12
  336.5 5.5 convolution_bitcast_fusion.4
  404.6 7.0 %collective-permute-done.29 = f32[32,2048]{1,0:T(8,128)S(1)} collective-permute-done((f32[32,2048]{1,0:T(8,128)S(1)}, f32[32,2048]{1,0:T(8,128)S(1)}, u32[]{:S(2)}, u32[]{:S(2)}) %collective-permute-start.29) | collective-permute-done | bytes 262176 | tf_op jit(solution)/shard_map/ppermute | solution.py:52
  411.8 4.6 collective-permute-done.83
  432.3 5.7 convolution_bitcast_fusion.10
  445.1 5.5 convolution_bitcast_fusion.2
  465.5 6.8 %collective-permute-done.36 = f32[32,1024]{1,0:T(8,128)S(1)} collective-permute-done((f32[32,1024]{1,0:T(8,128)S(1)}, f32[32,1024]{1,0:T(8,128)S(1)}, u32[]{:S(2)}, u32[]{:S(2)}) %collective-permute-start.36) | collective-permute-done | bytes 131104 | tf_op jit(solution)/shard_map/ppermute | solution.py:52
  480.1 5.3 collective-permute-done.38
  513.1 7.0 %collective-permute-done.42 = f32[32,2048]{1,0:T(8,128)S(1)} collective-permute-done((f32[32,2048]{1,0:T(8,128)S(1)}, f32[32,2048]{1,0:T(8,128)S(1)}, u32[]{:S(2)}, u32[]{:S(2)}) %collective-permute-start.42) | collective-permute-done | bytes 262176 | tf_op jit(solution)/shard_map/ppermute | solution.py:52
  520.3 4.6 collective-permute-done.96
  538.8 5.7 convolution_bitcast_fusion.8
  549.5 5.5 convolution_bitcast_fusion
  (569 shorter events, 330.9 us)
Async XLA Ops:
  5.4 26.2 %all-to-all-start = ((s32[8,24,2]{1,2,0:T(2,128)}), s32[8,24,2]{1,2,0:T(2,128)S(1)}, u32[]{:S(2)}, u32[]{:S(2)}) async-start(s32[8,24,2]{1,2,0:T(2,128)} %copy.126), calls=%async_computation | async-start | bytes 16384 | tf_op jit(solution)/shard_map/all_to_all | solution.py:119
  31.5 143.8 %all-to-all-start.1 = ((bf16[8,24,128,128]{3,2,1,0:T(8,128)(2,1)}), bf16[8,24,128,128]{3,2,1,0:T(8,128)(2,1)}, u32[]{:S(2)}, u32[]{:S(2)}) async-start(bf16[8,24,128,128]{3,2,1,0:T(8,128)(2,1)} %bitcast.330), calls=%async_computation.1 | async-start | bytes 12582912 | tf_op jit(solution)/shard_map/all_to_all | solution.py:112
  190.4 9.2 %collective-permute-start.57 = (f32[32,2048]{1,0:T(8,128)S(1)}, f32[32,2048]{1,0:T(8,128)S(1)}, u32[]{:S(2)}, u32[]{:S(2)}) collective-permute-start(f32[32,2048]{1,0:T(8,128)S(1)} %dynamic-slice_add_fusion.7), channel_id=1, source_target_pairs={{0,16},{8,24},{16,0},{24,8},{1,17},{9,25},{17,1},{25,9},{2,18},{10... | collective-permute-start | bytes 786440 | tf_op jit(solution)/shard_map/ppermute | solution.py:52
  192.1 12.2 %collective-permute-start.3 = (f32[32,2048]{1,0:T(8,128)S(1)}, f32[32,2048]{1,0:T(8,128)S(1)}, u32[]{:S(2)}, u32[]{:S(2)}) collective-permute-start(f32[32,2048]{1,0:T(8,128)S(1)} %dynamic-slice_add_fusion.15), channel_id=1, source_target_pairs={{0,16},{8,24},{16,0},{24,8},{1,17},{9,25},{17,1},{25,9},{2,18},{10... | collective-permute-start | bytes 786440 | tf_op jit(solution)/shard_map/ppermute | solution.py:52
  214.3 14.7 %collective-permute-start.7 = (f32[32]{0:T(128)S(1)}, f32[32]{0:T(128)S(1)}, u32[]{:S(2)}, u32[]{:S(2)}) collective-permute-start(f32[32]{0:T(128)S(1)} %add.495), channel_id=1, source_target_pairs={{0,4},{1,5},{2,6},{3,7},{4,0},{5,1},{6,2},{7,3},{8,12},{9,13},{10,... | collective-permute-start | bytes 392 | tf_op jit(solution)/shard_map/ppermute | solution.py:28
  227.5 11.4 %collective-permute-start.62 = (f32[32,2048]{1,0:T(8,128)}, f32[32,2048]{1,0:T(8,128)}, u32[]{:S(2)}, u32[]{:S(2)}) collective-permute-start(f32[32,2048]{1,0:T(8,128)} %constant_dynamic-slice_fusion.10), channel_id=1, source_target_pairs={{0,1},{1,0},{2,3},{3,2},{4,5},{5,4},{6,7},{7,6},{8,9},{9,8},{10,11... | collective-permute-start | bytes 786440 | tf_op jit(solution)/shard_map/ppermute | solution.py:51
  247.4 9.4 %collective-permute-start.64 = (f32[32,1024]{1,0:T(8,128)S(1)}, f32[32,1024]{1,0:T(8,128)S(1)}, u32[]{:S(2)}, u32[]{:S(2)}) collective-permute-start(f32[32,1024]{1,0:T(8,128)S(1)} %dynamic-slice_add_fusion.19), channel_id=1, source_target_pairs={{0,4},{1,5},{2,6},{3,7},{4,0},{5,1},{6,2},{7,3},{8,12},{9,13},{10,... | collective-permute-start | bytes 393224 | tf_op jit(solution)/shard_map/ppermute | solution.py:52
  276.6 9.9 %collective-permute-start.68 = (f32[32]{0:T(128)S(1)}, f32[32]{0:T(128)S(1)}, u32[]{:S(2)}, u32[]{:S(2)}) collective-permute-start(f32[32]{0:T(128)S(1)} %add.565), channel_id=1, source_target_pairs={{0,16},{8,24},{16,0},{24,8},{1,17},{9,25},{17,1},{25,9},{2,18},{10... | collective-permute-start | bytes 392 | tf_op jit(solution)/shard_map/ppermute | solution.py:28
  297.6 12.7 %collective-permute-start.70 = (f32[32,2048]{1,0:T(8,128)S(1)}, f32[32,2048]{1,0:T(8,128)S(1)}, u32[]{:S(2)}, u32[]{:S(2)}) collective-permute-start(f32[32,2048]{1,0:T(8,128)S(1)} %dynamic-slice_add_fusion.5), channel_id=1, source_target_pairs={{0,16},{8,24},{16,0},{24,8},{1,17},{9,25},{17,1},{25,9},{2,18},{10... | collective-permute-start | bytes 786440 | tf_op jit(solution)/shard_map/ppermute | solution.py:52
  319.4 15.1 %collective-permute-start.74 = (f32[32]{0:T(128)S(1)}, f32[32]{0:T(128)S(1)}, u32[]{:S(2)}, u32[]{:S(2)}) collective-permute-start(f32[32]{0:T(128)S(1)} %add.572), channel_id=1, source_target_pairs={{0,4},{1,5},{2,6},{3,7},{4,0},{5,1},{6,2},{7,3},{8,12},{9,13},{10,... | collective-permute-start | bytes 392 | tf_op jit(solution)/shard_map/ppermute | solution.py:28
  334.2 12.3 %collective-permute-start.21 = (f32[32,2048]{1,0:T(8,128)}, f32[32,2048]{1,0:T(8,128)}, u32[]{:S(2)}, u32[]{:S(2)}) collective-permute-start(f32[32,2048]{1,0:T(8,128)} %constant_dynamic-slice_fusion.19), channel_id=1, source_target_pairs={{0,1},{1,0},{2,3},{3,2},{4,5},{5,4},{6,7},{7,6},{8,9},{9,8},{10,11... | collective-permute-start | bytes 786440 | tf_op jit(solution)/shard_map/ppermute | solution.py:51
  367.2 9.3 %collective-permute-start.25 = (f32[32,2048]{1,0:T(8,128)S(1)}, f32[32,2048]{1,0:T(8,128)S(1)}, u32[]{:S(2)}, u32[]{:S(2)}) collective-permute-start(f32[32,2048]{1,0:T(8,128)S(1)} %maximum_select_fusion.25), channel_id=1, source_target_pairs={{0,1},{1,0},{2,3},{3,2},{4,5},{5,4},{6,7},{7,6},{8,9},{9,8},{10,11... | collective-permute-start | bytes 786440 | tf_op jit(solution)/shard_map/ppermute | solution.py:55
  382.2 10.8 %collective-permute-start.81 = (f32[32]{0:T(128)S(1)}, f32[32]{0:T(128)S(1)}, u32[]{:S(2)}, u32[]{:S(2)}) collective-permute-start(f32[32]{0:T(128)S(1)} %add.578), channel_id=1, source_target_pairs={{0,16},{8,24},{16,0},{24,8},{1,17},{9,25},{17,1},{25,9},{2,18},{10... | collective-permute-start | bytes 392 | tf_op jit(solution)/shard_map/ppermute | solution.py:28
  402.4 9.2 %collective-permute-start.29 = (f32[32,2048]{1,0:T(8,128)S(1)}, f32[32,2048]{1,0:T(8,128)S(1)}, u32[]{:S(2)}, u32[]{:S(2)}) collective-permute-start(f32[32,2048]{1,0:T(8,128)S(1)} %dynamic-slice_add_fusion.11), channel_id=1, source_target_pairs={{0,16},{8,24},{16,0},{24,8},{1,17},{9,25},{17,1},{25,9},{2,18},{10... | collective-permute-start | bytes 786440 | tf_op jit(solution)/shard_map/ppermute | solution.py:52
  404.1 12.3 %collective-permute-start.83 = (f32[32,2048]{1,0:T(8,128)S(1)}, f32[32,2048]{1,0:T(8,128)S(1)}, u32[]{:S(2)}, u32[]{:S(2)}) collective-permute-start(f32[32,2048]{1,0:T(8,128)S(1)} %dynamic-slice_add_fusion.3), channel_id=1, source_target_pairs={{0,16},{8,24},{16,0},{24,8},{1,17},{9,25},{17,1},{25,9},{2,18},{10... | collective-permute-start | bytes 786440 | tf_op jit(solution)/shard_map/ppermute | solution.py:52
  428.4 14.8 %collective-permute-start.87 = (f32[32]{0:T(128)S(1)}, f32[32]{0:T(128)S(1)}, u32[]{:S(2)}, u32[]{:S(2)}) collective-permute-start(f32[32]{0:T(128)S(1)} %add.586), channel_id=1, source_target_pairs={{0,4},{1,5},{2,6},{3,7},{4,0},{5,1},{6,2},{7,3},{8,12},{9,13},{10,... | collective-permute-start | bytes 392 | tf_op jit(solution)/shard_map/ppermute | solution.py:28
  441.5 12.3 %collective-permute-start.34 = (f32[32,2048]{1,0:T(8,128)}, f32[32,2048]{1,0:T(8,128)}, u32[]{:S(2)}, u32[]{:S(2)}) collective-permute-start(f32[32,2048]{1,0:T(8,128)} %constant_dynamic-slice_fusion.16), channel_id=1, source_target_pairs={{0,1},{1,0},{2,3},{3,2},{4,5},{5,4},{6,7},{7,6},{8,9},{9,8},{10,11... | collective-permute-start | bytes 786440 | tf_op jit(solution)/shard_map/ppermute | solution.py:51
  462.3 10.0 %collective-permute-start.36 = (f32[32,1024]{1,0:T(8,128)S(1)}, f32[32,1024]{1,0:T(8,128)S(1)}, u32[]{:S(2)}, u32[]{:S(2)}) collective-permute-start(f32[32,1024]{1,0:T(8,128)S(1)} %dynamic-slice_add_fusion.21), channel_id=1, source_target_pairs={{0,4},{1,5},{2,6},{3,7},{4,0},{5,1},{6,2},{7,3},{8,12},{9,13},{10,... | collective-permute-start | bytes 393224 | tf_op jit(solution)/shard_map/ppermute | solution.py:52
  491.0 10.7 %collective-permute-start.94 = (f32[32]{0:T(128)S(1)}, f32[32]{0:T(128)S(1)}, u32[]{:S(2)}, u32[]{:S(2)}) collective-permute-start(f32[32]{0:T(128)S(1)} %add.592), channel_id=1, source_target_pairs={{0,16},{8,24},{16,0},{24,8},{1,17},{9,25},{17,1},{25,9},{2,18},{10... | collective-permute-start | bytes 392 | tf_op jit(solution)/shard_map/ppermute | solution.py:28
  510.9 9.2 %collective-permute-start.42 = (f32[32,2048]{1,0:T(8,128)S(1)}, f32[32,2048]{1,0:T(8,128)S(1)}, u32[]{:S(2)}, u32[]{:S(2)}) collective-permute-start(f32[32,2048]{1,0:T(8,128)S(1)} %dynamic-slice_add_fusion.9), channel_id=1, source_target_pairs={{0,16},{8,24},{16,0},{24,8},{1,17},{9,25},{17,1},{25,9},{2,18},{10... | collective-permute-start | bytes 786440 | tf_op jit(solution)/shard_map/ppermute | solution.py:52
  512.6 12.3 %collective-permute-start.96 = (f32[32,2048]{1,0:T(8,128)S(1)}, f32[32,2048]{1,0:T(8,128)S(1)}, u32[]{:S(2)}, u32[]{:S(2)}) collective-permute-start(f32[32,2048]{1,0:T(8,128)S(1)} %dynamic-slice_add_fusion.1), channel_id=1, source_target_pairs={{0,16},{8,24},{16,0},{24,8},{1,17},{9,25},{17,1},{25,9},{2,18},{10... | collective-permute-start | bytes 786440 | tf_op jit(solution)/shard_map/ppermute | solution.py:52
  534.0 14.4 %collective-permute-start.100 = (f32[32]{0:T(128)S(1)}, f32[32]{0:T(128)S(1)}, u32[]{:S(2)}, u32[]{:S(2)}) collective-permute-start(f32[32]{0:T(128)S(1)} %add.600), channel_id=1, source_target_pairs={{0,4},{1,5},{2,6},{3,7},{4,0},{5,1},{6,2},{7,3},{8,12},{9,13},{10,... | collective-permute-start | bytes 392 | tf_op jit(solution)/shard_map/ppermute | solution.py:28
  548.1 11.5 %collective-permute-start.47 = (f32[32,2048]{1,0:T(8,128)}, f32[32,2048]{1,0:T(8,128)}, u32[]{:S(2)}, u32[]{:S(2)}) collective-permute-start(f32[32,2048]{1,0:T(8,128)} %constant_dynamic-slice_fusion.13), channel_id=1, source_target_pairs={{0,1},{1,0},{2,3},{3,2},{4,5},{5,4},{6,7},{7,6},{8,9},{9,8},{10,11... | collective-permute-start | bytes 786440 | tf_op jit(solution)/shard_map/ppermute | solution.py:51
  580.9 9.6 %collective-permute-start.51 = (f32[32,2048]{1,0:T(8,128)}, f32[32,2048]{1,0:T(8,128)}, u32[]{:S(2)}, u32[]{:S(2)}) collective-permute-start(f32[32,2048]{1,0:T(8,128)} %maximum_select_fusion.27), channel_id=1, source_target_pairs={{0,1},{1,0},{2,3},{3,2},{4,5},{5,4},{6,7},{7,6},{8,9},{9,8},{10,11... | collective-permute-start | bytes 786440 | tf_op jit(solution)/shard_map/ppermute | solution.py:55
  (145 other events, 1095.9 us)

commit v9 on v1

--- a/solution.py
+++ b/solution.py
@@ -5,6 +5,7 @@
 
 TC = 32
 ITERS = 4
+CHUNKS = 2
 
 
 EPSILON = 1e-06
@@ -22,11 +23,12 @@
     count = lax.axis_size(axis)
     if not is_power_of_two(count):
         return lax.psum(value, axis)
+    lanes = jnp.split(value, CHUNKS, axis=0)
     distance = 1
     while distance < count:
-        value = value + lax.ppermute(value, axis, partner_pairs(count, distance))
+        lanes = [lane + lax.ppermute(lane, axis, partner_pairs(count, distance)) for lane in lanes]
         distance *= 2
-    return value
+    return jnp.concatenate(lanes, axis=0)
 
 
 def big_sum(value, axis):
@@ -40,22 +42,30 @@
     while distance < count:
         distances.append(distance)
         distance *= 2
-    held = value
+    lanes = jnp.split(value, CHUNKS, axis=0)
+    last = distances.pop()
     for distance in distances:
-        half = held.shape[-1] // 2
         upper = (index // distance) % 2
-        keep = lax.dynamic_slice_in_dim(held, upper * half, half, held.ndim - 1)
-        give = lax.dynamic_slice_in_dim(held, (1 - upper) * half, half, held.ndim - 1)
-        held = keep + lax.ppermute(give, axis, partner_pairs(count, distance))
+        moved = []
+        for held in lanes:
+            half = held.shape[-1] // 2
+            keep = lax.dynamic_slice_in_dim(held, upper * half, half, held.ndim - 1)
+            give = lax.dynamic_slice_in_dim(held, (1 - upper) * half, half, held.ndim - 1)
+            moved.append(keep + lax.ppermute(give, axis, partner_pairs(count, distance)))
+        lanes = moved
+    lanes = [held + lax.ppermute(held, axis, partner_pairs(count, last)) for held in lanes]
     for distance in reversed(distances):
         upper = (index // distance) % 2
-        other = lax.ppermute(held, axis, partner_pairs(count, distance))
-        held = jnp.where(
-            upper == 1,
-            jnp.concatenate([other, held], axis=-1),
-            jnp.concatenate([held, other], axis=-1),
-        )
-    return held
+        moved = []
+        for held in lanes:
+            other = lax.ppermute(held, axis, partner_pairs(count, distance))
+            moved.append(jnp.where(
+                upper == 1,
+                jnp.concatenate([other, held], axis=-1),
+                jnp.concatenate([held, other], axis=-1),
+            ))
+        lanes = moved
+    return jnp.concatenate(lanes, axis=0)
 
 
 def gather_tiles(vector_bf, indices, block_size):
@@ -67,7 +77,7 @@
 def place_terms(weighted, indices, n_out):
     snapshots, number, block_size = weighted.shape
     onehot = (indices[:, None] == jnp.arange(n_out, dtype=jnp.int32)[None, :]).astype(jnp.float32)
-    summed = jnp.einsum("ksi,st->kti", weighted, onehot, precision=lax.Precision.HIGHEST)
+    summed = jnp.einsum("ksi,st->kti", weighted, onehot, precision=lax.Precision.HIGH)
     return summed.reshape(snapshots, n_out * block_size)
 
 

time: 662 us -> 601 us (0.908)
  waiting for transfers between devices: 430 us -> 307 us
  starting transfers between devices: 59.6 us -> 123 us
  matrix products: 103 us -> 92.8 us
  other arithmetic: 16.6 us -> 23.4 us
    ppermute x20 -> x24, waiting for transfers between devices: 116 us -> 35.9 us  [big_sum(): other = lax.ppermute(held, axis, partner_pairs(count, distance))]
    ppermute x42 -> x84, starting transfers between devices: 32.9 us -> 89.3 us  [the longest x44 40.5 us: small_sum(): lax.ppermute(lane, axis, partner_pairs(count, distance))]
    ppermute x42 -> x84, waiting for transfers between devices: 185 us -> 144 us  [the longest x16 63.6 us: big_sum(): lax.ppermute(held, axis, partner_pairs(count, last))]
    dot_general x8, matrix products: 47.9 us -> 37.9 us  [place_terms(): jnp.einsum('ksi,st->kti', weighted, onehot, precision=lax.Precision.HIGH)]
    ppermute x20 -> x24, starting transfers between devices: 12.7 us -> 19.5 us  [big_sum(): other = lax.ppermute(held, axis, partner_pairs(count, distance))]
  transfers between devices with their start and end apart: 64 -> 110, of which waited for: 63 -> 98; matrix products, arithmetic and copies ran while one was open for 3% -> 5% of each run, Pallas kernels for 0% -> 0%
where the time goes in v9:
time: 601 us; the launch traced here: 597 us
  waiting for transfers between devices  307 us (51%)
  starting transfers between devices  123 us (20%)
  matrix products  92.8 us (15%)
  local copies, waits for them, and re-layouts  48.9 us (8%)
  other arithmetic  23.4 us (4%)
    all_to_all x1, waiting for transfers between devices, per_device(): lax.all_to_all(outgoing.reshape(col_count, capacity, block_size, block_si...  127 us
    ppermute x16, waiting for transfers between devices, big_sum(): lax.ppermute(held, axis, partner_pairs(count, last))  63.6 us
    ppermute x44, waiting for transfers between devices, small_sum(): lax.ppermute(lane, axis, partner_pairs(count, distance))  42 us
    ppermute x44, starting transfers between devices, small_sum(): lax.ppermute(lane, axis, partner_pairs(count, distance))  40.5 us
    ppermute x24, waiting for transfers between devices, big_sum(): lax.ppermute(give, axis, partner_pairs(count, distance))  38.2 us
    dot_general x8, matrix products, place_terms(): jnp.einsum('ksi,st->kti', weighted, onehot, precision=lax.Precision.HIGH)  37.9 us
    ppermute x24, waiting for transfers between devices, big_sum(): other = lax.ppermute(held, axis, partner_pairs(count, distance))  35.9 us
    dot_general x4, matrix products, forward_terms(): jnp.einsum('sij,ksj->ksi', blocks, picked, preferred_element_type=jnp.flo...  32.6 us
  transfers between devices with their start and end apart: 110, of which 98 were waited for; matrix products, arithmetic and copies ran while one was open for 5% of the time, Pallas kernels for 0%

profile of v9, /device:TPU:0, one launch (start us, length us, event | category | flops | bytes accessed | tf_op | source)
XLA Modules:
  0.0 597.5 jit_solution(4243123663695650956)
XLA Ops:
  5.4 7.3 %all-to-all-start = ((s32[8,24,2]{1,2,0:T(2,128)}), s32[8,24,2]{1,2,0:T(2,128)S(1)}, u32[]{:S(2)}, u32[]{:S(2)}) async-start(s32[8,24,2]{1,2,0:T(2,128)} %copy.102), calls=%async_computation | async-start | bytes 16384 | tf_op jit(solution)/shard_map/all_to_all | solution.py:126
  16.9 12.7 %scatter_fusion = bf16[192,128,128]{2,1,0:T(8,128)(2,1)} fusion(bf16[192,128,128]{2,1,0:T(8,128)(2,1)} %broadcast_in_dim.14, s32[96]{0:T(128)S(1)} %fusion.137, bf16[96,128,128]{2,1,0:T(8,128)(2,1)S(1)} %copy-done.17), kind=kCustom, calls=%fused_computation.9 | custom fusion | bytes 9437568 | tf_op jit(solution)/shard_map/scatter | solution.py:111
  29.6 6.6 %all-to-all-start.1 = ((bf16[8,24,128,128]{3,2,1,0:T(8,128)(2,1)}), bf16[8,24,128,128]{3,2,1,0:T(8,128)(2,1)}, u32[]{:S(2)}, u32[]{:S(2)}) async-start(bf16[8,24,128,128]{3,2,1,0:T(8,128)(2,1)} %bitcast.274), calls=%async_computation.1 | async-start | bytes 12582912 | tf_op jit(solution)/shard_map/all_to_all | solution.py:119
  46.1 127.3 %all-to-all-done.1 = bf16[8,24,128,128]{3,2,1,0:T(8,128)(2,1)} async-done(((bf16[8,24,128,128]{3,2,1,0:T(8,128)(2,1)}), bf16[8,24,128,128]{3,2,1,0:T(8,128)(2,1)}, u32[]{:S(2)}, u32[]{:S(2)}) %all-to-all-start.1) | async-done | bytes 6291488 | tf_op jit(solution)/shard_map/all_to_all | solution.py:119
  173.4 5.6 fusion.48
  179.0 4.7 fusion.80
  187.9 7.0 %collective-permute-done.5 = f32[32,2048]{1,0:T(8,128)S(1)} collective-permute-done((f32[32,2048]{1,0:T(8,128)S(1)}, f32[32,2048]{1,0:T(8,128)S(1)}, u32[]{:S(2)}, u32[]{:S(2)}) %collective-permute-start.5) | collective-permute-done | bytes 262176 | tf_op jit(solution)/shard_map/ppermute | solution.py:56
  218.0 8.2 %fusion.51 = f32[64,192,128]{2,0,1:T(8,128)S(1)} fusion(bf16[192,128,128]{2,1,0:T(8,128)(2,1)} %bitcast.11, bf16[192,64,128]{2,1,0:T(8,128)(2,1)} %gather_fusion.1, pred[192]{0:T(512)(128)(4,1)S(1)} %get-tuple-element.91), kind=kOutput, calls=%fused_computation.59 | convolution fusion | flops 404226048 | bytes 15728832 | tf_op jit(solution)/shard_map/sij,ksj->ksi/dot_general | solution.py:86
  233.8 5.0 collective-permute-done.16
  276.7 5.6 fusion.54
  282.3 4.9 fusion.86
  291.4 7.0 %collective-permute-done.31 = f32[32,2048]{1,0:T(8,128)S(1)} collective-permute-done((f32[32,2048]{1,0:T(8,128)S(1)}, f32[32,2048]{1,0:T(8,128)S(1)}, u32[]{:S(2)}, u32[]{:S(2)}) %collective-permute-start.31) | collective-permute-done | bytes 262176 | tf_op jit(solution)/shard_map/ppermute | solution.py:56
  323.2 8.1 %fusion.57 = f32[64,192,128]{2,0,1:T(8,128)S(1)} fusion(bf16[192,128,128]{2,1,0:T(8,128)(2,1)} %bitcast.11, bf16[192,64,128]{2,1,0:T(8,128)(2,1)} %gather_fusion.3, pred[192]{0:T(512)(128)(4,1)S(1)} %get-tuple-element.91), kind=kOutput, calls=%fused_computation.61 | convolution fusion | flops 404226048 | bytes 15728832 | tf_op jit(solution)/shard_map/sij,ksj->ksi/dot_general | solution.py:86
  331.3 5.1 fusion.89
  339.2 4.9 collective-permute-done.42
  381.5 5.6 fusion.60
  396.1 7.0 %collective-permute-done.57 = f32[32,2048]{1,0:T(8,128)S(1)} collective-permute-done((f32[32,2048]{1,0:T(8,128)S(1)}, f32[32,2048]{1,0:T(8,128)S(1)}, u32[]{:S(2)}, u32[]{:S(2)}) %collective-permute-start.57) | collective-permute-done | bytes 262176 | tf_op jit(solution)/shard_map/ppermute | solution.py:56
  429.5 8.1 %fusion.63 = f32[64,192,128]{2,0,1:T(8,128)S(1)} fusion(bf16[192,128,128]{2,1,0:T(8,128)(2,1)} %bitcast.11, bf16[192,64,128]{2,1,0:T(8,128)(2,1)} %gather_fusion.5, pred[192]{0:T(512)(128)(4,1)S(1)} %get-tuple-element.91), kind=kOutput, calls=%fused_computation.63 | convolution fusion | flops 404226048 | bytes 15728832 | tf_op jit(solution)/shard_map/sij,ksj->ksi/dot_general | solution.py:86
  445.2 5.0 collective-permute-done.68
  488.5 5.6 fusion.66
  494.1 4.7 fusion.98
  503.0 7.0 %collective-permute-done.83 = f32[32,2048]{1,0:T(8,128)S(1)} collective-permute-done((f32[32,2048]{1,0:T(8,128)S(1)}, f32[32,2048]{1,0:T(8,128)S(1)}, u32[]{:S(2)}, u32[]{:S(2)}) %collective-permute-start.83) | collective-permute-done | bytes 262176 | tf_op jit(solution)/shard_map/ppermute | solution.py:56
  535.5 8.3 %fusion.69 = f32[64,192,128]{2,0,1:T(8,128)S(1)} fusion(bf16[192,128,128]{2,1,0:T(8,128)(2,1)} %bitcast.11, bf16[192,64,128]{2,1,0:T(8,128)(2,1)} %gather_fusion.7, pred[192]{0:T(512)(128)(4,1)S(1)} %get-tuple-element.91), kind=kOutput, calls=%fused_computation.65 | convolution fusion | flops 404226048 | bytes 15728832 | tf_op jit(solution)/shard_map/sij,ksj->ksi/dot_general | solution.py:86
  551.4 4.8 collective-permute-done.94
  (499 shorter events, 319.0 us)
Async XLA Ops:
  5.4 24.2 %all-to-all-start = ((s32[8,24,2]{1,2,0:T(2,128)}), s32[8,24,2]{1,2,0:T(2,128)S(1)}, u32[]{:S(2)}, u32[]{:S(2)}) async-start(s32[8,24,2]{1,2,0:T(2,128)} %copy.102), calls=%async_computation | async-start | bytes 16384 | tf_op jit(solution)/shard_map/all_to_all | solution.py:126
  29.6 143.8 %all-to-all-start.1 = ((bf16[8,24,128,128]{3,2,1,0:T(8,128)(2,1)}), bf16[8,24,128,128]{3,2,1,0:T(8,128)(2,1)}, u32[]{:S(2)}, u32[]{:S(2)}) async-start(bf16[8,24,128,128]{3,2,1,0:T(8,128)(2,1)} %bitcast.274), calls=%async_computation.1 | async-start | bytes 12582912 | tf_op jit(solution)/shard_map/all_to_all | solution.py:119
  185.7 9.2 %collective-permute-start.5 = (f32[32,2048]{1,0:T(8,128)S(1)}, f32[32,2048]{1,0:T(8,128)S(1)}, u32[]{:S(2)}, u32[]{:S(2)}) collective-permute-start(f32[32,2048]{1,0:T(8,128)S(1)} %dynamic-slice_add_fusion.15), channel_id=1, source_target_pairs={{0,16},{8,24},{16,0},{24,8},{1,17},{9,25},{17,1},{25,9},{2,18},{10... | collective-permute-start | bytes 786440 | tf_op jit(solution)/shard_map/ppermute | solution.py:56
  187.3 12.4 %collective-permute-start.8 = (f32[32,2048]{1,0:T(8,128)S(1)}, f32[32,2048]{1,0:T(8,128)S(1)}, u32[]{:S(2)}, u32[]{:S(2)}) collective-permute-start(f32[32,2048]{1,0:T(8,128)S(1)} %dynamic-slice_add_fusion.14), channel_id=1, source_target_pairs={{0,16},{8,24},{16,0},{24,8},{1,17},{9,25},{17,1},{25,9},{2,18},{10... | collective-permute-start | bytes 786440 | tf_op jit(solution)/shard_map/ppermute | solution.py:56
  231.3 7.5 %collective-permute-start.16 = (f32[32,2048]{1,0:T(8,128)S(1)}, f32[32,2048]{1,0:T(8,128)S(1)}, u32[]{:S(2)}, u32[]{:S(2)}) collective-permute-start(f32[32,2048]{1,0:T(8,128)S(1)} %constant_dynamic-slice_fusion.21), channel_id=1, source_target_pairs={{0,1},{1,0},{2,3},{3,2},{4,5},{5,4},{6,7},{7,6},{8,9},{9,8},{10,11... | collective-permute-start | bytes 786440 | tf_op jit(solution)/shard_map/ppermute | solution.py:54
  233.0 8.6 %collective-permute-start.21 = (f32[32,2048]{1,0:T(8,128)S(1)}, f32[32,2048]{1,0:T(8,128)S(1)}, u32[]{:S(2)}, u32[]{:S(2)}) collective-permute-start(f32[32,2048]{1,0:T(8,128)S(1)} %constant_dynamic-slice_fusion.19), channel_id=1, source_target_pairs={{0,1},{1,0},{2,3},{3,2},{4,5},{5,4},{6,7},{7,6},{8,9},{9,8},{10,11... | collective-permute-start | bytes 786440 | tf_op jit(solution)/shard_map/ppermute | solution.py:54
  244.4 7.5 %collective-permute-start.18 = (f32[32,1024]{1,0:T(8,128)S(1)}, f32[32,1024]{1,0:T(8,128)S(1)}, u32[]{:S(2)}, u32[]{:S(2)}) collective-permute-start(f32[32,1024]{1,0:T(8,128)S(1)} %dynamic-slice_add_fusion.23), channel_id=1, source_target_pairs={{0,4},{1,5},{2,6},{3,7},{4,0},{5,1},{6,2},{7,3},{8,12},{9,13},{10,... | collective-permute-start | bytes 393224 | tf_op jit(solution)/shard_map/ppermute | solution.py:56
  289.2 9.2 %collective-permute-start.31 = (f32[32,2048]{1,0:T(8,128)S(1)}, f32[32,2048]{1,0:T(8,128)S(1)}, u32[]{:S(2)}, u32[]{:S(2)}) collective-permute-start(f32[32,2048]{1,0:T(8,128)S(1)} %dynamic-slice_add_fusion.11), channel_id=1, source_target_pairs={{0,16},{8,24},{16,0},{24,8},{1,17},{9,25},{17,1},{25,9},{2,18},{10... | collective-permute-start | bytes 786440 | tf_op jit(solution)/shard_map/ppermute | solution.py:56
  289.9 13.4 %collective-permute-start.34 = (f32[32,2048]{1,0:T(8,128)S(1)}, f32[32,2048]{1,0:T(8,128)S(1)}, u32[]{:S(2)}, u32[]{:S(2)}) collective-permute-start(f32[32,2048]{1,0:T(8,128)S(1)} %dynamic-slice_add_fusion.10), channel_id=1, source_target_pairs={{0,16},{8,24},{16,0},{24,8},{1,17},{9,25},{17,1},{25,9},{2,18},{10... | collective-permute-start | bytes 786440 | tf_op jit(solution)/shard_map/ppermute | solution.py:56
  336.7 7.4 %collective-permute-start.42 = (f32[32,2048]{1,0:T(8,128)S(1)}, f32[32,2048]{1,0:T(8,128)S(1)}, u32[]{:S(2)}, u32[]{:S(2)}) collective-permute-start(f32[32,2048]{1,0:T(8,128)S(1)} %constant_dynamic-slice_fusion.15), channel_id=1, source_target_pairs={{0,1},{1,0},{2,3},{3,2},{4,5},{5,4},{6,7},{7,6},{8,9},{9,8},{10,11... | collective-permute-start | bytes 786440 | tf_op jit(solution)/shard_map/ppermute | solution.py:54
  338.8 8.1 %collective-permute-start.47 = (f32[32,2048]{1,0:T(8,128)S(1)}, f32[32,2048]{1,0:T(8,128)S(1)}, u32[]{:S(2)}, u32[]{:S(2)}) collective-permute-start(f32[32,2048]{1,0:T(8,128)S(1)} %constant_dynamic-slice_fusion.13), channel_id=1, source_target_pairs={{0,1},{1,0},{2,3},{3,2},{4,5},{5,4},{6,7},{7,6},{8,9},{9,8},{10,11... | collective-permute-start | bytes 786440 | tf_op jit(solution)/shard_map/ppermute | solution.py:54
  353.4 7.5 %collective-permute-start.49 = (f32[32,1024]{1,0:T(8,128)S(1)}, f32[32,1024]{1,0:T(8,128)S(1)}, u32[]{:S(2)}, u32[]{:S(2)}) collective-permute-start(f32[32,1024]{1,0:T(8,128)S(1)} %dynamic-slice_add_fusion.20), channel_id=1, source_target_pairs={{0,4},{1,5},{2,6},{3,7},{4,0},{5,1},{6,2},{7,3},{8,12},{9,13},{10,... | collective-permute-start | bytes 393224 | tf_op jit(solution)/shard_map/ppermute | solution.py:56
  361.9 7.6 %collective-permute-start.46 = (f32[32,2048]{1,0:T(8,128)S(1)}, f32[32,2048]{1,0:T(8,128)S(1)}, u32[]{:S(2)}, u32[]{:S(2)}) collective-permute-start(f32[32,2048]{1,0:T(8,128)S(1)} %maximum_select_fusion.26), channel_id=1, source_target_pairs={{0,1},{1,0},{2,3},{3,2},{4,5},{5,4},{6,7},{7,6},{8,9},{9,8},{10,11... | collective-permute-start | bytes 786440 | tf_op jit(solution)/shard_map/ppermute | solution.py:61
  393.9 9.2 %collective-permute-start.57 = (f32[32,2048]{1,0:T(8,128)S(1)}, f32[32,2048]{1,0:T(8,128)S(1)}, u32[]{:S(2)}, u32[]{:S(2)}) collective-permute-start(f32[32,2048]{1,0:T(8,128)S(1)} %dynamic-slice_add_fusion.7), channel_id=1, source_target_pairs={{0,16},{8,24},{16,0},{24,8},{1,17},{9,25},{17,1},{25,9},{2,18},{10... | collective-permute-start | bytes 786440 | tf_op jit(solution)/shard_map/ppermute | solution.py:56
  395.5 12.4 %collective-permute-start.60 = (f32[32,2048]{1,0:T(8,128)S(1)}, f32[32,2048]{1,0:T(8,128)S(1)}, u32[]{:S(2)}, u32[]{:S(2)}) collective-permute-start(f32[32,2048]{1,0:T(8,128)S(1)} %dynamic-slice_add_fusion.6), channel_id=1, source_target_pairs={{0,16},{8,24},{16,0},{24,8},{1,17},{9,25},{17,1},{25,9},{2,18},{10... | collective-permute-start | bytes 786440 | tf_op jit(solution)/shard_map/ppermute | solution.py:56
  442.7 7.5 %collective-permute-start.68 = (f32[32,2048]{1,0:T(8,128)S(1)}, f32[32,2048]{1,0:T(8,128)S(1)}, u32[]{:S(2)}, u32[]{:S(2)}) collective-permute-start(f32[32,2048]{1,0:T(8,128)S(1)} %constant_dynamic-slice_fusion.9), channel_id=1, source_target_pairs={{0,1},{1,0},{2,3},{3,2},{4,5},{5,4},{6,7},{7,6},{8,9},{9,8},{10,11... | collective-permute-start | bytes 786440 | tf_op jit(solution)/shard_map/ppermute | solution.py:54
  443.9 9.0 %collective-permute-start.73 = (f32[32,2048]{1,0:T(8,128)S(1)}, f32[32,2048]{1,0:T(8,128)S(1)}, u32[]{:S(2)}, u32[]{:S(2)}) collective-permute-start(f32[32,2048]{1,0:T(8,128)S(1)} %constant_dynamic-slice_fusion.7), channel_id=1, source_target_pairs={{0,1},{1,0},{2,3},{3,2},{4,5},{5,4},{6,7},{7,6},{8,9},{9,8},{10,11... | collective-permute-start | bytes 786440 | tf_op jit(solution)/shard_map/ppermute | solution.py:54
  455.8 7.5 %collective-permute-start.70 = (f32[32,1024]{1,0:T(8,128)S(1)}, f32[32,1024]{1,0:T(8,128)S(1)}, u32[]{:S(2)}, u32[]{:S(2)}) collective-permute-start(f32[32,1024]{1,0:T(8,128)S(1)} %dynamic-slice_add_fusion.19), channel_id=1, source_target_pairs={{0,4},{1,5},{2,6},{3,7},{4,0},{5,1},{6,2},{7,3},{8,12},{9,13},{10,... | collective-permute-start | bytes 393224 | tf_op jit(solution)/shard_map/ppermute | solution.py:56
  459.4 7.6 %collective-permute-start.75 = (f32[32,1024]{1,0:T(8,128)S(1)}, f32[32,1024]{1,0:T(8,128)S(1)}, u32[]{:S(2)}, u32[]{:S(2)}) collective-permute-start(f32[32,1024]{1,0:T(8,128)S(1)} %dynamic-slice_add_fusion.18), channel_id=1, source_target_pairs={{0,4},{1,5},{2,6},{3,7},{4,0},{5,1},{6,2},{7,3},{8,12},{9,13},{10,... | collective-permute-start | bytes 393224 | tf_op jit(solution)/shard_map/ppermute | solution.py:56
  500.8 9.2 %collective-permute-start.83 = (f32[32,2048]{1,0:T(8,128)S(1)}, f32[32,2048]{1,0:T(8,128)S(1)}, u32[]{:S(2)}, u32[]{:S(2)}) collective-permute-start(f32[32,2048]{1,0:T(8,128)S(1)} %dynamic-slice_add_fusion.3), channel_id=1, source_target_pairs={{0,16},{8,24},{16,0},{24,8},{1,17},{9,25},{17,1},{25,9},{2,18},{10... | collective-permute-start | bytes 786440 | tf_op jit(solution)/shard_map/ppermute | solution.py:56
  501.5 13.4 %collective-permute-start.86 = (f32[32,2048]{1,0:T(8,128)S(1)}, f32[32,2048]{1,0:T(8,128)S(1)}, u32[]{:S(2)}, u32[]{:S(2)}) collective-permute-start(f32[32,2048]{1,0:T(8,128)S(1)} %dynamic-slice_add_fusion.2), channel_id=1, source_target_pairs={{0,16},{8,24},{16,0},{24,8},{1,17},{9,25},{17,1},{25,9},{2,18},{10... | collective-permute-start | bytes 786440 | tf_op jit(solution)/shard_map/ppermute | solution.py:56
  548.9 7.3 %collective-permute-start.94 = (f32[32,2048]{1,0:T(8,128)S(1)}, f32[32,2048]{1,0:T(8,128)S(1)}, u32[]{:S(2)}, u32[]{:S(2)}) collective-permute-start(f32[32,2048]{1,0:T(8,128)S(1)} %constant_dynamic-slice_fusion.3), channel_id=1, source_target_pairs={{0,1},{1,0},{2,3},{3,2},{4,5},{5,4},{6,7},{7,6},{8,9},{9,8},{10,11... | collective-permute-start | bytes 786440 | tf_op jit(solution)/shard_map/ppermute | solution.py:54
  550.7 8.3 %collective-permute-start.99 = (f32[32,2048]{1,0:T(8,128)S(1)}, f32[32,2048]{1,0:T(8,128)S(1)}, u32[]{:S(2)}, u32[]{:S(2)}) collective-permute-start(f32[32,2048]{1,0:T(8,128)S(1)} %constant_dynamic-slice_fusion.1), channel_id=1, source_target_pairs={{0,1},{1,0},{2,3},{3,2},{4,5},{5,4},{6,7},{7,6},{8,9},{9,8},{10,11... | collective-permute-start | bytes 786440 | tf_op jit(solution)/shard_map/ppermute | solution.py:54
  565.7 7.6 %collective-permute-start.101 = (f32[32,1024]{1,0:T(8,128)S(1)}, f32[32,1024]{1,0:T(8,128)S(1)}, u32[]{:S(2)}, u32[]{:S(2)}) collective-permute-start(f32[32,1024]{1,0:T(8,128)S(1)} %dynamic-slice_add_fusion.16), channel_id=1, source_target_pairs={{0,4},{1,5},{2,6},{3,7},{4,0},{5,1},{6,2},{7,3},{8,12},{9,13},{10,... | collective-permute-start | bytes 393224 | tf_op jit(solution)/shard_map/ppermute | solution.py:56
  (111 other events, 1010.8 us)

commit v10 on v9

--- a/solution.py
+++ b/solution.py
@@ -5,7 +5,7 @@
 
 TC = 32
 ITERS = 4
-CHUNKS = 2
+CHUNKS = 4
 
 
 EPSILON = 1e-06

time: 601 us -> 621 us (1.033)
  starting transfers between devices: 123 us -> 206 us
  waiting for transfers between devices: 307 us -> 242 us
    ppermute x44 -> x88, starting transfers between devices: 40.5 us -> 81.3 us  [small_sum(): lax.ppermute(lane, axis, partner_pairs(count, distance))]
    ppermute x24 -> x48, waiting for transfers between devices: 38.2 us -> 12.9 us  [big_sum(): lax.ppermute(give, axis, partner_pairs(count, distance))]
    ppermute x16 -> x32, waiting for transfers between devices: 63.6 us -> 41.4 us  [big_sum(): lax.ppermute(held, axis, partner_pairs(count, last))]
    ppermute x24 -> x48, starting transfers between devices: 19.5 us -> 35 us  [big_sum(): other = lax.ppermute(held, axis, partner_pairs(count, distance))]
    ppermute x16 -> x32, starting transfers between devices: 23.6 us -> 38.9 us  [big_sum(): lax.ppermute(held, axis, partner_pairs(count, last))]
    ppermute x24 -> x48, waiting for transfers between devices: 35.9 us -> 23.5 us  [big_sum(): other = lax.ppermute(held, axis, partner_pairs(count, distance))]
    ppermute x24 -> x48, starting transfers between devices: 25.2 us -> 36.5 us  [big_sum(): lax.ppermute(give, axis, partner_pairs(count, distance))]
    ppermute x44 -> x88, waiting for transfers between devices: 42 us -> 39.3 us  [small_sum(): lax.ppermute(lane, axis, partner_pairs(count, distance))]
  transfers between devices with their start and end apart: 110 -> 218, of which waited for: 98 -> 121; matrix products, arithmetic and copies ran while one was open for 5% -> 5% of each run, Pallas kernels for 0% -> 0%
where the time goes in v10:
time: 621 us; the launch traced here: 618 us
  waiting for transfers between devices  242 us (39%)
  starting transfers between devices  206 us (33%)
  matrix products  93.2 us (15%)
  local copies, waits for them, and re-layouts  49.8 us (8%)
  other arithmetic  23.8 us (4%)
    all_to_all x1, waiting for transfers between devices, per_device(): lax.all_to_all(outgoing.reshape(col_count, capacity, block_size, block_si...  125 us
    ppermute x88, starting transfers between devices, small_sum(): lax.ppermute(lane, axis, partner_pairs(count, distance))  81.3 us
    ppermute x32, waiting for transfers between devices, big_sum(): lax.ppermute(held, axis, partner_pairs(count, last))  41.4 us
    ppermute x88, waiting for transfers between devices, small_sum(): lax.ppermute(lane, axis, partner_pairs(count, distance))  39.3 us
    ppermute x32, starting transfers between devices, big_sum(): lax.ppermute(held, axis, partner_pairs(count, last))  38.9 us
    dot_general x8, matrix products, place_terms(): jnp.einsum('ksi,st->kti', weighted, onehot, precision=lax.Precision.HIGH)  37.9 us
    ppermute x48, starting transfers between devices, big_sum(): lax.ppermute(give, axis, partner_pairs(count, distance))  36.5 us
    ppermute x48, starting transfers between devices, big_sum(): other = lax.ppermute(held, axis, partner_pairs(count, distance))  35 us
  transfers between devices with their start and end apart: 218, of which 121 were waited for; matrix products, arithmetic and copies ran while one was open for 5% of the time, Pallas kernels for 0%

profile of v10, /device:TPU:0, one launch (start us, length us, event | category | flops | bytes accessed | tf_op | source)
XLA Modules:
  0.0 617.7 jit_solution(14454765106330569804)
XLA Ops:
  5.4 7.3 %all-to-all-start = ((s32[8,24,2]{1,2,0:T(2,128)}), s32[8,24,2]{1,2,0:T(2,128)S(1)}, u32[]{:S(2)}, u32[]{:S(2)}) async-start(s32[8,24,2]{1,2,0:T(2,128)} %copy.166), calls=%async_computation | async-start | bytes 16384 | tf_op jit(solution)/shard_map/all_to_all | solution.py:126
  12.6 4.2 broadcast_in_dim.14
  16.8 12.7 %scatter_fusion = bf16[192,128,128]{2,1,0:T(8,128)(2,1)} fusion(bf16[192,128,128]{2,1,0:T(8,128)(2,1)} %broadcast_in_dim.14, s32[96]{0:T(128)S(1)} %fusion.137, bf16[96,128,128]{2,1,0:T(8,128)(2,1)S(1)} %copy-done.9), kind=kCustom, calls=%fused_computation.9 | custom fusion | bytes 9437568 | tf_op jit(solution)/shard_map/scatter | solution.py:111
  29.5 6.6 %all-to-all-start.1 = ((bf16[8,24,128,128]{3,2,1,0:T(8,128)(2,1)}), bf16[8,24,128,128]{3,2,1,0:T(8,128)(2,1)}, u32[]{:S(2)}, u32[]{:S(2)}) async-start(bf16[8,24,128,128]{3,2,1,0:T(8,128)(2,1)} %bitcast.418), calls=%async_computation.1 | async-start | bytes 12582912 | tf_op jit(solution)/shard_map/all_to_all | solution.py:119
  48.6 124.7 %all-to-all-done.1 = bf16[8,24,128,128]{3,2,1,0:T(8,128)(2,1)} async-done(((bf16[8,24,128,128]{3,2,1,0:T(8,128)(2,1)}), bf16[8,24,128,128]{3,2,1,0:T(8,128)(2,1)}, u32[]{:S(2)}, u32[]{:S(2)}) %all-to-all-start.1) | async-done | bytes 6291488 | tf_op jit(solution)/shard_map/all_to_all | solution.py:119
  173.3 5.6 fusion.48
  178.8 4.7 fusion.80
  212.6 2.8 collective-permute-start.25
  220.3 3.0 gather_fusion.1
  223.3 8.1 %fusion.51 = f32[64,192,128]{2,0,1:T(8,128)S(1)} fusion(bf16[192,128,128]{2,1,0:T(8,128)(2,1)} %bitcast.11, bf16[192,64,128]{2,1,0:T(8,128)(2,1)} %gather_fusion.1, pred[192]{0:T(512)(128)(4,1)S(1)} %get-tuple-element.144), kind=kOutput, calls=%fused_computation.59 | convolution fusion | flops 404226048 | bytes 15728832 | tf_op jit(solution)/shard_map/sij,ksj->ksi/dot_general | solution.py:86
  231.3 4.7 fusion.83
  278.5 3.0 gather_fusion.2
  281.5 5.6 fusion.54
  287.0 4.7 fusion.86
  333.8 8.4 %fusion.57 = f32[64,192,128]{2,0,1:T(8,128)S(1)} fusion(bf16[192,128,128]{2,1,0:T(8,128)(2,1)} %bitcast.11, bf16[192,64,128]{2,1,0:T(8,128)(2,1)} %gather_fusion.3, pred[192]{0:T(512)(128)(4,1)S(1)} %get-tuple-element.144), kind=kOutput, calls=%fused_computation.61 | convolution fusion | flops 404226048 | bytes 15728832 | tf_op jit(solution)/shard_map/sij,ksj->ksi/dot_general | solution.py:86
  342.3 4.7 fusion.89
  390.4 5.7 fusion.60
  396.2 4.7 fusion.92
  445.2 8.3 %fusion.63 = f32[64,192,128]{2,0,1:T(8,128)S(1)} fusion(bf16[192,128,128]{2,1,0:T(8,128)(2,1)} %bitcast.11, bf16[192,64,128]{2,1,0:T(8,128)(2,1)} %gather_fusion.5, pred[192]{0:T(512)(128)(4,1)S(1)} %get-tuple-element.144), kind=kOutput, calls=%fused_computation.63 | convolution fusion | flops 404226048 | bytes 15728832 | tf_op jit(solution)/shard_map/sij,ksj->ksi/dot_general | solution.py:86
  453.4 4.7 fusion.95
  502.5 5.6 fusion.66
  508.1 5.1 fusion.98
  556.7 8.1 %fusion.69 = f32[64,192,128]{2,0,1:T(8,128)S(1)} fusion(bf16[192,128,128]{2,1,0:T(8,128)(2,1)} %bitcast.11, bf16[192,64,128]{2,1,0:T(8,128)(2,1)} %gather_fusion.7, pred[192]{0:T(512)(128)(4,1)S(1)} %get-tuple-element.144), kind=kOutput, calls=%fused_computation.65 | convolution fusion | flops 404226048 | bytes 15728832 | tf_op jit(solution)/shard_map/sij,ksj->ksi/dot_general | solution.py:86
  564.8 4.8 fusion.101
  (885 shorter events, 356.8 us)
Async XLA Ops:
  5.4 24.1 %all-to-all-start = ((s32[8,24,2]{1,2,0:T(2,128)}), s32[8,24,2]{1,2,0:T(2,128)S(1)}, u32[]{:S(2)}, u32[]{:S(2)}) async-start(s32[8,24,2]{1,2,0:T(2,128)} %copy.166), calls=%async_computation | async-start | bytes 16384 | tf_op jit(solution)/shard_map/all_to_all | solution.py:126
  29.5 143.8 %all-to-all-start.1 = ((bf16[8,24,128,128]{3,2,1,0:T(8,128)(2,1)}), bf16[8,24,128,128]{3,2,1,0:T(8,128)(2,1)}, u32[]{:S(2)}, u32[]{:S(2)}) async-start(bf16[8,24,128,128]{3,2,1,0:T(8,128)(2,1)} %bitcast.418), calls=%async_computation.1 | async-start | bytes 12582912 | tf_op jit(solution)/shard_map/all_to_all | solution.py:119
  187.3 7.6 %collective-permute-start.18 = (f32[16,2048]{1,0:T(8,128)S(1)}, f32[16,2048]{1,0:T(8,128)S(1)}, u32[]{:S(2)}, u32[]{:S(2)}) collective-permute-start(f32[16,2048]{1,0:T(8,128)S(1)} %dynamic-slice_add_fusion.28), channel_id=1, source_target_pairs={{0,16},{8,24},{16,0},{24,8},{1,17},{9,25},{17,1},{25,9},{2,18},{10... | collective-permute-start | bytes 393224 | tf_op jit(solution)/shard_map/ppermute | solution.py:56
  187.8 9.8 %collective-permute-start.15 = (f32[16,2048]{1,0:T(8,128)S(1)}, f32[16,2048]{1,0:T(8,128)S(1)}, u32[]{:S(2)}, u32[]{:S(2)}) collective-permute-start(f32[16,2048]{1,0:T(8,128)S(1)} %dynamic-slice_add_fusion.29), channel_id=1, source_target_pairs={{0,16},{8,24},{16,0},{24,8},{1,17},{9,25},{17,1},{25,9},{2,18},{10... | collective-permute-start | bytes 393224 | tf_op jit(solution)/shard_map/ppermute | solution.py:56
  189.5 10.1 %collective-permute-start.12 = (f32[16,2048]{1,0:T(8,128)S(1)}, f32[16,2048]{1,0:T(8,128)S(1)}, u32[]{:S(2)}, u32[]{:S(2)}) collective-permute-start(f32[16,2048]{1,0:T(8,128)S(1)} %dynamic-slice_add_fusion.30), channel_id=1, source_target_pairs={{0,16},{8,24},{16,0},{24,8},{1,17},{9,25},{17,1},{25,9},{2,18},{10... | collective-permute-start | bytes 393224 | tf_op jit(solution)/shard_map/ppermute | solution.py:56
  192.0 7.7 %collective-permute-start.10 = (f32[16,2048]{1,0:T(8,128)S(1)}, f32[16,2048]{1,0:T(8,128)S(1)}, u32[]{:S(2)}, u32[]{:S(2)}) collective-permute-start(f32[16,2048]{1,0:T(8,128)S(1)} %add.935), channel_id=1, source_target_pairs={{0,8},{8,0},{16,24},{24,16},{1,9},{9,1},{17,25},{25,17},{2,10},{10... | collective-permute-start | bytes 393224 | tf_op jit(solution)/shard_map/ppermute | solution.py:61
  294.4 8.7 %collective-permute-start.70 = (f32[16,2048]{1,0:T(8,128)S(1)}, f32[16,2048]{1,0:T(8,128)S(1)}, u32[]{:S(2)}, u32[]{:S(2)}) collective-permute-start(f32[16,2048]{1,0:T(8,128)S(1)} %dynamic-slice_add_fusion.20), channel_id=1, source_target_pairs={{0,16},{8,24},{16,0},{24,8},{1,17},{9,25},{17,1},{25,9},{2,18},{10... | collective-permute-start | bytes 393224 | tf_op jit(solution)/shard_map/ppermute | solution.py:56
  296.1 9.8 %collective-permute-start.67 = (f32[16,2048]{1,0:T(8,128)S(1)}, f32[16,2048]{1,0:T(8,128)S(1)}, u32[]{:S(2)}, u32[]{:S(2)}) collective-permute-start(f32[16,2048]{1,0:T(8,128)S(1)} %dynamic-slice_add_fusion.21), channel_id=1, source_target_pairs={{0,16},{8,24},{16,0},{24,8},{1,17},{9,25},{17,1},{25,9},{2,18},{10... | collective-permute-start | bytes 393224 | tf_op jit(solution)/shard_map/ppermute | solution.py:56
  296.7 11.2 %collective-permute-start.64 = (f32[16,2048]{1,0:T(8,128)S(1)}, f32[16,2048]{1,0:T(8,128)S(1)}, u32[]{:S(2)}, u32[]{:S(2)}) collective-permute-start(f32[16,2048]{1,0:T(8,128)S(1)} %dynamic-slice_add_fusion.22), channel_id=1, source_target_pairs={{0,16},{8,24},{16,0},{24,8},{1,17},{9,25},{17,1},{25,9},{2,18},{10... | collective-permute-start | bytes 393224 | tf_op jit(solution)/shard_map/ppermute | solution.py:56
  300.3 7.6 %collective-permute-start.62 = (f32[16,2048]{1,0:T(8,128)S(1)}, f32[16,2048]{1,0:T(8,128)S(1)}, u32[]{:S(2)}, u32[]{:S(2)}) collective-permute-start(f32[16,2048]{1,0:T(8,128)S(1)} %add.984), channel_id=1, source_target_pairs={{0,8},{8,0},{16,24},{24,16},{1,9},{9,1},{17,25},{25,17},{2,10},{10... | collective-permute-start | bytes 393224 | tf_op jit(solution)/shard_map/ppermute | solution.py:61
  356.7 6.8 %collective-permute-start.90 = (f32[16,1024]{1,0:T(8,128)S(1)}, f32[16,1024]{1,0:T(8,128)S(1)}, u32[]{:S(2)}, u32[]{:S(2)}) collective-permute-start(f32[16,1024]{1,0:T(8,128)S(1)} %constant_dynamic-slice_fusion.28), channel_id=1, source_target_pairs={{0,2},{1,3},{2,0},{3,1},{4,6},{5,7},{6,4},{7,5},{8,10},{9,11},{10,... | collective-permute-start | bytes 196616 | tf_op jit(solution)/shard_map/ppermute | solution.py:54
  357.6 6.9 %collective-permute-start.86 = (f32[16,1024]{1,0:T(8,128)S(1)}, f32[16,1024]{1,0:T(8,128)S(1)}, u32[]{:S(2)}, u32[]{:S(2)}) collective-permute-start(f32[16,1024]{1,0:T(8,128)S(1)} %dynamic-slice_add_fusion.43), channel_id=1, source_target_pairs={{0,4},{1,5},{2,6},{3,7},{4,0},{5,1},{6,2},{7,3},{8,12},{9,13},{10,... | collective-permute-start | bytes 196616 | tf_op jit(solution)/shard_map/ppermute | solution.py:56
  404.6 7.6 %collective-permute-start.122 = (f32[16,2048]{1,0:T(8,128)S(1)}, f32[16,2048]{1,0:T(8,128)S(1)}, u32[]{:S(2)}, u32[]{:S(2)}) collective-permute-start(f32[16,2048]{1,0:T(8,128)S(1)} %dynamic-slice_add_fusion.12), channel_id=1, source_target_pairs={{0,16},{8,24},{16,0},{24,8},{1,17},{9,25},{17,1},{25,9},{2,18},{10... | collective-permute-start | bytes 393224 | tf_op jit(solution)/shard_map/ppermute | solution.py:56
  405.2 9.8 %collective-permute-start.119 = (f32[16,2048]{1,0:T(8,128)S(1)}, f32[16,2048]{1,0:T(8,128)S(1)}, u32[]{:S(2)}, u32[]{:S(2)}) collective-permute-start(f32[16,2048]{1,0:T(8,128)S(1)} %dynamic-slice_add_fusion.13), channel_id=1, source_target_pairs={{0,16},{8,24},{16,0},{24,8},{1,17},{9,25},{17,1},{25,9},{2,18},{10... | collective-permute-start | bytes 393224 | tf_op jit(solution)/shard_map/ppermute | solution.py:56
  406.8 10.1 %collective-permute-start.116 = (f32[16,2048]{1,0:T(8,128)S(1)}, f32[16,2048]{1,0:T(8,128)S(1)}, u32[]{:S(2)}, u32[]{:S(2)}) collective-permute-start(f32[16,2048]{1,0:T(8,128)S(1)} %dynamic-slice_add_fusion.14), channel_id=1, source_target_pairs={{0,16},{8,24},{16,0},{24,8},{1,17},{9,25},{17,1},{25,9},{2,18},{10... | collective-permute-start | bytes 393224 | tf_op jit(solution)/shard_map/ppermute | solution.py:56
  409.4 7.7 %collective-permute-start.114 = (f32[16,2048]{1,0:T(8,128)S(1)}, f32[16,2048]{1,0:T(8,128)S(1)}, u32[]{:S(2)}, u32[]{:S(2)}) collective-permute-start(f32[16,2048]{1,0:T(8,128)S(1)} %add.1028), channel_id=1, source_target_pairs={{0,8},{8,0},{16,24},{24,16},{1,9},{9,1},{17,25},{25,17},{2,10},{10... | collective-permute-start | bytes 393224 | tf_op jit(solution)/shard_map/ppermute | solution.py:61
  468.6 6.9 %collective-permute-start.138 = (f32[16,1024]{1,0:T(8,128)S(1)}, f32[16,1024]{1,0:T(8,128)S(1)}, u32[]{:S(2)}, u32[]{:S(2)}) collective-permute-start(f32[16,1024]{1,0:T(8,128)S(1)} %dynamic-slice_add_fusion.39), channel_id=1, source_target_pairs={{0,4},{1,5},{2,6},{3,7},{4,0},{5,1},{6,2},{7,3},{8,12},{9,13},{10,... | collective-permute-start | bytes 196616 | tf_op jit(solution)/shard_map/ppermute | solution.py:56
  515.9 8.6 %collective-permute-start.174 = (f32[16,2048]{1,0:T(8,128)S(1)}, f32[16,2048]{1,0:T(8,128)S(1)}, u32[]{:S(2)}, u32[]{:S(2)}) collective-permute-start(f32[16,2048]{1,0:T(8,128)S(1)} %dynamic-slice_add_fusion.4), channel_id=1, source_target_pairs={{0,16},{8,24},{16,0},{24,8},{1,17},{9,25},{17,1},{25,9},{2,18},{10... | collective-permute-start | bytes 393224 | tf_op jit(solution)/shard_map/ppermute | solution.py:56
  517.5 9.8 %collective-permute-start.171 = (f32[16,2048]{1,0:T(8,128)S(1)}, f32[16,2048]{1,0:T(8,128)S(1)}, u32[]{:S(2)}, u32[]{:S(2)}) collective-permute-start(f32[16,2048]{1,0:T(8,128)S(1)} %dynamic-slice_add_fusion.5), channel_id=1, source_target_pairs={{0,16},{8,24},{16,0},{24,8},{1,17},{9,25},{17,1},{25,9},{2,18},{10... | collective-permute-start | bytes 393224 | tf_op jit(solution)/shard_map/ppermute | solution.py:56
  518.1 11.2 %collective-permute-start.168 = (f32[16,2048]{1,0:T(8,128)S(1)}, f32[16,2048]{1,0:T(8,128)S(1)}, u32[]{:S(2)}, u32[]{:S(2)}) collective-permute-start(f32[16,2048]{1,0:T(8,128)S(1)} %dynamic-slice_add_fusion.6), channel_id=1, source_target_pairs={{0,16},{8,24},{16,0},{24,8},{1,17},{9,25},{17,1},{25,9},{2,18},{10... | collective-permute-start | bytes 393224 | tf_op jit(solution)/shard_map/ppermute | solution.py:56
  521.7 7.7 %collective-permute-start.166 = (f32[16,2048]{1,0:T(8,128)S(1)}, f32[16,2048]{1,0:T(8,128)S(1)}, u32[]{:S(2)}, u32[]{:S(2)}) collective-permute-start(f32[16,2048]{1,0:T(8,128)S(1)} %add.1073), channel_id=1, source_target_pairs={{0,8},{8,0},{16,24},{24,16},{1,9},{9,1},{17,25},{25,17},{2,10},{10... | collective-permute-start | bytes 393224 | tf_op jit(solution)/shard_map/ppermute | solution.py:61
  580.2 6.9 %collective-permute-start.190 = (f32[16,1024]{1,0:T(8,128)S(1)}, f32[16,1024]{1,0:T(8,128)S(1)}, u32[]{:S(2)}, u32[]{:S(2)}) collective-permute-start(f32[16,1024]{1,0:T(8,128)S(1)} %dynamic-slice_add_fusion.35), channel_id=1, source_target_pairs={{0,4},{1,5},{2,6},{3,7},{4,0},{5,1},{6,2},{7,3},{8,12},{9,13},{10,... | collective-permute-start | bytes 196616 | tf_op jit(solution)/shard_map/ppermute | solution.py:56
  587.1 6.8 %collective-permute-start.191 = (f32[16,1024]{1,0:T(8,128)S(1)}, f32[16,1024]{1,0:T(8,128)}, u32[]{:S(2)}, u32[]{:S(2)}) collective-permute-start(f32[16,1024]{1,0:T(8,128)S(1)} %add.1095), channel_id=1, source_target_pairs={{0,2},{1,3},{2,0},{3,1},{4,6},{5,7},{6,4},{7,5},{8,10},{9,11},{10,... | collective-permute-start | bytes 196616 | tf_op jit(solution)/shard_map/ppermute | solution.py:61
  588.7 7.2 %collective-permute-start.206 = (f32[16,1024]{1,0:T(8,128)S(1)}, f32[16,1024]{1,0:T(8,128)S(1)}, u32[]{:S(2)}, u32[]{:S(2)}) collective-permute-start(f32[16,1024]{1,0:T(8,128)S(1)} %add.1104), channel_id=1, source_target_pairs={{0,2},{1,3},{2,0},{3,1},{4,6},{5,7},{6,4},{7,5},{8,10},{9,11},{10,... | collective-permute-start | bytes 196616 | tf_op jit(solution)/shard_map/ppermute | solution.py:61
  (227 other events, 1640.0 us)

commit v11 on v9

--- a/solution.py
+++ b/solution.py
@@ -23,12 +23,11 @@
     count = lax.axis_size(axis)
     if not is_power_of_two(count):
         return lax.psum(value, axis)
-    lanes = jnp.split(value, CHUNKS, axis=0)
     distance = 1
     while distance < count:
-        lanes = [lane + lax.ppermute(lane, axis, partner_pairs(count, distance)) for lane in lanes]
+        value = value + lax.ppermute(value, axis, partner_pairs(count, distance))
         distance *= 2
-    return jnp.concatenate(lanes, axis=0)
+    return value
 
 
 def big_sum(value, axis):

time: 601 us -> 583 us (0.970)
  starting transfers between devices: 123 us -> 66.9 us
  waiting for transfers between devices: 307 us -> 352 us
  other arithmetic: 23.4 us -> 17 us
    ppermute x44 -> x22, starting transfers between devices: 40.5 us -> 14.7 us  [small_sum(): value = value + lax.ppermute(value, axis, partner_pairs(count, distance))]
    ppermute x24, waiting for transfers between devices: 38.2 us -> 54.2 us  [big_sum(): lax.ppermute(give, axis, partner_pairs(count, distance))]
    ppermute x44 -> x22, waiting for transfers between devices: 42 us -> 54.5 us  [small_sum(): value = value + lax.ppermute(value, axis, partner_pairs(count, distance))]
    ppermute x24, starting transfers between devices: 25.2 us -> 13.9 us  [big_sum(): lax.ppermute(give, axis, partner_pairs(count, distance))]
    ppermute x24, starting transfers between devices: 19.5 us -> 9.82 us  [big_sum(): other = lax.ppermute(held, axis, partner_pairs(count, distance))]
    ppermute x16, starting transfers between devices: 23.6 us -> 15 us  [big_sum(): lax.ppermute(held, axis, partner_pairs(count, last))]
    ppermute x16, waiting for transfers between devices: 63.6 us -> 71.6 us  [big_sum(): lax.ppermute(held, axis, partner_pairs(count, last))]
    ppermute x24, waiting for transfers between devices: 35.9 us -> 42.4 us  [big_sum(): other = lax.ppermute(held, axis, partner_pairs(count, distance))]
  transfers between devices with their start and end apart: 110 -> 88, of which waited for: 98 -> 79; matrix products, arithmetic and copies ran while one was open for 5% -> 4% of each run, Pallas kernels for 0% -> 0%
where the time goes in v11:
time: 583 us; the launch traced here: 580 us
  waiting for transfers between devices  352 us (60%)
  matrix products  92.7 us (16%)
  starting transfers between devices  66.9 us (11%)
  local copies, waits for them, and re-layouts  49 us (8%)
  other arithmetic  17 us (3%)
    all_to_all x1, waiting for transfers between devices, per_device(): lax.all_to_all(outgoing.reshape(col_count, capacity, block_size, block_si...  130 us
    ppermute x16, waiting for transfers between devices, big_sum(): lax.ppermute(held, axis, partner_pairs(count, last))  71.6 us
    ppermute x22, waiting for transfers between devices, small_sum(): value = value + lax.ppermute(value, axis, partner_pairs(count, distance))  54.5 us
    ppermute x24, waiting for transfers between devices, big_sum(): lax.ppermute(give, axis, partner_pairs(count, distance))  54.2 us
    ppermute x24, waiting for transfers between devices, big_sum(): other = lax.ppermute(held, axis, partner_pairs(count, distance))  42.4 us
    dot_general x8, matrix products, place_terms(): jnp.einsum('ksi,st->kti', weighted, onehot, precision=lax.Precision.HIGH)  37.8 us
    dot_general x4, matrix products, forward_terms(): jnp.einsum('sij,ksj->ksi', blocks, picked, preferred_element_type=jnp.flo...  32.6 us
    gather x8, local copies, waits for them, and re-layouts, gather_tiles(): return jnp.take(vector_tiles, indices, axis=1)  22.7 us
  transfers between devices with their start and end apart: 88, of which 79 were waited for; matrix products, arithmetic and copies ran while one was open for 4% of the time, Pallas kernels for 0%

profile of v11, /device:TPU:0, one launch (start us, length us, event | category | flops | bytes accessed | tf_op | source)
XLA Modules:
  0.0 580.3 jit_solution(651249470991116027)
XLA Ops:
  5.4 7.3 %all-to-all-start = ((s32[8,24,2]{1,2,0:T(2,128)}), s32[8,24,2]{1,2,0:T(2,128)S(1)}, u32[]{:S(2)}, u32[]{:S(2)}) async-start(s32[8,24,2]{1,2,0:T(2,128)} %copy.102), calls=%async_computation | async-start | bytes 16384 | tf_op jit(solution)/shard_map/all_to_all | solution.py:125
  17.0 12.8 %scatter_fusion = bf16[192,128,128]{2,1,0:T(8,128)(2,1)} fusion(bf16[192,128,128]{2,1,0:T(8,128)(2,1)} %broadcast_in_dim.14, s32[96]{0:T(128)S(1)} %fusion.137, bf16[96,128,128]{2,1,0:T(8,128)(2,1)S(1)} %copy-done.17), kind=kCustom, calls=%fused_computation.9 | custom fusion | bytes 9437568 | tf_op jit(solution)/shard_map/scatter | solution.py:110
  29.8 6.2 %all-to-all-start.1 = ((bf16[8,24,128,128]{3,2,1,0:T(8,128)(2,1)}), bf16[8,24,128,128]{3,2,1,0:T(8,128)(2,1)}, u32[]{:S(2)}, u32[]{:S(2)}) async-start(bf16[8,24,128,128]{3,2,1,0:T(8,128)(2,1)} %bitcast.274), calls=%async_computation.1 | async-start | bytes 12582912 | tf_op jit(solution)/shard_map/all_to_all | solution.py:118
  43.9 129.7 %all-to-all-done.1 = bf16[8,24,128,128]{3,2,1,0:T(8,128)(2,1)} async-done(((bf16[8,24,128,128]{3,2,1,0:T(8,128)(2,1)}), bf16[8,24,128,128]{3,2,1,0:T(8,128)(2,1)}, u32[]{:S(2)}, u32[]{:S(2)}) %all-to-all-start.1) | async-done | bytes 6291488 | tf_op jit(solution)/shard_map/all_to_all | solution.py:118
  173.6 5.6 fusion.48
  179.2 4.7 fusion.80
  188.1 7.0 %collective-permute-done.3 = f32[32,2048]{1,0:T(8,128)S(1)} collective-permute-done((f32[32,2048]{1,0:T(8,128)S(1)}, f32[32,2048]{1,0:T(8,128)S(1)}, u32[]{:S(2)}, u32[]{:S(2)}) %collective-permute-start.3) | collective-permute-done | bytes 262176 | tf_op jit(solution)/shard_map/ppermute | solution.py:55
  216.5 8.3 %fusion.51 = f32[64,192,128]{2,0,1:T(8,128)S(1)} fusion(bf16[192,128,128]{2,1,0:T(8,128)(2,1)} %bitcast.11, bf16[192,64,128]{2,1,0:T(8,128)(2,1)} %gather_fusion.1, pred[192]{0:T(512)(128)(4,1)S(1)} %get-tuple-element.55), kind=kOutput, calls=%fused_computation.59 | convolution fusion | flops 404226048 | bytes 15728832 | tf_op jit(solution)/shard_map/sij,ksj->ksi/dot_general | solution.py:85
  232.3 5.3 collective-permute-done.11
  274.1 5.6 fusion.54
  279.7 5.1 fusion.86
  289.0 7.0 %collective-permute-done.24 = f32[32,2048]{1,0:T(8,128)S(1)} collective-permute-done((f32[32,2048]{1,0:T(8,128)S(1)}, f32[32,2048]{1,0:T(8,128)S(1)}, u32[]{:S(2)}, u32[]{:S(2)}) %collective-permute-start.24) | collective-permute-done | bytes 262176 | tf_op jit(solution)/shard_map/ppermute | solution.py:55
  318.7 8.1 %fusion.57 = f32[64,192,128]{2,0,1:T(8,128)S(1)} fusion(bf16[192,128,128]{2,1,0:T(8,128)(2,1)} %bitcast.11, bf16[192,64,128]{2,1,0:T(8,128)(2,1)} %gather_fusion.3, pred[192]{0:T(512)(128)(4,1)S(1)} %get-tuple-element.55), kind=kOutput, calls=%fused_computation.61 | convolution fusion | flops 404226048 | bytes 15728832 | tf_op jit(solution)/shard_map/sij,ksj->ksi/dot_general | solution.py:85
  326.7 4.8 fusion.89
  334.5 5.3 collective-permute-done.32
  375.8 5.6 fusion.60
  390.2 7.0 %collective-permute-done.45 = f32[32,2048]{1,0:T(8,128)S(1)} collective-permute-done((f32[32,2048]{1,0:T(8,128)S(1)}, f32[32,2048]{1,0:T(8,128)S(1)}, u32[]{:S(2)}, u32[]{:S(2)}) %collective-permute-start.45) | collective-permute-done | bytes 262176 | tf_op jit(solution)/shard_map/ppermute | solution.py:55
  420.9 8.1 %fusion.63 = f32[64,192,128]{2,0,1:T(8,128)S(1)} fusion(bf16[192,128,128]{2,1,0:T(8,128)(2,1)} %bitcast.11, bf16[192,64,128]{2,1,0:T(8,128)(2,1)} %gather_fusion.5, pred[192]{0:T(512)(128)(4,1)S(1)} %get-tuple-element.55), kind=kOutput, calls=%fused_computation.63 | convolution fusion | flops 404226048 | bytes 15728832 | tf_op jit(solution)/shard_map/sij,ksj->ksi/dot_general | solution.py:85
  436.5 5.3 collective-permute-done.53
  478.4 5.6 fusion.66
  484.0 4.7 fusion.98
  492.9 7.0 %collective-permute-done.66 = f32[32,2048]{1,0:T(8,128)S(1)} collective-permute-done((f32[32,2048]{1,0:T(8,128)S(1)}, f32[32,2048]{1,0:T(8,128)S(1)}, u32[]{:S(2)}, u32[]{:S(2)}) %collective-permute-start.66) | collective-permute-done | bytes 262176 | tf_op jit(solution)/shard_map/ppermute | solution.py:55
  523.0 8.2 %fusion.69 = f32[64,192,128]{2,0,1:T(8,128)S(1)} fusion(bf16[192,128,128]{2,1,0:T(8,128)(2,1)} %bitcast.11, bf16[192,64,128]{2,1,0:T(8,128)(2,1)} %gather_fusion.7, pred[192]{0:T(512)(128)(4,1)S(1)} %get-tuple-element.55), kind=kOutput, calls=%fused_computation.65 | convolution fusion | flops 404226048 | bytes 15728832 | tf_op jit(solution)/shard_map/sij,ksj->ksi/dot_general | solution.py:85
  538.8 5.3 collective-permute-done.74
  (410 shorter events, 298.6 us)
Async XLA Ops:
  5.4 24.4 %all-to-all-start = ((s32[8,24,2]{1,2,0:T(2,128)}), s32[8,24,2]{1,2,0:T(2,128)S(1)}, u32[]{:S(2)}, u32[]{:S(2)}) async-start(s32[8,24,2]{1,2,0:T(2,128)} %copy.102), calls=%async_computation | async-start | bytes 16384 | tf_op jit(solution)/shard_map/all_to_all | solution.py:125
  29.8 143.8 %all-to-all-start.1 = ((bf16[8,24,128,128]{3,2,1,0:T(8,128)(2,1)}), bf16[8,24,128,128]{3,2,1,0:T(8,128)(2,1)}, u32[]{:S(2)}, u32[]{:S(2)}) async-start(bf16[8,24,128,128]{3,2,1,0:T(8,128)(2,1)} %bitcast.274), calls=%async_computation.1 | async-start | bytes 12582912 | tf_op jit(solution)/shard_map/all_to_all | solution.py:118
  185.9 9.2 %collective-permute-start.3 = (f32[32,2048]{1,0:T(8,128)S(1)}, f32[32,2048]{1,0:T(8,128)S(1)}, u32[]{:S(2)}, u32[]{:S(2)}) collective-permute-start(f32[32,2048]{1,0:T(8,128)S(1)} %dynamic-slice_add_fusion.15), channel_id=1, source_target_pairs={{0,16},{8,24},{16,0},{24,8},{1,17},{9,25},{17,1},{25,9},{2,18},{10... | collective-permute-start | bytes 786440 | tf_op jit(solution)/shard_map/ppermute | solution.py:55
  187.5 12.4 %collective-permute-start.6 = (f32[32,2048]{1,0:T(8,128)S(1)}, f32[32,2048]{1,0:T(8,128)S(1)}, u32[]{:S(2)}, u32[]{:S(2)}) collective-permute-start(f32[32,2048]{1,0:T(8,128)S(1)} %dynamic-slice_add_fusion.14), channel_id=1, source_target_pairs={{0,16},{8,24},{16,0},{24,8},{1,17},{9,25},{17,1},{25,9},{2,18},{10... | collective-permute-start | bytes 786440 | tf_op jit(solution)/shard_map/ppermute | solution.py:55
  229.8 7.8 %collective-permute-start.11 = (f32[32,2048]{1,0:T(8,128)S(1)}, f32[32,2048]{1,0:T(8,128)S(1)}, u32[]{:S(2)}, u32[]{:S(2)}) collective-permute-start(f32[32,2048]{1,0:T(8,128)S(1)} %constant_dynamic-slice_fusion.21), channel_id=1, source_target_pairs={{0,1},{1,0},{2,3},{3,2},{4,5},{5,4},{6,7},{7,6},{8,9},{9,8},{10,11... | collective-permute-start | bytes 786440 | tf_op jit(solution)/shard_map/ppermute | solution.py:53
  231.7 8.7 %collective-permute-start.16 = (f32[32,2048]{1,0:T(8,128)S(1)}, f32[32,2048]{1,0:T(8,128)S(1)}, u32[]{:S(2)}, u32[]{:S(2)}) collective-permute-start(f32[32,2048]{1,0:T(8,128)S(1)} %constant_dynamic-slice_fusion.19), channel_id=1, source_target_pairs={{0,1},{1,0},{2,3},{3,2},{4,5},{5,4},{6,7},{7,6},{8,9},{9,8},{10,11... | collective-permute-start | bytes 786440 | tf_op jit(solution)/shard_map/ppermute | solution.py:53
  243.1 7.4 %collective-permute-start.13 = (f32[32,1024]{1,0:T(8,128)S(1)}, f32[32,1024]{1,0:T(8,128)S(1)}, u32[]{:S(2)}, u32[]{:S(2)}) collective-permute-start(f32[32,1024]{1,0:T(8,128)S(1)} %dynamic-slice_add_fusion.23), channel_id=1, source_target_pairs={{0,4},{1,5},{2,6},{3,7},{4,0},{5,1},{6,2},{7,3},{8,12},{9,13},{10,... | collective-permute-start | bytes 393224 | tf_op jit(solution)/shard_map/ppermute | solution.py:55
  286.8 9.2 %collective-permute-start.24 = (f32[32,2048]{1,0:T(8,128)S(1)}, f32[32,2048]{1,0:T(8,128)S(1)}, u32[]{:S(2)}, u32[]{:S(2)}) collective-permute-start(f32[32,2048]{1,0:T(8,128)S(1)} %dynamic-slice_add_fusion.11), channel_id=1, source_target_pairs={{0,16},{8,24},{16,0},{24,8},{1,17},{9,25},{17,1},{25,9},{2,18},{10... | collective-permute-start | bytes 786440 | tf_op jit(solution)/shard_map/ppermute | solution.py:55
  288.5 12.4 %collective-permute-start.27 = (f32[32,2048]{1,0:T(8,128)S(1)}, f32[32,2048]{1,0:T(8,128)S(1)}, u32[]{:S(2)}, u32[]{:S(2)}) collective-permute-start(f32[32,2048]{1,0:T(8,128)S(1)} %dynamic-slice_add_fusion.10), channel_id=1, source_target_pairs={{0,16},{8,24},{16,0},{24,8},{1,17},{9,25},{17,1},{25,9},{2,18},{10... | collective-permute-start | bytes 786440 | tf_op jit(solution)/shard_map/ppermute | solution.py:55
  332.0 7.8 %collective-permute-start.32 = (f32[32,2048]{1,0:T(8,128)S(1)}, f32[32,2048]{1,0:T(8,128)S(1)}, u32[]{:S(2)}, u32[]{:S(2)}) collective-permute-start(f32[32,2048]{1,0:T(8,128)S(1)} %constant_dynamic-slice_fusion.15), channel_id=1, source_target_pairs={{0,1},{1,0},{2,3},{3,2},{4,5},{5,4},{6,7},{7,6},{8,9},{9,8},{10,11... | collective-permute-start | bytes 786440 | tf_op jit(solution)/shard_map/ppermute | solution.py:53
  333.3 9.3 %collective-permute-start.37 = (f32[32,2048]{1,0:T(8,128)S(1)}, f32[32,2048]{1,0:T(8,128)S(1)}, u32[]{:S(2)}, u32[]{:S(2)}) collective-permute-start(f32[32,2048]{1,0:T(8,128)S(1)} %constant_dynamic-slice_fusion.13), channel_id=1, source_target_pairs={{0,1},{1,0},{2,3},{3,2},{4,5},{5,4},{6,7},{7,6},{8,9},{9,8},{10,11... | collective-permute-start | bytes 786440 | tf_op jit(solution)/shard_map/ppermute | solution.py:53
  342.6 7.1 %collective-permute-start.38 = (f32[32,1024]{1,0:T(8,128)S(1)}, f32[32,1024]{1,0:T(8,128)S(1)}, u32[]{:S(2)}, u32[]{:S(2)}) collective-permute-start(f32[32,1024]{1,0:T(8,128)S(1)} %constant_dynamic-slice_fusion.12), channel_id=1, source_target_pairs={{0,2},{1,3},{2,0},{3,1},{4,6},{5,7},{6,4},{7,5},{8,10},{9,11},{10,... | collective-permute-start | bytes 393224 | tf_op jit(solution)/shard_map/ppermute | solution.py:53
  345.3 7.4 %collective-permute-start.34 = (f32[32,1024]{1,0:T(8,128)S(1)}, f32[32,1024]{1,0:T(8,128)S(1)}, u32[]{:S(2)}, u32[]{:S(2)}) collective-permute-start(f32[32,1024]{1,0:T(8,128)S(1)} %dynamic-slice_add_fusion.21), channel_id=1, source_target_pairs={{0,4},{1,5},{2,6},{3,7},{4,0},{5,1},{6,2},{7,3},{8,12},{9,13},{10,... | collective-permute-start | bytes 393224 | tf_op jit(solution)/shard_map/ppermute | solution.py:55
  388.0 9.2 %collective-permute-start.45 = (f32[32,2048]{1,0:T(8,128)S(1)}, f32[32,2048]{1,0:T(8,128)S(1)}, u32[]{:S(2)}, u32[]{:S(2)}) collective-permute-start(f32[32,2048]{1,0:T(8,128)S(1)} %dynamic-slice_add_fusion.7), channel_id=1, source_target_pairs={{0,16},{8,24},{16,0},{24,8},{1,17},{9,25},{17,1},{25,9},{2,18},{10... | collective-permute-start | bytes 786440 | tf_op jit(solution)/shard_map/ppermute | solution.py:55
  389.7 12.4 %collective-permute-start.48 = (f32[32,2048]{1,0:T(8,128)S(1)}, f32[32,2048]{1,0:T(8,128)S(1)}, u32[]{:S(2)}, u32[]{:S(2)}) collective-permute-start(f32[32,2048]{1,0:T(8,128)S(1)} %dynamic-slice_add_fusion.6), channel_id=1, source_target_pairs={{0,16},{8,24},{16,0},{24,8},{1,17},{9,25},{17,1},{25,9},{2,18},{10... | collective-permute-start | bytes 786440 | tf_op jit(solution)/shard_map/ppermute | solution.py:55
  434.0 7.8 %collective-permute-start.53 = (f32[32,2048]{1,0:T(8,128)S(1)}, f32[32,2048]{1,0:T(8,128)S(1)}, u32[]{:S(2)}, u32[]{:S(2)}) collective-permute-start(f32[32,2048]{1,0:T(8,128)S(1)} %constant_dynamic-slice_fusion.9), channel_id=1, source_target_pairs={{0,1},{1,0},{2,3},{3,2},{4,5},{5,4},{6,7},{7,6},{8,9},{9,8},{10,11... | collective-permute-start | bytes 786440 | tf_op jit(solution)/shard_map/ppermute | solution.py:53
  435.5 9.1 %collective-permute-start.58 = (f32[32,2048]{1,0:T(8,128)S(1)}, f32[32,2048]{1,0:T(8,128)S(1)}, u32[]{:S(2)}, u32[]{:S(2)}) collective-permute-start(f32[32,2048]{1,0:T(8,128)S(1)} %constant_dynamic-slice_fusion.7), channel_id=1, source_target_pairs={{0,1},{1,0},{2,3},{3,2},{4,5},{5,4},{6,7},{7,6},{8,9},{9,8},{10,11... | collective-permute-start | bytes 786440 | tf_op jit(solution)/shard_map/ppermute | solution.py:53
  447.3 7.4 %collective-permute-start.55 = (f32[32,1024]{1,0:T(8,128)S(1)}, f32[32,1024]{1,0:T(8,128)S(1)}, u32[]{:S(2)}, u32[]{:S(2)}) collective-permute-start(f32[32,1024]{1,0:T(8,128)S(1)} %dynamic-slice_add_fusion.19), channel_id=1, source_target_pairs={{0,4},{1,5},{2,6},{3,7},{4,0},{5,1},{6,2},{7,3},{8,12},{9,13},{10,... | collective-permute-start | bytes 393224 | tf_op jit(solution)/shard_map/ppermute | solution.py:55
  490.7 9.2 %collective-permute-start.66 = (f32[32,2048]{1,0:T(8,128)S(1)}, f32[32,2048]{1,0:T(8,128)S(1)}, u32[]{:S(2)}, u32[]{:S(2)}) collective-permute-start(f32[32,2048]{1,0:T(8,128)S(1)} %dynamic-slice_add_fusion.3), channel_id=1, source_target_pairs={{0,16},{8,24},{16,0},{24,8},{1,17},{9,25},{17,1},{25,9},{2,18},{10... | collective-permute-start | bytes 786440 | tf_op jit(solution)/shard_map/ppermute | solution.py:55
  492.4 12.4 %collective-permute-start.69 = (f32[32,2048]{1,0:T(8,128)S(1)}, f32[32,2048]{1,0:T(8,128)S(1)}, u32[]{:S(2)}, u32[]{:S(2)}) collective-permute-start(f32[32,2048]{1,0:T(8,128)S(1)} %dynamic-slice_add_fusion.2), channel_id=1, source_target_pairs={{0,16},{8,24},{16,0},{24,8},{1,17},{9,25},{17,1},{25,9},{2,18},{10... | collective-permute-start | bytes 786440 | tf_op jit(solution)/shard_map/ppermute | solution.py:55
  536.3 7.8 %collective-permute-start.74 = (f32[32,2048]{1,0:T(8,128)S(1)}, f32[32,2048]{1,0:T(8,128)S(1)}, u32[]{:S(2)}, u32[]{:S(2)}) collective-permute-start(f32[32,2048]{1,0:T(8,128)S(1)} %constant_dynamic-slice_fusion.3), channel_id=1, source_target_pairs={{0,1},{1,0},{2,3},{3,2},{4,5},{5,4},{6,7},{7,6},{8,9},{9,8},{10,11... | collective-permute-start | bytes 786440 | tf_op jit(solution)/shard_map/ppermute | solution.py:53
  537.7 9.2 %collective-permute-start.79 = (f32[32,2048]{1,0:T(8,128)S(1)}, f32[32,2048]{1,0:T(8,128)S(1)}, u32[]{:S(2)}, u32[]{:S(2)}) collective-permute-start(f32[32,2048]{1,0:T(8,128)S(1)} %constant_dynamic-slice_fusion.1), channel_id=1, source_target_pairs={{0,1},{1,0},{2,3},{3,2},{4,5},{5,4},{6,7},{7,6},{8,9},{9,8},{10,11... | collective-permute-start | bytes 786440 | tf_op jit(solution)/shard_map/ppermute | solution.py:53
  546.9 7.2 %collective-permute-start.80 = (f32[32,1024]{1,0:T(8,128)S(1)}, f32[32,1024]{1,0:T(8,128)S(1)}, u32[]{:S(2)}, u32[]{:S(2)}) collective-permute-start(f32[32,1024]{1,0:T(8,128)S(1)} %constant_dynamic-slice_fusion), channel_id=1, source_target_pairs={{0,2},{1,3},{2,0},{3,1},{4,6},{5,7},{6,4},{7,5},{8,10},{9,11},{10,... | collective-permute-start | bytes 393224 | tf_op jit(solution)/shard_map/ppermute | solution.py:53
  549.6 7.4 %collective-permute-start.76 = (f32[32,1024]{1,0:T(8,128)S(1)}, f32[32,1024]{1,0:T(8,128)S(1)}, u32[]{:S(2)}, u32[]{:S(2)}) collective-permute-start(f32[32,1024]{1,0:T(8,128)S(1)} %dynamic-slice_add_fusion.17), channel_id=1, source_target_pairs={{0,4},{1,5},{2,6},{3,7},{4,0},{5,1},{6,2},{7,3},{8,12},{9,13},{10,... | collective-permute-start | bytes 393224 | tf_op jit(solution)/shard_map/ppermute | solution.py:55
  (82 other events, 501.2 us)

commit v12 on v11

--- a/solution.py
+++ b/solution.py
@@ -30,7 +30,7 @@
     return value
 
 
-def big_sum(value, axis):
+def big_sum(value, axis, lane_count):
     count = lax.axis_size(axis)
     width = value.shape[-1]
     if not is_power_of_two(count) or width % (128 * count):
@@ -41,7 +41,7 @@
     while distance < count:
         distances.append(distance)
         distance *= 2
-    lanes = jnp.split(value, CHUNKS, axis=0)
+    lanes = jnp.split(value, lane_count, axis=0)
     last = distances.pop()
     for distance in distances:
         upper = (index // distance) % 2
@@ -135,7 +135,7 @@
         return backward_terms(left_bf, work_blocks, work_rows, work_cols, TC)
 
     def sum_right(partial_value):
-        return big_sum(partial_value, "row")
+        return big_sum(partial_value, "row", 1)
 
     def finish_left(unscaled, need_form):
         squares = jnp.sum(unscaled * unscaled, axis=1)
@@ -164,7 +164,7 @@
     for iteration in range(ITERS):
         last_turn = iteration + 1 == ITERS
         unscaled = (
-            big_sum(forward_terms(right_bf, work_blocks, work_rows, work_cols, row_tiles), "col")
+            big_sum(forward_terms(right_bf, work_blocks, work_rows, work_cols, row_tiles), "col", CHUNKS)
             - alpha_norm[:, None] * left_vec
         )
         beta_norm, left_vec, left_bf = finish_left(unscaled, not last_turn)

time: 583 us -> 597 us (1.024); the launches traced: 580 us -> 587 us
  waiting for transfers between devices: 352 us -> 364 us
    ppermute x24 -> x20, waiting for transfers between devices: 54.2 us -> 59.3 us  [big_sum(): lax.ppermute(give, axis, partner_pairs(count, distance))]
    ppermute x16 -> x12, waiting for transfers between devices: 71.6 us -> 75 us  [big_sum(): lax.ppermute(held, axis, partner_pairs(count, last))]
    ppermute x16 -> x12, starting transfers between devices: 15 us -> 12.4 us  [big_sum(): lax.ppermute(held, axis, partner_pairs(count, last))]
    ppermute x24 -> x20, starting transfers between devices: 13.9 us -> 11.7 us  [big_sum(): lax.ppermute(give, axis, partner_pairs(count, distance))]
    ppermute x24 -> x20, waiting for transfers between devices: 42.4 us -> 44.4 us  [big_sum(): other = lax.ppermute(held, axis, partner_pairs(count, distance))]
  transfers between devices with their start and end apart: 88 -> 76, of which waited for: 79 -> 75; matrix products, arithmetic and copies ran while one was open for 4% -> 4% of each run, Pallas kernels for 0% -> 0%
where the time goes in v12:
time: 597 us; the launch traced here: 587 us
  waiting for transfers between devices  364 us (61%)
  matrix products  92.9 us (16%)
  starting transfers between devices  61.2 us (10%)
  local copies, waits for them, and re-layouts  49.9 us (8%)
  other arithmetic  17 us (3%)
    all_to_all x1, waiting for transfers between devices, per_device(): lax.all_to_all(outgoing.reshape(col_count, capacity, block_size, block_si...  130 us
    ppermute x12, waiting for transfers between devices, big_sum(): lax.ppermute(held, axis, partner_pairs(count, last))  75 us
    ppermute x20, waiting for transfers between devices, big_sum(): lax.ppermute(give, axis, partner_pairs(count, distance))  59.3 us
    ppermute x22, waiting for transfers between devices, small_sum(): value = value + lax.ppermute(value, axis, partner_pairs(count, distance))  55.2 us
    ppermute x20, waiting for transfers between devices, big_sum(): other = lax.ppermute(held, axis, partner_pairs(count, distance))  44.4 us
    dot_general x8, matrix products, place_terms(): jnp.einsum('ksi,st->kti', weighted, onehot, precision=lax.Precision.HIGH)  37.9 us
    dot_general x4, matrix products, forward_terms(): jnp.einsum('sij,ksj->ksi', blocks, picked, preferred_element_type=jnp.flo...  32.6 us
    dot_general x4, matrix products, backward_terms(): jnp.einsum('sji,ksj->ksi', blocks, picked, preferred_element_type=jnp.flo...  22.4 us
  transfers between devices with their start and end apart: 76, of which 75 were waited for; matrix products, arithmetic and copies ran while one was open for 4% of the time, Pallas kernels for 0%

profile of v12, /device:TPU:0, one launch (start us, length us, event | category | flops | bytes accessed | tf_op | source)
XLA Modules:
  0.0 586.7 jit_solution(4443217365923910591)
XLA Ops:
  5.4 7.3 %all-to-all-start = ((s32[8,24,2]{1,2,0:T(2,128)}), s32[8,24,2]{1,2,0:T(2,128)S(1)}, u32[]{:S(2)}, u32[]{:S(2)}) async-start(s32[8,24,2]{1,2,0:T(2,128)} %copy.70), calls=%async_computation | async-start | bytes 16384 | tf_op jit(solution)/shard_map/all_to_all | solution.py:125
  16.9 14.7 %scatter_fusion = bf16[192,128,128]{2,1,0:T(8,128)(2,1)} fusion(bf16[192,128,128]{2,1,0:T(8,128)(2,1)} %broadcast_in_dim.14, s32[96]{0:T(128)S(1)} %fusion.132, bf16[96,128,128]{2,1,0:T(8,128)(2,1)} %param.8), kind=kCustom, calls=%fused_computation.9 | custom fusion | bytes 9437568 | tf_op jit(solution)/shard_map/scatter | solution.py:110
  31.7 6.1 %all-to-all-start.1 = ((bf16[8,24,128,128]{3,2,1,0:T(8,128)(2,1)}), bf16[8,24,128,128]{3,2,1,0:T(8,128)(2,1)}, u32[]{:S(2)}, u32[]{:S(2)}) async-start(bf16[8,24,128,128]{3,2,1,0:T(8,128)(2,1)} %bitcast.214), calls=%async_computation.1 | async-start | bytes 12582912 | tf_op jit(solution)/shard_map/all_to_all | solution.py:118
  45.7 129.7 %all-to-all-done.1 = bf16[8,24,128,128]{3,2,1,0:T(8,128)(2,1)} async-done(((bf16[8,24,128,128]{3,2,1,0:T(8,128)(2,1)}), bf16[8,24,128,128]{3,2,1,0:T(8,128)(2,1)}, u32[]{:S(2)}, u32[]{:S(2)}) %all-to-all-start.1) | async-done | bytes 6291488 | tf_op jit(solution)/shard_map/all_to_all | solution.py:118
  175.4 5.6 fusion.48
  189.9 12.5 %collective-permute-done.3 = f32[64,2048]{1,0:T(8,128)S(1)} collective-permute-done((f32[64,2048]{1,0:T(8,128)S(1)}, f32[64,2048]{1,0:T(8,128)S(1)}, u32[]{:S(2)}, u32[]{:S(2)}) %collective-permute-start.3) | collective-permute-done | bytes 524320 | tf_op jit(solution)/shard_map/ppermute | solution.py:55
  219.3 8.4 %fusion.51 = f32[64,192,128]{2,0,1:T(8,128)S(1)} fusion(bf16[192,128,128]{2,1,0:T(8,128)(2,1)} %bitcast.11, bf16[192,64,128]{2,1,0:T(8,128)(2,1)} %gather_fusion.1, pred[192]{0:T(512)(128)(4,1)S(1)} %get-tuple-element.47), kind=kOutput, calls=%fused_computation.59 | convolution fusion | flops 404226048 | bytes 15728832 | tf_op jit(solution)/shard_map/sij,ksj->ksi/dot_general | solution.py:85
  235.3 5.3 collective-permute-done.8
  277.1 5.6 fusion.54
  282.6 4.9 fusion.10
  291.8 12.5 %collective-permute-done.21 = f32[64,2048]{1,0:T(8,128)S(1)} collective-permute-done((f32[64,2048]{1,0:T(8,128)S(1)}, f32[64,2048]{1,0:T(8,128)S(1)}, u32[]{:S(2)}, u32[]{:S(2)}) %collective-permute-start.21) | collective-permute-done | bytes 524320 | tf_op jit(solution)/shard_map/ppermute | solution.py:55
  322.6 8.1 %fusion.57 = f32[64,192,128]{2,0,1:T(8,128)S(1)} fusion(bf16[192,128,128]{2,1,0:T(8,128)(2,1)} %bitcast.11, bf16[192,64,128]{2,1,0:T(8,128)(2,1)} %gather_fusion.3, pred[192]{0:T(512)(128)(4,1)S(1)} %get-tuple-element.47), kind=kOutput, calls=%fused_computation.61 | convolution fusion | flops 404226048 | bytes 15728832 | tf_op jit(solution)/shard_map/sij,ksj->ksi/dot_general | solution.py:85
  330.7 4.9 fusion.83
  338.5 5.3 collective-permute-done.26
  379.7 5.6 fusion.60
  385.3 4.7 fusion.6
  394.2 12.5 %collective-permute-done.39 = f32[64,2048]{1,0:T(8,128)S(1)} collective-permute-done((f32[64,2048]{1,0:T(8,128)S(1)}, f32[64,2048]{1,0:T(8,128)S(1)}, u32[]{:S(2)}, u32[]{:S(2)}) %collective-permute-start.39) | collective-permute-done | bytes 524320 | tf_op jit(solution)/shard_map/ppermute | solution.py:55
  426.4 8.1 %fusion.63 = f32[64,192,128]{2,0,1:T(8,128)S(1)} fusion(bf16[192,128,128]{2,1,0:T(8,128)(2,1)} %bitcast.11, bf16[192,64,128]{2,1,0:T(8,128)(2,1)} %gather_fusion.5, pred[192]{0:T(512)(128)(4,1)S(1)} %get-tuple-element.47), kind=kOutput, calls=%fused_computation.63 | convolution fusion | flops 404226048 | bytes 15728832 | tf_op jit(solution)/shard_map/sij,ksj->ksi/dot_general | solution.py:85
  442.1 5.3 collective-permute-done.44
  483.5 5.7 fusion.66
  498.2 12.5 %collective-permute-done.57 = f32[64,2048]{1,0:T(8,128)S(1)} collective-permute-done((f32[64,2048]{1,0:T(8,128)S(1)}, f32[64,2048]{1,0:T(8,128)S(1)}, u32[]{:S(2)}, u32[]{:S(2)}) %collective-permute-start.57) | collective-permute-done | bytes 524320 | tf_op jit(solution)/shard_map/ppermute | solution.py:55
  529.3 8.1 %fusion.69 = f32[64,192,128]{2,0,1:T(8,128)S(1)} fusion(bf16[192,128,128]{2,1,0:T(8,128)(2,1)} %bitcast.11, bf16[192,64,128]{2,1,0:T(8,128)(2,1)} %gather_fusion.7, pred[192]{0:T(512)(128)(4,1)S(1)} %get-tuple-element.47), kind=kOutput, calls=%fused_computation.65 | convolution fusion | flops 404226048 | bytes 15728832 | tf_op jit(solution)/shard_map/sij,ksj->ksi/dot_general | solution.py:85
  537.4 4.9 fusion.89
  545.2 5.3 collective-permute-done.62
  (340 shorter events, 281.4 us)
Async XLA Ops:
  5.4 26.3 %all-to-all-start = ((s32[8,24,2]{1,2,0:T(2,128)}), s32[8,24,2]{1,2,0:T(2,128)S(1)}, u32[]{:S(2)}, u32[]{:S(2)}) async-start(s32[8,24,2]{1,2,0:T(2,128)} %copy.70), calls=%async_computation | async-start | bytes 16384 | tf_op jit(solution)/shard_map/all_to_all | solution.py:125
  31.7 143.8 %all-to-all-start.1 = ((bf16[8,24,128,128]{3,2,1,0:T(8,128)(2,1)}), bf16[8,24,128,128]{3,2,1,0:T(8,128)(2,1)}, u32[]{:S(2)}, u32[]{:S(2)}) async-start(bf16[8,24,128,128]{3,2,1,0:T(8,128)(2,1)} %bitcast.214), calls=%async_computation.1 | async-start | bytes 12582912 | tf_op jit(solution)/shard_map/all_to_all | solution.py:118
  188.4 14.0 %collective-permute-start.3 = (f32[64,2048]{1,0:T(8,128)S(1)}, f32[64,2048]{1,0:T(8,128)S(1)}, u32[]{:S(2)}, u32[]{:S(2)}) collective-permute-start(f32[64,2048]{1,0:T(8,128)S(1)} %dynamic-slice_add_fusion.3), channel_id=1, source_target_pairs={{0,16},{8,24},{16,0},{24,8},{1,17},{9,25},{17,1},{25,9},{2,18},{10... | collective-permute-start | bytes 1572872 | tf_op jit(solution)/shard_map/ppermute | solution.py:55
  232.8 7.8 %collective-permute-start.8 = (f32[32,2048]{1,0:T(8,128)S(1)}, f32[32,2048]{1,0:T(8,128)S(1)}, u32[]{:S(2)}, u32[]{:S(2)}) collective-permute-start(f32[32,2048]{1,0:T(8,128)S(1)} %constant_dynamic-slice_fusion.18), channel_id=1, source_target_pairs={{0,1},{1,0},{2,3},{3,2},{4,5},{5,4},{6,7},{7,6},{8,9},{9,8},{10,11... | collective-permute-start | bytes 786440 | tf_op jit(solution)/shard_map/ppermute | solution.py:53
  234.7 8.7 %collective-permute-start.13 = (f32[32,2048]{1,0:T(8,128)S(1)}, f32[32,2048]{1,0:T(8,128)S(1)}, u32[]{:S(2)}, u32[]{:S(2)}) collective-permute-start(f32[32,2048]{1,0:T(8,128)S(1)} %constant_dynamic-slice_fusion.16), channel_id=1, source_target_pairs={{0,1},{1,0},{2,3},{3,2},{4,5},{5,4},{6,7},{7,6},{8,9},{9,8},{10,11... | collective-permute-start | bytes 786440 | tf_op jit(solution)/shard_map/ppermute | solution.py:53
  243.5 6.9 %collective-permute-start.14 = (f32[32,1024]{1,0:T(8,128)S(1)}, f32[32,1024]{1,0:T(8,128)S(1)}, u32[]{:S(2)}, u32[]{:S(2)}) collective-permute-start(f32[32,1024]{1,0:T(8,128)S(1)} %constant_dynamic-slice_fusion.15), channel_id=1, source_target_pairs={{0,2},{1,3},{2,0},{3,1},{4,6},{5,7},{6,4},{7,5},{8,10},{9,11},{10,... | collective-permute-start | bytes 393224 | tf_op jit(solution)/shard_map/ppermute | solution.py:53
  246.1 7.4 %collective-permute-start.10 = (f32[32,1024]{1,0:T(8,128)S(1)}, f32[32,1024]{1,0:T(8,128)S(1)}, u32[]{:S(2)}, u32[]{:S(2)}) collective-permute-start(f32[32,1024]{1,0:T(8,128)S(1)} %dynamic-slice_add_fusion.19), channel_id=1, source_target_pairs={{0,4},{1,5},{2,6},{3,7},{4,0},{5,1},{6,2},{7,3},{8,12},{9,13},{10,... | collective-permute-start | bytes 393224 | tf_op jit(solution)/shard_map/ppermute | solution.py:55
  250.4 7.0 %collective-permute-start.15 = (f32[32,1024]{1,0:T(8,128)S(1)}, f32[32,1024]{1,0:T(8,128)S(1)}, u32[]{:S(2)}, u32[]{:S(2)}) collective-permute-start(f32[32,1024]{1,0:T(8,128)S(1)} %dynamic-slice_add_fusion.18), channel_id=1, source_target_pairs={{0,4},{1,5},{2,6},{3,7},{4,0},{5,1},{6,2},{7,3},{8,12},{9,13},{10,... | collective-permute-start | bytes 393224 | tf_op jit(solution)/shard_map/ppermute | solution.py:55
  290.2 14.0 %collective-permute-start.21 = (f32[64,2048]{1,0:T(8,128)S(1)}, f32[64,2048]{1,0:T(8,128)S(1)}, u32[]{:S(2)}, u32[]{:S(2)}) collective-permute-start(f32[64,2048]{1,0:T(8,128)S(1)} %dynamic-slice_add_fusion.2), channel_id=1, source_target_pairs={{0,16},{8,24},{16,0},{24,8},{1,17},{9,25},{17,1},{25,9},{2,18},{10... | collective-permute-start | bytes 1572872 | tf_op jit(solution)/shard_map/ppermute | solution.py:55
  336.0 7.8 %collective-permute-start.26 = (f32[32,2048]{1,0:T(8,128)S(1)}, f32[32,2048]{1,0:T(8,128)S(1)}, u32[]{:S(2)}, u32[]{:S(2)}) collective-permute-start(f32[32,2048]{1,0:T(8,128)S(1)} %constant_dynamic-slice_fusion.13), channel_id=1, source_target_pairs={{0,1},{1,0},{2,3},{3,2},{4,5},{5,4},{6,7},{7,6},{8,9},{9,8},{10,11... | collective-permute-start | bytes 786440 | tf_op jit(solution)/shard_map/ppermute | solution.py:53
  337.2 9.3 %collective-permute-start.31 = (f32[32,2048]{1,0:T(8,128)S(1)}, f32[32,2048]{1,0:T(8,128)S(1)}, u32[]{:S(2)}, u32[]{:S(2)}) collective-permute-start(f32[32,2048]{1,0:T(8,128)S(1)} %constant_dynamic-slice_fusion.11), channel_id=1, source_target_pairs={{0,1},{1,0},{2,3},{3,2},{4,5},{5,4},{6,7},{7,6},{8,9},{9,8},{10,11... | collective-permute-start | bytes 786440 | tf_op jit(solution)/shard_map/ppermute | solution.py:53
  346.6 7.1 %collective-permute-start.32 = (f32[32,1024]{1,0:T(8,128)S(1)}, f32[32,1024]{1,0:T(8,128)S(1)}, u32[]{:S(2)}, u32[]{:S(2)}) collective-permute-start(f32[32,1024]{1,0:T(8,128)S(1)} %constant_dynamic-slice_fusion.10), channel_id=1, source_target_pairs={{0,2},{1,3},{2,0},{3,1},{4,6},{5,7},{6,4},{7,5},{8,10},{9,11},{10,... | collective-permute-start | bytes 393224 | tf_op jit(solution)/shard_map/ppermute | solution.py:53
  349.3 7.4 %collective-permute-start.28 = (f32[32,1024]{1,0:T(8,128)S(1)}, f32[32,1024]{1,0:T(8,128)S(1)}, u32[]{:S(2)}, u32[]{:S(2)}) collective-permute-start(f32[32,1024]{1,0:T(8,128)S(1)} %dynamic-slice_add_fusion.17), channel_id=1, source_target_pairs={{0,4},{1,5},{2,6},{3,7},{4,0},{5,1},{6,2},{7,3},{8,12},{9,13},{10,... | collective-permute-start | bytes 393224 | tf_op jit(solution)/shard_map/ppermute | solution.py:55
  392.7 14.0 %collective-permute-start.39 = (f32[64,2048]{1,0:T(8,128)S(1)}, f32[64,2048]{1,0:T(8,128)S(1)}, u32[]{:S(2)}, u32[]{:S(2)}) collective-permute-start(f32[64,2048]{1,0:T(8,128)S(1)} %dynamic-slice_add_fusion.1), channel_id=1, source_target_pairs={{0,16},{8,24},{16,0},{24,8},{1,17},{9,25},{17,1},{25,9},{2,18},{10... | collective-permute-start | bytes 1572872 | tf_op jit(solution)/shard_map/ppermute | solution.py:55
  439.6 7.8 %collective-permute-start.44 = (f32[32,2048]{1,0:T(8,128)S(1)}, f32[32,2048]{1,0:T(8,128)S(1)}, u32[]{:S(2)}, u32[]{:S(2)}) collective-permute-start(f32[32,2048]{1,0:T(8,128)S(1)} %constant_dynamic-slice_fusion.8), channel_id=1, source_target_pairs={{0,1},{1,0},{2,3},{3,2},{4,5},{5,4},{6,7},{7,6},{8,9},{9,8},{10,11... | collective-permute-start | bytes 786440 | tf_op jit(solution)/shard_map/ppermute | solution.py:53
  441.1 9.1 %collective-permute-start.49 = (f32[32,2048]{1,0:T(8,128)S(1)}, f32[32,2048]{1,0:T(8,128)S(1)}, u32[]{:S(2)}, u32[]{:S(2)}) collective-permute-start(f32[32,2048]{1,0:T(8,128)S(1)} %constant_dynamic-slice_fusion.6), channel_id=1, source_target_pairs={{0,1},{1,0},{2,3},{3,2},{4,5},{5,4},{6,7},{7,6},{8,9},{9,8},{10,11... | collective-permute-start | bytes 786440 | tf_op jit(solution)/shard_map/ppermute | solution.py:53
  450.2 7.1 %collective-permute-start.50 = (f32[32,1024]{1,0:T(8,128)S(1)}, f32[32,1024]{1,0:T(8,128)S(1)}, u32[]{:S(2)}, u32[]{:S(2)}) collective-permute-start(f32[32,1024]{1,0:T(8,128)S(1)} %constant_dynamic-slice_fusion.5), channel_id=1, source_target_pairs={{0,2},{1,3},{2,0},{3,1},{4,6},{5,7},{6,4},{7,5},{8,10},{9,11},{10,... | collective-permute-start | bytes 393224 | tf_op jit(solution)/shard_map/ppermute | solution.py:53
  452.9 7.4 %collective-permute-start.46 = (f32[32,1024]{1,0:T(8,128)S(1)}, f32[32,1024]{1,0:T(8,128)S(1)}, u32[]{:S(2)}, u32[]{:S(2)}) collective-permute-start(f32[32,1024]{1,0:T(8,128)S(1)} %dynamic-slice_add_fusion.15), channel_id=1, source_target_pairs={{0,4},{1,5},{2,6},{3,7},{4,0},{5,1},{6,2},{7,3},{8,12},{9,13},{10,... | collective-permute-start | bytes 393224 | tf_op jit(solution)/shard_map/ppermute | solution.py:55
  457.3 6.5 %collective-permute-start.51 = (f32[32,1024]{1,0:T(8,128)S(1)}, f32[32,1024]{1,0:T(8,128)S(1)}, u32[]{:S(2)}, u32[]{:S(2)}) collective-permute-start(f32[32,1024]{1,0:T(8,128)S(1)} %dynamic-slice_add_fusion.14), channel_id=1, source_target_pairs={{0,4},{1,5},{2,6},{3,7},{4,0},{5,1},{6,2},{7,3},{8,12},{9,13},{10,... | collective-permute-start | bytes 393224 | tf_op jit(solution)/shard_map/ppermute | solution.py:55
  496.7 14.0 %collective-permute-start.57 = (f32[64,2048]{1,0:T(8,128)S(1)}, f32[64,2048]{1,0:T(8,128)S(1)}, u32[]{:S(2)}, u32[]{:S(2)}) collective-permute-start(f32[64,2048]{1,0:T(8,128)S(1)} %dynamic-slice_add_fusion), channel_id=1, source_target_pairs={{0,16},{8,24},{16,0},{24,8},{1,17},{9,25},{17,1},{25,9},{2,18},{10... | collective-permute-start | bytes 1572872 | tf_op jit(solution)/shard_map/ppermute | solution.py:55
  542.7 7.8 %collective-permute-start.62 = (f32[32,2048]{1,0:T(8,128)S(1)}, f32[32,2048]{1,0:T(8,128)S(1)}, u32[]{:S(2)}, u32[]{:S(2)}) collective-permute-start(f32[32,2048]{1,0:T(8,128)S(1)} %constant_dynamic-slice_fusion.3), channel_id=1, source_target_pairs={{0,1},{1,0},{2,3},{3,2},{4,5},{5,4},{6,7},{7,6},{8,9},{9,8},{10,11... | collective-permute-start | bytes 786440 | tf_op jit(solution)/shard_map/ppermute | solution.py:53
  544.0 9.3 %collective-permute-start.67 = (f32[32,2048]{1,0:T(8,128)S(1)}, f32[32,2048]{1,0:T(8,128)S(1)}, u32[]{:S(2)}, u32[]{:S(2)}) collective-permute-start(f32[32,2048]{1,0:T(8,128)S(1)} %constant_dynamic-slice_fusion.1), channel_id=1, source_target_pairs={{0,1},{1,0},{2,3},{3,2},{4,5},{5,4},{6,7},{7,6},{8,9},{9,8},{10,11... | collective-permute-start | bytes 786440 | tf_op jit(solution)/shard_map/ppermute | solution.py:53
  553.3 7.2 %collective-permute-start.68 = (f32[32,1024]{1,0:T(8,128)S(1)}, f32[32,1024]{1,0:T(8,128)S(1)}, u32[]{:S(2)}, u32[]{:S(2)}) collective-permute-start(f32[32,1024]{1,0:T(8,128)S(1)} %constant_dynamic-slice_fusion), channel_id=1, source_target_pairs={{0,2},{1,3},{2,0},{3,1},{4,6},{5,7},{6,4},{7,5},{8,10},{9,11},{10,... | collective-permute-start | bytes 393224 | tf_op jit(solution)/shard_map/ppermute | solution.py:53
  556.0 7.4 %collective-permute-start.64 = (f32[32,1024]{1,0:T(8,128)S(1)}, f32[32,1024]{1,0:T(8,128)S(1)}, u32[]{:S(2)}, u32[]{:S(2)}) collective-permute-start(f32[32,1024]{1,0:T(8,128)S(1)} %dynamic-slice_add_fusion.13), channel_id=1, source_target_pairs={{0,4},{1,5},{2,6},{3,7},{4,0},{5,1},{6,2},{7,3},{8,12},{9,13},{10,... | collective-permute-start | bytes 393224 | tf_op jit(solution)/shard_map/ppermute | solution.py:55
  (69 other events, 491.2 us)

commit v13 on v11

--- a/solution.py
+++ b/solution.py
@@ -101,19 +101,19 @@
     own_count = blocks.shape[0]
     capacity = 2 * own_count // col_count
     target = targets[:, 0]
+    slot_count = col_count * capacity
     matches = (target[:, None] == jnp.arange(col_count, dtype=jnp.int32)[None, :]).astype(jnp.int32)
     before = jnp.cumsum(matches, axis=0) - matches
     slot_index = target * capacity + jnp.sum(before * matches, axis=1)
-    outgoing = (
-        jnp.zeros((col_count * capacity, block_size, block_size), blocks.dtype)
-        .at[slot_index]
-        .set(blocks)
-    )
-    places = (
-        jnp.zeros((col_count * capacity, 2), jnp.int32)
-        .at[slot_index]
-        .set(jnp.stack([tile_rows, tile_cols], axis=1))
-    )
+    pick = slot_index[:, None] == jnp.arange(slot_count, dtype=jnp.int32)[None, :]
+    source = jnp.sum(jnp.where(pick, jnp.arange(own_count, dtype=jnp.int32)[:, None], 0), axis=0)
+    source = jnp.where(jnp.any(pick, axis=0), source, own_count)
+    padded = jnp.concatenate([blocks, jnp.zeros((1, block_size, block_size), blocks.dtype)], axis=0)
+    outgoing = jnp.take(padded, source, axis=0, mode="clip")
+    padded_places = jnp.concatenate(
+        [jnp.stack([tile_rows, tile_cols], axis=1), jnp.zeros((1, 2), jnp.int32)], axis=0
+    )
+    places = jnp.take(padded_places, source, axis=0, mode="clip")
     arrived, arrived_places = (
         lax.all_to_all(
             outgoing.reshape(col_count, capacity, block_size, block_size),

time: 583 us -> 577 us (0.990)
  local copies, waits for them, and re-layouts: 49 us -> 41.9 us
    scatter x2 -> x0, local copies, waits for them, and re-layouts: 13.7 us -> none  [the longest x1 12.8 us: per_device(): outgoing = jnp.zeros((col_count * capacity, block_size, block_size), bloc...]
    gather x0 -> x2, local copies, waits for them, and re-layouts: none -> 8.69 us  [the longest x1 7.99 us: per_device(): outgoing = jnp.take(padded, source, axis=0, mode='clip')]
  transfers between devices with their start and end apart: 88 -> 88, of which waited for: 79 -> 79; matrix products, arithmetic and copies ran while one was open for 4% -> 3% of each run, Pallas kernels for 0% -> 0%
where the time goes in v13:
time: 577 us; the launch traced here: 574 us
  waiting for transfers between devices  353 us (61%)
  matrix products  92.7 us (16%)
  starting transfers between devices  66.7 us (12%)
  local copies, waits for them, and re-layouts  41.9 us (7%)
  other arithmetic  17.3 us (3%)
    all_to_all x1, waiting for transfers between devices, per_device(): lax.all_to_all(outgoing.reshape(col_count, capacity, block_size, block_si...  130 us
    ppermute x16, waiting for transfers between devices, big_sum(): lax.ppermute(held, axis, partner_pairs(count, last))  71.6 us
    ppermute x22, waiting for transfers between devices, small_sum(): value = value + lax.ppermute(value, axis, partner_pairs(count, distance))  54.7 us
    ppermute x24, waiting for transfers between devices, big_sum(): lax.ppermute(give, axis, partner_pairs(count, distance))  54.2 us
    ppermute x24, waiting for transfers between devices, big_sum(): other = lax.ppermute(held, axis, partner_pairs(count, distance))  42.5 us
    dot_general x8, matrix products, place_terms(): jnp.einsum('ksi,st->kti', weighted, onehot, precision=lax.Precision.HIGH)  37.8 us
    dot_general x4, matrix products, forward_terms(): jnp.einsum('sij,ksj->ksi', blocks, picked, preferred_element_type=jnp.flo...  32.6 us
    gather x8, local copies, waits for them, and re-layouts, gather_tiles(): return jnp.take(vector_tiles, indices, axis=1)  22.8 us
  transfers between devices with their start and end apart: 88, of which 79 were waited for; matrix products, arithmetic and copies ran while one was open for 3% of the time, Pallas kernels for 0%

profile of v13, /device:TPU:0, one launch (start us, length us, event | category | flops | bytes accessed | tf_op | source)
XLA Modules:
  0.0 573.5 jit_solution(10187728203670934070)
XLA Ops:
  5.5 7.3 %all-to-all-start = ((s32[8,24,2]{1,2,0:T(2,128)}), s32[8,24,2]{1,2,0:T(2,128)S(1)}, u32[]{:S(2)}, u32[]{:S(2)}) async-start(s32[8,24,2]{1,2,0:T(2,128)} %copy.153), calls=%async_computation | async-start | bytes 16384 | tf_op jit(solution)/shard_map/all_to_all | solution.py:125
  14.8 8.0 %gather_fusion.1 = bf16[192,128,128]{2,1,0:T(8,128)(2,1)} fusion(bf16[97,128,128]{2,1,0:T(8,128)(2,1)S(1)} %concatenate.273, s32[1024]{0:T(1024)S(1)} %pad_clamp_fusion.2), kind=kCustom, calls=%fused_computation.9 | custom fusion | bytes 12583680 | tf_op jit(solution)/shard_map/jit(_take)/gather | solution.py:112
  22.8 6.3 %all-to-all-start.1 = ((bf16[8,24,128,128]{3,2,1,0:T(8,128)(2,1)}), bf16[8,24,128,128]{3,2,1,0:T(8,128)(2,1)}, u32[]{:S(2)}, u32[]{:S(2)}) async-start(bf16[8,24,128,128]{3,2,1,0:T(8,128)(2,1)} %bitcast.272), calls=%async_computation.1 | async-start | bytes 12582912 | tf_op jit(solution)/shard_map/all_to_all | solution.py:118
  37.1 129.6 %all-to-all-done.1 = bf16[8,24,128,128]{3,2,1,0:T(8,128)(2,1)} async-done(((bf16[8,24,128,128]{3,2,1,0:T(8,128)(2,1)}), bf16[8,24,128,128]{3,2,1,0:T(8,128)(2,1)}, u32[]{:S(2)}, u32[]{:S(2)}) %all-to-all-start.1) | async-done | bytes 6291488 | tf_op jit(solution)/shard_map/all_to_all | solution.py:118
  166.6 5.6 fusion.48
  172.2 4.7 fusion.80
  181.2 7.0 %collective-permute-done.3 = f32[32,2048]{1,0:T(8,128)S(1)} collective-permute-done((f32[32,2048]{1,0:T(8,128)S(1)}, f32[32,2048]{1,0:T(8,128)S(1)}, u32[]{:S(2)}, u32[]{:S(2)}) %collective-permute-start.3) | collective-permute-done | bytes 262176 | tf_op jit(solution)/shard_map/ppermute | solution.py:55
  209.5 8.3 %fusion.51 = f32[64,192,128]{2,0,1:T(8,128)S(1)} fusion(bf16[192,128,128]{2,1,0:T(8,128)(2,1)} %bitcast.11, bf16[192,64,128]{2,1,0:T(8,128)(2,1)} %gather_fusion.3, pred[192]{0:T(512)(128)(4,1)S(1)} %get-tuple-element.55), kind=kOutput, calls=%fused_computation.59 | convolution fusion | flops 404226048 | bytes 15728832 | tf_op jit(solution)/shard_map/sij,ksj->ksi/dot_general | solution.py:85
  225.4 5.3 collective-permute-done.11
  267.2 5.6 fusion.54
  272.7 5.1 fusion.86
  282.1 7.0 %collective-permute-done.24 = f32[32,2048]{1,0:T(8,128)S(1)} collective-permute-done((f32[32,2048]{1,0:T(8,128)S(1)}, f32[32,2048]{1,0:T(8,128)S(1)}, u32[]{:S(2)}, u32[]{:S(2)}) %collective-permute-start.24) | collective-permute-done | bytes 262176 | tf_op jit(solution)/shard_map/ppermute | solution.py:55
  311.8 8.1 %fusion.57 = f32[64,192,128]{2,0,1:T(8,128)S(1)} fusion(bf16[192,128,128]{2,1,0:T(8,128)(2,1)} %bitcast.11, bf16[192,64,128]{2,1,0:T(8,128)(2,1)} %gather_fusion.5, pred[192]{0:T(512)(128)(4,1)S(1)} %get-tuple-element.55), kind=kOutput, calls=%fused_computation.61 | convolution fusion | flops 404226048 | bytes 15728832 | tf_op jit(solution)/shard_map/sij,ksj->ksi/dot_general | solution.py:85
  319.8 4.8 fusion.89
  327.6 5.3 collective-permute-done.32
  368.9 5.6 fusion.60
  383.3 7.0 %collective-permute-done.45 = f32[32,2048]{1,0:T(8,128)S(1)} collective-permute-done((f32[32,2048]{1,0:T(8,128)S(1)}, f32[32,2048]{1,0:T(8,128)S(1)}, u32[]{:S(2)}, u32[]{:S(2)}) %collective-permute-start.45) | collective-permute-done | bytes 262176 | tf_op jit(solution)/shard_map/ppermute | solution.py:55
  414.1 8.1 %fusion.63 = f32[64,192,128]{2,0,1:T(8,128)S(1)} fusion(bf16[192,128,128]{2,1,0:T(8,128)(2,1)} %bitcast.11, bf16[192,64,128]{2,1,0:T(8,128)(2,1)} %gather_fusion.7, pred[192]{0:T(512)(128)(4,1)S(1)} %get-tuple-element.55), kind=kOutput, calls=%fused_computation.63 | convolution fusion | flops 404226048 | bytes 15728832 | tf_op jit(solution)/shard_map/sij,ksj->ksi/dot_general | solution.py:85
  429.7 5.3 collective-permute-done.53
  471.6 5.6 fusion.66
  477.2 4.7 fusion.98
  486.1 7.0 %collective-permute-done.66 = f32[32,2048]{1,0:T(8,128)S(1)} collective-permute-done((f32[32,2048]{1,0:T(8,128)S(1)}, f32[32,2048]{1,0:T(8,128)S(1)}, u32[]{:S(2)}, u32[]{:S(2)}) %collective-permute-start.66) | collective-permute-done | bytes 262176 | tf_op jit(solution)/shard_map/ppermute | solution.py:55
  516.2 8.2 %fusion.69 = f32[64,192,128]{2,0,1:T(8,128)S(1)} fusion(bf16[192,128,128]{2,1,0:T(8,128)(2,1)} %bitcast.11, bf16[192,64,128]{2,1,0:T(8,128)(2,1)} %gather_fusion.9, pred[192]{0:T(512)(128)(4,1)S(1)} %get-tuple-element.55), kind=kOutput, calls=%fused_computation.65 | convolution fusion | flops 404226048 | bytes 15728832 | tf_op jit(solution)/shard_map/sij,ksj->ksi/dot_general | solution.py:85
  532.0 5.3 collective-permute-done.74
  (413 shorter events, 296.7 us)
Async XLA Ops:
  5.5 17.4 %all-to-all-start = ((s32[8,24,2]{1,2,0:T(2,128)}), s32[8,24,2]{1,2,0:T(2,128)S(1)}, u32[]{:S(2)}, u32[]{:S(2)}) async-start(s32[8,24,2]{1,2,0:T(2,128)} %copy.153), calls=%async_computation | async-start | bytes 16384 | tf_op jit(solution)/shard_map/all_to_all | solution.py:125
  22.8 143.8 %all-to-all-start.1 = ((bf16[8,24,128,128]{3,2,1,0:T(8,128)(2,1)}), bf16[8,24,128,128]{3,2,1,0:T(8,128)(2,1)}, u32[]{:S(2)}, u32[]{:S(2)}) async-start(bf16[8,24,128,128]{3,2,1,0:T(8,128)(2,1)} %bitcast.272), calls=%async_computation.1 | async-start | bytes 12582912 | tf_op jit(solution)/shard_map/all_to_all | solution.py:118
  179.0 9.2 %collective-permute-start.3 = (f32[32,2048]{1,0:T(8,128)S(1)}, f32[32,2048]{1,0:T(8,128)S(1)}, u32[]{:S(2)}, u32[]{:S(2)}) collective-permute-start(f32[32,2048]{1,0:T(8,128)S(1)} %dynamic-slice_add_fusion.15), channel_id=1, source_target_pairs={{0,16},{8,24},{16,0},{24,8},{1,17},{9,25},{17,1},{25,9},{2,18},{10... | collective-permute-start | bytes 786440 | tf_op jit(solution)/shard_map/ppermute | solution.py:55
  180.6 12.4 %collective-permute-start.6 = (f32[32,2048]{1,0:T(8,128)S(1)}, f32[32,2048]{1,0:T(8,128)S(1)}, u32[]{:S(2)}, u32[]{:S(2)}) collective-permute-start(f32[32,2048]{1,0:T(8,128)S(1)} %dynamic-slice_add_fusion.14), channel_id=1, source_target_pairs={{0,16},{8,24},{16,0},{24,8},{1,17},{9,25},{17,1},{25,9},{2,18},{10... | collective-permute-start | bytes 786440 | tf_op jit(solution)/shard_map/ppermute | solution.py:55
  222.9 7.8 %collective-permute-start.11 = (f32[32,2048]{1,0:T(8,128)S(1)}, f32[32,2048]{1,0:T(8,128)S(1)}, u32[]{:S(2)}, u32[]{:S(2)}) collective-permute-start(f32[32,2048]{1,0:T(8,128)S(1)} %constant_dynamic-slice_fusion.21), channel_id=1, source_target_pairs={{0,1},{1,0},{2,3},{3,2},{4,5},{5,4},{6,7},{7,6},{8,9},{9,8},{10,11... | collective-permute-start | bytes 786440 | tf_op jit(solution)/shard_map/ppermute | solution.py:53
  224.8 8.7 %collective-permute-start.16 = (f32[32,2048]{1,0:T(8,128)S(1)}, f32[32,2048]{1,0:T(8,128)S(1)}, u32[]{:S(2)}, u32[]{:S(2)}) collective-permute-start(f32[32,2048]{1,0:T(8,128)S(1)} %constant_dynamic-slice_fusion.19), channel_id=1, source_target_pairs={{0,1},{1,0},{2,3},{3,2},{4,5},{5,4},{6,7},{7,6},{8,9},{9,8},{10,11... | collective-permute-start | bytes 786440 | tf_op jit(solution)/shard_map/ppermute | solution.py:53
  236.2 7.4 %collective-permute-start.13 = (f32[32,1024]{1,0:T(8,128)S(1)}, f32[32,1024]{1,0:T(8,128)S(1)}, u32[]{:S(2)}, u32[]{:S(2)}) collective-permute-start(f32[32,1024]{1,0:T(8,128)S(1)} %dynamic-slice_add_fusion.23), channel_id=1, source_target_pairs={{0,4},{1,5},{2,6},{3,7},{4,0},{5,1},{6,2},{7,3},{8,12},{9,13},{10,... | collective-permute-start | bytes 393224 | tf_op jit(solution)/shard_map/ppermute | solution.py:55
  279.9 9.2 %collective-permute-start.24 = (f32[32,2048]{1,0:T(8,128)S(1)}, f32[32,2048]{1,0:T(8,128)S(1)}, u32[]{:S(2)}, u32[]{:S(2)}) collective-permute-start(f32[32,2048]{1,0:T(8,128)S(1)} %dynamic-slice_add_fusion.11), channel_id=1, source_target_pairs={{0,16},{8,24},{16,0},{24,8},{1,17},{9,25},{17,1},{25,9},{2,18},{10... | collective-permute-start | bytes 786440 | tf_op jit(solution)/shard_map/ppermute | solution.py:55
  281.5 12.4 %collective-permute-start.27 = (f32[32,2048]{1,0:T(8,128)S(1)}, f32[32,2048]{1,0:T(8,128)S(1)}, u32[]{:S(2)}, u32[]{:S(2)}) collective-permute-start(f32[32,2048]{1,0:T(8,128)S(1)} %dynamic-slice_add_fusion.10), channel_id=1, source_target_pairs={{0,16},{8,24},{16,0},{24,8},{1,17},{9,25},{17,1},{25,9},{2,18},{10... | collective-permute-start | bytes 786440 | tf_op jit(solution)/shard_map/ppermute | solution.py:55
  325.1 7.8 %collective-permute-start.32 = (f32[32,2048]{1,0:T(8,128)S(1)}, f32[32,2048]{1,0:T(8,128)S(1)}, u32[]{:S(2)}, u32[]{:S(2)}) collective-permute-start(f32[32,2048]{1,0:T(8,128)S(1)} %constant_dynamic-slice_fusion.15), channel_id=1, source_target_pairs={{0,1},{1,0},{2,3},{3,2},{4,5},{5,4},{6,7},{7,6},{8,9},{9,8},{10,11... | collective-permute-start | bytes 786440 | tf_op jit(solution)/shard_map/ppermute | solution.py:53
  326.4 9.3 %collective-permute-start.37 = (f32[32,2048]{1,0:T(8,128)S(1)}, f32[32,2048]{1,0:T(8,128)S(1)}, u32[]{:S(2)}, u32[]{:S(2)}) collective-permute-start(f32[32,2048]{1,0:T(8,128)S(1)} %constant_dynamic-slice_fusion.13), channel_id=1, source_target_pairs={{0,1},{1,0},{2,3},{3,2},{4,5},{5,4},{6,7},{7,6},{8,9},{9,8},{10,11... | collective-permute-start | bytes 786440 | tf_op jit(solution)/shard_map/ppermute | solution.py:53
  335.7 7.1 %collective-permute-start.38 = (f32[32,1024]{1,0:T(8,128)S(1)}, f32[32,1024]{1,0:T(8,128)S(1)}, u32[]{:S(2)}, u32[]{:S(2)}) collective-permute-start(f32[32,1024]{1,0:T(8,128)S(1)} %constant_dynamic-slice_fusion.12), channel_id=1, source_target_pairs={{0,2},{1,3},{2,0},{3,1},{4,6},{5,7},{6,4},{7,5},{8,10},{9,11},{10,... | collective-permute-start | bytes 393224 | tf_op jit(solution)/shard_map/ppermute | solution.py:53
  338.4 7.4 %collective-permute-start.34 = (f32[32,1024]{1,0:T(8,128)S(1)}, f32[32,1024]{1,0:T(8,128)S(1)}, u32[]{:S(2)}, u32[]{:S(2)}) collective-permute-start(f32[32,1024]{1,0:T(8,128)S(1)} %dynamic-slice_add_fusion.21), channel_id=1, source_target_pairs={{0,4},{1,5},{2,6},{3,7},{4,0},{5,1},{6,2},{7,3},{8,12},{9,13},{10,... | collective-permute-start | bytes 393224 | tf_op jit(solution)/shard_map/ppermute | solution.py:55
  381.1 9.2 %collective-permute-start.45 = (f32[32,2048]{1,0:T(8,128)S(1)}, f32[32,2048]{1,0:T(8,128)S(1)}, u32[]{:S(2)}, u32[]{:S(2)}) collective-permute-start(f32[32,2048]{1,0:T(8,128)S(1)} %dynamic-slice_add_fusion.7), channel_id=1, source_target_pairs={{0,16},{8,24},{16,0},{24,8},{1,17},{9,25},{17,1},{25,9},{2,18},{10... | collective-permute-start | bytes 786440 | tf_op jit(solution)/shard_map/ppermute | solution.py:55
  382.7 12.4 %collective-permute-start.48 = (f32[32,2048]{1,0:T(8,128)S(1)}, f32[32,2048]{1,0:T(8,128)S(1)}, u32[]{:S(2)}, u32[]{:S(2)}) collective-permute-start(f32[32,2048]{1,0:T(8,128)S(1)} %dynamic-slice_add_fusion.6), channel_id=1, source_target_pairs={{0,16},{8,24},{16,0},{24,8},{1,17},{9,25},{17,1},{25,9},{2,18},{10... | collective-permute-start | bytes 786440 | tf_op jit(solution)/shard_map/ppermute | solution.py:55
  427.2 7.8 %collective-permute-start.53 = (f32[32,2048]{1,0:T(8,128)S(1)}, f32[32,2048]{1,0:T(8,128)S(1)}, u32[]{:S(2)}, u32[]{:S(2)}) collective-permute-start(f32[32,2048]{1,0:T(8,128)S(1)} %constant_dynamic-slice_fusion.9), channel_id=1, source_target_pairs={{0,1},{1,0},{2,3},{3,2},{4,5},{5,4},{6,7},{7,6},{8,9},{9,8},{10,11... | collective-permute-start | bytes 786440 | tf_op jit(solution)/shard_map/ppermute | solution.py:53
  428.7 9.1 %collective-permute-start.58 = (f32[32,2048]{1,0:T(8,128)S(1)}, f32[32,2048]{1,0:T(8,128)S(1)}, u32[]{:S(2)}, u32[]{:S(2)}) collective-permute-start(f32[32,2048]{1,0:T(8,128)S(1)} %constant_dynamic-slice_fusion.7), channel_id=1, source_target_pairs={{0,1},{1,0},{2,3},{3,2},{4,5},{5,4},{6,7},{7,6},{8,9},{9,8},{10,11... | collective-permute-start | bytes 786440 | tf_op jit(solution)/shard_map/ppermute | solution.py:53
  440.5 7.4 %collective-permute-start.55 = (f32[32,1024]{1,0:T(8,128)S(1)}, f32[32,1024]{1,0:T(8,128)S(1)}, u32[]{:S(2)}, u32[]{:S(2)}) collective-permute-start(f32[32,1024]{1,0:T(8,128)S(1)} %dynamic-slice_add_fusion.19), channel_id=1, source_target_pairs={{0,4},{1,5},{2,6},{3,7},{4,0},{5,1},{6,2},{7,3},{8,12},{9,13},{10,... | collective-permute-start | bytes 393224 | tf_op jit(solution)/shard_map/ppermute | solution.py:55
  483.9 9.2 %collective-permute-start.66 = (f32[32,2048]{1,0:T(8,128)S(1)}, f32[32,2048]{1,0:T(8,128)S(1)}, u32[]{:S(2)}, u32[]{:S(2)}) collective-permute-start(f32[32,2048]{1,0:T(8,128)S(1)} %dynamic-slice_add_fusion.3), channel_id=1, source_target_pairs={{0,16},{8,24},{16,0},{24,8},{1,17},{9,25},{17,1},{25,9},{2,18},{10... | collective-permute-start | bytes 786440 | tf_op jit(solution)/shard_map/ppermute | solution.py:55
  485.5 12.4 %collective-permute-start.69 = (f32[32,2048]{1,0:T(8,128)S(1)}, f32[32,2048]{1,0:T(8,128)S(1)}, u32[]{:S(2)}, u32[]{:S(2)}) collective-permute-start(f32[32,2048]{1,0:T(8,128)S(1)} %dynamic-slice_add_fusion.2), channel_id=1, source_target_pairs={{0,16},{8,24},{16,0},{24,8},{1,17},{9,25},{17,1},{25,9},{2,18},{10... | collective-permute-start | bytes 786440 | tf_op jit(solution)/shard_map/ppermute | solution.py:55
  529.5 7.8 %collective-permute-start.74 = (f32[32,2048]{1,0:T(8,128)S(1)}, f32[32,2048]{1,0:T(8,128)S(1)}, u32[]{:S(2)}, u32[]{:S(2)}) collective-permute-start(f32[32,2048]{1,0:T(8,128)S(1)} %constant_dynamic-slice_fusion.3), channel_id=1, source_target_pairs={{0,1},{1,0},{2,3},{3,2},{4,5},{5,4},{6,7},{7,6},{8,9},{9,8},{10,11... | collective-permute-start | bytes 786440 | tf_op jit(solution)/shard_map/ppermute | solution.py:53
  530.9 9.2 %collective-permute-start.79 = (f32[32,2048]{1,0:T(8,128)S(1)}, f32[32,2048]{1,0:T(8,128)S(1)}, u32[]{:S(2)}, u32[]{:S(2)}) collective-permute-start(f32[32,2048]{1,0:T(8,128)S(1)} %constant_dynamic-slice_fusion.1), channel_id=1, source_target_pairs={{0,1},{1,0},{2,3},{3,2},{4,5},{5,4},{6,7},{7,6},{8,9},{9,8},{10,11... | collective-permute-start | bytes 786440 | tf_op jit(solution)/shard_map/ppermute | solution.py:53
  540.2 7.2 %collective-permute-start.80 = (f32[32,1024]{1,0:T(8,128)S(1)}, f32[32,1024]{1,0:T(8,128)S(1)}, u32[]{:S(2)}, u32[]{:S(2)}) collective-permute-start(f32[32,1024]{1,0:T(8,128)S(1)} %constant_dynamic-slice_fusion), channel_id=1, source_target_pairs={{0,2},{1,3},{2,0},{3,1},{4,6},{5,7},{6,4},{7,5},{8,10},{9,11},{10,... | collective-permute-start | bytes 393224 | tf_op jit(solution)/shard_map/ppermute | solution.py:53
  542.8 7.4 %collective-permute-start.76 = (f32[32,1024]{1,0:T(8,128)S(1)}, f32[32,1024]{1,0:T(8,128)S(1)}, u32[]{:S(2)}, u32[]{:S(2)}) collective-permute-start(f32[32,1024]{1,0:T(8,128)S(1)} %dynamic-slice_add_fusion.17), channel_id=1, source_target_pairs={{0,4},{1,5},{2,6},{3,7},{4,0},{5,1},{6,2},{7,3},{8,12},{9,13},{10,... | collective-permute-start | bytes 393224 | tf_op jit(solution)/shard_map/ppermute | solution.py:55
  (81 other events, 497.0 us)

commit v14 on v13

--- a/solution.py
+++ b/solution.py
@@ -43,6 +43,8 @@
         distance *= 2
     lanes = jnp.split(value, CHUNKS, axis=0)
     last = distances.pop()
+    if len(distances) > 1:
+        distances[0], distances[1] = distances[1], distances[0]
     for distance in distances:
         upper = (index // distance) % 2
         moved = []

time: 577 us -> 577 us (level)
  waiting for transfers between devices: 353 us -> 311 us
  starting transfers between devices: 66.7 us -> 108 us
    ppermute x24, starting transfers between devices: 9.72 us -> 29.8 us  [big_sum(): other = lax.ppermute(held, axis, partner_pairs(count, distance))]
    ppermute x24, waiting for transfers between devices: 54.2 us -> 39.3 us  [big_sum(): lax.ppermute(give, axis, partner_pairs(count, distance))]
    ppermute x24, starting transfers between devices: 13.9 us -> 26.8 us  [big_sum(): lax.ppermute(give, axis, partner_pairs(count, distance))]
    ppermute x24, waiting for transfers between devices: 42.5 us -> 31.9 us  [big_sum(): other = lax.ppermute(held, axis, partner_pairs(count, distance))]
    ppermute x22, waiting for transfers between devices: 54.7 us -> 46.5 us  [small_sum(): value = value + lax.ppermute(value, axis, partner_pairs(count, distance))]
    ppermute x22, starting transfers between devices: 14.5 us -> 22.6 us  [small_sum(): value = value + lax.ppermute(value, axis, partner_pairs(count, distance))]
    ppermute x16, waiting for transfers between devices: 71.6 us -> 64 us  [big_sum(): lax.ppermute(held, axis, partner_pairs(count, last))]
  transfers between devices with their start and end apart: 88 -> 88, of which waited for: 79 -> 73; matrix products, arithmetic and copies ran while one was open for 3% -> 3% of each run, Pallas kernels for 0% -> 0%
where the time goes in v14:
time: 577 us; the launch traced here: 573 us
  waiting for transfers between devices  311 us (54%)
  starting transfers between devices  108 us (19%)
  matrix products  92.7 us (16%)
  local copies, waits for them, and re-layouts  41.9 us (7%)
  other arithmetic  17.1 us (3%)
    all_to_all x1, waiting for transfers between devices, per_device(): lax.all_to_all(outgoing.reshape(col_count, capacity, block_size, block_si...  130 us
    ppermute x16, waiting for transfers between devices, big_sum(): lax.ppermute(held, axis, partner_pairs(count, last))  64 us
    ppermute x22, waiting for transfers between devices, small_sum(): value = value + lax.ppermute(value, axis, partner_pairs(count, distance))  46.5 us
    ppermute x24, waiting for transfers between devices, big_sum(): lax.ppermute(give, axis, partner_pairs(count, distance))  39.3 us
    dot_general x8, matrix products, place_terms(): jnp.einsum('ksi,st->kti', weighted, onehot, precision=lax.Precision.HIGH)  37.8 us
    dot_general x4, matrix products, forward_terms(): jnp.einsum('sij,ksj->ksi', blocks, picked, preferred_element_type=jnp.flo...  32.6 us
    ppermute x24, waiting for transfers between devices, big_sum(): other = lax.ppermute(held, axis, partner_pairs(count, distance))  31.9 us
    ppermute x24, starting transfers between devices, big_sum(): other = lax.ppermute(held, axis, partner_pairs(count, distance))  29.8 us
  transfers between devices with their start and end apart: 88, of which 73 were waited for; matrix products, arithmetic and copies ran while one was open for 3% of the time, Pallas kernels for 0%

profile of v14, /device:TPU:0, one launch (start us, length us, event | category | flops | bytes accessed | tf_op | source)
XLA Modules:
  0.0 573.2 jit_solution(4019954950127747759)
XLA Ops:
  5.5 7.3 %all-to-all-start = ((s32[8,24,2]{1,2,0:T(2,128)}), s32[8,24,2]{1,2,0:T(2,128)S(1)}, u32[]{:S(2)}, u32[]{:S(2)}) async-start(s32[8,24,2]{1,2,0:T(2,128)} %copy.153), calls=%async_computation | async-start | bytes 16384 | tf_op jit(solution)/shard_map/all_to_all | solution.py:127
  14.8 8.0 %gather_fusion.1 = bf16[192,128,128]{2,1,0:T(8,128)(2,1)} fusion(bf16[97,128,128]{2,1,0:T(8,128)(2,1)S(1)} %concatenate.273, s32[1024]{0:T(1024)S(1)} %pad_clamp_fusion.2), kind=kCustom, calls=%fused_computation.9 | custom fusion | bytes 12583680 | tf_op jit(solution)/shard_map/jit(_take)/gather | solution.py:114
  22.9 6.3 %all-to-all-start.1 = ((bf16[8,24,128,128]{3,2,1,0:T(8,128)(2,1)}), bf16[8,24,128,128]{3,2,1,0:T(8,128)(2,1)}, u32[]{:S(2)}, u32[]{:S(2)}) async-start(bf16[8,24,128,128]{3,2,1,0:T(8,128)(2,1)} %bitcast.272), calls=%async_computation.1 | async-start | bytes 12582912 | tf_op jit(solution)/shard_map/all_to_all | solution.py:120
  37.1 129.6 %all-to-all-done.1 = bf16[8,24,128,128]{3,2,1,0:T(8,128)(2,1)} async-done(((bf16[8,24,128,128]{3,2,1,0:T(8,128)(2,1)}), bf16[8,24,128,128]{3,2,1,0:T(8,128)(2,1)}, u32[]{:S(2)}, u32[]{:S(2)}) %all-to-all-start.1) | async-done | bytes 6291488 | tf_op jit(solution)/shard_map/all_to_all | solution.py:120
  166.7 5.6 fusion.48
  172.2 4.7 fusion.80
  181.2 7.0 %collective-permute-done.3 = f32[32,2048]{1,0:T(8,128)S(1)} collective-permute-done((f32[32,2048]{1,0:T(8,128)S(1)}, f32[32,2048]{1,0:T(8,128)S(1)}, u32[]{:S(2)}, u32[]{:S(2)}) %collective-permute-start.3) | collective-permute-done | bytes 262176 | tf_op jit(solution)/shard_map/ppermute | solution.py:57
  209.6 8.3 %fusion.51 = f32[64,192,128]{2,0,1:T(8,128)S(1)} fusion(bf16[192,128,128]{2,1,0:T(8,128)(2,1)} %bitcast.11, bf16[192,64,128]{2,1,0:T(8,128)(2,1)} %gather_fusion.3, pred[192]{0:T(512)(128)(4,1)S(1)} %get-tuple-element.55), kind=kOutput, calls=%fused_computation.59 | convolution fusion | flops 404226048 | bytes 15728832 | tf_op jit(solution)/shard_map/sij,ksj->ksi/dot_general | solution.py:87
  225.4 5.3 collective-permute-done.11
  265.5 5.6 fusion.54
  271.1 5.1 fusion.86
  280.4 7.0 %collective-permute-done.24 = f32[32,2048]{1,0:T(8,128)S(1)} collective-permute-done((f32[32,2048]{1,0:T(8,128)S(1)}, f32[32,2048]{1,0:T(8,128)S(1)}, u32[]{:S(2)}, u32[]{:S(2)}) %collective-permute-start.24) | collective-permute-done | bytes 262176 | tf_op jit(solution)/shard_map/ppermute | solution.py:57
  310.1 8.1 %fusion.57 = f32[64,192,128]{2,0,1:T(8,128)S(1)} fusion(bf16[192,128,128]{2,1,0:T(8,128)(2,1)} %bitcast.11, bf16[192,64,128]{2,1,0:T(8,128)(2,1)} %gather_fusion.5, pred[192]{0:T(512)(128)(4,1)S(1)} %get-tuple-element.55), kind=kOutput, calls=%fused_computation.61 | convolution fusion | flops 404226048 | bytes 15728832 | tf_op jit(solution)/shard_map/sij,ksj->ksi/dot_general | solution.py:87
  318.2 4.8 fusion.89
  325.9 5.3 collective-permute-done.32
  366.9 5.6 fusion.60
  381.4 7.0 %collective-permute-done.45 = f32[32,2048]{1,0:T(8,128)S(1)} collective-permute-done((f32[32,2048]{1,0:T(8,128)S(1)}, f32[32,2048]{1,0:T(8,128)S(1)}, u32[]{:S(2)}, u32[]{:S(2)}) %collective-permute-start.45) | collective-permute-done | bytes 262176 | tf_op jit(solution)/shard_map/ppermute | solution.py:57
  412.1 8.1 %fusion.63 = f32[64,192,128]{2,0,1:T(8,128)S(1)} fusion(bf16[192,128,128]{2,1,0:T(8,128)(2,1)} %bitcast.11, bf16[192,64,128]{2,1,0:T(8,128)(2,1)} %gather_fusion.7, pred[192]{0:T(512)(128)(4,1)S(1)} %get-tuple-element.55), kind=kOutput, calls=%fused_computation.63 | convolution fusion | flops 404226048 | bytes 15728832 | tf_op jit(solution)/shard_map/sij,ksj->ksi/dot_general | solution.py:87
  427.7 5.6 collective-permute-done.53
  470.2 5.6 fusion.66
  475.8 4.7 fusion.98
  484.8 7.0 %collective-permute-done.66 = f32[32,2048]{1,0:T(8,128)S(1)} collective-permute-done((f32[32,2048]{1,0:T(8,128)S(1)}, f32[32,2048]{1,0:T(8,128)S(1)}, u32[]{:S(2)}, u32[]{:S(2)}) %collective-permute-start.66) | collective-permute-done | bytes 262176 | tf_op jit(solution)/shard_map/ppermute | solution.py:57
  514.9 8.2 %fusion.69 = f32[64,192,128]{2,0,1:T(8,128)S(1)} fusion(bf16[192,128,128]{2,1,0:T(8,128)(2,1)} %bitcast.11, bf16[192,64,128]{2,1,0:T(8,128)(2,1)} %gather_fusion.9, pred[192]{0:T(512)(128)(4,1)S(1)} %get-tuple-element.55), kind=kOutput, calls=%fused_computation.65 | convolution fusion | flops 404226048 | bytes 15728832 | tf_op jit(solution)/shard_map/sij,ksj->ksi/dot_general | solution.py:87
  530.7 5.5 collective-permute-done.74
  (413 shorter events, 295.6 us)
Async XLA Ops:
  5.5 17.4 %all-to-all-start = ((s32[8,24,2]{1,2,0:T(2,128)}), s32[8,24,2]{1,2,0:T(2,128)S(1)}, u32[]{:S(2)}, u32[]{:S(2)}) async-start(s32[8,24,2]{1,2,0:T(2,128)} %copy.153), calls=%async_computation | async-start | bytes 16384 | tf_op jit(solution)/shard_map/all_to_all | solution.py:127
  22.9 143.8 %all-to-all-start.1 = ((bf16[8,24,128,128]{3,2,1,0:T(8,128)(2,1)}), bf16[8,24,128,128]{3,2,1,0:T(8,128)(2,1)}, u32[]{:S(2)}, u32[]{:S(2)}) async-start(bf16[8,24,128,128]{3,2,1,0:T(8,128)(2,1)} %bitcast.272), calls=%async_computation.1 | async-start | bytes 12582912 | tf_op jit(solution)/shard_map/all_to_all | solution.py:120
  179.0 9.2 %collective-permute-start.3 = (f32[32,2048]{1,0:T(8,128)S(1)}, f32[32,2048]{1,0:T(8,128)S(1)}, u32[]{:S(2)}, u32[]{:S(2)}) collective-permute-start(f32[32,2048]{1,0:T(8,128)S(1)} %dynamic-slice_add_fusion.15), channel_id=1, source_target_pairs={{0,16},{8,24},{16,0},{24,8},{1,17},{9,25},{17,1},{25,9},{2,18},{10... | collective-permute-start | bytes 786440 | tf_op jit(solution)/shard_map/ppermute | solution.py:57
  180.6 12.5 %collective-permute-start.6 = (f32[32,2048]{1,0:T(8,128)S(1)}, f32[32,2048]{1,0:T(8,128)S(1)}, u32[]{:S(2)}, u32[]{:S(2)}) collective-permute-start(f32[32,2048]{1,0:T(8,128)S(1)} %dynamic-slice_add_fusion.14), channel_id=1, source_target_pairs={{0,16},{8,24},{16,0},{24,8},{1,17},{9,25},{17,1},{25,9},{2,18},{10... | collective-permute-start | bytes 786440 | tf_op jit(solution)/shard_map/ppermute | solution.py:57
  222.9 7.8 %collective-permute-start.11 = (f32[32,2048]{1,0:T(8,128)S(1)}, f32[32,2048]{1,0:T(8,128)S(1)}, u32[]{:S(2)}, u32[]{:S(2)}) collective-permute-start(f32[32,2048]{1,0:T(8,128)S(1)} %constant_dynamic-slice_fusion.21), channel_id=1, source_target_pairs={{0,2},{1,3},{2,0},{3,1},{4,6},{5,7},{6,4},{7,5},{8,10},{9,11},{10,... | collective-permute-start | bytes 786440 | tf_op jit(solution)/shard_map/ppermute | solution.py:55
  223.4 10.1 %collective-permute-start.16 = (f32[32,2048]{1,0:T(8,128)S(1)}, f32[32,2048]{1,0:T(8,128)S(1)}, u32[]{:S(2)}, u32[]{:S(2)}) collective-permute-start(f32[32,2048]{1,0:T(8,128)S(1)} %constant_dynamic-slice_fusion.19), channel_id=1, source_target_pairs={{0,2},{1,3},{2,0},{3,1},{4,6},{5,7},{6,4},{7,5},{8,10},{9,11},{10,... | collective-permute-start | bytes 786440 | tf_op jit(solution)/shard_map/ppermute | solution.py:55
  235.8 7.1 %collective-permute-start.13 = (f32[32,1024]{1,0:T(8,128)S(1)}, f32[32,1024]{1,0:T(8,128)S(1)}, u32[]{:S(2)}, u32[]{:S(2)}) collective-permute-start(f32[32,1024]{1,0:T(8,128)S(1)} %dynamic-slice_add_fusion.23), channel_id=1, source_target_pairs={{0,4},{1,5},{2,6},{3,7},{4,0},{5,1},{6,2},{7,3},{8,12},{9,13},{10,... | collective-permute-start | bytes 393224 | tf_op jit(solution)/shard_map/ppermute | solution.py:57
  238.6 7.2 %collective-permute-start.18 = (f32[32,1024]{1,0:T(8,128)S(1)}, f32[32,1024]{1,0:T(8,128)S(1)}, u32[]{:S(2)}, u32[]{:S(2)}) collective-permute-start(f32[32,1024]{1,0:T(8,128)S(1)} %dynamic-slice_add_fusion.22), channel_id=1, source_target_pairs={{0,4},{1,5},{2,6},{3,7},{4,0},{5,1},{6,2},{7,3},{8,12},{9,13},{10,... | collective-permute-start | bytes 393224 | tf_op jit(solution)/shard_map/ppermute | solution.py:57
  278.2 9.2 %collective-permute-start.24 = (f32[32,2048]{1,0:T(8,128)S(1)}, f32[32,2048]{1,0:T(8,128)S(1)}, u32[]{:S(2)}, u32[]{:S(2)}) collective-permute-start(f32[32,2048]{1,0:T(8,128)S(1)} %dynamic-slice_add_fusion.11), channel_id=1, source_target_pairs={{0,16},{8,24},{16,0},{24,8},{1,17},{9,25},{17,1},{25,9},{2,18},{10... | collective-permute-start | bytes 786440 | tf_op jit(solution)/shard_map/ppermute | solution.py:57
  279.8 12.5 %collective-permute-start.27 = (f32[32,2048]{1,0:T(8,128)S(1)}, f32[32,2048]{1,0:T(8,128)S(1)}, u32[]{:S(2)}, u32[]{:S(2)}) collective-permute-start(f32[32,2048]{1,0:T(8,128)S(1)} %dynamic-slice_add_fusion.10), channel_id=1, source_target_pairs={{0,16},{8,24},{16,0},{24,8},{1,17},{9,25},{17,1},{25,9},{2,18},{10... | collective-permute-start | bytes 786440 | tf_op jit(solution)/shard_map/ppermute | solution.py:57
  323.4 7.8 %collective-permute-start.32 = (f32[32,2048]{1,0:T(8,128)S(1)}, f32[32,2048]{1,0:T(8,128)S(1)}, u32[]{:S(2)}, u32[]{:S(2)}) collective-permute-start(f32[32,2048]{1,0:T(8,128)S(1)} %constant_dynamic-slice_fusion.15), channel_id=1, source_target_pairs={{0,2},{1,3},{2,0},{3,1},{4,6},{5,7},{6,4},{7,5},{8,10},{9,11},{10,... | collective-permute-start | bytes 786440 | tf_op jit(solution)/shard_map/ppermute | solution.py:55
  324.3 9.7 %collective-permute-start.37 = (f32[32,2048]{1,0:T(8,128)S(1)}, f32[32,2048]{1,0:T(8,128)S(1)}, u32[]{:S(2)}, u32[]{:S(2)}) collective-permute-start(f32[32,2048]{1,0:T(8,128)S(1)} %constant_dynamic-slice_fusion.13), channel_id=1, source_target_pairs={{0,2},{1,3},{2,0},{3,1},{4,6},{5,7},{6,4},{7,5},{8,10},{9,11},{10,... | collective-permute-start | bytes 786440 | tf_op jit(solution)/shard_map/ppermute | solution.py:55
  336.4 7.3 %collective-permute-start.34 = (f32[32,1024]{1,0:T(8,128)S(1)}, f32[32,1024]{1,0:T(8,128)S(1)}, u32[]{:S(2)}, u32[]{:S(2)}) collective-permute-start(f32[32,1024]{1,0:T(8,128)S(1)} %dynamic-slice_add_fusion.21), channel_id=1, source_target_pairs={{0,4},{1,5},{2,6},{3,7},{4,0},{5,1},{6,2},{7,3},{8,12},{9,13},{10,... | collective-permute-start | bytes 393224 | tf_op jit(solution)/shard_map/ppermute | solution.py:57
  379.2 9.2 %collective-permute-start.45 = (f32[32,2048]{1,0:T(8,128)S(1)}, f32[32,2048]{1,0:T(8,128)S(1)}, u32[]{:S(2)}, u32[]{:S(2)}) collective-permute-start(f32[32,2048]{1,0:T(8,128)S(1)} %dynamic-slice_add_fusion.7), channel_id=1, source_target_pairs={{0,16},{8,24},{16,0},{24,8},{1,17},{9,25},{17,1},{25,9},{2,18},{10... | collective-permute-start | bytes 786440 | tf_op jit(solution)/shard_map/ppermute | solution.py:57
  380.6 12.5 %collective-permute-start.48 = (f32[32,2048]{1,0:T(8,128)S(1)}, f32[32,2048]{1,0:T(8,128)S(1)}, u32[]{:S(2)}, u32[]{:S(2)}) collective-permute-start(f32[32,2048]{1,0:T(8,128)S(1)} %dynamic-slice_add_fusion.6), channel_id=1, source_target_pairs={{0,16},{8,24},{16,0},{24,8},{1,17},{9,25},{17,1},{25,9},{2,18},{10... | collective-permute-start | bytes 786440 | tf_op jit(solution)/shard_map/ppermute | solution.py:57
  425.2 8.1 %collective-permute-start.53 = (f32[32,2048]{1,0:T(8,128)S(1)}, f32[32,2048]{1,0:T(8,128)S(1)}, u32[]{:S(2)}, u32[]{:S(2)}) collective-permute-start(f32[32,2048]{1,0:T(8,128)S(1)} %constant_dynamic-slice_fusion.9), channel_id=1, source_target_pairs={{0,2},{1,3},{2,0},{3,1},{4,6},{5,7},{6,4},{7,5},{8,10},{9,11},{10,... | collective-permute-start | bytes 786440 | tf_op jit(solution)/shard_map/ppermute | solution.py:55
  427.1 8.9 %collective-permute-start.58 = (f32[32,2048]{1,0:T(8,128)S(1)}, f32[32,2048]{1,0:T(8,128)S(1)}, u32[]{:S(2)}, u32[]{:S(2)}) collective-permute-start(f32[32,2048]{1,0:T(8,128)S(1)} %constant_dynamic-slice_fusion.7), channel_id=1, source_target_pairs={{0,2},{1,3},{2,0},{3,1},{4,6},{5,7},{6,4},{7,5},{8,10},{9,11},{10,... | collective-permute-start | bytes 786440 | tf_op jit(solution)/shard_map/ppermute | solution.py:55
  439.0 7.3 %collective-permute-start.55 = (f32[32,1024]{1,0:T(8,128)S(1)}, f32[32,1024]{1,0:T(8,128)S(1)}, u32[]{:S(2)}, u32[]{:S(2)}) collective-permute-start(f32[32,1024]{1,0:T(8,128)S(1)} %dynamic-slice_add_fusion.19), channel_id=1, source_target_pairs={{0,4},{1,5},{2,6},{3,7},{4,0},{5,1},{6,2},{7,3},{8,12},{9,13},{10,... | collective-permute-start | bytes 393224 | tf_op jit(solution)/shard_map/ppermute | solution.py:57
  482.6 9.2 %collective-permute-start.66 = (f32[32,2048]{1,0:T(8,128)S(1)}, f32[32,2048]{1,0:T(8,128)S(1)}, u32[]{:S(2)}, u32[]{:S(2)}) collective-permute-start(f32[32,2048]{1,0:T(8,128)S(1)} %dynamic-slice_add_fusion.3), channel_id=1, source_target_pairs={{0,16},{8,24},{16,0},{24,8},{1,17},{9,25},{17,1},{25,9},{2,18},{10... | collective-permute-start | bytes 786440 | tf_op jit(solution)/shard_map/ppermute | solution.py:57
  484.0 12.6 %collective-permute-start.69 = (f32[32,2048]{1,0:T(8,128)S(1)}, f32[32,2048]{1,0:T(8,128)S(1)}, u32[]{:S(2)}, u32[]{:S(2)}) collective-permute-start(f32[32,2048]{1,0:T(8,128)S(1)} %dynamic-slice_add_fusion.2), channel_id=1, source_target_pairs={{0,16},{8,24},{16,0},{24,8},{1,17},{9,25},{17,1},{25,9},{2,18},{10... | collective-permute-start | bytes 786440 | tf_op jit(solution)/shard_map/ppermute | solution.py:57
  528.2 8.1 %collective-permute-start.74 = (f32[32,2048]{1,0:T(8,128)S(1)}, f32[32,2048]{1,0:T(8,128)S(1)}, u32[]{:S(2)}, u32[]{:S(2)}) collective-permute-start(f32[32,2048]{1,0:T(8,128)S(1)} %constant_dynamic-slice_fusion.3), channel_id=1, source_target_pairs={{0,2},{1,3},{2,0},{3,1},{4,6},{5,7},{6,4},{7,5},{8,10},{9,11},{10,... | collective-permute-start | bytes 786440 | tf_op jit(solution)/shard_map/ppermute | solution.py:55
  530.6 9.1 %collective-permute-start.79 = (f32[32,2048]{1,0:T(8,128)S(1)}, f32[32,2048]{1,0:T(8,128)S(1)}, u32[]{:S(2)}, u32[]{:S(2)}) collective-permute-start(f32[32,2048]{1,0:T(8,128)S(1)} %constant_dynamic-slice_fusion.1), channel_id=1, source_target_pairs={{0,2},{1,3},{2,0},{3,1},{4,6},{5,7},{6,4},{7,5},{8,10},{9,11},{10,... | collective-permute-start | bytes 786440 | tf_op jit(solution)/shard_map/ppermute | solution.py:55
  541.8 7.3 %collective-permute-start.76 = (f32[32,1024]{1,0:T(8,128)S(1)}, f32[32,1024]{1,0:T(8,128)S(1)}, u32[]{:S(2)}, u32[]{:S(2)}) collective-permute-start(f32[32,1024]{1,0:T(8,128)S(1)} %dynamic-slice_add_fusion.17), channel_id=1, source_target_pairs={{0,4},{1,5},{2,6},{3,7},{4,0},{5,1},{6,2},{7,3},{8,12},{9,13},{10,... | collective-permute-start | bytes 393224 | tf_op jit(solution)/shard_map/ppermute | solution.py:57
  557.6 7.3 %collective-permute-start.83 = (f32[32,2048]{1,0:T(8,128)S(1)}, f32[32,2048]{1,0:T(8,128)S(1)}, u32[]{:S(2)}, u32[]{:S(2)}) collective-permute-start(f32[32,2048]{1,0:T(8,128)S(1)} %maximum_select_fusion.31), channel_id=1, source_target_pairs={{0,2},{1,3},{2,0},{3,1},{4,6},{5,7},{6,4},{7,5},{8,10},{9,11},{10,... | collective-permute-start | bytes 786440 | tf_op jit(solution)/shard_map/ppermute | solution.py:62
  (81 other events, 498.1 us)

commit v15 on v13

--- a/solution.py
+++ b/solution.py
@@ -43,20 +43,23 @@
         distance *= 2
     lanes = jnp.split(value, CHUNKS, axis=0)
     last = distances.pop()
-    for distance in distances:
-        upper = (index // distance) % 2
+    orders = [distances[lane % len(distances):] + distances[:lane % len(distances)] if distances else [] for lane in range(CHUNKS)]
+    for step in range(len(distances)):
         moved = []
-        for held in lanes:
+        for lane, held in enumerate(lanes):
+            distance = orders[lane][step]
+            upper = (index // distance) % 2
             half = held.shape[-1] // 2
             keep = lax.dynamic_slice_in_dim(held, upper * half, half, held.ndim - 1)
             give = lax.dynamic_slice_in_dim(held, (1 - upper) * half, half, held.ndim - 1)
             moved.append(keep + lax.ppermute(give, axis, partner_pairs(count, distance)))
         lanes = moved
     lanes = [held + lax.ppermute(held, axis, partner_pairs(count, last)) for held in lanes]
-    for distance in reversed(distances):
-        upper = (index // distance) % 2
+    for step in reversed(range(len(distances))):
         moved = []
-        for held in lanes:
+        for lane, held in enumerate(lanes):
+            distance = orders[lane][step]
+            upper = (index // distance) % 2
             other = lax.ppermute(held, axis, partner_pairs(count, distance))
             moved.append(jnp.where(
                 upper == 1,

time: 577 us -> 575 us (level)
  waiting for transfers between devices: 353 us -> 334 us
  starting transfers between devices: 66.7 us -> 82.8 us
    ppermute x24, waiting for transfers between devices: 54.2 us -> 42.3 us  [big_sum(): lax.ppermute(give, axis, partner_pairs(count, distance))]
    ppermute x24, starting transfers between devices: 9.72 us -> 18.9 us  [big_sum(): other = lax.ppermute(held, axis, partner_pairs(count, distance))]
  transfers between devices with their start and end apart: 88 -> 88, of which waited for: 79 -> 75; matrix products, arithmetic and copies ran while one was open for 3% -> 3% of each run, Pallas kernels for 0% -> 0%
where the time goes in v15:
time: 575 us; the launch traced here: 571 us
  waiting for transfers between devices  334 us (58%)
  matrix products  92.7 us (16%)
  starting transfers between devices  82.8 us (14%)
  local copies, waits for them, and re-layouts  41.9 us (7%)
  other arithmetic  17.3 us (3%)
    all_to_all x1, waiting for transfers between devices, per_device(): lax.all_to_all(outgoing.reshape(col_count, capacity, block_size, block_si...  130 us
    ppermute x16, waiting for transfers between devices, big_sum(): lax.ppermute(held, axis, partner_pairs(count, last))  71.3 us
    ppermute x22, waiting for transfers between devices, small_sum(): value = value + lax.ppermute(value, axis, partner_pairs(count, distance))  52.2 us
    ppermute x24, waiting for transfers between devices, big_sum(): lax.ppermute(give, axis, partner_pairs(count, distance))  42.3 us
    ppermute x24, waiting for transfers between devices, big_sum(): other = lax.ppermute(held, axis, partner_pairs(count, distance))  38.5 us
    dot_general x8, matrix products, place_terms(): jnp.einsum('ksi,st->kti', weighted, onehot, precision=lax.Precision.HIGH)  37.8 us
    dot_general x4, matrix products, forward_terms(): jnp.einsum('sij,ksj->ksi', blocks, picked, preferred_element_type=jnp.flo...  32.6 us
    gather x8, local copies, waits for them, and re-layouts, gather_tiles(): return jnp.take(vector_tiles, indices, axis=1)  22.8 us
  transfers between devices with their start and end apart: 88, of which 75 were waited for; matrix products, arithmetic and copies ran while one was open for 3% of the time, Pallas kernels for 0%

profile of v15, /device:TPU:0, one launch (start us, length us, event | category | flops | bytes accessed | tf_op | source)
XLA Modules:
  0.0 571.0 jit_solution(15103606523810819692)
XLA Ops:
  5.5 7.3 %all-to-all-start = ((s32[8,24,2]{1,2,0:T(2,128)}), s32[8,24,2]{1,2,0:T(2,128)S(1)}, u32[]{:S(2)}, u32[]{:S(2)}) async-start(s32[8,24,2]{1,2,0:T(2,128)} %copy.153), calls=%async_computation | async-start | bytes 16384 | tf_op jit(solution)/shard_map/all_to_all | solution.py:128
  14.8 8.0 %gather_fusion.1 = bf16[192,128,128]{2,1,0:T(8,128)(2,1)} fusion(bf16[97,128,128]{2,1,0:T(8,128)(2,1)S(1)} %concatenate.273, s32[1024]{0:T(1024)S(1)} %pad_clamp_fusion.2), kind=kCustom, calls=%fused_computation.9 | custom fusion | bytes 12583680 | tf_op jit(solution)/shard_map/jit(_take)/gather | solution.py:115
  22.8 6.3 %all-to-all-start.1 = ((bf16[8,24,128,128]{3,2,1,0:T(8,128)(2,1)}), bf16[8,24,128,128]{3,2,1,0:T(8,128)(2,1)}, u32[]{:S(2)}, u32[]{:S(2)}) async-start(bf16[8,24,128,128]{3,2,1,0:T(8,128)(2,1)} %bitcast.272), calls=%async_computation.1 | async-start | bytes 12582912 | tf_op jit(solution)/shard_map/all_to_all | solution.py:121
  37.1 129.6 %all-to-all-done.1 = bf16[8,24,128,128]{3,2,1,0:T(8,128)(2,1)} async-done(((bf16[8,24,128,128]{3,2,1,0:T(8,128)(2,1)}), bf16[8,24,128,128]{3,2,1,0:T(8,128)(2,1)}, u32[]{:S(2)}, u32[]{:S(2)}) %all-to-all-start.1) | async-done | bytes 6291488 | tf_op jit(solution)/shard_map/all_to_all | solution.py:121
  166.7 5.6 fusion.48
  181.2 7.0 %collective-permute-done.3 = f32[32,2048]{1,0:T(8,128)S(1)} collective-permute-done((f32[32,2048]{1,0:T(8,128)S(1)}, f32[32,2048]{1,0:T(8,128)S(1)}, u32[]{:S(2)}, u32[]{:S(2)}) %collective-permute-start.3) | collective-permute-done | bytes 262176 | tf_op jit(solution)/shard_map/ppermute | solution.py:57
  209.5 8.3 %fusion.51 = f32[64,192,128]{2,0,1:T(8,128)S(1)} fusion(bf16[192,128,128]{2,1,0:T(8,128)(2,1)} %bitcast.11, bf16[192,64,128]{2,1,0:T(8,128)(2,1)} %gather_fusion.3, pred[192]{0:T(512)(128)(4,1)S(1)} %get-tuple-element.55), kind=kOutput, calls=%fused_computation.59 | convolution fusion | flops 404226048 | bytes 15728832 | tf_op jit(solution)/shard_map/sij,ksj->ksi/dot_general | solution.py:88
  266.6 5.6 fusion.54
  272.2 5.1 fusion.86
  281.5 7.0 %collective-permute-done.24 = f32[32,2048]{1,0:T(8,128)S(1)} collective-permute-done((f32[32,2048]{1,0:T(8,128)S(1)}, f32[32,2048]{1,0:T(8,128)S(1)}, u32[]{:S(2)}, u32[]{:S(2)}) %collective-permute-start.24) | collective-permute-done | bytes 262176 | tf_op jit(solution)/shard_map/ppermute | solution.py:57
  311.2 8.1 %fusion.57 = f32[64,192,128]{2,0,1:T(8,128)S(1)} fusion(bf16[192,128,128]{2,1,0:T(8,128)(2,1)} %bitcast.11, bf16[192,64,128]{2,1,0:T(8,128)(2,1)} %gather_fusion.5, pred[192]{0:T(512)(128)(4,1)S(1)} %get-tuple-element.55), kind=kOutput, calls=%fused_computation.61 | convolution fusion | flops 404226048 | bytes 15728832 | tf_op jit(solution)/shard_map/sij,ksj->ksi/dot_general | solution.py:88
  319.3 4.8 fusion.89
  325.9 6.0 %collective-permute-done.32 = f32[32,2048]{1,0:T(8,128)S(1)} collective-permute-done((f32[32,2048]{1,0:T(8,128)S(1)}, f32[32,2048]{1,0:T(8,128)S(1)}, u32[]{:S(2)}, u32[]{:S(2)}) %collective-permute-start.32) | collective-permute-done | bytes 262176 | tf_op jit(solution)/shard_map/ppermute | solution.py:55
  340.3 5.7 collective-permute-done.34
  353.3 5.3 collective-permute-done.36
  367.1 5.6 fusion.60
  381.6 7.0 %collective-permute-done.45 = f32[32,2048]{1,0:T(8,128)S(1)} collective-permute-done((f32[32,2048]{1,0:T(8,128)S(1)}, f32[32,2048]{1,0:T(8,128)S(1)}, u32[]{:S(2)}, u32[]{:S(2)}) %collective-permute-start.45) | collective-permute-done | bytes 262176 | tf_op jit(solution)/shard_map/ppermute | solution.py:57
  412.3 8.1 %fusion.63 = f32[64,192,128]{2,0,1:T(8,128)S(1)} fusion(bf16[192,128,128]{2,1,0:T(8,128)(2,1)} %bitcast.11, bf16[192,64,128]{2,1,0:T(8,128)(2,1)} %gather_fusion.7, pred[192]{0:T(512)(128)(4,1)S(1)} %get-tuple-element.55), kind=kOutput, calls=%fused_computation.63 | convolution fusion | flops 404226048 | bytes 15728832 | tf_op jit(solution)/shard_map/sij,ksj->ksi/dot_general | solution.py:88
  470.0 5.6 fusion.66
  484.5 7.0 %collective-permute-done.66 = f32[32,2048]{1,0:T(8,128)S(1)} collective-permute-done((f32[32,2048]{1,0:T(8,128)S(1)}, f32[32,2048]{1,0:T(8,128)S(1)}, u32[]{:S(2)}, u32[]{:S(2)}) %collective-permute-start.66) | collective-permute-done | bytes 262176 | tf_op jit(solution)/shard_map/ppermute | solution.py:57
  514.6 8.2 %fusion.69 = f32[64,192,128]{2,0,1:T(8,128)S(1)} fusion(bf16[192,128,128]{2,1,0:T(8,128)(2,1)} %bitcast.11, bf16[192,64,128]{2,1,0:T(8,128)(2,1)} %gather_fusion.9, pred[192]{0:T(512)(128)(4,1)S(1)} %get-tuple-element.55), kind=kOutput, calls=%fused_computation.65 | convolution fusion | flops 404226048 | bytes 15728832 | tf_op jit(solution)/shard_map/sij,ksj->ksi/dot_general | solution.py:88
  529.8 5.4 collective-permute-done.74
  544.1 5.7 collective-permute-done.76
  557.0 4.8 collective-permute-done.78
  (413 shorter events, 291.8 us)
Async XLA Ops:
  5.5 17.4 %all-to-all-start = ((s32[8,24,2]{1,2,0:T(2,128)}), s32[8,24,2]{1,2,0:T(2,128)S(1)}, u32[]{:S(2)}, u32[]{:S(2)}) async-start(s32[8,24,2]{1,2,0:T(2,128)} %copy.153), calls=%async_computation | async-start | bytes 16384 | tf_op jit(solution)/shard_map/all_to_all | solution.py:128
  22.8 143.8 %all-to-all-start.1 = ((bf16[8,24,128,128]{3,2,1,0:T(8,128)(2,1)}), bf16[8,24,128,128]{3,2,1,0:T(8,128)(2,1)}, u32[]{:S(2)}, u32[]{:S(2)}) async-start(bf16[8,24,128,128]{3,2,1,0:T(8,128)(2,1)} %bitcast.272), calls=%async_computation.1 | async-start | bytes 12582912 | tf_op jit(solution)/shard_map/all_to_all | solution.py:121
  179.0 9.2 %collective-permute-start.3 = (f32[32,2048]{1,0:T(8,128)S(1)}, f32[32,2048]{1,0:T(8,128)S(1)}, u32[]{:S(2)}, u32[]{:S(2)}) collective-permute-start(f32[32,2048]{1,0:T(8,128)S(1)} %dynamic-slice_add_fusion.15), channel_id=1, source_target_pairs={{0,16},{8,24},{16,0},{24,8},{1,17},{9,25},{17,1},{25,9},{2,18},{10... | collective-permute-start | bytes 786440 | tf_op jit(solution)/shard_map/ppermute | solution.py:57
  180.6 12.4 %collective-permute-start.6 = (f32[32,2048]{1,0:T(8,128)S(1)}, f32[32,2048]{1,0:T(8,128)S(1)}, u32[]{:S(2)}, u32[]{:S(2)}) collective-permute-start(f32[32,2048]{1,0:T(8,128)S(1)} %dynamic-slice_add_fusion.14), channel_id=1, source_target_pairs={{0,16},{8,24},{16,0},{24,8},{1,17},{9,25},{17,1},{25,9},{2,18},{10... | collective-permute-start | bytes 786440 | tf_op jit(solution)/shard_map/ppermute | solution.py:57
  224.8 7.0 %collective-permute-start.16 = (f32[32,2048]{1,0:T(8,128)S(1)}, f32[32,2048]{1,0:T(8,128)S(1)}, u32[]{:S(2)}, u32[]{:S(2)}) collective-permute-start(f32[32,2048]{1,0:T(8,128)S(1)} %constant_dynamic-slice_fusion.19), channel_id=1, source_target_pairs={{0,2},{1,3},{2,0},{3,1},{4,6},{5,7},{6,4},{7,5},{8,10},{9,11},{10,... | collective-permute-start | bytes 786440 | tf_op jit(solution)/shard_map/ppermute | solution.py:55
  237.5 7.4 %collective-permute-start.18 = (f32[32,1024]{1,0:T(8,128)S(1)}, f32[32,1024]{1,0:T(8,128)S(1)}, u32[]{:S(2)}, u32[]{:S(2)}) collective-permute-start(f32[32,1024]{1,0:T(8,128)S(1)} %dynamic-slice_add_fusion.22), channel_id=1, source_target_pairs={{0,4},{1,5},{2,6},{3,7},{4,0},{5,1},{6,2},{7,3},{8,12},{9,13},{10,... | collective-permute-start | bytes 393224 | tf_op jit(solution)/shard_map/ppermute | solution.py:57
  245.0 7.0 %collective-permute-start.19 = (f32[32,1024]{1,0:T(8,128)S(1)}, f32[32,1024]{1,0:T(8,128)S(1)}, u32[]{:S(2)}, u32[]{:S(2)}) collective-permute-start(f32[32,1024]{1,0:T(8,128)S(1)} %add.407), channel_id=1, source_target_pairs={{0,1},{1,0},{2,3},{3,2},{4,5},{5,4},{6,7},{7,6},{8,9},{9,8},{10,11... | collective-permute-start | bytes 393224 | tf_op jit(solution)/shard_map/ppermute | solution.py:63
  247.6 8.7 %collective-permute-start.15 = (f32[32,2048]{1,0:T(8,128)S(1)}, f32[32,2048]{1,0:T(8,128)S(1)}, u32[]{:S(2)}, u32[]{:S(2)}) collective-permute-start(f32[32,2048]{1,0:T(8,128)S(1)} %maximum_select_fusion.24), channel_id=1, source_target_pairs={{0,1},{1,0},{2,3},{3,2},{4,5},{5,4},{6,7},{7,6},{8,9},{9,8},{10,11... | collective-permute-start | bytes 786440 | tf_op jit(solution)/shard_map/ppermute | solution.py:63
  279.3 9.2 %collective-permute-start.24 = (f32[32,2048]{1,0:T(8,128)S(1)}, f32[32,2048]{1,0:T(8,128)S(1)}, u32[]{:S(2)}, u32[]{:S(2)}) collective-permute-start(f32[32,2048]{1,0:T(8,128)S(1)} %dynamic-slice_add_fusion.11), channel_id=1, source_target_pairs={{0,16},{8,24},{16,0},{24,8},{1,17},{9,25},{17,1},{25,9},{2,18},{10... | collective-permute-start | bytes 786440 | tf_op jit(solution)/shard_map/ppermute | solution.py:57
  280.9 12.4 %collective-permute-start.27 = (f32[32,2048]{1,0:T(8,128)S(1)}, f32[32,2048]{1,0:T(8,128)S(1)}, u32[]{:S(2)}, u32[]{:S(2)}) collective-permute-start(f32[32,2048]{1,0:T(8,128)S(1)} %dynamic-slice_add_fusion.10), channel_id=1, source_target_pairs={{0,16},{8,24},{16,0},{24,8},{1,17},{9,25},{17,1},{25,9},{2,18},{10... | collective-permute-start | bytes 786440 | tf_op jit(solution)/shard_map/ppermute | solution.py:57
  324.5 7.4 %collective-permute-start.32 = (f32[32,2048]{1,0:T(8,128)S(1)}, f32[32,2048]{1,0:T(8,128)S(1)}, u32[]{:S(2)}, u32[]{:S(2)}) collective-permute-start(f32[32,2048]{1,0:T(8,128)S(1)} %constant_dynamic-slice_fusion.15), channel_id=1, source_target_pairs={{0,1},{1,0},{2,3},{3,2},{4,5},{5,4},{6,7},{7,6},{8,9},{9,8},{10,11... | collective-permute-start | bytes 786440 | tf_op jit(solution)/shard_map/ppermute | solution.py:55
  325.1 7.8 %collective-permute-start.37 = (f32[32,2048]{1,0:T(8,128)S(1)}, f32[32,2048]{1,0:T(8,128)S(1)}, u32[]{:S(2)}, u32[]{:S(2)}) collective-permute-start(f32[32,2048]{1,0:T(8,128)S(1)} %constant_dynamic-slice_fusion.13), channel_id=1, source_target_pairs={{0,2},{1,3},{2,0},{3,1},{4,6},{5,7},{6,4},{7,5},{8,10},{9,11},{10,... | collective-permute-start | bytes 786440 | tf_op jit(solution)/shard_map/ppermute | solution.py:55
  337.3 8.7 %collective-permute-start.34 = (f32[32,1024]{1,0:T(8,128)S(1)}, f32[32,1024]{1,0:T(8,128)S(1)}, u32[]{:S(2)}, u32[]{:S(2)}) collective-permute-start(f32[32,1024]{1,0:T(8,128)S(1)} %dynamic-slice_add_fusion.21), channel_id=1, source_target_pairs={{0,4},{1,5},{2,6},{3,7},{4,0},{5,1},{6,2},{7,3},{8,12},{9,13},{10,... | collective-permute-start | bytes 393224 | tf_op jit(solution)/shard_map/ppermute | solution.py:57
  338.1 9.3 %collective-permute-start.39 = (f32[32,1024]{1,0:T(8,128)S(1)}, f32[32,1024]{1,0:T(8,128)S(1)}, u32[]{:S(2)}, u32[]{:S(2)}) collective-permute-start(f32[32,1024]{1,0:T(8,128)S(1)} %dynamic-slice_add_fusion.20), channel_id=1, source_target_pairs={{0,4},{1,5},{2,6},{3,7},{4,0},{5,1},{6,2},{7,3},{8,12},{9,13},{10,... | collective-permute-start | bytes 393224 | tf_op jit(solution)/shard_map/ppermute | solution.py:57
  379.4 9.2 %collective-permute-start.45 = (f32[32,2048]{1,0:T(8,128)S(1)}, f32[32,2048]{1,0:T(8,128)S(1)}, u32[]{:S(2)}, u32[]{:S(2)}) collective-permute-start(f32[32,2048]{1,0:T(8,128)S(1)} %dynamic-slice_add_fusion.7), channel_id=1, source_target_pairs={{0,16},{8,24},{16,0},{24,8},{1,17},{9,25},{17,1},{25,9},{2,18},{10... | collective-permute-start | bytes 786440 | tf_op jit(solution)/shard_map/ppermute | solution.py:57
  381.0 12.4 %collective-permute-start.48 = (f32[32,2048]{1,0:T(8,128)S(1)}, f32[32,2048]{1,0:T(8,128)S(1)}, u32[]{:S(2)}, u32[]{:S(2)}) collective-permute-start(f32[32,2048]{1,0:T(8,128)S(1)} %dynamic-slice_add_fusion.6), channel_id=1, source_target_pairs={{0,16},{8,24},{16,0},{24,8},{1,17},{9,25},{17,1},{25,9},{2,18},{10... | collective-permute-start | bytes 786440 | tf_op jit(solution)/shard_map/ppermute | solution.py:57
  440.5 7.8 %collective-permute-start.60 = (f32[32,1024]{1,0:T(8,128)S(1)}, f32[32,1024]{1,0:T(8,128)S(1)}, u32[]{:S(2)}, u32[]{:S(2)}) collective-permute-start(f32[32,1024]{1,0:T(8,128)S(1)} %dynamic-slice_add_fusion.18), channel_id=1, source_target_pairs={{0,4},{1,5},{2,6},{3,7},{4,0},{5,1},{6,2},{7,3},{8,12},{9,13},{10,... | collective-permute-start | bytes 393224 | tf_op jit(solution)/shard_map/ppermute | solution.py:57
  451.2 8.1 %collective-permute-start.57 = (f32[32,2048]{1,0:T(8,128)S(1)}, f32[32,2048]{1,0:T(8,128)S(1)}, u32[]{:S(2)}, u32[]{:S(2)}) collective-permute-start(f32[32,2048]{1,0:T(8,128)S(1)} %maximum_select_fusion.28), channel_id=1, source_target_pairs={{0,1},{1,0},{2,3},{3,2},{4,5},{5,4},{6,7},{7,6},{8,9},{9,8},{10,11... | collective-permute-start | bytes 786440 | tf_op jit(solution)/shard_map/ppermute | solution.py:63
  482.3 9.2 %collective-permute-start.66 = (f32[32,2048]{1,0:T(8,128)S(1)}, f32[32,2048]{1,0:T(8,128)S(1)}, u32[]{:S(2)}, u32[]{:S(2)}) collective-permute-start(f32[32,2048]{1,0:T(8,128)S(1)} %dynamic-slice_add_fusion.3), channel_id=1, source_target_pairs={{0,16},{8,24},{16,0},{24,8},{1,17},{9,25},{17,1},{25,9},{2,18},{10... | collective-permute-start | bytes 786440 | tf_op jit(solution)/shard_map/ppermute | solution.py:57
  483.9 12.4 %collective-permute-start.69 = (f32[32,2048]{1,0:T(8,128)S(1)}, f32[32,2048]{1,0:T(8,128)S(1)}, u32[]{:S(2)}, u32[]{:S(2)}) collective-permute-start(f32[32,2048]{1,0:T(8,128)S(1)} %dynamic-slice_add_fusion.2), channel_id=1, source_target_pairs={{0,16},{8,24},{16,0},{24,8},{1,17},{9,25},{17,1},{25,9},{2,18},{10... | collective-permute-start | bytes 786440 | tf_op jit(solution)/shard_map/ppermute | solution.py:57
  527.9 7.3 %collective-permute-start.74 = (f32[32,2048]{1,0:T(8,128)S(1)}, f32[32,2048]{1,0:T(8,128)S(1)}, u32[]{:S(2)}, u32[]{:S(2)}) collective-permute-start(f32[32,2048]{1,0:T(8,128)S(1)} %constant_dynamic-slice_fusion.3), channel_id=1, source_target_pairs={{0,1},{1,0},{2,3},{3,2},{4,5},{5,4},{6,7},{7,6},{8,9},{9,8},{10,11... | collective-permute-start | bytes 786440 | tf_op jit(solution)/shard_map/ppermute | solution.py:55
  529.0 7.8 %collective-permute-start.79 = (f32[32,2048]{1,0:T(8,128)S(1)}, f32[32,2048]{1,0:T(8,128)S(1)}, u32[]{:S(2)}, u32[]{:S(2)}) collective-permute-start(f32[32,2048]{1,0:T(8,128)S(1)} %constant_dynamic-slice_fusion.1), channel_id=1, source_target_pairs={{0,2},{1,3},{2,0},{3,1},{4,6},{5,7},{6,4},{7,5},{8,10},{9,11},{10,... | collective-permute-start | bytes 786440 | tf_op jit(solution)/shard_map/ppermute | solution.py:55
  541.0 8.7 %collective-permute-start.76 = (f32[32,1024]{1,0:T(8,128)S(1)}, f32[32,1024]{1,0:T(8,128)S(1)}, u32[]{:S(2)}, u32[]{:S(2)}) collective-permute-start(f32[32,1024]{1,0:T(8,128)S(1)} %dynamic-slice_add_fusion.17), channel_id=1, source_target_pairs={{0,4},{1,5},{2,6},{3,7},{4,0},{5,1},{6,2},{7,3},{8,12},{9,13},{10,... | collective-permute-start | bytes 393224 | tf_op jit(solution)/shard_map/ppermute | solution.py:57
  541.9 9.2 %collective-permute-start.81 = (f32[32,1024]{1,0:T(8,128)S(1)}, f32[32,1024]{1,0:T(8,128)S(1)}, u32[]{:S(2)}, u32[]{:S(2)}) collective-permute-start(f32[32,1024]{1,0:T(8,128)S(1)} %dynamic-slice_add_fusion.16), channel_id=1, source_target_pairs={{0,4},{1,5},{2,6},{3,7},{4,0},{5,1},{6,2},{7,3},{8,12},{9,13},{10,... | collective-permute-start | bytes 393224 | tf_op jit(solution)/shard_map/ppermute | solution.py:57
  (81 other events, 500.1 us)

commit v16 on v15

--- a/solution.py
+++ b/solution.py
@@ -73,7 +73,9 @@
 def gather_tiles(vector_bf, indices, block_size):
     snapshots, extent = vector_bf.shape
     vector_tiles = vector_bf.reshape(snapshots, extent // block_size, block_size)
-    return jnp.take(vector_tiles, indices, axis=1)
+    onehot = (indices[:, None] == jnp.arange(extent // block_size, dtype=jnp.int32)[None, :]).astype(vector_bf.dtype)
+    picked = jnp.einsum("ktj,st->ksj", vector_tiles, onehot, preferred_element_type=jnp.float32)
+    return picked.astype(vector_bf.dtype)
 
 
 def place_terms(weighted, indices, n_out):

time: 575 us -> 582 us (1.012)
  matrix products: 92.7 us -> 121 us
  local copies, waits for them, and re-layouts: 41.9 us -> 22.5 us
  starting transfers between devices: 82.8 us -> 76.8 us
    gather x8 -> x0, local copies, waits for them, and re-layouts: 22.8 us -> none  [gather_tiles(): return jnp.take(vector_tiles, indices, axis=1)]
    dot_general x4, matrix products: 22.2 us -> 36.8 us  [backward_terms(): jnp.einsum('sji,ksj->ksi', blocks, picked, preferred_element_type=jnp.flo...]
    dot_general x0 -> x8, matrix products: none -> 10.6 us  [gather_tiles(): jnp.einsum('ktj,st->ksj', vector_tiles, onehot, preferred_element_type=jn...]
    ppermute x24, starting transfers between devices: 18.9 us -> 12.5 us  [big_sum(): other = lax.ppermute(held, axis, partner_pairs(count, distance))]
  transfers between devices with their start and end apart: 88 -> 88, of which waited for: 75 -> 74; matrix products, arithmetic and copies ran while one was open for 3% -> 4% of each run, Pallas kernels for 0% -> 0%
where the time goes in v16:
time: 582 us; the launch traced here: 575 us
  waiting for transfers between devices  338 us (58%)
  matrix products  121 us (21%)
  starting transfers between devices  76.8 us (13%)
  local copies, waits for them, and re-layouts  22.5 us (4%)
  other arithmetic  13.1 us (2%)
    all_to_all x1, waiting for transfers between devices, per_device(): lax.all_to_all(outgoing.reshape(col_count, capacity, block_size, block_si...  129 us
    ppermute x16, waiting for transfers between devices, big_sum(): lax.ppermute(held, axis, partner_pairs(count, last))  73.2 us
    ppermute x22, waiting for transfers between devices, small_sum(): value = value + lax.ppermute(value, axis, partner_pairs(count, distance))  52.7 us
    ppermute x24, waiting for transfers between devices, big_sum(): other = lax.ppermute(held, axis, partner_pairs(count, distance))  42.1 us
    ppermute x24, waiting for transfers between devices, big_sum(): lax.ppermute(give, axis, partner_pairs(count, distance))  40.9 us
    dot_general x8, matrix products, place_terms(): jnp.einsum('ksi,st->kti', weighted, onehot, precision=lax.Precision.HIGH)  37.3 us
    dot_general x4, matrix products, backward_terms(): jnp.einsum('sji,ksj->ksi', blocks, picked, preferred_element_type=jnp.flo...  36.8 us
    dot_general x4, matrix products, forward_terms(): jnp.einsum('sij,ksj->ksi', blocks, picked, preferred_element_type=jnp.flo...  36.8 us
  transfers between devices with their start and end apart: 88, of which 74 were waited for; matrix products, arithmetic and copies ran while one was open for 4% of the time, Pallas kernels for 0%

profile of v16, /device:TPU:0, one launch (start us, length us, event | category | flops | bytes accessed | tf_op | source)
XLA Modules:
  0.0 574.8 jit_solution(2791942827879257173)
XLA Ops:
  5.5 7.3 %all-to-all-start = ((s32[8,24,2]{1,2,0:T(2,128)}), s32[8,24,2]{1,2,0:T(2,128)S(1)}, u32[]{:S(2)}, u32[]{:S(2)}) async-start(s32[8,24,2]{1,2,0:T(2,128)} %copy.50), calls=%async_computation | async-start | bytes 16384 | tf_op jit(solution)/shard_map/all_to_all | solution.py:130
  14.8 8.0 %gather_fusion.1 = bf16[192,128,128]{2,1,0:T(8,128)(2,1)} fusion(bf16[97,128,128]{2,1,0:T(8,128)(2,1)S(1)} %concatenate.273, s32[1024]{0:T(1024)S(1)} %pad_clamp_fusion), kind=kCustom, calls=%fused_computation.1 | custom fusion | bytes 12583680 | tf_op jit(solution)/shard_map/jit(_take)/gather | solution.py:117
  22.8 6.1 %all-to-all-start.1 = ((bf16[8,24,128,128]{3,2,1,0:T(8,128)(2,1)}), bf16[8,24,128,128]{3,2,1,0:T(8,128)(2,1)}, u32[]{:S(2)}, u32[]{:S(2)}) async-start(bf16[8,24,128,128]{3,2,1,0:T(8,128)(2,1)} %bitcast.204), calls=%async_computation.1 | async-start | bytes 12582912 | tf_op jit(solution)/shard_map/all_to_all | solution.py:123
  37.1 129.5 %all-to-all-done.1 = bf16[8,24,128,128]{3,2,1,0:T(8,128)(2,1)} async-done(((bf16[8,24,128,128]{3,2,1,0:T(8,128)(2,1)}), bf16[8,24,128,128]{3,2,1,0:T(8,128)(2,1)}, u32[]{:S(2)}, u32[]{:S(2)}) %all-to-all-start.1) | async-done | bytes 6291488 | tf_op jit(solution)/shard_map/all_to_all | solution.py:123
  166.6 9.2 %fusion.32 = f32[64,192,128]{2,0,1:T(8,128)S(1)} fusion(bf16[192,128,128]{2,1,0:T(8,128)(2,1)} %bitcast.12, bf16[64,192,128]{2,1,0:T(8,128)(2,1)S(1)} %convert_bitcast_fusion.7), kind=kOutput, calls=%fused_computation.42 | convolution fusion | flops 402653184 | bytes 15728640 | tf_op jit(solution)/shard_map/sji,ksj->ksi/dot_general | solution.py:96
  184.7 7.0 %collective-permute-done.3 = f32[32,2048]{1,0:T(8,128)S(1)} collective-permute-done((f32[32,2048]{1,0:T(8,128)S(1)}, f32[32,2048]{1,0:T(8,128)S(1)}, u32[]{:S(2)}, u32[]{:S(2)}) %collective-permute-start.3) | collective-permute-done | bytes 262176 | tf_op jit(solution)/shard_map/ppermute | solution.py:57
  211.1 9.3 %fusion.35 = f32[64,192,128]{2,0,1:T(8,128)S(1)} fusion(bf16[192,128,128]{2,1,0:T(8,128)(2,1)} %bitcast.12, bf16[64,192,128]{2,1,0:T(8,128)(2,1)S(1)} %convert_bitcast_fusion.6), kind=kOutput, calls=%fused_computation.43 | convolution fusion | flops 402653184 | bytes 15728640 | tf_op jit(solution)/shard_map/sij,ksj->ksi/dot_general | solution.py:90
  268.8 9.1 %fusion.38 = f32[64,192,128]{2,0,1:T(8,128)S(1)} fusion(bf16[192,128,128]{2,1,0:T(8,128)(2,1)} %bitcast.12, bf16[64,192,128]{2,1,0:T(8,128)(2,1)S(1)} %convert_bitcast_fusion.5), kind=kOutput, calls=%fused_computation.44 | convolution fusion | flops 402653184 | bytes 15728640 | tf_op jit(solution)/shard_map/sji,ksj->ksi/dot_general | solution.py:96
  286.9 7.0 %collective-permute-done.24 = f32[32,2048]{1,0:T(8,128)S(1)} collective-permute-done((f32[32,2048]{1,0:T(8,128)S(1)}, f32[32,2048]{1,0:T(8,128)S(1)}, u32[]{:S(2)}, u32[]{:S(2)}) %collective-permute-start.24) | collective-permute-done | bytes 262176 | tf_op jit(solution)/shard_map/ppermute | solution.py:57
  313.4 9.1 %fusion.41 = f32[64,192,128]{2,0,1:T(8,128)S(1)} fusion(bf16[192,128,128]{2,1,0:T(8,128)(2,1)} %bitcast.12, bf16[64,192,128]{2,1,0:T(8,128)(2,1)S(1)} %convert_bitcast_fusion.4), kind=kOutput, calls=%fused_computation.45 | convolution fusion | flops 402653184 | bytes 15728640 | tf_op jit(solution)/shard_map/sij,ksj->ksi/dot_general | solution.py:90
  329.1 6.0 %collective-permute-done.32 = f32[32,2048]{1,0:T(8,128)S(1)} collective-permute-done((f32[32,2048]{1,0:T(8,128)S(1)}, f32[32,2048]{1,0:T(8,128)S(1)}, u32[]{:S(2)}, u32[]{:S(2)}) %collective-permute-start.32) | collective-permute-done | bytes 262176 | tf_op jit(solution)/shard_map/ppermute | solution.py:55
  344.1 5.5 collective-permute-done.34
  356.8 4.8 collective-permute-done.36
  368.9 9.4 %fusion.44 = f32[64,192,128]{2,0,1:T(8,128)S(1)} fusion(bf16[192,128,128]{2,1,0:T(8,128)(2,1)} %bitcast.12, bf16[64,192,128]{2,1,0:T(8,128)(2,1)S(1)} %convert_bitcast_fusion.3), kind=kOutput, calls=%fused_computation.46 | convolution fusion | flops 402653184 | bytes 15728640 | tf_op jit(solution)/shard_map/sji,ksj->ksi/dot_general | solution.py:96
  387.3 7.0 %collective-permute-done.45 = f32[32,2048]{1,0:T(8,128)S(1)} collective-permute-done((f32[32,2048]{1,0:T(8,128)S(1)}, f32[32,2048]{1,0:T(8,128)S(1)}, u32[]{:S(2)}, u32[]{:S(2)}) %collective-permute-start.45) | collective-permute-done | bytes 262176 | tf_op jit(solution)/shard_map/ppermute | solution.py:57
  394.4 4.7 collective-permute-done.48
  414.4 9.1 %fusion.47 = f32[64,192,128]{2,0,1:T(8,128)S(1)} fusion(bf16[192,128,128]{2,1,0:T(8,128)(2,1)} %bitcast.12, bf16[64,192,128]{2,1,0:T(8,128)(2,1)S(1)} %convert_bitcast_fusion.2), kind=kOutput, calls=%fused_computation.47 | convolution fusion | flops 402653184 | bytes 15728640 | tf_op jit(solution)/shard_map/sij,ksj->ksi/dot_general | solution.py:90
  445.1 5.7 collective-permute-done.55
  458.0 4.8 collective-permute-done.57
  470.4 9.2 %fusion.50 = f32[64,192,128]{2,0,1:T(8,128)S(1)} fusion(bf16[192,128,128]{2,1,0:T(8,128)(2,1)} %bitcast.12, bf16[64,192,128]{2,1,0:T(8,128)(2,1)S(1)} %convert_bitcast_fusion.1), kind=kOutput, calls=%fused_computation.48 | convolution fusion | flops 402653184 | bytes 15728640 | tf_op jit(solution)/shard_map/sji,ksj->ksi/dot_general | solution.py:96
  488.5 7.0 %collective-permute-done.66 = f32[32,2048]{1,0:T(8,128)S(1)} collective-permute-done((f32[32,2048]{1,0:T(8,128)S(1)}, f32[32,2048]{1,0:T(8,128)S(1)}, u32[]{:S(2)}, u32[]{:S(2)}) %collective-permute-start.66) | collective-permute-done | bytes 262176 | tf_op jit(solution)/shard_map/ppermute | solution.py:57
  516.8 9.2 %fusion.53 = f32[64,192,128]{2,0,1:T(8,128)S(1)} fusion(bf16[192,128,128]{2,1,0:T(8,128)(2,1)} %bitcast.12, bf16[64,192,128]{2,1,0:T(8,128)(2,1)S(1)} %convert_bitcast_fusion), kind=kOutput, calls=%fused_computation.49 | convolution fusion | flops 402653184 | bytes 15728640 | tf_op jit(solution)/shard_map/sij,ksj->ksi/dot_general | solution.py:90
  547.6 5.3 collective-permute-done.76
  560.2 4.8 collective-permute-done.78
  (385 shorter events, 278.1 us)
Async XLA Ops:
  5.5 17.4 %all-to-all-start = ((s32[8,24,2]{1,2,0:T(2,128)}), s32[8,24,2]{1,2,0:T(2,128)S(1)}, u32[]{:S(2)}, u32[]{:S(2)}) async-start(s32[8,24,2]{1,2,0:T(2,128)} %copy.50), calls=%async_computation | async-start | bytes 16384 | tf_op jit(solution)/shard_map/all_to_all | solution.py:130
  22.8 143.8 %all-to-all-start.1 = ((bf16[8,24,128,128]{3,2,1,0:T(8,128)(2,1)}), bf16[8,24,128,128]{3,2,1,0:T(8,128)(2,1)}, u32[]{:S(2)}, u32[]{:S(2)}) async-start(bf16[8,24,128,128]{3,2,1,0:T(8,128)(2,1)} %bitcast.204), calls=%async_computation.1 | async-start | bytes 12582912 | tf_op jit(solution)/shard_map/all_to_all | solution.py:123
  182.5 9.2 %collective-permute-start.3 = (f32[32,2048]{1,0:T(8,128)S(1)}, f32[32,2048]{1,0:T(8,128)S(1)}, u32[]{:S(2)}, u32[]{:S(2)}) collective-permute-start(f32[32,2048]{1,0:T(8,128)S(1)} %dynamic-slice_add_fusion.15), channel_id=1, source_target_pairs={{0,16},{8,24},{16,0},{24,8},{1,17},{9,25},{17,1},{25,9},{2,18},{10... | collective-permute-start | bytes 786440 | tf_op jit(solution)/shard_map/ppermute | solution.py:57
  184.1 12.4 %collective-permute-start.6 = (f32[32,2048]{1,0:T(8,128)S(1)}, f32[32,2048]{1,0:T(8,128)S(1)}, u32[]{:S(2)}, u32[]{:S(2)}) collective-permute-start(f32[32,2048]{1,0:T(8,128)S(1)} %dynamic-slice_add_fusion.14), channel_id=1, source_target_pairs={{0,16},{8,24},{16,0},{24,8},{1,17},{9,25},{17,1},{25,9},{2,18},{10... | collective-permute-start | bytes 786440 | tf_op jit(solution)/shard_map/ppermute | solution.py:57
  229.2 7.1 %collective-permute-start.16 = (f32[32,2048]{1,0:T(8,128)S(1)}, f32[32,2048]{1,0:T(8,128)S(1)}, u32[]{:S(2)}, u32[]{:S(2)}) collective-permute-start(f32[32,2048]{1,0:T(8,128)S(1)} %constant_dynamic-slice_fusion.19), channel_id=1, source_target_pairs={{0,2},{1,3},{2,0},{3,1},{4,6},{5,7},{6,4},{7,5},{8,10},{9,11},{10,... | collective-permute-start | bytes 786440 | tf_op jit(solution)/shard_map/ppermute | solution.py:55
  241.4 7.9 %collective-permute-start.18 = (f32[32,1024]{1,0:T(8,128)S(1)}, f32[32,1024]{1,0:T(8,128)S(1)}, u32[]{:S(2)}, u32[]{:S(2)}) collective-permute-start(f32[32,1024]{1,0:T(8,128)S(1)} %dynamic-slice_add_fusion.22), channel_id=1, source_target_pairs={{0,4},{1,5},{2,6},{3,7},{4,0},{5,1},{6,2},{7,3},{8,12},{9,13},{10,... | collective-permute-start | bytes 393224 | tf_op jit(solution)/shard_map/ppermute | solution.py:57
  252.6 7.6 %collective-permute-start.15 = (f32[32,2048]{1,0:T(8,128)S(1)}, f32[32,2048]{1,0:T(8,128)S(1)}, u32[]{:S(2)}, u32[]{:S(2)}) collective-permute-start(f32[32,2048]{1,0:T(8,128)S(1)} %maximum_select_fusion.24), channel_id=1, source_target_pairs={{0,1},{1,0},{2,3},{3,2},{4,5},{5,4},{6,7},{7,6},{8,9},{9,8},{10,11... | collective-permute-start | bytes 786440 | tf_op jit(solution)/shard_map/ppermute | solution.py:63
  284.7 9.2 %collective-permute-start.24 = (f32[32,2048]{1,0:T(8,128)S(1)}, f32[32,2048]{1,0:T(8,128)S(1)}, u32[]{:S(2)}, u32[]{:S(2)}) collective-permute-start(f32[32,2048]{1,0:T(8,128)S(1)} %dynamic-slice_add_fusion.11), channel_id=1, source_target_pairs={{0,16},{8,24},{16,0},{24,8},{1,17},{9,25},{17,1},{25,9},{2,18},{10... | collective-permute-start | bytes 786440 | tf_op jit(solution)/shard_map/ppermute | solution.py:57
  286.3 12.5 %collective-permute-start.27 = (f32[32,2048]{1,0:T(8,128)S(1)}, f32[32,2048]{1,0:T(8,128)S(1)}, u32[]{:S(2)}, u32[]{:S(2)}) collective-permute-start(f32[32,2048]{1,0:T(8,128)S(1)} %dynamic-slice_add_fusion.10), channel_id=1, source_target_pairs={{0,16},{8,24},{16,0},{24,8},{1,17},{9,25},{17,1},{25,9},{2,18},{10... | collective-permute-start | bytes 786440 | tf_op jit(solution)/shard_map/ppermute | solution.py:57
  327.7 7.4 %collective-permute-start.32 = (f32[32,2048]{1,0:T(8,128)S(1)}, f32[32,2048]{1,0:T(8,128)S(1)}, u32[]{:S(2)}, u32[]{:S(2)}) collective-permute-start(f32[32,2048]{1,0:T(8,128)S(1)} %constant_dynamic-slice_fusion.15), channel_id=1, source_target_pairs={{0,1},{1,0},{2,3},{3,2},{4,5},{5,4},{6,7},{7,6},{8,9},{9,8},{10,11... | collective-permute-start | bytes 786440 | tf_op jit(solution)/shard_map/ppermute | solution.py:55
  328.3 7.8 %collective-permute-start.37 = (f32[32,2048]{1,0:T(8,128)S(1)}, f32[32,2048]{1,0:T(8,128)S(1)}, u32[]{:S(2)}, u32[]{:S(2)}) collective-permute-start(f32[32,2048]{1,0:T(8,128)S(1)} %constant_dynamic-slice_fusion.13), channel_id=1, source_target_pairs={{0,2},{1,3},{2,0},{3,1},{4,6},{5,7},{6,4},{7,5},{8,10},{9,11},{10,... | collective-permute-start | bytes 786440 | tf_op jit(solution)/shard_map/ppermute | solution.py:55
  341.0 8.6 %collective-permute-start.34 = (f32[32,1024]{1,0:T(8,128)S(1)}, f32[32,1024]{1,0:T(8,128)S(1)}, u32[]{:S(2)}, u32[]{:S(2)}) collective-permute-start(f32[32,1024]{1,0:T(8,128)S(1)} %dynamic-slice_add_fusion.21), channel_id=1, source_target_pairs={{0,4},{1,5},{2,6},{3,7},{4,0},{5,1},{6,2},{7,3},{8,12},{9,13},{10,... | collective-permute-start | bytes 393224 | tf_op jit(solution)/shard_map/ppermute | solution.py:57
  341.3 9.7 %collective-permute-start.39 = (f32[32,1024]{1,0:T(8,128)S(1)}, f32[32,1024]{1,0:T(8,128)S(1)}, u32[]{:S(2)}, u32[]{:S(2)}) collective-permute-start(f32[32,1024]{1,0:T(8,128)S(1)} %dynamic-slice_add_fusion.20), channel_id=1, source_target_pairs={{0,4},{1,5},{2,6},{3,7},{4,0},{5,1},{6,2},{7,3},{8,12},{9,13},{10,... | collective-permute-start | bytes 393224 | tf_op jit(solution)/shard_map/ppermute | solution.py:57
  385.1 9.2 %collective-permute-start.45 = (f32[32,2048]{1,0:T(8,128)S(1)}, f32[32,2048]{1,0:T(8,128)S(1)}, u32[]{:S(2)}, u32[]{:S(2)}) collective-permute-start(f32[32,2048]{1,0:T(8,128)S(1)} %dynamic-slice_add_fusion.7), channel_id=1, source_target_pairs={{0,16},{8,24},{16,0},{24,8},{1,17},{9,25},{17,1},{25,9},{2,18},{10... | collective-permute-start | bytes 786440 | tf_op jit(solution)/shard_map/ppermute | solution.py:57
  386.6 12.5 %collective-permute-start.48 = (f32[32,2048]{1,0:T(8,128)S(1)}, f32[32,2048]{1,0:T(8,128)S(1)}, u32[]{:S(2)}, u32[]{:S(2)}) collective-permute-start(f32[32,2048]{1,0:T(8,128)S(1)} %dynamic-slice_add_fusion.6), channel_id=1, source_target_pairs={{0,16},{8,24},{16,0},{24,8},{1,17},{9,25},{17,1},{25,9},{2,18},{10... | collective-permute-start | bytes 786440 | tf_op jit(solution)/shard_map/ppermute | solution.py:57
  430.3 7.2 %collective-permute-start.58 = (f32[32,2048]{1,0:T(8,128)S(1)}, f32[32,2048]{1,0:T(8,128)S(1)}, u32[]{:S(2)}, u32[]{:S(2)}) collective-permute-start(f32[32,2048]{1,0:T(8,128)S(1)} %constant_dynamic-slice_fusion.7), channel_id=1, source_target_pairs={{0,2},{1,3},{2,0},{3,1},{4,6},{5,7},{6,4},{7,5},{8,10},{9,11},{10,... | collective-permute-start | bytes 786440 | tf_op jit(solution)/shard_map/ppermute | solution.py:55
  442.0 8.7 %collective-permute-start.55 = (f32[32,1024]{1,0:T(8,128)S(1)}, f32[32,1024]{1,0:T(8,128)S(1)}, u32[]{:S(2)}, u32[]{:S(2)}) collective-permute-start(f32[32,1024]{1,0:T(8,128)S(1)} %dynamic-slice_add_fusion.19), channel_id=1, source_target_pairs={{0,4},{1,5},{2,6},{3,7},{4,0},{5,1},{6,2},{7,3},{8,12},{9,13},{10,... | collective-permute-start | bytes 393224 | tf_op jit(solution)/shard_map/ppermute | solution.py:57
  442.8 9.5 %collective-permute-start.60 = (f32[32,1024]{1,0:T(8,128)S(1)}, f32[32,1024]{1,0:T(8,128)S(1)}, u32[]{:S(2)}, u32[]{:S(2)}) collective-permute-start(f32[32,1024]{1,0:T(8,128)S(1)} %dynamic-slice_add_fusion.18), channel_id=1, source_target_pairs={{0,4},{1,5},{2,6},{3,7},{4,0},{5,1},{6,2},{7,3},{8,12},{9,13},{10,... | collective-permute-start | bytes 393224 | tf_op jit(solution)/shard_map/ppermute | solution.py:57
  486.3 9.2 %collective-permute-start.66 = (f32[32,2048]{1,0:T(8,128)S(1)}, f32[32,2048]{1,0:T(8,128)S(1)}, u32[]{:S(2)}, u32[]{:S(2)}) collective-permute-start(f32[32,2048]{1,0:T(8,128)S(1)} %dynamic-slice_add_fusion.3), channel_id=1, source_target_pairs={{0,16},{8,24},{16,0},{24,8},{1,17},{9,25},{17,1},{25,9},{2,18},{10... | collective-permute-start | bytes 786440 | tf_op jit(solution)/shard_map/ppermute | solution.py:57
  487.9 12.4 %collective-permute-start.69 = (f32[32,2048]{1,0:T(8,128)S(1)}, f32[32,2048]{1,0:T(8,128)S(1)}, u32[]{:S(2)}, u32[]{:S(2)}) collective-permute-start(f32[32,2048]{1,0:T(8,128)S(1)} %dynamic-slice_add_fusion.2), channel_id=1, source_target_pairs={{0,16},{8,24},{16,0},{24,8},{1,17},{9,25},{17,1},{25,9},{2,18},{10... | collective-permute-start | bytes 786440 | tf_op jit(solution)/shard_map/ppermute | solution.py:57
  531.1 7.0 %collective-permute-start.74 = (f32[32,2048]{1,0:T(8,128)S(1)}, f32[32,2048]{1,0:T(8,128)S(1)}, u32[]{:S(2)}, u32[]{:S(2)}) collective-permute-start(f32[32,2048]{1,0:T(8,128)S(1)} %constant_dynamic-slice_fusion.3), channel_id=1, source_target_pairs={{0,1},{1,0},{2,3},{3,2},{4,5},{5,4},{6,7},{7,6},{8,9},{9,8},{10,11... | collective-permute-start | bytes 786440 | tf_op jit(solution)/shard_map/ppermute | solution.py:55
  532.5 7.5 %collective-permute-start.79 = (f32[32,2048]{1,0:T(8,128)S(1)}, f32[32,2048]{1,0:T(8,128)S(1)}, u32[]{:S(2)}, u32[]{:S(2)}) collective-permute-start(f32[32,2048]{1,0:T(8,128)S(1)} %constant_dynamic-slice_fusion.1), channel_id=1, source_target_pairs={{0,2},{1,3},{2,0},{3,1},{4,6},{5,7},{6,4},{7,5},{8,10},{9,11},{10,... | collective-permute-start | bytes 786440 | tf_op jit(solution)/shard_map/ppermute | solution.py:55
  544.5 8.4 %collective-permute-start.76 = (f32[32,1024]{1,0:T(8,128)S(1)}, f32[32,1024]{1,0:T(8,128)S(1)}, u32[]{:S(2)}, u32[]{:S(2)}) collective-permute-start(f32[32,1024]{1,0:T(8,128)S(1)} %dynamic-slice_add_fusion.17), channel_id=1, source_target_pairs={{0,4},{1,5},{2,6},{3,7},{4,0},{5,1},{6,2},{7,3},{8,12},{9,13},{10,... | collective-permute-start | bytes 393224 | tf_op jit(solution)/shard_map/ppermute | solution.py:57
  545.4 8.9 %collective-permute-start.81 = (f32[32,1024]{1,0:T(8,128)S(1)}, f32[32,1024]{1,0:T(8,128)S(1)}, u32[]{:S(2)}, u32[]{:S(2)}) collective-permute-start(f32[32,1024]{1,0:T(8,128)S(1)} %dynamic-slice_add_fusion.16), channel_id=1, source_target_pairs={{0,4},{1,5},{2,6},{3,7},{4,0},{5,1},{6,2},{7,3},{8,12},{9,13},{10,... | collective-permute-start | bytes 393224 | tf_op jit(solution)/shard_map/ppermute | solution.py:57
  (70 other events, 393.0 us)

commit v17 on v15

--- a/solution.py
+++ b/solution.py
@@ -19,8 +19,25 @@
     return count & (count - 1) == 0
 
 
+def gathered_sum(value, axis):
+    count = lax.axis_size(axis)
+    me = lax.axis_index(axis)
+    arrived = [value] + [
+        lax.ppermute(value, axis, [(i, (i + shift) % count) for i in range(count)])
+        for shift in range(1, count)
+    ]
+    stacked = jnp.stack(arrived, axis=0)
+    ordered = jnp.take(stacked, (me - jnp.arange(count)) % count, axis=0)
+    total = ordered[0]
+    for source in range(1, count):
+        total = total + ordered[source]
+    return total
+
+
 def small_sum(value, axis):
     count = lax.axis_size(axis)
+    if axis == "col":
+        return gathered_sum(value, axis)
     if not is_power_of_two(count):
         return lax.psum(value, axis)
     distance = 1

time: 575 us -> 596 us (1.037)
  other arithmetic: 17.3 us -> 26.7 us
  starting transfers between devices: 82.8 us -> 89.7 us
    ppermute x22 -> x10, waiting for transfers between devices: 52.2 us -> 15.7 us  [small_sum(): value = value + lax.ppermute(value, axis, partner_pairs(count, distance))]
    ppermute x0 -> x28, starting transfers between devices: none -> 33.5 us  [gathered_sum(): lax.ppermute(value, axis, [(i, (i + shift) % count) for i in range(count)])]
    ppermute x0 -> x28, waiting for transfers between devices: none -> 19.5 us  [gathered_sum(): lax.ppermute(value, axis, [(i, (i + shift) % count) for i in range(count)])]
    ppermute x24, starting transfers between devices: 18.9 us -> 3.54 us  [big_sum(): other = lax.ppermute(held, axis, partner_pairs(count, distance))]
    ppermute x24, waiting for transfers between devices: 38.5 us -> 53.3 us  [big_sum(): other = lax.ppermute(held, axis, partner_pairs(count, distance))]
    ppermute x22 -> x10, starting transfers between devices: 17 us -> 7.8 us  [small_sum(): value = value + lax.ppermute(value, axis, partner_pairs(count, distance))]
  transfers between devices with their start and end apart: 88 -> 104, of which waited for: 75 -> 77; matrix products, arithmetic and copies ran while one was open for 3% -> 4% of each run, Pallas kernels for 0% -> 0%
where the time goes in v17:
time: 596 us; the launch traced here: 592 us
  waiting for transfers between devices  336 us (56%)
  matrix products  92.6 us (16%)
  starting transfers between devices  89.7 us (15%)
  local copies, waits for them, and re-layouts  44.4 us (7%)
  other arithmetic  26.7 us (4%)
    all_to_all x1, waiting for transfers between devices, per_device(): lax.all_to_all(outgoing.reshape(col_count, capacity, block_size, block_si...  130 us
    ppermute x16, waiting for transfers between devices, big_sum(): lax.ppermute(held, axis, partner_pairs(count, last))  77.1 us
    ppermute x24, waiting for transfers between devices, big_sum(): other = lax.ppermute(held, axis, partner_pairs(count, distance))  53.3 us
    ppermute x24, waiting for transfers between devices, big_sum(): lax.ppermute(give, axis, partner_pairs(count, distance))  40.8 us
    dot_general x8, matrix products, place_terms(): jnp.einsum('ksi,st->kti', weighted, onehot, precision=lax.Precision.HIGH)  37.3 us
    ppermute x28, starting transfers between devices, gathered_sum(): lax.ppermute(value, axis, [(i, (i + shift) % count) for i in range(count)])  33.5 us
    dot_general x4, matrix products, forward_terms(): jnp.einsum('sij,ksj->ksi', blocks, picked, preferred_element_type=jnp.flo...  32.3 us
    dot_general x4, matrix products, backward_terms(): jnp.einsum('sji,ksj->ksi', blocks, picked, preferred_element_type=jnp.flo...  23.1 us
  transfers between devices with their start and end apart: 104, of which 77 were waited for; matrix products, arithmetic and copies ran while one was open for 4% of the time, Pallas kernels for 0%

profile of v17, /device:TPU:0, one launch (start us, length us, event | category | flops | bytes accessed | tf_op | source)
XLA Modules:
  0.0 592.0 jit_solution(6845593364588866658)
XLA Ops:
  5.5 7.3 %all-to-all-start = ((s32[8,24,2]{1,2,0:T(2,128)}), s32[8,24,2]{1,2,0:T(2,128)S(1)}, u32[]{:S(2)}, u32[]{:S(2)}) async-start(s32[8,24,2]{1,2,0:T(2,128)} %copy.153), calls=%async_computation | async-start | bytes 16384 | tf_op jit(solution)/shard_map/all_to_all | solution.py:145
  14.9 8.0 %gather_fusion.1 = bf16[192,128,128]{2,1,0:T(8,128)(2,1)} fusion(bf16[97,128,128]{2,1,0:T(8,128)(2,1)S(1)} %concatenate.273, s32[1024]{0:T(1024)S(1)} %pad_clamp_fusion.3), kind=kCustom, calls=%fused_computation.13 | custom fusion | bytes 12583680 | tf_op jit(solution)/shard_map/jit(_take)/gather | solution.py:132
  22.9 6.7 %all-to-all-start.1 = ((bf16[8,24,128,128]{3,2,1,0:T(8,128)(2,1)}), bf16[8,24,128,128]{3,2,1,0:T(8,128)(2,1)}, u32[]{:S(2)}, u32[]{:S(2)}) async-start(bf16[8,24,128,128]{3,2,1,0:T(8,128)(2,1)} %bitcast.328), calls=%async_computation.1 | async-start | bytes 12582912 | tf_op jit(solution)/shard_map/all_to_all | solution.py:138
  37.5 129.7 %all-to-all-done.1 = bf16[8,24,128,128]{3,2,1,0:T(8,128)(2,1)} async-done(((bf16[8,24,128,128]{3,2,1,0:T(8,128)(2,1)}), bf16[8,24,128,128]{3,2,1,0:T(8,128)(2,1)}, u32[]{:S(2)}, u32[]{:S(2)}) %all-to-all-start.1) | async-done | bytes 6291488 | tf_op jit(solution)/shard_map/all_to_all | solution.py:138
  167.1 5.6 fusion.48
  181.6 7.0 %collective-permute-done.3 = f32[32,2048]{1,0:T(8,128)S(1)} collective-permute-done((f32[32,2048]{1,0:T(8,128)S(1)}, f32[32,2048]{1,0:T(8,128)S(1)}, u32[]{:S(2)}, u32[]{:S(2)}) %collective-permute-start.3) | collective-permute-done | bytes 262176 | tf_op jit(solution)/shard_map/ppermute | solution.py:74
  213.7 8.1 %fusion.51 = f32[64,192,128]{2,0,1:T(8,128)S(1)} fusion(bf16[192,128,128]{2,1,0:T(8,128)(2,1)} %bitcast.11, bf16[192,64,128]{2,1,0:T(8,128)(2,1)} %gather_fusion.4, pred[192]{0:T(512)(128)(4,1)S(1)} %get-tuple-element.56), kind=kOutput, calls=%fused_computation.63 | convolution fusion | flops 404226048 | bytes 15728832 | tf_op jit(solution)/shard_map/sij,ksj->ksi/dot_general | solution.py:105
  242.3 6.3 %collective-permute-done.17 = f32[32,1024]{1,0:T(8,128)S(1)} collective-permute-done((f32[32,1024]{1,0:T(8,128)S(1)}, f32[32,1024]{1,0:T(8,128)S(1)}, u32[]{:S(2)}, u32[]{:S(2)}) %collective-permute-start.17) | collective-permute-done | bytes 131104 | tf_op jit(solution)/shard_map/ppermute | solution.py:74
  271.2 5.8 fusion.54
  285.9 7.0 %collective-permute-done.28 = f32[32,2048]{1,0:T(8,128)S(1)} collective-permute-done((f32[32,2048]{1,0:T(8,128)S(1)}, f32[32,2048]{1,0:T(8,128)S(1)}, u32[]{:S(2)}, u32[]{:S(2)}) %collective-permute-start.28) | collective-permute-done | bytes 262176 | tf_op jit(solution)/shard_map/ppermute | solution.py:74
  320.8 8.1 %fusion.57 = f32[64,192,128]{2,0,1:T(8,128)S(1)} fusion(bf16[192,128,128]{2,1,0:T(8,128)(2,1)} %bitcast.11, bf16[192,64,128]{2,1,0:T(8,128)(2,1)} %gather_fusion.7, pred[192]{0:T(512)(128)(4,1)S(1)} %get-tuple-element.56), kind=kOutput, calls=%fused_computation.65 | convolution fusion | flops 404226048 | bytes 15728832 | tf_op jit(solution)/shard_map/sij,ksj->ksi/dot_general | solution.py:105
  334.5 6.3 %collective-permute-done.40 = f32[32,2048]{1,0:T(8,128)S(1)} collective-permute-done((f32[32,2048]{1,0:T(8,128)S(1)}, f32[32,2048]{1,0:T(8,128)S(1)}, u32[]{:S(2)}, u32[]{:S(2)}) %collective-permute-start.40) | collective-permute-done | bytes 262176 | tf_op jit(solution)/shard_map/ppermute | solution.py:72
  349.0 6.4 %collective-permute-done.42 = f32[32,1024]{1,0:T(8,128)S(1)} collective-permute-done((f32[32,1024]{1,0:T(8,128)S(1)}, f32[32,1024]{1,0:T(8,128)S(1)}, u32[]{:S(2)}, u32[]{:S(2)}) %collective-permute-start.42) | collective-permute-done | bytes 131104 | tf_op jit(solution)/shard_map/ppermute | solution.py:74
  377.9 5.7 fusion.60
  392.5 7.0 %collective-permute-done.53 = f32[32,2048]{1,0:T(8,128)S(1)} collective-permute-done((f32[32,2048]{1,0:T(8,128)S(1)}, f32[32,2048]{1,0:T(8,128)S(1)}, u32[]{:S(2)}, u32[]{:S(2)}) %collective-permute-start.53) | collective-permute-done | bytes 262176 | tf_op jit(solution)/shard_map/ppermute | solution.py:74
  428.4 8.1 %fusion.63 = f32[64,192,128]{2,0,1:T(8,128)S(1)} fusion(bf16[192,128,128]{2,1,0:T(8,128)(2,1)} %bitcast.11, bf16[192,64,128]{2,1,0:T(8,128)(2,1)} %gather_fusion.10, pred[192]{0:T(512)(128)(4,1)S(1)} %get-tuple-element.56), kind=kOutput, calls=%fused_computation.67 | convolution fusion | flops 404226048 | bytes 15728832 | tf_op jit(solution)/shard_map/sij,ksj->ksi/dot_general | solution.py:105
  442.1 6.2 %collective-permute-done.65 = f32[32,2048]{1,0:T(8,128)S(1)} collective-permute-done((f32[32,2048]{1,0:T(8,128)S(1)}, f32[32,2048]{1,0:T(8,128)S(1)}, u32[]{:S(2)}, u32[]{:S(2)}) %collective-permute-start.65) | collective-permute-done | bytes 262176 | tf_op jit(solution)/shard_map/ppermute | solution.py:72
  456.6 6.4 %collective-permute-done.67 = f32[32,1024]{1,0:T(8,128)S(1)} collective-permute-done((f32[32,1024]{1,0:T(8,128)S(1)}, f32[32,1024]{1,0:T(8,128)S(1)}, u32[]{:S(2)}, u32[]{:S(2)}) %collective-permute-start.67) | collective-permute-done | bytes 131104 | tf_op jit(solution)/shard_map/ppermute | solution.py:74
  484.7 6.0 %fusion.66 = f32[64,192,128]{2,0,1:T(8,128)S(1)} fusion(bf16[192,128,128]{2,1,0:T(8,128)(2,1)} %bitcast.11, bf16[192,64,128]{2,1,0:T(8,128)(2,1)} %gather_fusion.11, pred[192]{0:T(512)(128)(4,1)S(1)} %get-tuple-element.57), kind=kOutput, calls=%fused_computation.68 | convolution fusion | flops 404226048 | bytes 15728832 | tf_op jit(solution)/shard_map/sji,ksj->ksi/dot_general | solution.py:111
  490.6 4.7 fusion.98
  499.6 7.0 %collective-permute-done.78 = f32[32,2048]{1,0:T(8,128)S(1)} collective-permute-done((f32[32,2048]{1,0:T(8,128)S(1)}, f32[32,2048]{1,0:T(8,128)S(1)}, u32[]{:S(2)}, u32[]{:S(2)}) %collective-permute-start.78) | collective-permute-done | bytes 262176 | tf_op jit(solution)/shard_map/ppermute | solution.py:74
  535.3 8.1 %fusion.69 = f32[64,192,128]{2,0,1:T(8,128)S(1)} fusion(bf16[192,128,128]{2,1,0:T(8,128)(2,1)} %bitcast.11, bf16[192,64,128]{2,1,0:T(8,128)(2,1)} %gather_fusion.13, pred[192]{0:T(512)(128)(4,1)S(1)} %get-tuple-element.56), kind=kOutput, calls=%fused_computation.69 | convolution fusion | flops 404226048 | bytes 15728832 | tf_op jit(solution)/shard_map/sij,ksj->ksi/dot_general | solution.py:105
  549.0 6.3 %collective-permute-done.90 = f32[32,2048]{1,0:T(8,128)S(1)} collective-permute-done((f32[32,2048]{1,0:T(8,128)S(1)}, f32[32,2048]{1,0:T(8,128)S(1)}, u32[]{:S(2)}, u32[]{:S(2)}) %collective-permute-start.90) | collective-permute-done | bytes 262176 | tf_op jit(solution)/shard_map/ppermute | solution.py:72
  563.5 6.0 %collective-permute-done.92 = f32[32,1024]{1,0:T(8,128)S(1)} collective-permute-done((f32[32,1024]{1,0:T(8,128)S(1)}, f32[32,1024]{1,0:T(8,128)S(1)}, u32[]{:S(2)}, u32[]{:S(2)}) %collective-permute-start.92) | collective-permute-done | bytes 131104 | tf_op jit(solution)/shard_map/ppermute | solution.py:74
  (446 shorter events, 305.9 us)
Async XLA Ops:
  5.5 17.4 %all-to-all-start = ((s32[8,24,2]{1,2,0:T(2,128)}), s32[8,24,2]{1,2,0:T(2,128)S(1)}, u32[]{:S(2)}, u32[]{:S(2)}) async-start(s32[8,24,2]{1,2,0:T(2,128)} %copy.153), calls=%async_computation | async-start | bytes 16384 | tf_op jit(solution)/shard_map/all_to_all | solution.py:145
  22.9 144.2 %all-to-all-start.1 = ((bf16[8,24,128,128]{3,2,1,0:T(8,128)(2,1)}), bf16[8,24,128,128]{3,2,1,0:T(8,128)(2,1)}, u32[]{:S(2)}, u32[]{:S(2)}) async-start(bf16[8,24,128,128]{3,2,1,0:T(8,128)(2,1)} %bitcast.328), calls=%async_computation.1 | async-start | bytes 12582912 | tf_op jit(solution)/shard_map/all_to_all | solution.py:138
  179.4 9.2 %collective-permute-start.3 = (f32[32,2048]{1,0:T(8,128)S(1)}, f32[32,2048]{1,0:T(8,128)S(1)}, u32[]{:S(2)}, u32[]{:S(2)}) collective-permute-start(f32[32,2048]{1,0:T(8,128)S(1)} %dynamic-slice_add_fusion.15), channel_id=1, source_target_pairs={{0,16},{8,24},{16,0},{24,8},{1,17},{9,25},{17,1},{25,9},{2,18},{10... | collective-permute-start | bytes 786440 | tf_op jit(solution)/shard_map/ppermute | solution.py:74
  181.0 12.4 %collective-permute-start.6 = (f32[32,2048]{1,0:T(8,128)S(1)}, f32[32,2048]{1,0:T(8,128)S(1)}, u32[]{:S(2)}, u32[]{:S(2)}) collective-permute-start(f32[32,2048]{1,0:T(8,128)S(1)} %dynamic-slice_add_fusion.14), channel_id=1, source_target_pairs={{0,16},{8,24},{16,0},{24,8},{1,17},{9,25},{17,1},{25,9},{2,18},{10... | collective-permute-start | bytes 786440 | tf_op jit(solution)/shard_map/ppermute | solution.py:74
  238.5 10.1 %collective-permute-start.17 = (f32[32,1024]{1,0:T(8,128)S(1)}, f32[32,1024]{1,0:T(8,128)S(1)}, u32[]{:S(2)}, u32[]{:S(2)}) collective-permute-start(f32[32,1024]{1,0:T(8,128)S(1)} %dynamic-slice_add_fusion.23), channel_id=1, source_target_pairs={{0,4},{1,5},{2,6},{3,7},{4,0},{5,1},{6,2},{7,3},{8,12},{9,13},{10,... | collective-permute-start | bytes 393224 | tf_op jit(solution)/shard_map/ppermute | solution.py:74
  283.7 9.2 %collective-permute-start.28 = (f32[32,2048]{1,0:T(8,128)S(1)}, f32[32,2048]{1,0:T(8,128)S(1)}, u32[]{:S(2)}, u32[]{:S(2)}) collective-permute-start(f32[32,2048]{1,0:T(8,128)S(1)} %dynamic-slice_add_fusion.11), channel_id=1, source_target_pairs={{0,16},{8,24},{16,0},{24,8},{1,17},{9,25},{17,1},{25,9},{2,18},{10... | collective-permute-start | bytes 786440 | tf_op jit(solution)/shard_map/ppermute | solution.py:74
  285.3 12.4 %collective-permute-start.31 = (f32[32,2048]{1,0:T(8,128)S(1)}, f32[32,2048]{1,0:T(8,128)S(1)}, u32[]{:S(2)}, u32[]{:S(2)}) collective-permute-start(f32[32,2048]{1,0:T(8,128)S(1)} %dynamic-slice_add_fusion.10), channel_id=1, source_target_pairs={{0,16},{8,24},{16,0},{24,8},{1,17},{9,25},{17,1},{25,9},{2,18},{10... | collective-permute-start | bytes 786440 | tf_op jit(solution)/shard_map/ppermute | solution.py:74
  301.1 8.8 %collective-permute-start.37 = (f32[64]{0:T(128)S(1)}, f32[64]{0:T(128)S(1)}, u32[]{:S(2)}, u32[]{:S(2)}) collective-permute-start(f32[64]{0:T(128)S(1)} %get-tuple-element.27), channel_id=1, source_target_pairs={{0,5},{1,6},{2,7},{3,0},{4,1},{5,2},{6,3},{7,4},{8,13},{9,14},{10,... | collective-permute-start | bytes 776 | tf_op jit(solution)/shard_map/ppermute | solution.py:26
  334.4 7.8 %collective-permute-start.45 = (f32[32,2048]{1,0:T(8,128)S(1)}, f32[32,2048]{1,0:T(8,128)S(1)}, u32[]{:S(2)}, u32[]{:S(2)}) collective-permute-start(f32[32,2048]{1,0:T(8,128)S(1)} %constant_dynamic-slice_fusion.13), channel_id=1, source_target_pairs={{0,2},{1,3},{2,0},{3,1},{4,6},{5,7},{6,4},{7,5},{8,10},{9,11},{10,... | collective-permute-start | bytes 786440 | tf_op jit(solution)/shard_map/ppermute | solution.py:72
  345.9 9.4 %collective-permute-start.42 = (f32[32,1024]{1,0:T(8,128)S(1)}, f32[32,1024]{1,0:T(8,128)S(1)}, u32[]{:S(2)}, u32[]{:S(2)}) collective-permute-start(f32[32,1024]{1,0:T(8,128)S(1)} %dynamic-slice_add_fusion.21), channel_id=1, source_target_pairs={{0,4},{1,5},{2,6},{3,7},{4,0},{5,1},{6,2},{7,3},{8,12},{9,13},{10,... | collective-permute-start | bytes 393224 | tf_op jit(solution)/shard_map/ppermute | solution.py:74
  347.6 9.1 %collective-permute-start.47 = (f32[32,1024]{1,0:T(8,128)S(1)}, f32[32,1024]{1,0:T(8,128)S(1)}, u32[]{:S(2)}, u32[]{:S(2)}) collective-permute-start(f32[32,1024]{1,0:T(8,128)S(1)} %dynamic-slice_add_fusion.20), channel_id=1, source_target_pairs={{0,4},{1,5},{2,6},{3,7},{4,0},{5,1},{6,2},{7,3},{8,12},{9,13},{10,... | collective-permute-start | bytes 393224 | tf_op jit(solution)/shard_map/ppermute | solution.py:74
  390.3 9.2 %collective-permute-start.53 = (f32[32,2048]{1,0:T(8,128)S(1)}, f32[32,2048]{1,0:T(8,128)S(1)}, u32[]{:S(2)}, u32[]{:S(2)}) collective-permute-start(f32[32,2048]{1,0:T(8,128)S(1)} %dynamic-slice_add_fusion.7), channel_id=1, source_target_pairs={{0,16},{8,24},{16,0},{24,8},{1,17},{9,25},{17,1},{25,9},{2,18},{10... | collective-permute-start | bytes 786440 | tf_op jit(solution)/shard_map/ppermute | solution.py:74
  391.9 12.4 %collective-permute-start.56 = (f32[32,2048]{1,0:T(8,128)S(1)}, f32[32,2048]{1,0:T(8,128)S(1)}, u32[]{:S(2)}, u32[]{:S(2)}) collective-permute-start(f32[32,2048]{1,0:T(8,128)S(1)} %dynamic-slice_add_fusion.6), channel_id=1, source_target_pairs={{0,16},{8,24},{16,0},{24,8},{1,17},{9,25},{17,1},{25,9},{2,18},{10... | collective-permute-start | bytes 786440 | tf_op jit(solution)/shard_map/ppermute | solution.py:74
  408.5 8.9 %collective-permute-start.62 = (f32[64]{0:T(128)S(1)}, f32[64]{0:T(128)S(1)}, u32[]{:S(2)}, u32[]{:S(2)}) collective-permute-start(f32[64]{0:T(128)S(1)} %get-tuple-element.21), channel_id=1, source_target_pairs={{0,5},{1,6},{2,7},{3,0},{4,1},{5,2},{6,3},{7,4},{8,13},{9,14},{10,... | collective-permute-start | bytes 776 | tf_op jit(solution)/shard_map/ppermute | solution.py:26
  442.0 7.8 %collective-permute-start.70 = (f32[32,2048]{1,0:T(8,128)S(1)}, f32[32,2048]{1,0:T(8,128)S(1)}, u32[]{:S(2)}, u32[]{:S(2)}) collective-permute-start(f32[32,2048]{1,0:T(8,128)S(1)} %constant_dynamic-slice_fusion.7), channel_id=1, source_target_pairs={{0,2},{1,3},{2,0},{3,1},{4,6},{5,7},{6,4},{7,5},{8,10},{9,11},{10,... | collective-permute-start | bytes 786440 | tf_op jit(solution)/shard_map/ppermute | solution.py:72
  453.5 9.5 %collective-permute-start.67 = (f32[32,1024]{1,0:T(8,128)S(1)}, f32[32,1024]{1,0:T(8,128)S(1)}, u32[]{:S(2)}, u32[]{:S(2)}) collective-permute-start(f32[32,1024]{1,0:T(8,128)S(1)} %dynamic-slice_add_fusion.19), channel_id=1, source_target_pairs={{0,4},{1,5},{2,6},{3,7},{4,0},{5,1},{6,2},{7,3},{8,12},{9,13},{10,... | collective-permute-start | bytes 393224 | tf_op jit(solution)/shard_map/ppermute | solution.py:74
  454.9 9.4 %collective-permute-start.72 = (f32[32,1024]{1,0:T(8,128)S(1)}, f32[32,1024]{1,0:T(8,128)S(1)}, u32[]{:S(2)}, u32[]{:S(2)}) collective-permute-start(f32[32,1024]{1,0:T(8,128)S(1)} %dynamic-slice_add_fusion.18), channel_id=1, source_target_pairs={{0,4},{1,5},{2,6},{3,7},{4,0},{5,1},{6,2},{7,3},{8,12},{9,13},{10,... | collective-permute-start | bytes 393224 | tf_op jit(solution)/shard_map/ppermute | solution.py:74
  497.4 9.2 %collective-permute-start.78 = (f32[32,2048]{1,0:T(8,128)S(1)}, f32[32,2048]{1,0:T(8,128)S(1)}, u32[]{:S(2)}, u32[]{:S(2)}) collective-permute-start(f32[32,2048]{1,0:T(8,128)S(1)} %dynamic-slice_add_fusion.3), channel_id=1, source_target_pairs={{0,16},{8,24},{16,0},{24,8},{1,17},{9,25},{17,1},{25,9},{2,18},{10... | collective-permute-start | bytes 786440 | tf_op jit(solution)/shard_map/ppermute | solution.py:74
  499.0 12.4 %collective-permute-start.81 = (f32[32,2048]{1,0:T(8,128)S(1)}, f32[32,2048]{1,0:T(8,128)S(1)}, u32[]{:S(2)}, u32[]{:S(2)}) collective-permute-start(f32[32,2048]{1,0:T(8,128)S(1)} %dynamic-slice_add_fusion.2), channel_id=1, source_target_pairs={{0,16},{8,24},{16,0},{24,8},{1,17},{9,25},{17,1},{25,9},{2,18},{10... | collective-permute-start | bytes 786440 | tf_op jit(solution)/shard_map/ppermute | solution.py:74
  515.1 8.5 %collective-permute-start.88 = (f32[64]{0:T(128)S(1)}, f32[64]{0:T(128)S(1)}, u32[]{:S(2)}, u32[]{:S(2)}) collective-permute-start(f32[64]{0:T(128)S(1)} %get-tuple-element.14), channel_id=1, source_target_pairs={{0,6},{1,7},{2,0},{3,1},{4,2},{5,3},{6,4},{7,5},{8,14},{9,15},{10,... | collective-permute-start | bytes 776 | tf_op jit(solution)/shard_map/ppermute | solution.py:26
  516.4 8.4 %collective-permute-start.87 = (f32[64]{0:T(128)S(1)}, f32[64]{0:T(128)S(1)}, u32[]{:S(2)}, u32[]{:S(2)}) collective-permute-start(f32[64]{0:T(128)S(1)} %get-tuple-element.14), channel_id=1, source_target_pairs={{0,5},{1,6},{2,7},{3,0},{4,1},{5,2},{6,3},{7,4},{8,13},{9,14},{10,... | collective-permute-start | bytes 776 | tf_op jit(solution)/shard_map/ppermute | solution.py:26
  548.9 7.8 %collective-permute-start.95 = (f32[32,2048]{1,0:T(8,128)S(1)}, f32[32,2048]{1,0:T(8,128)S(1)}, u32[]{:S(2)}, u32[]{:S(2)}) collective-permute-start(f32[32,2048]{1,0:T(8,128)S(1)} %constant_dynamic-slice_fusion.1), channel_id=1, source_target_pairs={{0,2},{1,3},{2,0},{3,1},{4,6},{5,7},{6,4},{7,5},{8,10},{9,11},{10,... | collective-permute-start | bytes 786440 | tf_op jit(solution)/shard_map/ppermute | solution.py:72
  560.4 9.1 %collective-permute-start.92 = (f32[32,1024]{1,0:T(8,128)S(1)}, f32[32,1024]{1,0:T(8,128)S(1)}, u32[]{:S(2)}, u32[]{:S(2)}) collective-permute-start(f32[32,1024]{1,0:T(8,128)S(1)} %dynamic-slice_add_fusion.17), channel_id=1, source_target_pairs={{0,4},{1,5},{2,6},{3,7},{4,0},{5,1},{6,2},{7,3},{8,12},{9,13},{10,... | collective-permute-start | bytes 393224 | tf_op jit(solution)/shard_map/ppermute | solution.py:74
  561.9 9.0 %collective-permute-start.97 = (f32[32,1024]{1,0:T(8,128)S(1)}, f32[32,1024]{1,0:T(8,128)S(1)}, u32[]{:S(2)}, u32[]{:S(2)}) collective-permute-start(f32[32,1024]{1,0:T(8,128)S(1)} %dynamic-slice_add_fusion.16), channel_id=1, source_target_pairs={{0,4},{1,5},{2,6},{3,7},{4,0},{5,1},{6,2},{7,3},{8,12},{9,13},{10,... | collective-permute-start | bytes 393224 | tf_op jit(solution)/shard_map/ppermute | solution.py:74
  (94 other events, 583.0 us)

commit v18 on v15

--- a/solution.py
+++ b/solution.py
@@ -42,9 +42,9 @@
         distances.append(distance)
         distance *= 2
     lanes = jnp.split(value, CHUNKS, axis=0)
-    last = distances.pop()
-    orders = [distances[lane % len(distances):] + distances[:lane % len(distances)] if distances else [] for lane in range(CHUNKS)]
-    for step in range(len(distances)):
+    orders = [distances[lane % len(distances):] + distances[:lane % len(distances)] for lane in range(CHUNKS)]
+    lasts = [order.pop() for order in orders]
+    for step in range(len(distances) - 1):
         moved = []
         for lane, held in enumerate(lanes):
             distance = orders[lane][step]
@@ -54,8 +54,8 @@
             give = lax.dynamic_slice_in_dim(held, (1 - upper) * half, half, held.ndim - 1)
             moved.append(keep + lax.ppermute(give, axis, partner_pairs(count, distance)))
         lanes = moved
-    lanes = [held + lax.ppermute(held, axis, partner_pairs(count, last)) for held in lanes]
-    for step in reversed(range(len(distances))):
+    lanes = [held + lax.ppermute(held, axis, partner_pairs(count, last)) for held, last in zip(lanes, lasts)]
+    for step in reversed(range(len(distances) - 1)):
         moved = []
         for lane, held in enumerate(lanes):
             distance = orders[lane][step]

time: 575 us -> 614 us (1.068)
  waiting for transfers between devices: 334 us -> 378 us
    ppermute x24, waiting for transfers between devices: 42.3 us -> 82.4 us  [big_sum(): lax.ppermute(give, axis, partner_pairs(count, distance))]
    ppermute x24, waiting for transfers between devices: 38.5 us -> 72.8 us  [big_sum(): other = lax.ppermute(held, axis, partner_pairs(count, distance))]
    ppermute x16, waiting for transfers between devices: 71.3 us -> 40.5 us  [big_sum(): lax.ppermute(held, axis, partner_pairs(count, last))]
  transfers between devices with their start and end apart: 88 -> 88, of which waited for: 75 -> 72; matrix products, arithmetic and copies ran while one was open for 3% -> 3% of each run, Pallas kernels for 0% -> 0%
where the time goes in v18:
time: 614 us; the launch traced here: 611 us
  waiting for transfers between devices  378 us (62%)
  matrix products  92.7 us (15%)
  starting transfers between devices  78.7 us (13%)
  local copies, waits for them, and re-layouts  41.9 us (7%)
  other arithmetic  17.1 us (3%)
    all_to_all x1, waiting for transfers between devices, per_device(): lax.all_to_all(outgoing.reshape(col_count, capacity, block_size, block_si...  130 us
    ppermute x24, waiting for transfers between devices, big_sum(): lax.ppermute(give, axis, partner_pairs(count, distance))  82.4 us
    ppermute x24, waiting for transfers between devices, big_sum(): other = lax.ppermute(held, axis, partner_pairs(count, distance))  72.8 us
    ppermute x22, waiting for transfers between devices, small_sum(): value = value + lax.ppermute(value, axis, partner_pairs(count, distance))  52.5 us
    ppermute x16, waiting for transfers between devices, big_sum(): lax.ppermute(held, axis, partner_pairs(count, last))  40.5 us
    dot_general x8, matrix products, place_terms(): jnp.einsum('ksi,st->kti', weighted, onehot, precision=lax.Precision.HIGH)  37.8 us
    dot_general x4, matrix products, forward_terms(): jnp.einsum('sij,ksj->ksi', blocks, picked, preferred_element_type=jnp.flo...  32.6 us
    gather x8, local copies, waits for them, and re-layouts, gather_tiles(): return jnp.take(vector_tiles, indices, axis=1)  22.8 us
  transfers between devices with their start and end apart: 88, of which 72 were waited for; matrix products, arithmetic and copies ran while one was open for 3% of the time, Pallas kernels for 0%

profile of v18, /device:TPU:0, one launch (start us, length us, event | category | flops | bytes accessed | tf_op | source)
XLA Modules:
  0.0 610.8 jit_solution(9256200788318725773)
XLA Ops:
  5.5 7.3 %all-to-all-start = ((s32[8,24,2]{1,2,0:T(2,128)}), s32[8,24,2]{1,2,0:T(2,128)S(1)}, u32[]{:S(2)}, u32[]{:S(2)}) async-start(s32[8,24,2]{1,2,0:T(2,128)} %copy.153), calls=%async_computation | async-start | bytes 16384 | tf_op jit(solution)/shard_map/all_to_all | solution.py:128
  14.8 8.0 %gather_fusion.1 = bf16[192,128,128]{2,1,0:T(8,128)(2,1)} fusion(bf16[97,128,128]{2,1,0:T(8,128)(2,1)S(1)} %concatenate.273, s32[1024]{0:T(1024)S(1)} %pad_clamp_fusion.2), kind=kCustom, calls=%fused_computation.9 | custom fusion | bytes 12583680 | tf_op jit(solution)/shard_map/jit(_take)/gather | solution.py:115
  22.8 6.3 %all-to-all-start.1 = ((bf16[8,24,128,128]{3,2,1,0:T(8,128)(2,1)}), bf16[8,24,128,128]{3,2,1,0:T(8,128)(2,1)}, u32[]{:S(2)}, u32[]{:S(2)}) async-start(bf16[8,24,128,128]{3,2,1,0:T(8,128)(2,1)} %bitcast.272), calls=%async_computation.1 | async-start | bytes 12582912 | tf_op jit(solution)/shard_map/all_to_all | solution.py:121
  37.1 129.5 %all-to-all-done.1 = bf16[8,24,128,128]{3,2,1,0:T(8,128)(2,1)} async-done(((bf16[8,24,128,128]{3,2,1,0:T(8,128)(2,1)}), bf16[8,24,128,128]{3,2,1,0:T(8,128)(2,1)}, u32[]{:S(2)}, u32[]{:S(2)}) %all-to-all-start.1) | async-done | bytes 6291488 | tf_op jit(solution)/shard_map/all_to_all | solution.py:121
  166.6 5.6 fusion.48
  180.5 6.4 %collective-permute-done.5 = f32[32,2048]{1,0:T(8,128)S(1)} collective-permute-done((f32[32,2048]{1,0:T(8,128)S(1)}, f32[32,2048]{1,0:T(8,128)S(1)}, u32[]{:S(2)}, u32[]{:S(2)}) %collective-permute-start.5) | collective-permute-done | bytes 262176 | tf_op jit(solution)/shard_map/ppermute | solution.py:55
  194.0 7.1 %collective-permute-done.7 = f32[32,2048]{1,0:T(8,128)S(1)} collective-permute-done((f32[32,2048]{1,0:T(8,128)S(1)}, f32[32,2048]{1,0:T(8,128)S(1)}, u32[]{:S(2)}, u32[]{:S(2)}) %collective-permute-start.7) | collective-permute-done | bytes 262176 | tf_op jit(solution)/shard_map/ppermute | solution.py:63
  216.0 8.3 %fusion.51 = f32[64,192,128]{2,0,1:T(8,128)S(1)} fusion(bf16[192,128,128]{2,1,0:T(8,128)(2,1)} %bitcast.11, bf16[192,64,128]{2,1,0:T(8,128)(2,1)} %gather_fusion.3, pred[192]{0:T(512)(128)(4,1)S(1)} %get-tuple-element.55), kind=kOutput, calls=%fused_computation.59 | convolution fusion | flops 404226048 | bytes 15728832 | tf_op jit(solution)/shard_map/sij,ksj->ksi/dot_general | solution.py:88
  231.4 7.0 %collective-permute-done.16 = f32[32,2048]{1,0:T(8,128)S(1)} collective-permute-done((f32[32,2048]{1,0:T(8,128)S(1)}, f32[32,2048]{1,0:T(8,128)S(1)}, u32[]{:S(2)}, u32[]{:S(2)}) %collective-permute-start.16) | collective-permute-done | bytes 262176 | tf_op jit(solution)/shard_map/ppermute | solution.py:55
  241.7 7.3 %collective-permute-done.17 = f32[32,1024]{1,0:T(8,128)S(1)} collective-permute-done((f32[32,1024]{1,0:T(8,128)S(1)}, f32[32,1024]{1,0:T(8,128)S(1)}, u32[]{:S(2)}, u32[]{:S(2)}) %collective-permute-start.17) | collective-permute-done | bytes 131104 | tf_op jit(solution)/shard_map/ppermute | solution.py:55
  276.8 5.6 fusion.54
  291.1 6.4 %collective-permute-done.26 = f32[32,2048]{1,0:T(8,128)S(1)} collective-permute-done((f32[32,2048]{1,0:T(8,128)S(1)}, f32[32,2048]{1,0:T(8,128)S(1)}, u32[]{:S(2)}, u32[]{:S(2)}) %collective-permute-start.26) | collective-permute-done | bytes 262176 | tf_op jit(solution)/shard_map/ppermute | solution.py:55
  304.5 7.1 %collective-permute-done.28 = f32[32,2048]{1,0:T(8,128)S(1)} collective-permute-done((f32[32,2048]{1,0:T(8,128)S(1)}, f32[32,2048]{1,0:T(8,128)S(1)}, u32[]{:S(2)}, u32[]{:S(2)}) %collective-permute-start.28) | collective-permute-done | bytes 262176 | tf_op jit(solution)/shard_map/ppermute | solution.py:63
  327.9 8.1 %fusion.57 = f32[64,192,128]{2,0,1:T(8,128)S(1)} fusion(bf16[192,128,128]{2,1,0:T(8,128)(2,1)} %bitcast.11, bf16[192,64,128]{2,1,0:T(8,128)(2,1)} %gather_fusion.5, pred[192]{0:T(512)(128)(4,1)S(1)} %get-tuple-element.55), kind=kOutput, calls=%fused_computation.61 | convolution fusion | flops 404226048 | bytes 15728832 | tf_op jit(solution)/shard_map/sij,ksj->ksi/dot_general | solution.py:88
  354.9 6.7 %collective-permute-done.38 = f32[32,1024]{1,0:T(8,128)S(1)} collective-permute-done((f32[32,1024]{1,0:T(8,128)S(1)}, f32[32,1024]{1,0:T(8,128)S(1)}, u32[]{:S(2)}, u32[]{:S(2)}) %collective-permute-start.38) | collective-permute-done | bytes 131104 | tf_op jit(solution)/shard_map/ppermute | solution.py:55
  388.1 5.6 fusion.60
  402.0 6.4 %collective-permute-done.47 = f32[32,2048]{1,0:T(8,128)S(1)} collective-permute-done((f32[32,2048]{1,0:T(8,128)S(1)}, f32[32,2048]{1,0:T(8,128)S(1)}, u32[]{:S(2)}, u32[]{:S(2)}) %collective-permute-start.47) | collective-permute-done | bytes 262176 | tf_op jit(solution)/shard_map/ppermute | solution.py:55
  415.5 7.1 %collective-permute-done.49 = f32[32,2048]{1,0:T(8,128)S(1)} collective-permute-done((f32[32,2048]{1,0:T(8,128)S(1)}, f32[32,2048]{1,0:T(8,128)S(1)}, u32[]{:S(2)}, u32[]{:S(2)}) %collective-permute-start.49) | collective-permute-done | bytes 262176 | tf_op jit(solution)/shard_map/ppermute | solution.py:63
  439.8 8.1 %fusion.63 = f32[64,192,128]{2,0,1:T(8,128)S(1)} fusion(bf16[192,128,128]{2,1,0:T(8,128)(2,1)} %bitcast.11, bf16[192,64,128]{2,1,0:T(8,128)(2,1)} %gather_fusion.7, pred[192]{0:T(512)(128)(4,1)S(1)} %get-tuple-element.55), kind=kOutput, calls=%fused_computation.63 | convolution fusion | flops 404226048 | bytes 15728832 | tf_op jit(solution)/shard_map/sij,ksj->ksi/dot_general | solution.py:88
  454.2 5.2 collective-permute-done.53
  499.4 5.6 fusion.66
  513.4 6.3 %collective-permute-done.68 = f32[32,2048]{1,0:T(8,128)S(1)} collective-permute-done((f32[32,2048]{1,0:T(8,128)S(1)}, f32[32,2048]{1,0:T(8,128)S(1)}, u32[]{:S(2)}, u32[]{:S(2)}) %collective-permute-start.68) | collective-permute-done | bytes 262176 | tf_op jit(solution)/shard_map/ppermute | solution.py:55
  526.8 7.1 %collective-permute-done.70 = f32[32,2048]{1,0:T(8,128)S(1)} collective-permute-done((f32[32,2048]{1,0:T(8,128)S(1)}, f32[32,2048]{1,0:T(8,128)S(1)}, u32[]{:S(2)}, u32[]{:S(2)}) %collective-permute-start.70) | collective-permute-done | bytes 262176 | tf_op jit(solution)/shard_map/ppermute | solution.py:63
  550.5 8.2 %fusion.69 = f32[64,192,128]{2,0,1:T(8,128)S(1)} fusion(bf16[192,128,128]{2,1,0:T(8,128)(2,1)} %bitcast.11, bf16[192,64,128]{2,1,0:T(8,128)(2,1)} %gather_fusion.9, pred[192]{0:T(512)(128)(4,1)S(1)} %get-tuple-element.55), kind=kOutput, calls=%fused_computation.65 | convolution fusion | flops 404226048 | bytes 15728832 | tf_op jit(solution)/shard_map/sij,ksj->ksi/dot_general | solution.py:88
  (413 shorter events, 322.1 us)
Async XLA Ops:
  5.5 17.4 %all-to-all-start = ((s32[8,24,2]{1,2,0:T(2,128)}), s32[8,24,2]{1,2,0:T(2,128)S(1)}, u32[]{:S(2)}, u32[]{:S(2)}) async-start(s32[8,24,2]{1,2,0:T(2,128)} %copy.153), calls=%async_computation | async-start | bytes 16384 | tf_op jit(solution)/shard_map/all_to_all | solution.py:128
  22.8 143.8 %all-to-all-start.1 = ((bf16[8,24,128,128]{3,2,1,0:T(8,128)(2,1)}), bf16[8,24,128,128]{3,2,1,0:T(8,128)(2,1)}, u32[]{:S(2)}, u32[]{:S(2)}) async-start(bf16[8,24,128,128]{3,2,1,0:T(8,128)(2,1)} %bitcast.272), calls=%async_computation.1 | async-start | bytes 12582912 | tf_op jit(solution)/shard_map/all_to_all | solution.py:121
  177.8 9.2 %collective-permute-start.5 = (f32[32,2048]{1,0:T(8,128)S(1)}, f32[32,2048]{1,0:T(8,128)S(1)}, u32[]{:S(2)}, u32[]{:S(2)}) collective-permute-start(f32[32,2048]{1,0:T(8,128)S(1)} %constant_dynamic-slice_fusion.22), channel_id=1, source_target_pairs={{0,16},{8,24},{16,0},{24,8},{1,17},{9,25},{17,1},{25,9},{2,18},{10... | collective-permute-start | bytes 786440 | tf_op jit(solution)/shard_map/ppermute | solution.py:55
  179.4 12.8 %collective-permute-start.3 = (f32[32,2048]{1,0:T(8,128)S(1)}, f32[32,2048]{1,0:T(8,128)S(1)}, u32[]{:S(2)}, u32[]{:S(2)}) collective-permute-start(f32[32,2048]{1,0:T(8,128)S(1)} %dynamic-slice_add_fusion.15), channel_id=1, source_target_pairs={{0,16},{8,24},{16,0},{24,8},{1,17},{9,25},{17,1},{25,9},{2,18},{10... | collective-permute-start | bytes 786440 | tf_op jit(solution)/shard_map/ppermute | solution.py:57
  192.3 8.8 %collective-permute-start.7 = (f32[32,2048]{1,0:T(8,128)S(1)}, f32[32,2048]{1,0:T(8,128)S(1)}, u32[]{:S(2)}, u32[]{:S(2)}) collective-permute-start(f32[32,2048]{1,0:T(8,128)S(1)} %add.400), channel_id=1, source_target_pairs={{0,16},{8,24},{16,0},{24,8},{1,17},{9,25},{17,1},{25,9},{2,18},{10... | collective-permute-start | bytes 786440 | tf_op jit(solution)/shard_map/ppermute | solution.py:63
  229.4 9.0 %collective-permute-start.16 = (f32[32,2048]{1,0:T(8,128)S(1)}, f32[32,2048]{1,0:T(8,128)S(1)}, u32[]{:S(2)}, u32[]{:S(2)}) collective-permute-start(f32[32,2048]{1,0:T(8,128)S(1)} %constant_dynamic-slice_fusion.19), channel_id=1, source_target_pairs={{0,2},{1,3},{2,0},{3,1},{4,6},{5,7},{6,4},{7,5},{8,10},{9,11},{10,... | collective-permute-start | bytes 786440 | tf_op jit(solution)/shard_map/ppermute | solution.py:55
  229.9 9.2 %collective-permute-start.11 = (f32[32,2048]{1,0:T(8,128)S(1)}, f32[32,2048]{1,0:T(8,128)S(1)}, u32[]{:S(2)}, u32[]{:S(2)}) collective-permute-start(f32[32,2048]{1,0:T(8,128)S(1)} %constant_dynamic-slice_fusion.21), channel_id=1, source_target_pairs={{0,1},{1,0},{2,3},{3,2},{4,5},{5,4},{6,7},{7,6},{8,9},{9,8},{10,11... | collective-permute-start | bytes 786440 | tf_op jit(solution)/shard_map/ppermute | solution.py:55
  238.4 10.6 %collective-permute-start.17 = (f32[32,1024]{1,0:T(8,128)S(1)}, f32[32,1024]{1,0:T(8,128)S(1)}, u32[]{:S(2)}, u32[]{:S(2)}) collective-permute-start(f32[32,1024]{1,0:T(8,128)S(1)} %constant_dynamic-slice_fusion.18), channel_id=1, source_target_pairs={{0,4},{1,5},{2,6},{3,7},{4,0},{5,1},{6,2},{7,3},{8,12},{9,13},{10,... | collective-permute-start | bytes 393224 | tf_op jit(solution)/shard_map/ppermute | solution.py:55
  239.1 11.0 %collective-permute-start.12 = (f32[32,1024]{1,0:T(8,128)S(1)}, f32[32,1024]{1,0:T(8,128)S(1)}, u32[]{:S(2)}, u32[]{:S(2)}) collective-permute-start(f32[32,1024]{1,0:T(8,128)S(1)} %constant_dynamic-slice_fusion.20), channel_id=1, source_target_pairs={{0,2},{1,3},{2,0},{3,1},{4,6},{5,7},{6,4},{7,5},{8,10},{9,11},{10,... | collective-permute-start | bytes 393224 | tf_op jit(solution)/shard_map/ppermute | solution.py:55
  288.3 9.2 %collective-permute-start.26 = (f32[32,2048]{1,0:T(8,128)S(1)}, f32[32,2048]{1,0:T(8,128)S(1)}, u32[]{:S(2)}, u32[]{:S(2)}) collective-permute-start(f32[32,2048]{1,0:T(8,128)S(1)} %constant_dynamic-slice_fusion.16), channel_id=1, source_target_pairs={{0,16},{8,24},{16,0},{24,8},{1,17},{9,25},{17,1},{25,9},{2,18},{10... | collective-permute-start | bytes 786440 | tf_op jit(solution)/shard_map/ppermute | solution.py:55
  289.9 12.8 %collective-permute-start.24 = (f32[32,2048]{1,0:T(8,128)S(1)}, f32[32,2048]{1,0:T(8,128)S(1)}, u32[]{:S(2)}, u32[]{:S(2)}) collective-permute-start(f32[32,2048]{1,0:T(8,128)S(1)} %dynamic-slice_add_fusion.11), channel_id=1, source_target_pairs={{0,16},{8,24},{16,0},{24,8},{1,17},{9,25},{17,1},{25,9},{2,18},{10... | collective-permute-start | bytes 786440 | tf_op jit(solution)/shard_map/ppermute | solution.py:57
  302.9 8.8 %collective-permute-start.28 = (f32[32,2048]{1,0:T(8,128)S(1)}, f32[32,2048]{1,0:T(8,128)S(1)}, u32[]{:S(2)}, u32[]{:S(2)}) collective-permute-start(f32[32,2048]{1,0:T(8,128)S(1)} %add.429), channel_id=1, source_target_pairs={{0,16},{8,24},{16,0},{24,8},{1,17},{9,25},{17,1},{25,9},{2,18},{10... | collective-permute-start | bytes 786440 | tf_op jit(solution)/shard_map/ppermute | solution.py:63
  342.6 8.5 %collective-permute-start.37 = (f32[32,2048]{1,0:T(8,128)S(1)}, f32[32,2048]{1,0:T(8,128)S(1)}, u32[]{:S(2)}, u32[]{:S(2)}) collective-permute-start(f32[32,2048]{1,0:T(8,128)S(1)} %constant_dynamic-slice_fusion.13), channel_id=1, source_target_pairs={{0,2},{1,3},{2,0},{3,1},{4,6},{5,7},{6,4},{7,5},{8,10},{9,11},{10,... | collective-permute-start | bytes 786440 | tf_op jit(solution)/shard_map/ppermute | solution.py:55
  351.2 10.4 %collective-permute-start.38 = (f32[32,1024]{1,0:T(8,128)S(1)}, f32[32,1024]{1,0:T(8,128)S(1)}, u32[]{:S(2)}, u32[]{:S(2)}) collective-permute-start(f32[32,1024]{1,0:T(8,128)S(1)} %constant_dynamic-slice_fusion.12), channel_id=1, source_target_pairs={{0,4},{1,5},{2,6},{3,7},{4,0},{5,1},{6,2},{7,3},{8,12},{9,13},{10,... | collective-permute-start | bytes 393224 | tf_op jit(solution)/shard_map/ppermute | solution.py:55
  353.6 10.3 %collective-permute-start.34 = (f32[32,1024]{1,0:T(8,128)S(1)}, f32[32,1024]{1,0:T(8,128)S(1)}, u32[]{:S(2)}, u32[]{:S(2)}) collective-permute-start(f32[32,1024]{1,0:T(8,128)S(1)} %dynamic-slice_add_fusion.21), channel_id=1, source_target_pairs={{0,4},{1,5},{2,6},{3,7},{4,0},{5,1},{6,2},{7,3},{8,12},{9,13},{10,... | collective-permute-start | bytes 393224 | tf_op jit(solution)/shard_map/ppermute | solution.py:57
  399.2 9.2 %collective-permute-start.47 = (f32[32,2048]{1,0:T(8,128)S(1)}, f32[32,2048]{1,0:T(8,128)S(1)}, u32[]{:S(2)}, u32[]{:S(2)}) collective-permute-start(f32[32,2048]{1,0:T(8,128)S(1)} %constant_dynamic-slice_fusion.10), channel_id=1, source_target_pairs={{0,16},{8,24},{16,0},{24,8},{1,17},{9,25},{17,1},{25,9},{2,18},{10... | collective-permute-start | bytes 786440 | tf_op jit(solution)/shard_map/ppermute | solution.py:55
  400.8 12.7 %collective-permute-start.45 = (f32[32,2048]{1,0:T(8,128)S(1)}, f32[32,2048]{1,0:T(8,128)S(1)}, u32[]{:S(2)}, u32[]{:S(2)}) collective-permute-start(f32[32,2048]{1,0:T(8,128)S(1)} %dynamic-slice_add_fusion.7), channel_id=1, source_target_pairs={{0,16},{8,24},{16,0},{24,8},{1,17},{9,25},{17,1},{25,9},{2,18},{10... | collective-permute-start | bytes 786440 | tf_op jit(solution)/shard_map/ppermute | solution.py:57
  413.8 8.8 %collective-permute-start.49 = (f32[32,2048]{1,0:T(8,128)S(1)}, f32[32,2048]{1,0:T(8,128)S(1)}, u32[]{:S(2)}, u32[]{:S(2)}) collective-permute-start(f32[32,2048]{1,0:T(8,128)S(1)} %add.448), channel_id=1, source_target_pairs={{0,16},{8,24},{16,0},{24,8},{1,17},{9,25},{17,1},{25,9},{2,18},{10... | collective-permute-start | bytes 786440 | tf_op jit(solution)/shard_map/ppermute | solution.py:63
  454.2 8.7 %collective-permute-start.58 = (f32[32,2048]{1,0:T(8,128)S(1)}, f32[32,2048]{1,0:T(8,128)S(1)}, u32[]{:S(2)}, u32[]{:S(2)}) collective-permute-start(f32[32,2048]{1,0:T(8,128)S(1)} %constant_dynamic-slice_fusion.7), channel_id=1, source_target_pairs={{0,2},{1,3},{2,0},{3,1},{4,6},{5,7},{6,4},{7,5},{8,10},{9,11},{10,... | collective-permute-start | bytes 786440 | tf_op jit(solution)/shard_map/ppermute | solution.py:55
  464.5 11.1 %collective-permute-start.55 = (f32[32,1024]{1,0:T(8,128)S(1)}, f32[32,1024]{1,0:T(8,128)S(1)}, u32[]{:S(2)}, u32[]{:S(2)}) collective-permute-start(f32[32,1024]{1,0:T(8,128)S(1)} %dynamic-slice_add_fusion.19), channel_id=1, source_target_pairs={{0,4},{1,5},{2,6},{3,7},{4,0},{5,1},{6,2},{7,3},{8,12},{9,13},{10,... | collective-permute-start | bytes 393224 | tf_op jit(solution)/shard_map/ppermute | solution.py:57
  510.5 9.2 %collective-permute-start.68 = (f32[32,2048]{1,0:T(8,128)S(1)}, f32[32,2048]{1,0:T(8,128)S(1)}, u32[]{:S(2)}, u32[]{:S(2)}) collective-permute-start(f32[32,2048]{1,0:T(8,128)S(1)} %constant_dynamic-slice_fusion.4), channel_id=1, source_target_pairs={{0,16},{8,24},{16,0},{24,8},{1,17},{9,25},{17,1},{25,9},{2,18},{10... | collective-permute-start | bytes 786440 | tf_op jit(solution)/shard_map/ppermute | solution.py:55
  512.2 12.7 %collective-permute-start.66 = (f32[32,2048]{1,0:T(8,128)S(1)}, f32[32,2048]{1,0:T(8,128)S(1)}, u32[]{:S(2)}, u32[]{:S(2)}) collective-permute-start(f32[32,2048]{1,0:T(8,128)S(1)} %dynamic-slice_add_fusion.3), channel_id=1, source_target_pairs={{0,16},{8,24},{16,0},{24,8},{1,17},{9,25},{17,1},{25,9},{2,18},{10... | collective-permute-start | bytes 786440 | tf_op jit(solution)/shard_map/ppermute | solution.py:57
  525.1 8.8 %collective-permute-start.70 = (f32[32,2048]{1,0:T(8,128)S(1)}, f32[32,2048]{1,0:T(8,128)S(1)}, u32[]{:S(2)}, u32[]{:S(2)}) collective-permute-start(f32[32,2048]{1,0:T(8,128)S(1)} %add.467), channel_id=1, source_target_pairs={{0,16},{8,24},{16,0},{24,8},{1,17},{9,25},{17,1},{25,9},{2,18},{10... | collective-permute-start | bytes 786440 | tf_op jit(solution)/shard_map/ppermute | solution.py:63
  576.6 9.9 %collective-permute-start.76 = (f32[32,1024]{1,0:T(8,128)S(1)}, f32[32,1024]{1,0:T(8,128)S(1)}, u32[]{:S(2)}, u32[]{:S(2)}) collective-permute-start(f32[32,1024]{1,0:T(8,128)S(1)} %dynamic-slice_add_fusion.17), channel_id=1, source_target_pairs={{0,4},{1,5},{2,6},{3,7},{4,0},{5,1},{6,2},{7,3},{8,12},{9,13},{10,... | collective-permute-start | bytes 393224 | tf_op jit(solution)/shard_map/ppermute | solution.py:57
  (81 other events, 571.1 us)

commit v19 on v18

--- a/solution.py
+++ b/solution.py
@@ -42,9 +42,13 @@
         distances.append(distance)
         distance *= 2
     lanes = jnp.split(value, CHUNKS, axis=0)
-    orders = [distances[lane % len(distances):] + distances[:lane % len(distances)] for lane in range(CHUNKS)]
+    if len(distances) == 2:
+        orders = [distances[lane % 2:] + distances[:lane % 2] for lane in range(CHUNKS)]
+    else:
+        orders = [distances[:-1][lane % (len(distances) - 1):] + distances[:-1][:lane % (len(distances) - 1)] + distances[-1:] for lane in range(CHUNKS)]
     lasts = [order.pop() for order in orders]
-    for step in range(len(distances) - 1):
+    distances = distances[:-1]
+    for step in range(len(distances)):
         moved = []
         for lane, held in enumerate(lanes):
             distance = orders[lane][step]
@@ -55,7 +59,7 @@
             moved.append(keep + lax.ppermute(give, axis, partner_pairs(count, distance)))
         lanes = moved
     lanes = [held + lax.ppermute(held, axis, partner_pairs(count, last)) for held, last in zip(lanes, lasts)]
-    for step in reversed(range(len(distances) - 1)):
+    for step in reversed(range(len(distances))):
         moved = []
         for lane, held in enumerate(lanes):
             distance = orders[lane][step]

time: 614 us -> 601 us (0.979)
  waiting for transfers between devices: 378 us -> 355 us
  starting transfers between devices: 78.7 us -> 88.3 us
    ppermute x24, waiting for transfers between devices: 82.4 us -> 67 us  [big_sum(): lax.ppermute(give, axis, partner_pairs(count, distance))]
    ppermute x24, waiting for transfers between devices: 72.8 us -> 65.9 us  [big_sum(): other = lax.ppermute(held, axis, partner_pairs(count, distance))]
  transfers between devices with their start and end apart: 88 -> 88, of which waited for: 72 -> 69; matrix products, arithmetic and copies ran while one was open for 3% -> 3% of each run, Pallas kernels for 0% -> 0%
where the time goes in v19:
time: 601 us; the launch traced here: 597 us
  waiting for transfers between devices  355 us (59%)
  matrix products  92.7 us (15%)
  starting transfers between devices  88.3 us (15%)
  local copies, waits for them, and re-layouts  41.9 us (7%)
  other arithmetic  17.1 us (3%)
    all_to_all x1, waiting for transfers between devices, per_device(): lax.all_to_all(outgoing.reshape(col_count, capacity, block_size, block_si...  130 us
    ppermute x24, waiting for transfers between devices, big_sum(): lax.ppermute(give, axis, partner_pairs(count, distance))  67 us
    ppermute x24, waiting for transfers between devices, big_sum(): other = lax.ppermute(held, axis, partner_pairs(count, distance))  65.9 us
    ppermute x22, waiting for transfers between devices, small_sum(): value = value + lax.ppermute(value, axis, partner_pairs(count, distance))  50.7 us
    ppermute x16, waiting for transfers between devices, big_sum(): lax.ppermute(held, axis, partner_pairs(count, last))  41.8 us
    dot_general x8, matrix products, place_terms(): jnp.einsum('ksi,st->kti', weighted, onehot, precision=lax.Precision.HIGH)  37.8 us
    dot_general x4, matrix products, forward_terms(): jnp.einsum('sij,ksj->ksi', blocks, picked, preferred_element_type=jnp.flo...  32.6 us
    gather x8, local copies, waits for them, and re-layouts, gather_tiles(): return jnp.take(vector_tiles, indices, axis=1)  22.8 us
  transfers between devices with their start and end apart: 88, of which 69 were waited for; matrix products, arithmetic and copies ran while one was open for 3% of the time, Pallas kernels for 0%

profile of v19, /device:TPU:0, one launch (start us, length us, event | category | flops | bytes accessed | tf_op | source)
XLA Modules:
  0.0 597.5 jit_solution(4478955228760696742)
XLA Ops:
  5.5 7.3 %all-to-all-start = ((s32[8,24,2]{1,2,0:T(2,128)}), s32[8,24,2]{1,2,0:T(2,128)S(1)}, u32[]{:S(2)}, u32[]{:S(2)}) async-start(s32[8,24,2]{1,2,0:T(2,128)} %copy.153), calls=%async_computation | async-start | bytes 16384 | tf_op jit(solution)/shard_map/all_to_all | solution.py:132
  14.8 8.0 %gather_fusion.1 = bf16[192,128,128]{2,1,0:T(8,128)(2,1)} fusion(bf16[97,128,128]{2,1,0:T(8,128)(2,1)S(1)} %concatenate.273, s32[1024]{0:T(1024)S(1)} %pad_clamp_fusion.2), kind=kCustom, calls=%fused_computation.9 | custom fusion | bytes 12583680 | tf_op jit(solution)/shard_map/jit(_take)/gather | solution.py:119
  22.9 6.3 %all-to-all-start.1 = ((bf16[8,24,128,128]{3,2,1,0:T(8,128)(2,1)}), bf16[8,24,128,128]{3,2,1,0:T(8,128)(2,1)}, u32[]{:S(2)}, u32[]{:S(2)}) async-start(bf16[8,24,128,128]{3,2,1,0:T(8,128)(2,1)} %bitcast.272), calls=%async_computation.1 | async-start | bytes 12582912 | tf_op jit(solution)/shard_map/all_to_all | solution.py:125
  37.1 129.6 %all-to-all-done.1 = bf16[8,24,128,128]{3,2,1,0:T(8,128)(2,1)} async-done(((bf16[8,24,128,128]{3,2,1,0:T(8,128)(2,1)}), bf16[8,24,128,128]{3,2,1,0:T(8,128)(2,1)}, u32[]{:S(2)}, u32[]{:S(2)}) %all-to-all-start.1) | async-done | bytes 6291488 | tf_op jit(solution)/shard_map/all_to_all | solution.py:125
  166.7 5.6 fusion.48
  180.5 6.4 %collective-permute-done.5 = f32[32,2048]{1,0:T(8,128)S(1)} collective-permute-done((f32[32,2048]{1,0:T(8,128)S(1)}, f32[32,2048]{1,0:T(8,128)S(1)}, u32[]{:S(2)}, u32[]{:S(2)}) %collective-permute-start.5) | collective-permute-done | bytes 262176 | tf_op jit(solution)/shard_map/ppermute | solution.py:59
  194.0 7.1 %collective-permute-done.7 = f32[32,2048]{1,0:T(8,128)S(1)} collective-permute-done((f32[32,2048]{1,0:T(8,128)S(1)}, f32[32,2048]{1,0:T(8,128)S(1)}, u32[]{:S(2)}, u32[]{:S(2)}) %collective-permute-start.7) | collective-permute-done | bytes 262176 | tf_op jit(solution)/shard_map/ppermute | solution.py:67
  216.0 8.3 %fusion.51 = f32[64,192,128]{2,0,1:T(8,128)S(1)} fusion(bf16[192,128,128]{2,1,0:T(8,128)(2,1)} %bitcast.11, bf16[192,64,128]{2,1,0:T(8,128)(2,1)} %gather_fusion.3, pred[192]{0:T(512)(128)(4,1)S(1)} %get-tuple-element.55), kind=kOutput, calls=%fused_computation.59 | convolution fusion | flops 404226048 | bytes 15728832 | tf_op jit(solution)/shard_map/sij,ksj->ksi/dot_general | solution.py:92
  273.1 5.6 fusion.54
  287.3 6.4 %collective-permute-done.26 = f32[32,2048]{1,0:T(8,128)S(1)} collective-permute-done((f32[32,2048]{1,0:T(8,128)S(1)}, f32[32,2048]{1,0:T(8,128)S(1)}, u32[]{:S(2)}, u32[]{:S(2)}) %collective-permute-start.26) | collective-permute-done | bytes 262176 | tf_op jit(solution)/shard_map/ppermute | solution.py:59
  300.8 7.1 %collective-permute-done.28 = f32[32,2048]{1,0:T(8,128)S(1)} collective-permute-done((f32[32,2048]{1,0:T(8,128)S(1)}, f32[32,2048]{1,0:T(8,128)S(1)}, u32[]{:S(2)}, u32[]{:S(2)}) %collective-permute-start.28) | collective-permute-done | bytes 262176 | tf_op jit(solution)/shard_map/ppermute | solution.py:67
  324.2 8.1 %fusion.57 = f32[64,192,128]{2,0,1:T(8,128)S(1)} fusion(bf16[192,128,128]{2,1,0:T(8,128)(2,1)} %bitcast.11, bf16[192,64,128]{2,1,0:T(8,128)(2,1)} %gather_fusion.5, pred[192]{0:T(512)(128)(4,1)S(1)} %get-tuple-element.55), kind=kOutput, calls=%fused_computation.61 | convolution fusion | flops 404226048 | bytes 15728832 | tf_op jit(solution)/shard_map/sij,ksj->ksi/dot_general | solution.py:92
  339.4 5.7 collective-permute-done.32
  346.9 5.9 collective-permute-done.33
  380.9 5.6 fusion.60
  394.8 6.4 %collective-permute-done.47 = f32[32,2048]{1,0:T(8,128)S(1)} collective-permute-done((f32[32,2048]{1,0:T(8,128)S(1)}, f32[32,2048]{1,0:T(8,128)S(1)}, u32[]{:S(2)}, u32[]{:S(2)}) %collective-permute-start.47) | collective-permute-done | bytes 262176 | tf_op jit(solution)/shard_map/ppermute | solution.py:59
  408.2 7.1 %collective-permute-done.49 = f32[32,2048]{1,0:T(8,128)S(1)} collective-permute-done((f32[32,2048]{1,0:T(8,128)S(1)}, f32[32,2048]{1,0:T(8,128)S(1)}, u32[]{:S(2)}, u32[]{:S(2)}) %collective-permute-start.49) | collective-permute-done | bytes 262176 | tf_op jit(solution)/shard_map/ppermute | solution.py:67
  432.6 8.1 %fusion.63 = f32[64,192,128]{2,0,1:T(8,128)S(1)} fusion(bf16[192,128,128]{2,1,0:T(8,128)(2,1)} %bitcast.11, bf16[192,64,128]{2,1,0:T(8,128)(2,1)} %gather_fusion.7, pred[192]{0:T(512)(128)(4,1)S(1)} %get-tuple-element.55), kind=kOutput, calls=%fused_computation.63 | convolution fusion | flops 404226048 | bytes 15728832 | tf_op jit(solution)/shard_map/sij,ksj->ksi/dot_general | solution.py:92
  447.4 5.6 collective-permute-done.53
  489.3 5.6 fusion.66
  503.2 6.4 %collective-permute-done.68 = f32[32,2048]{1,0:T(8,128)S(1)} collective-permute-done((f32[32,2048]{1,0:T(8,128)S(1)}, f32[32,2048]{1,0:T(8,128)S(1)}, u32[]{:S(2)}, u32[]{:S(2)}) %collective-permute-start.68) | collective-permute-done | bytes 262176 | tf_op jit(solution)/shard_map/ppermute | solution.py:59
  516.7 7.1 %collective-permute-done.70 = f32[32,2048]{1,0:T(8,128)S(1)} collective-permute-done((f32[32,2048]{1,0:T(8,128)S(1)}, f32[32,2048]{1,0:T(8,128)S(1)}, u32[]{:S(2)}, u32[]{:S(2)}) %collective-permute-start.70) | collective-permute-done | bytes 262176 | tf_op jit(solution)/shard_map/ppermute | solution.py:67
  540.4 8.2 %fusion.69 = f32[64,192,128]{2,0,1:T(8,128)S(1)} fusion(bf16[192,128,128]{2,1,0:T(8,128)(2,1)} %bitcast.11, bf16[192,64,128]{2,1,0:T(8,128)(2,1)} %gather_fusion.9, pred[192]{0:T(512)(128)(4,1)S(1)} %get-tuple-element.55), kind=kOutput, calls=%fused_computation.65 | convolution fusion | flops 404226048 | bytes 15728832 | tf_op jit(solution)/shard_map/sij,ksj->ksi/dot_general | solution.py:92
  556.0 5.4 collective-permute-done.74
  (413 shorter events, 312.3 us)
Async XLA Ops:
  5.5 17.4 %all-to-all-start = ((s32[8,24,2]{1,2,0:T(2,128)}), s32[8,24,2]{1,2,0:T(2,128)S(1)}, u32[]{:S(2)}, u32[]{:S(2)}) async-start(s32[8,24,2]{1,2,0:T(2,128)} %copy.153), calls=%async_computation | async-start | bytes 16384 | tf_op jit(solution)/shard_map/all_to_all | solution.py:132
  22.9 143.8 %all-to-all-start.1 = ((bf16[8,24,128,128]{3,2,1,0:T(8,128)(2,1)}), bf16[8,24,128,128]{3,2,1,0:T(8,128)(2,1)}, u32[]{:S(2)}, u32[]{:S(2)}) async-start(bf16[8,24,128,128]{3,2,1,0:T(8,128)(2,1)} %bitcast.272), calls=%async_computation.1 | async-start | bytes 12582912 | tf_op jit(solution)/shard_map/all_to_all | solution.py:125
  177.8 9.2 %collective-permute-start.5 = (f32[32,2048]{1,0:T(8,128)S(1)}, f32[32,2048]{1,0:T(8,128)S(1)}, u32[]{:S(2)}, u32[]{:S(2)}) collective-permute-start(f32[32,2048]{1,0:T(8,128)S(1)} %constant_dynamic-slice_fusion.22), channel_id=1, source_target_pairs={{0,16},{8,24},{16,0},{24,8},{1,17},{9,25},{17,1},{25,9},{2,18},{10... | collective-permute-start | bytes 786440 | tf_op jit(solution)/shard_map/ppermute | solution.py:59
  179.4 12.8 %collective-permute-start.3 = (f32[32,2048]{1,0:T(8,128)S(1)}, f32[32,2048]{1,0:T(8,128)S(1)}, u32[]{:S(2)}, u32[]{:S(2)}) collective-permute-start(f32[32,2048]{1,0:T(8,128)S(1)} %dynamic-slice_add_fusion.15), channel_id=1, source_target_pairs={{0,16},{8,24},{16,0},{24,8},{1,17},{9,25},{17,1},{25,9},{2,18},{10... | collective-permute-start | bytes 786440 | tf_op jit(solution)/shard_map/ppermute | solution.py:61
  192.4 8.8 %collective-permute-start.7 = (f32[32,2048]{1,0:T(8,128)S(1)}, f32[32,2048]{1,0:T(8,128)S(1)}, u32[]{:S(2)}, u32[]{:S(2)}) collective-permute-start(f32[32,2048]{1,0:T(8,128)S(1)} %add.397), channel_id=1, source_target_pairs={{0,16},{8,24},{16,0},{24,8},{1,17},{9,25},{17,1},{25,9},{2,18},{10... | collective-permute-start | bytes 786440 | tf_op jit(solution)/shard_map/ppermute | solution.py:67
  243.8 9.0 %collective-permute-start.18 = (f32[32,1024]{1,0:T(8,128)S(1)}, f32[32,1024]{1,0:T(8,128)S(1)}, u32[]{:S(2)}, u32[]{:S(2)}) collective-permute-start(f32[32,1024]{1,0:T(8,128)S(1)} %dynamic-slice_add_fusion.22), channel_id=1, source_target_pairs={{0,4},{1,5},{2,6},{3,7},{4,0},{5,1},{6,2},{7,3},{8,12},{9,13},{10,... | collective-permute-start | bytes 393224 | tf_op jit(solution)/shard_map/ppermute | solution.py:61
  284.6 9.2 %collective-permute-start.26 = (f32[32,2048]{1,0:T(8,128)S(1)}, f32[32,2048]{1,0:T(8,128)S(1)}, u32[]{:S(2)}, u32[]{:S(2)}) collective-permute-start(f32[32,2048]{1,0:T(8,128)S(1)} %constant_dynamic-slice_fusion.16), channel_id=1, source_target_pairs={{0,16},{8,24},{16,0},{24,8},{1,17},{9,25},{17,1},{25,9},{2,18},{10... | collective-permute-start | bytes 786440 | tf_op jit(solution)/shard_map/ppermute | solution.py:59
  286.2 12.8 %collective-permute-start.24 = (f32[32,2048]{1,0:T(8,128)S(1)}, f32[32,2048]{1,0:T(8,128)S(1)}, u32[]{:S(2)}, u32[]{:S(2)}) collective-permute-start(f32[32,2048]{1,0:T(8,128)S(1)} %dynamic-slice_add_fusion.11), channel_id=1, source_target_pairs={{0,16},{8,24},{16,0},{24,8},{1,17},{9,25},{17,1},{25,9},{2,18},{10... | collective-permute-start | bytes 786440 | tf_op jit(solution)/shard_map/ppermute | solution.py:61
  299.2 8.8 %collective-permute-start.28 = (f32[32,2048]{1,0:T(8,128)S(1)}, f32[32,2048]{1,0:T(8,128)S(1)}, u32[]{:S(2)}, u32[]{:S(2)}) collective-permute-start(f32[32,2048]{1,0:T(8,128)S(1)} %add.425), channel_id=1, source_target_pairs={{0,16},{8,24},{16,0},{24,8},{1,17},{9,25},{17,1},{25,9},{2,18},{10... | collective-permute-start | bytes 786440 | tf_op jit(solution)/shard_map/ppermute | solution.py:67
  337.5 7.6 %collective-permute-start.32 = (f32[32,2048]{1,0:T(8,128)S(1)}, f32[32,2048]{1,0:T(8,128)S(1)}, u32[]{:S(2)}, u32[]{:S(2)}) collective-permute-start(f32[32,2048]{1,0:T(8,128)S(1)} %constant_dynamic-slice_fusion.15), channel_id=1, source_target_pairs={{0,1},{1,0},{2,3},{3,2},{4,5},{5,4},{6,7},{7,6},{8,9},{9,8},{10,11... | collective-permute-start | bytes 786440 | tf_op jit(solution)/shard_map/ppermute | solution.py:59
  345.1 7.7 %collective-permute-start.33 = (f32[32,1024]{1,0:T(8,128)S(1)}, f32[32,1024]{1,0:T(8,128)S(1)}, u32[]{:S(2)}, u32[]{:S(2)}) collective-permute-start(f32[32,1024]{1,0:T(8,128)S(1)} %constant_dynamic-slice_fusion.14), channel_id=1, source_target_pairs={{0,2},{1,3},{2,0},{3,1},{4,6},{5,7},{6,4},{7,5},{8,10},{9,11},{10,... | collective-permute-start | bytes 393224 | tf_op jit(solution)/shard_map/ppermute | solution.py:59
  353.0 8.2 %collective-permute-start.39 = (f32[32,1024]{1,0:T(8,128)S(1)}, f32[32,1024]{1,0:T(8,128)S(1)}, u32[]{:S(2)}, u32[]{:S(2)}) collective-permute-start(f32[32,1024]{1,0:T(8,128)S(1)} %dynamic-slice_add_fusion.20), channel_id=1, source_target_pairs={{0,4},{1,5},{2,6},{3,7},{4,0},{5,1},{6,2},{7,3},{8,12},{9,13},{10,... | collective-permute-start | bytes 393224 | tf_op jit(solution)/shard_map/ppermute | solution.py:61
  392.0 9.2 %collective-permute-start.47 = (f32[32,2048]{1,0:T(8,128)S(1)}, f32[32,2048]{1,0:T(8,128)S(1)}, u32[]{:S(2)}, u32[]{:S(2)}) collective-permute-start(f32[32,2048]{1,0:T(8,128)S(1)} %constant_dynamic-slice_fusion.10), channel_id=1, source_target_pairs={{0,16},{8,24},{16,0},{24,8},{1,17},{9,25},{17,1},{25,9},{2,18},{10... | collective-permute-start | bytes 786440 | tf_op jit(solution)/shard_map/ppermute | solution.py:59
  393.6 12.8 %collective-permute-start.45 = (f32[32,2048]{1,0:T(8,128)S(1)}, f32[32,2048]{1,0:T(8,128)S(1)}, u32[]{:S(2)}, u32[]{:S(2)}) collective-permute-start(f32[32,2048]{1,0:T(8,128)S(1)} %dynamic-slice_add_fusion.7), channel_id=1, source_target_pairs={{0,16},{8,24},{16,0},{24,8},{1,17},{9,25},{17,1},{25,9},{2,18},{10... | collective-permute-start | bytes 786440 | tf_op jit(solution)/shard_map/ppermute | solution.py:61
  406.5 8.8 %collective-permute-start.49 = (f32[32,2048]{1,0:T(8,128)S(1)}, f32[32,2048]{1,0:T(8,128)S(1)}, u32[]{:S(2)}, u32[]{:S(2)}) collective-permute-start(f32[32,2048]{1,0:T(8,128)S(1)} %add.444), channel_id=1, source_target_pairs={{0,16},{8,24},{16,0},{24,8},{1,17},{9,25},{17,1},{25,9},{2,18},{10... | collective-permute-start | bytes 786440 | tf_op jit(solution)/shard_map/ppermute | solution.py:67
  461.2 7.4 %collective-permute-start.60 = (f32[32,1024]{1,0:T(8,128)S(1)}, f32[32,1024]{1,0:T(8,128)S(1)}, u32[]{:S(2)}, u32[]{:S(2)}) collective-permute-start(f32[32,1024]{1,0:T(8,128)S(1)} %dynamic-slice_add_fusion.18), channel_id=1, source_target_pairs={{0,4},{1,5},{2,6},{3,7},{4,0},{5,1},{6,2},{7,3},{8,12},{9,13},{10,... | collective-permute-start | bytes 393224 | tf_op jit(solution)/shard_map/ppermute | solution.py:61
  464.3 8.0 %collective-permute-start.56 = (f32[32,1024]{1,0:T(8,128)S(1)}, f32[32,1024]{1,0:T(8,128)S(1)}, u32[]{:S(2)}, u32[]{:S(2)}) collective-permute-start(f32[32,1024]{1,0:T(8,128)S(1)} %add.451), channel_id=1, source_target_pairs={{0,2},{1,3},{2,0},{3,1},{4,6},{5,7},{6,4},{7,5},{8,10},{9,11},{10,... | collective-permute-start | bytes 393224 | tf_op jit(solution)/shard_map/ppermute | solution.py:67
  500.4 9.2 %collective-permute-start.68 = (f32[32,2048]{1,0:T(8,128)S(1)}, f32[32,2048]{1,0:T(8,128)S(1)}, u32[]{:S(2)}, u32[]{:S(2)}) collective-permute-start(f32[32,2048]{1,0:T(8,128)S(1)} %constant_dynamic-slice_fusion.4), channel_id=1, source_target_pairs={{0,16},{8,24},{16,0},{24,8},{1,17},{9,25},{17,1},{25,9},{2,18},{10... | collective-permute-start | bytes 786440 | tf_op jit(solution)/shard_map/ppermute | solution.py:59
  502.1 12.7 %collective-permute-start.66 = (f32[32,2048]{1,0:T(8,128)S(1)}, f32[32,2048]{1,0:T(8,128)S(1)}, u32[]{:S(2)}, u32[]{:S(2)}) collective-permute-start(f32[32,2048]{1,0:T(8,128)S(1)} %dynamic-slice_add_fusion.3), channel_id=1, source_target_pairs={{0,16},{8,24},{16,0},{24,8},{1,17},{9,25},{17,1},{25,9},{2,18},{10... | collective-permute-start | bytes 786440 | tf_op jit(solution)/shard_map/ppermute | solution.py:61
  515.0 8.8 %collective-permute-start.70 = (f32[32,2048]{1,0:T(8,128)S(1)}, f32[32,2048]{1,0:T(8,128)S(1)}, u32[]{:S(2)}, u32[]{:S(2)}) collective-permute-start(f32[32,2048]{1,0:T(8,128)S(1)} %add.463), channel_id=1, source_target_pairs={{0,16},{8,24},{16,0},{24,8},{1,17},{9,25},{17,1},{25,9},{2,18},{10... | collective-permute-start | bytes 786440 | tf_op jit(solution)/shard_map/ppermute | solution.py:67
  553.7 7.6 %collective-permute-start.74 = (f32[32,2048]{1,0:T(8,128)S(1)}, f32[32,2048]{1,0:T(8,128)S(1)}, u32[]{:S(2)}, u32[]{:S(2)}) collective-permute-start(f32[32,2048]{1,0:T(8,128)S(1)} %constant_dynamic-slice_fusion.3), channel_id=1, source_target_pairs={{0,1},{1,0},{2,3},{3,2},{4,5},{5,4},{6,7},{7,6},{8,9},{9,8},{10,11... | collective-permute-start | bytes 786440 | tf_op jit(solution)/shard_map/ppermute | solution.py:59
  562.3 7.4 %collective-permute-start.80 = (f32[32,1024]{1,0:T(8,128)S(1)}, f32[32,1024]{1,0:T(8,128)S(1)}, u32[]{:S(2)}, u32[]{:S(2)}) collective-permute-start(f32[32,1024]{1,0:T(8,128)S(1)} %constant_dynamic-slice_fusion), channel_id=1, source_target_pairs={{0,1},{1,0},{2,3},{3,2},{4,5},{5,4},{6,7},{7,6},{8,9},{9,8},{10,11... | collective-permute-start | bytes 393224 | tf_op jit(solution)/shard_map/ppermute | solution.py:59
  567.8 8.3 %collective-permute-start.76 = (f32[32,1024]{1,0:T(8,128)S(1)}, f32[32,1024]{1,0:T(8,128)S(1)}, u32[]{:S(2)}, u32[]{:S(2)}) collective-permute-start(f32[32,1024]{1,0:T(8,128)S(1)} %dynamic-slice_add_fusion.17), channel_id=1, source_target_pairs={{0,4},{1,5},{2,6},{3,7},{4,0},{5,1},{6,2},{7,3},{8,12},{9,13},{10,... | collective-permute-start | bytes 393224 | tf_op jit(solution)/shard_map/ppermute | solution.py:61
  569.7 7.9 %collective-permute-start.81 = (f32[32,1024]{1,0:T(8,128)S(1)}, f32[32,1024]{1,0:T(8,128)S(1)}, u32[]{:S(2)}, u32[]{:S(2)}) collective-permute-start(f32[32,1024]{1,0:T(8,128)S(1)} %dynamic-slice_add_fusion.16), channel_id=1, source_target_pairs={{0,4},{1,5},{2,6},{3,7},{4,0},{5,1},{6,2},{7,3},{8,12},{9,13},{10,... | collective-permute-start | bytes 393224 | tf_op jit(solution)/shard_map/ppermute | solution.py:61
  (81 other events, 557.2 us)

commit v20 on v15

--- a/solution.py
+++ b/solution.py
@@ -23,11 +23,12 @@
     count = lax.axis_size(axis)
     if not is_power_of_two(count):
         return lax.psum(value, axis)
+    lanes = jnp.split(value, CHUNKS if axis == "col" else 1, axis=0)
     distance = 1
     while distance < count:
-        value = value + lax.ppermute(value, axis, partner_pairs(count, distance))
+        lanes = [lane + lax.ppermute(lane, axis, partner_pairs(count, distance)) for lane in lanes]
         distance *= 2
-    return value
+    return jnp.concatenate(lanes, axis=0)
 
 
 def big_sum(value, axis):

time: 575 us -> 583 us (1.014)
  starting transfers between devices: 82.8 us -> 127 us
  waiting for transfers between devices: 334 us -> 298 us
    ppermute x22 -> x34, starting transfers between devices: 17 us -> 35.6 us  [small_sum(): lax.ppermute(lane, axis, partner_pairs(count, distance))]
    ppermute x24, waiting for transfers between devices: 42.3 us -> 23.7 us  [big_sum(): lax.ppermute(give, axis, partner_pairs(count, distance))]
    ppermute x24, starting transfers between devices: 14.1 us -> 31.5 us  [big_sum(): lax.ppermute(give, axis, partner_pairs(count, distance))]
    ppermute x22 -> x34, waiting for transfers between devices: 52.2 us -> 39.3 us  [small_sum(): lax.ppermute(lane, axis, partner_pairs(count, distance))]
  transfers between devices with their start and end apart: 88 -> 100, of which waited for: 75 -> 79; matrix products, arithmetic and copies ran while one was open for 3% -> 3% of each run, Pallas kernels for 0% -> 0%
where the time goes in v20:
time: 583 us; the launch traced here: 579 us
  waiting for transfers between devices  298 us (51%)
  starting transfers between devices  127 us (22%)
  matrix products  92.8 us (16%)
  local copies, waits for them, and re-layouts  41.8 us (7%)
  other arithmetic  17.8 us (3%)
    all_to_all x1, waiting for transfers between devices, per_device(): lax.all_to_all(outgoing.reshape(col_count, capacity, block_size, block_si...  129 us
    ppermute x16, waiting for transfers between devices, big_sum(): lax.ppermute(held, axis, partner_pairs(count, last))  66.5 us
    ppermute x34, waiting for transfers between devices, small_sum(): lax.ppermute(lane, axis, partner_pairs(count, distance))  39.3 us
    ppermute x24, waiting for transfers between devices, big_sum(): other = lax.ppermute(held, axis, partner_pairs(count, distance))  39.1 us
    dot_general x8, matrix products, place_terms(): jnp.einsum('ksi,st->kti', weighted, onehot, precision=lax.Precision.HIGH)  37.9 us
    ppermute x34, starting transfers between devices, small_sum(): lax.ppermute(lane, axis, partner_pairs(count, distance))  35.6 us
    dot_general x4, matrix products, forward_terms(): jnp.einsum('sij,ksj->ksi', blocks, picked, preferred_element_type=jnp.flo...  32.6 us
    ppermute x24, starting transfers between devices, big_sum(): lax.ppermute(give, axis, partner_pairs(count, distance))  31.5 us
  transfers between devices with their start and end apart: 100, of which 79 were waited for; matrix products, arithmetic and copies ran while one was open for 3% of the time, Pallas kernels for 0%

profile of v20, /device:TPU:0, one launch (start us, length us, event | category | flops | bytes accessed | tf_op | source)
XLA Modules:
  0.0 579.4 jit_solution(6488506011152620313)
XLA Ops:
  5.5 7.3 %all-to-all-start = ((s32[8,24,2]{1,2,0:T(2,128)}), s32[8,24,2]{1,2,0:T(2,128)S(1)}, u32[]{:S(2)}, u32[]{:S(2)}) async-start(s32[8,24,2]{1,2,0:T(2,128)} %copy.153), calls=%async_computation | async-start | bytes 16384 | tf_op jit(solution)/shard_map/all_to_all | solution.py:129
  14.8 7.9 %gather_fusion.1 = bf16[192,128,128]{2,1,0:T(8,128)(2,1)} fusion(bf16[97,128,128]{2,1,0:T(8,128)(2,1)S(1)} %concatenate.301, s32[1024]{0:T(1024)S(1)} %pad_clamp_fusion.2), kind=kCustom, calls=%fused_computation.9 | custom fusion | bytes 12583680 | tf_op jit(solution)/shard_map/jit(_take)/gather | solution.py:116
  22.8 6.6 %all-to-all-start.1 = ((bf16[8,24,128,128]{3,2,1,0:T(8,128)(2,1)}), bf16[8,24,128,128]{3,2,1,0:T(8,128)(2,1)}, u32[]{:S(2)}, u32[]{:S(2)}) async-start(bf16[8,24,128,128]{3,2,1,0:T(8,128)(2,1)} %bitcast.272), calls=%async_computation.1 | async-start | bytes 12582912 | tf_op jit(solution)/shard_map/all_to_all | solution.py:122
  37.3 129.3 %all-to-all-done.1 = bf16[8,24,128,128]{3,2,1,0:T(8,128)(2,1)} async-done(((bf16[8,24,128,128]{3,2,1,0:T(8,128)(2,1)}), bf16[8,24,128,128]{3,2,1,0:T(8,128)(2,1)}, u32[]{:S(2)}, u32[]{:S(2)}) %all-to-all-start.1) | async-done | bytes 6291488 | tf_op jit(solution)/shard_map/all_to_all | solution.py:122
  166.6 5.6 fusion.48
  172.2 4.7 fusion.80
  181.1 7.0 %collective-permute-done.3 = f32[32,2048]{1,0:T(8,128)S(1)} collective-permute-done((f32[32,2048]{1,0:T(8,128)S(1)}, f32[32,2048]{1,0:T(8,128)S(1)}, u32[]{:S(2)}, u32[]{:S(2)}) %collective-permute-start.3) | collective-permute-done | bytes 262176 | tf_op jit(solution)/shard_map/ppermute | solution.py:58
  188.3 4.7 collective-permute-done.6
  211.2 8.2 %fusion.51 = f32[64,192,128]{2,0,1:T(8,128)S(1)} fusion(bf16[192,128,128]{2,1,0:T(8,128)(2,1)} %bitcast.11, bf16[192,64,128]{2,1,0:T(8,128)(2,1)} %gather_fusion.3, pred[192]{0:T(512)(128)(4,1)S(1)} %get-tuple-element.71), kind=kOutput, calls=%fused_computation.59 | convolution fusion | flops 404226048 | bytes 15728832 | tf_op jit(solution)/shard_map/sij,ksj->ksi/dot_general | solution.py:89
  268.7 5.6 fusion.54
  274.3 4.9 fusion.86
  283.4 7.0 %collective-permute-done.27 = f32[32,2048]{1,0:T(8,128)S(1)} collective-permute-done((f32[32,2048]{1,0:T(8,128)S(1)}, f32[32,2048]{1,0:T(8,128)S(1)}, u32[]{:S(2)}, u32[]{:S(2)}) %collective-permute-start.27) | collective-permute-done | bytes 262176 | tf_op jit(solution)/shard_map/ppermute | solution.py:58
  290.6 4.7 collective-permute-done.30
  315.0 8.1 %fusion.57 = f32[64,192,128]{2,0,1:T(8,128)S(1)} fusion(bf16[192,128,128]{2,1,0:T(8,128)(2,1)} %bitcast.11, bf16[192,64,128]{2,1,0:T(8,128)(2,1)} %gather_fusion.5, pred[192]{0:T(512)(128)(4,1)S(1)} %get-tuple-element.71), kind=kOutput, calls=%fused_computation.61 | convolution fusion | flops 404226048 | bytes 15728832 | tf_op jit(solution)/shard_map/sij,ksj->ksi/dot_general | solution.py:89
  323.0 5.1 fusion.89
  372.1 5.6 fusion.60
  386.6 6.9 %collective-permute-done.51 = f32[32,2048]{1,0:T(8,128)S(1)} collective-permute-done((f32[32,2048]{1,0:T(8,128)S(1)}, f32[32,2048]{1,0:T(8,128)S(1)}, u32[]{:S(2)}, u32[]{:S(2)}) %collective-permute-start.51) | collective-permute-done | bytes 262176 | tf_op jit(solution)/shard_map/ppermute | solution.py:58
  393.7 4.7 collective-permute-done.54
  419.1 8.1 %fusion.63 = f32[64,192,128]{2,0,1:T(8,128)S(1)} fusion(bf16[192,128,128]{2,1,0:T(8,128)(2,1)} %bitcast.11, bf16[192,64,128]{2,1,0:T(8,128)(2,1)} %gather_fusion.7, pred[192]{0:T(512)(128)(4,1)S(1)} %get-tuple-element.71), kind=kOutput, calls=%fused_computation.63 | convolution fusion | flops 404226048 | bytes 15728832 | tf_op jit(solution)/shard_map/sij,ksj->ksi/dot_general | solution.py:89
  476.3 5.6 fusion.66
  481.9 4.7 fusion.98
  490.8 7.0 %collective-permute-done.75 = f32[32,2048]{1,0:T(8,128)S(1)} collective-permute-done((f32[32,2048]{1,0:T(8,128)S(1)}, f32[32,2048]{1,0:T(8,128)S(1)}, u32[]{:S(2)}, u32[]{:S(2)}) %collective-permute-start.75) | collective-permute-done | bytes 262176 | tf_op jit(solution)/shard_map/ppermute | solution.py:58
  498.0 4.7 collective-permute-done.78
  522.0 8.3 %fusion.69 = f32[64,192,128]{2,0,1:T(8,128)S(1)} fusion(bf16[192,128,128]{2,1,0:T(8,128)(2,1)} %bitcast.11, bf16[192,64,128]{2,1,0:T(8,128)(2,1)} %gather_fusion.9, pred[192]{0:T(512)(128)(4,1)S(1)} %get-tuple-element.71), kind=kOutput, calls=%fused_computation.65 | convolution fusion | flops 404226048 | bytes 15728832 | tf_op jit(solution)/shard_map/sij,ksj->ksi/dot_general | solution.py:89
  (453 shorter events, 304.8 us)
Async XLA Ops:
  5.5 17.3 %all-to-all-start = ((s32[8,24,2]{1,2,0:T(2,128)}), s32[8,24,2]{1,2,0:T(2,128)S(1)}, u32[]{:S(2)}, u32[]{:S(2)}) async-start(s32[8,24,2]{1,2,0:T(2,128)} %copy.153), calls=%async_computation | async-start | bytes 16384 | tf_op jit(solution)/shard_map/all_to_all | solution.py:129
  22.8 143.8 %all-to-all-start.1 = ((bf16[8,24,128,128]{3,2,1,0:T(8,128)(2,1)}), bf16[8,24,128,128]{3,2,1,0:T(8,128)(2,1)}, u32[]{:S(2)}, u32[]{:S(2)}) async-start(bf16[8,24,128,128]{3,2,1,0:T(8,128)(2,1)} %bitcast.272), calls=%async_computation.1 | async-start | bytes 12582912 | tf_op jit(solution)/shard_map/all_to_all | solution.py:122
  178.9 9.2 %collective-permute-start.3 = (f32[32,2048]{1,0:T(8,128)S(1)}, f32[32,2048]{1,0:T(8,128)S(1)}, u32[]{:S(2)}, u32[]{:S(2)}) collective-permute-start(f32[32,2048]{1,0:T(8,128)S(1)} %dynamic-slice_add_fusion.15), channel_id=1, source_target_pairs={{0,16},{8,24},{16,0},{24,8},{1,17},{9,25},{17,1},{25,9},{2,18},{10... | collective-permute-start | bytes 786440 | tf_op jit(solution)/shard_map/ppermute | solution.py:58
  180.5 12.5 %collective-permute-start.6 = (f32[32,2048]{1,0:T(8,128)S(1)}, f32[32,2048]{1,0:T(8,128)S(1)}, u32[]{:S(2)}, u32[]{:S(2)}) collective-permute-start(f32[32,2048]{1,0:T(8,128)S(1)} %dynamic-slice_add_fusion.14), channel_id=1, source_target_pairs={{0,16},{8,24},{16,0},{24,8},{1,17},{9,25},{17,1},{25,9},{2,18},{10... | collective-permute-start | bytes 786440 | tf_op jit(solution)/shard_map/ppermute | solution.py:58
  226.2 7.5 %collective-permute-start.19 = (f32[32,2048]{1,0:T(8,128)S(1)}, f32[32,2048]{1,0:T(8,128)S(1)}, u32[]{:S(2)}, u32[]{:S(2)}) collective-permute-start(f32[32,2048]{1,0:T(8,128)S(1)} %constant_dynamic-slice_fusion.19), channel_id=1, source_target_pairs={{0,2},{1,3},{2,0},{3,1},{4,6},{5,7},{6,4},{7,5},{8,10},{9,11},{10,... | collective-permute-start | bytes 786440 | tf_op jit(solution)/shard_map/ppermute | solution.py:56
  233.8 7.1 %collective-permute-start.20 = (f32[32,1024]{1,0:T(8,128)S(1)}, f32[32,1024]{1,0:T(8,128)S(1)}, u32[]{:S(2)}, u32[]{:S(2)}) collective-permute-start(f32[32,1024]{1,0:T(8,128)S(1)} %constant_dynamic-slice_fusion.18), channel_id=1, source_target_pairs={{0,1},{1,0},{2,3},{3,2},{4,5},{5,4},{6,7},{7,6},{8,9},{9,8},{10,11... | collective-permute-start | bytes 393224 | tf_op jit(solution)/shard_map/ppermute | solution.py:56
  240.9 7.5 %collective-permute-start.21 = (f32[32,1024]{1,0:T(8,128)S(1)}, f32[32,1024]{1,0:T(8,128)S(1)}, u32[]{:S(2)}, u32[]{:S(2)}) collective-permute-start(f32[32,1024]{1,0:T(8,128)S(1)} %dynamic-slice_add_fusion.22), channel_id=1, source_target_pairs={{0,4},{1,5},{2,6},{3,7},{4,0},{5,1},{6,2},{7,3},{8,12},{9,13},{10,... | collective-permute-start | bytes 393224 | tf_op jit(solution)/shard_map/ppermute | solution.py:58
  244.0 7.2 %collective-permute-start.17 = (f32[32,1024]{1,0:T(8,128)S(1)}, f32[32,1024]{1,0:T(8,128)S(1)}, u32[]{:S(2)}, u32[]{:S(2)}) collective-permute-start(f32[32,1024]{1,0:T(8,128)S(1)} %add.455), channel_id=1, source_target_pairs={{0,2},{1,3},{2,0},{3,1},{4,6},{5,7},{6,4},{7,5},{8,10},{9,11},{10,... | collective-permute-start | bytes 393224 | tf_op jit(solution)/shard_map/ppermute | solution.py:64
  251.2 7.2 %collective-permute-start.18 = (f32[32,2048]{1,0:T(8,128)S(1)}, f32[32,2048]{1,0:T(8,128)S(1)}, u32[]{:S(2)}, u32[]{:S(2)}) collective-permute-start(f32[32,2048]{1,0:T(8,128)S(1)} %maximum_select_fusion.24), channel_id=1, source_target_pairs={{0,1},{1,0},{2,3},{3,2},{4,5},{5,4},{6,7},{7,6},{8,9},{9,8},{10,11... | collective-permute-start | bytes 786440 | tf_op jit(solution)/shard_map/ppermute | solution.py:64
  281.3 9.2 %collective-permute-start.27 = (f32[32,2048]{1,0:T(8,128)S(1)}, f32[32,2048]{1,0:T(8,128)S(1)}, u32[]{:S(2)}, u32[]{:S(2)}) collective-permute-start(f32[32,2048]{1,0:T(8,128)S(1)} %dynamic-slice_add_fusion.11), channel_id=1, source_target_pairs={{0,16},{8,24},{16,0},{24,8},{1,17},{9,25},{17,1},{25,9},{2,18},{10... | collective-permute-start | bytes 786440 | tf_op jit(solution)/shard_map/ppermute | solution.py:58
  282.8 12.5 %collective-permute-start.30 = (f32[32,2048]{1,0:T(8,128)S(1)}, f32[32,2048]{1,0:T(8,128)S(1)}, u32[]{:S(2)}, u32[]{:S(2)}) collective-permute-start(f32[32,2048]{1,0:T(8,128)S(1)} %dynamic-slice_add_fusion.10), channel_id=1, source_target_pairs={{0,16},{8,24},{16,0},{24,8},{1,17},{9,25},{17,1},{25,9},{2,18},{10... | collective-permute-start | bytes 786440 | tf_op jit(solution)/shard_map/ppermute | solution.py:58
  330.4 8.0 %collective-permute-start.43 = (f32[32,2048]{1,0:T(8,128)S(1)}, f32[32,2048]{1,0:T(8,128)S(1)}, u32[]{:S(2)}, u32[]{:S(2)}) collective-permute-start(f32[32,2048]{1,0:T(8,128)S(1)} %constant_dynamic-slice_fusion.13), channel_id=1, source_target_pairs={{0,2},{1,3},{2,0},{3,1},{4,6},{5,7},{6,4},{7,5},{8,10},{9,11},{10,... | collective-permute-start | bytes 786440 | tf_op jit(solution)/shard_map/ppermute | solution.py:56
  344.6 7.8 %collective-permute-start.45 = (f32[32,1024]{1,0:T(8,128)S(1)}, f32[32,1024]{1,0:T(8,128)S(1)}, u32[]{:S(2)}, u32[]{:S(2)}) collective-permute-start(f32[32,1024]{1,0:T(8,128)S(1)} %dynamic-slice_add_fusion.20), channel_id=1, source_target_pairs={{0,4},{1,5},{2,6},{3,7},{4,0},{5,1},{6,2},{7,3},{8,12},{9,13},{10,... | collective-permute-start | bytes 393224 | tf_op jit(solution)/shard_map/ppermute | solution.py:58
  347.5 7.6 %collective-permute-start.41 = (f32[32,1024]{1,0:T(8,128)S(1)}, f32[32,1024]{1,0:T(8,128)S(1)}, u32[]{:S(2)}, u32[]{:S(2)}) collective-permute-start(f32[32,1024]{1,0:T(8,128)S(1)} %add.480), channel_id=1, source_target_pairs={{0,2},{1,3},{2,0},{3,1},{4,6},{5,7},{6,4},{7,5},{8,10},{9,11},{10,... | collective-permute-start | bytes 393224 | tf_op jit(solution)/shard_map/ppermute | solution.py:64
  384.3 9.2 %collective-permute-start.51 = (f32[32,2048]{1,0:T(8,128)S(1)}, f32[32,2048]{1,0:T(8,128)S(1)}, u32[]{:S(2)}, u32[]{:S(2)}) collective-permute-start(f32[32,2048]{1,0:T(8,128)S(1)} %dynamic-slice_add_fusion.7), channel_id=1, source_target_pairs={{0,16},{8,24},{16,0},{24,8},{1,17},{9,25},{17,1},{25,9},{2,18},{10... | collective-permute-start | bytes 786440 | tf_op jit(solution)/shard_map/ppermute | solution.py:58
  385.9 12.5 %collective-permute-start.54 = (f32[32,2048]{1,0:T(8,128)S(1)}, f32[32,2048]{1,0:T(8,128)S(1)}, u32[]{:S(2)}, u32[]{:S(2)}) collective-permute-start(f32[32,2048]{1,0:T(8,128)S(1)} %dynamic-slice_add_fusion.6), channel_id=1, source_target_pairs={{0,16},{8,24},{16,0},{24,8},{1,17},{9,25},{17,1},{25,9},{2,18},{10... | collective-permute-start | bytes 786440 | tf_op jit(solution)/shard_map/ppermute | solution.py:58
  433.4 8.8 %collective-permute-start.67 = (f32[32,2048]{1,0:T(8,128)S(1)}, f32[32,2048]{1,0:T(8,128)S(1)}, u32[]{:S(2)}, u32[]{:S(2)}) collective-permute-start(f32[32,2048]{1,0:T(8,128)S(1)} %constant_dynamic-slice_fusion.7), channel_id=1, source_target_pairs={{0,2},{1,3},{2,0},{3,1},{4,6},{5,7},{6,4},{7,5},{8,10},{9,11},{10,... | collective-permute-start | bytes 786440 | tf_op jit(solution)/shard_map/ppermute | solution.py:56
  448.7 7.7 %collective-permute-start.69 = (f32[32,1024]{1,0:T(8,128)S(1)}, f32[32,1024]{1,0:T(8,128)S(1)}, u32[]{:S(2)}, u32[]{:S(2)}) collective-permute-start(f32[32,1024]{1,0:T(8,128)S(1)} %dynamic-slice_add_fusion.18), channel_id=1, source_target_pairs={{0,4},{1,5},{2,6},{3,7},{4,0},{5,1},{6,2},{7,3},{8,12},{9,13},{10,... | collective-permute-start | bytes 393224 | tf_op jit(solution)/shard_map/ppermute | solution.py:58
  451.7 7.5 %collective-permute-start.65 = (f32[32,1024]{1,0:T(8,128)S(1)}, f32[32,1024]{1,0:T(8,128)S(1)}, u32[]{:S(2)}, u32[]{:S(2)}) collective-permute-start(f32[32,1024]{1,0:T(8,128)S(1)} %add.502), channel_id=1, source_target_pairs={{0,2},{1,3},{2,0},{3,1},{4,6},{5,7},{6,4},{7,5},{8,10},{9,11},{10,... | collective-permute-start | bytes 393224 | tf_op jit(solution)/shard_map/ppermute | solution.py:64
  488.6 9.2 %collective-permute-start.75 = (f32[32,2048]{1,0:T(8,128)S(1)}, f32[32,2048]{1,0:T(8,128)S(1)}, u32[]{:S(2)}, u32[]{:S(2)}) collective-permute-start(f32[32,2048]{1,0:T(8,128)S(1)} %dynamic-slice_add_fusion.3), channel_id=1, source_target_pairs={{0,16},{8,24},{16,0},{24,8},{1,17},{9,25},{17,1},{25,9},{2,18},{10... | collective-permute-start | bytes 786440 | tf_op jit(solution)/shard_map/ppermute | solution.py:58
  490.2 12.5 %collective-permute-start.78 = (f32[32,2048]{1,0:T(8,128)S(1)}, f32[32,2048]{1,0:T(8,128)S(1)}, u32[]{:S(2)}, u32[]{:S(2)}) collective-permute-start(f32[32,2048]{1,0:T(8,128)S(1)} %dynamic-slice_add_fusion.2), channel_id=1, source_target_pairs={{0,16},{8,24},{16,0},{24,8},{1,17},{9,25},{17,1},{25,9},{2,18},{10... | collective-permute-start | bytes 786440 | tf_op jit(solution)/shard_map/ppermute | solution.py:58
  537.3 7.3 %collective-permute-start.91 = (f32[32,2048]{1,0:T(8,128)S(1)}, f32[32,2048]{1,0:T(8,128)S(1)}, u32[]{:S(2)}, u32[]{:S(2)}) collective-permute-start(f32[32,2048]{1,0:T(8,128)S(1)} %constant_dynamic-slice_fusion.1), channel_id=1, source_target_pairs={{0,2},{1,3},{2,0},{3,1},{4,6},{5,7},{6,4},{7,5},{8,10},{9,11},{10,... | collective-permute-start | bytes 786440 | tf_op jit(solution)/shard_map/ppermute | solution.py:56
  551.2 7.9 %collective-permute-start.93 = (f32[32,1024]{1,0:T(8,128)S(1)}, f32[32,1024]{1,0:T(8,128)S(1)}, u32[]{:S(2)}, u32[]{:S(2)}) collective-permute-start(f32[32,1024]{1,0:T(8,128)S(1)} %dynamic-slice_add_fusion.16), channel_id=1, source_target_pairs={{0,4},{1,5},{2,6},{3,7},{4,0},{5,1},{6,2},{7,3},{8,12},{9,13},{10,... | collective-permute-start | bytes 393224 | tf_op jit(solution)/shard_map/ppermute | solution.py:58
  554.2 7.6 %collective-permute-start.89 = (f32[32,1024]{1,0:T(8,128)S(1)}, f32[32,1024]{1,0:T(8,128)S(1)}, u32[]{:S(2)}, u32[]{:S(2)}) collective-permute-start(f32[32,1024]{1,0:T(8,128)S(1)} %add.524), channel_id=1, source_target_pairs={{0,2},{1,3},{2,0},{3,1},{4,6},{5,7},{6,4},{7,5},{8,10},{9,11},{10,... | collective-permute-start | bytes 393224 | tf_op jit(solution)/shard_map/ppermute | solution.py:64
  (93 other events, 568.8 us)
